TPU v7x, 256 devices: a whole 4x4x8 slice. The times are simulated.
256 devices in a mesh: gx: 16 (over z, y_hi), gy: 16 (over y_lo, x, core).
Axes of the slice: x: 4, y: 4 (y_hi: 2, y_lo: 2; y = y_hi * 2 + y_lo), z: 8, core: 2. Of those that a mesh axis runs over, the one named last changes fastest.
Arguments:
- field: float32 [32, 64, 256, 128], P(None, 'gx', 'gy'), may hold values from -6 to 6
- rates: float32 [32], replicated, may hold values from 0.2 to 1
- mixing: float32 [32, 32], replicated, may hold values from -1 to 1
- secretion: float32 [32, 16, 64, 256], P(None, 'gx', 'gy'), may hold values from -6 to 6
- positions: float32 [3, 16, 64, 256], P(None, 'gx', 'gy'), may hold values from 0 to 256, as said below
- stiffness: float32 [16, 64, 256], P('gx', 'gy'), may hold values from 0.5 to 2
- occupancy: int32 [16, 64, 256], P('gx', 'gy'), may hold values from 0 to 1
- offsets: int32 [16, 64, 256], P('gx', 'gy'), may hold values from 0 to 127
- migrant_state: float32 [8, 560, 2048], P(None, 'gx', 'gy'), may hold values from -6 to 6
- migrant_live: int32 [8, 16, 2048], P(None, 'gx', 'gy'), may hold values 0 or 1
Outputs:
- new_field: float32 [32, 64, 256, 128], P(None, 'gx', 'gy')
- displacement: float32 [3, 16, 64, 256], P(None, 'gx', 'gy')
- arrived: float32 [8, 560, 2048], P(None, 'gx', 'gy')
Inputs may be any that keep to these rules, and one draw needn't show every extreme that they name: `positions`: a slot's coordinates lie inside the box of its bin.
All inputs are finite; a program needn't handle non-finite values. No bound on the sum of `migrant_live` on one device may be relied on, other than what follows from the above.
Results may differ from a plain program's by a relative error of at most 0.0003.
Values sent between devices are 32-bit elements; how exact they have to be, the bound alone decides.
No kernel may reach another device: no remote copies, remote signals or barrier semaphores. Data moves between devices by JAX's collectives and lax.ppermute only.
A program may use at most 64 MiB of HBM per device.

v0:
```python
import jax
import jax.numpy as jnp
from jax import lax
from jax.sharding import PartitionSpec as P

BIN_XY = 4
BIN_Z = 8
SLOTS = 16
SUBSTEPS = 4


time_step = 0.15
move_step = 0.1
spread_sq = 8.0
shifts = ((-1, -1), (-1, 0), (-1, 1), (0, -1), (0, 1), (1, -1), (1, 0), (1, 1))


def padded_2(cells, sides, width):
    for axis, dim in sides:
        count = lax.axis_size(axis)
        ends = count - 1
        head = lax.slice_in_dim(cells, 0, width, axis=dim)
        tail = lax.slice_in_dim(cells, cells.shape[dim] - width, cells.shape[dim], axis=dim)
        cells = jnp.concatenate(
            [
                lax.ppermute(tail, axis, [(i, (i + 1) % count) for i in range(ends)]),
                cells,
                lax.ppermute(head, axis, [((i + 1) % count, i) for i in range(ends)]),
            ],
            axis=dim,
        )
    return cells


def shifted(block, axis, distance):
    devices = range(lax.axis_size(axis))
    route = [(i - distance, i) for i in devices if i - distance in devices]
    return lax.ppermute(block, axis, route)


def advance(padded, source, rates, mixing):
    center = padded[:, 1:-1, 1:-1, :]
    deeper = jnp.pad(center, ((0, 0), (0, 0), (0, 0), (1, 1)))
    beside = padded[:, 2:, 1:-1, :] + padded[:, :-2, 1:-1, :]
    beside = beside + padded[:, 1:-1, 2:, :] + padded[:, 1:-1, :-2, :]
    beside = beside + deeper[:, :, :, 2:] + deeper[:, :, :, :-2]
    laplace = beside - 6.0 * center
    species = center.shape[0]
    mixed = jnp.dot(mixing, center.reshape(species, -1), precision=lax.Precision.HIGHEST).reshape(
        center.shape
    )
    return (
        center
        + time_step * (rates[:, None, None, None] * laplace)
        + time_step * mixed
        + time_step * source
    )


def deposit(secretion, occupancy, offsets):
    species, bins_x, bins_y, lanes = secretion.shape
    layers = lanes // SLOTS
    cells = BIN_XY * BIN_XY * BIN_Z
    count = bins_x * bins_y * layers
    rates_slot = secretion.reshape(species, count, SLOTS)
    place = offsets.reshape(count, SLOTS)
    alive = occupancy.reshape(count, SLOTS).astype(jnp.float32)
    voxel_ids = lax.broadcasted_iota(jnp.int32, (count, SLOTS, cells), 2)
    onehot = (place[:, :, None] == voxel_ids).astype(jnp.float32) * alive[:, :, None]
    filled = jnp.einsum("snk,nkc->snc", rates_slot, onehot, precision=lax.Precision.HIGHEST)
    filled = filled.reshape(species, bins_x, bins_y, layers, BIN_XY, BIN_XY, BIN_Z)
    filled = jnp.transpose(filled, (0, 1, 4, 2, 5, 3, 6))
    return filled.reshape(species, bins_x * BIN_XY, bins_y * BIN_XY, layers * BIN_Z)


def pair_forces(points, padded, occupancy):
    planes, bins_x, bins_y, lanes = points.shape
    layers = lanes // SLOTS
    boxed = padded.reshape(planes, bins_x + 2, bins_y + 2, layers, SLOTS)
    boxed = jnp.pad(boxed, ((0, 0), (0, 0), (0, 0), (1, 1), (0, 0)))
    owned = points.reshape(planes, bins_x, bins_y, layers, SLOTS)[:3, :, :, :, :, None]
    force = jnp.zeros((3, bins_x, bins_y, layers, SLOTS), jnp.float32)
    for offset_x in range(3):
        nearby = jnp.concatenate(
            [
                boxed[
                    :,
                    offset_x : offset_x + bins_x,
                    offset_y : offset_y + bins_y,
                    offset_z : offset_z + layers,
                    :,
                ]
                for offset_y in range(3)
                for offset_z in range(3)
            ],
            axis=-1,
        )
        apart = owned - nearby[:3, :, :, :, None, :]
        strength = nearby[3][:, :, :, None, :] * jnp.exp(
            -jnp.sum(apart * apart, axis=0) / spread_sq
        )
        force = force + jnp.sum(apart * strength[None], axis=-1)
    active = occupancy.reshape(1, bins_x, bins_y, layers, SLOTS).astype(jnp.float32)
    return (move_step * active * force).reshape(3, bins_x, bins_y, lanes)


def on_device(
    field,
    rates,
    mixing,
    secretion,
    positions,
    stiffness,
    occupancy,
    offsets,
    migrant_state,
    migrant_live,
):
    weight = stiffness * occupancy.astype(jnp.float32)
    points = jnp.concatenate([positions, weight[None]], axis=0)
    bordered = padded_2(points, (("gx", 1), ("gy", 2)), 1)
    payload = migrant_state * migrant_live.astype(jnp.float32)
    moving = [payload[index] for index in range(8)]
    for stride in (1, -1):
        picked = [index for index in range(8) if shifts[index][0] == stride]
        landed = shifted(jnp.stack([moving[index] for index in picked]), "gx", stride)
        for place, index in enumerate(picked):
            moving[index] = landed[place]
    for stride in (1, -1):
        picked = [index for index in range(8) if shifts[index][1] == stride]
        landed = shifted(jnp.stack([moving[index] for index in picked]), "gy", stride)
        for place, index in enumerate(picked):
            moving[index] = landed[place]
    arrived = jnp.stack(moving)
    source = deposit(secretion, occupancy, offsets)
    current = field
    for substep in range(SUBSTEPS):
        padded = padded_2(current, (("gx", 1), ("gy", 2)), 1)
        current = advance(padded, source, rates, mixing)
    displacement = pair_forces(points, bordered, occupancy)
    return (current, displacement, arrived)


def solution(mesh):
    return jax.shard_map(
        on_device,
        mesh=mesh,
        in_specs=(
            P(None, "gx", "gy", None),
            P(),
            P(),
            P(None, "gx", "gy", None),
            P(None, "gx", "gy", None),
            P("gx", "gy", None),
            P("gx", "gy", None),
            P("gx", "gy", None),
            P(None, "gx", "gy"),
            P(None, "gx", "gy"),
        ),
        out_specs=(P(None, "gx", "gy", None), P(None, "gx", "gy", None), P(None, "gx", "gy")),
        check_vma=False,
    )
```

profile of v0, /device:TPU:120, one launch (start us, length us, event | category | flops | bytes accessed | tf_op | source)
XLA Modules:
  0.0 177.9 jit_solution(807722046056961635)
XLA Ops:
  2.2 3.1 %collective-permute-start.17 = (f32[4,1,4,256]{3,2,1,0:T(4,128)S(1)}, f32[4,1,4,256]{3,2,1,0:T(4,128)S(1)}, u32[]{:S(2)}, u32[]{:S(2)}) collective-permute-start(f32[4,1,4,256]{3,2,1,0:T(4,128)S(1)} %pad_maximum_fusion.40), channel_id=1, source_target_pairs={{16,0},{32,16},{48,32},{64,48},{80,64},{96,80},{112,96},{128,112},... | collective-permute-start | bytes 49160 | tf_op jit(solution)/shard_map/ppermute | solution.py:28
  5.3 6.3 %collective-permute-start.16 = (f32[4,1,4,256]{3,2,1,0:T(4,128)S(1)}, f32[4,1,4,256]{3,2,1,0:T(4,128)S(1)}, u32[]{:S(2)}, u32[]{:S(2)}) collective-permute-start(f32[4,1,4,256]{3,2,1,0:T(4,128)S(1)} %pad_maximum_fusion.40), channel_id=1, source_target_pairs={{0,16},{16,32},{32,48},{48,64},{64,80},{80,96},{96,112},{112,128},... | collective-permute-start | bytes 49160 | tf_op jit(solution)/shard_map/ppermute | solution.py:26
  14.4 3.6 %collective-permute-start.1 = (f32[32,1,16,128]{3,0,2,1:T(8,128)}, f32[32,1,16,128]{3,0,2,1:T(8,128)}, u32[]{:S(2)}, u32[]{:S(2)}) collective-permute-start(f32[32,1,16,128]{3,0,2,1:T(8,128)} %get-tuple-element.35), channel_id=1, source_target_pairs={{0,16},{16,32},{32,48},{48,64},{64,80},{80,96},{96,112},{112,128},... | collective-permute-start | bytes 786440 | tf_op jit(solution)/shard_map/ppermute | solution.py:26
  18.0 3.7 %collective-permute-start = (f32[32,1,16,128]{3,0,2,1:T(8,128)}, f32[32,1,16,128]{3,0,2,1:T(8,128)}, u32[]{:S(2)}, u32[]{:S(2)}) collective-permute-start(f32[32,1,16,128]{3,0,2,1:T(8,128)} %get-tuple-element.34), channel_id=1, source_target_pairs={{16,0},{32,16},{48,32},{64,48},{80,64},{96,80},{112,96},{128,112},... | collective-permute-start | bytes 786440 | tf_op jit(solution)/shard_map/ppermute | solution.py:28
  22.5 1.9 %collective-permute-start.20 = (f32[3,35,128]{2,1,0:T(8,128)}, f32[3,35,128]{2,1,0:T(8,128)}, u32[]{:S(2)}, u32[]{:S(2)}) collective-permute-start(f32[3,35,128]{2,1,0:T(8,128)} %get-tuple-element.65), channel_id=1, source_target_pairs={{16,0},{32,16},{48,32},{64,48},{80,64},{96,80},{112,96},{128,112},... | collective-permute-start | bytes 161288 | tf_op jit(solution)/shard_map/ppermute | solution.py:38
  24.8 2.2 %fusion.9 = f32[32,64,128]{2,0,1:T(8,128)S(1)} fusion(f32[32,64,16]{0,2,1:T(8,128)S(1)} %bitcast.97, f32[64,16]{1,0:T(8,128)S(1)} %convert_element_type.30, s32[64,16]{1,0:T(8,128)S(1)} %eq.10), kind=kOutput, calls=%fused_computation.45 | convolution fusion | flops 50855936 | bytes 1187840 | tf_op jit(solution)/shard_map/snk,nkc->snc/dot_general | solution.py:70
  27.0 3.2 %collective-permute-start.19 = (f32[4,3,1,256]{3,2,1,0:T(1,128)S(1)}, f32[4,3,1,256]{3,2,1,0:T(1,128)S(1)}, u32[]{:S(2)}, u32[]{:S(2)}) collective-permute-start(f32[4,3,1,256]{3,2,1,0:T(1,128)S(1)} %get-tuple-element.72), channel_id=1, source_target_pairs={{1,0},{2,1},{3,2},{4,3},{5,4},{6,5},{7,6},{8,7},{9,8},{10,9},{11,1... | collective-permute-start | bytes 36872 | tf_op jit(solution)/shard_map/ppermute | solution.py:28
  30.2 1.9 %collective-permute-start.18 = (f32[4,3,1,256]{3,2,1,0:T(1,128)S(1)}, f32[4,3,1,256]{3,2,1,0:T(1,128)S(1)}, u32[]{:S(2)}, u32[]{:S(2)}) collective-permute-start(f32[4,3,1,256]{3,2,1,0:T(1,128)S(1)} %get-tuple-element.71), channel_id=1, source_target_pairs={{0,1},{1,2},{2,3},{3,4},{4,5},{5,6},{6,7},{7,8},{8,9},{9,10},{10,1... | collective-permute-start | bytes 36872 | tf_op jit(solution)/shard_map/ppermute | solution.py:26
  32.8 2.7 %copy.90 = f32[32,64,128]{0,2,1:T(8,128)} copy(f32[32,64,128]{2,0,1:T(8,128)S(1)} %fusion.9) | data formatting | bytes 2097152 | tf_op jit(solution)/shard_map/mul | solution.py:56
  35.5 4.8 %copy.91 = f32[32,1,4,4,4,16,8]{0,6,5,4,3,2,1:T(8,128)} copy(f32[32,1,4,4,4,16,8]{0,6,4,2,5,3,1:T(8,128)} %bitcast.88) | data formatting | bytes 2097152 | tf_op jit(solution)/shard_map/mul | solution.py:56
  40.3 2.9 %copy.92 = f32[32,4,16,128]{3,0,2,1:T(8,128)S(1)} copy(f32[32,4,16,128]{0,3,2,1:T(8,128)} %bitcast.89) | data formatting | bytes 2097152 | tf_op jit(solution)/shard_map/mul | solution.py:56
  45.0 7.9 %collective-permute-start.21 = (f32[3,35,128]{2,1,0:T(8,128)}, f32[3,35,128]{2,1,0:T(8,128)}, u32[]{:S(2)}, u32[]{:S(2)}) collective-permute-start(f32[3,35,128]{2,1,0:T(8,128)} %get-tuple-element.66), channel_id=1, source_target_pairs={{0,16},{16,32},{32,48},{48,64},{64,80},{80,96},{96,112},{112,128},... | collective-permute-start | bytes 161288 | tf_op jit(solution)/shard_map/ppermute | solution.py:38
  62.6 2.0 %fusion.3 = (f32[3,4,16,16]{3,2,1,0:T(8,128)S(1)}, f32[4,16,16,144]{3,2,1,0:T(8,128)S(1)}, f32[3,4,16,16]{3,2,1,0:T(8,128)S(1)}) fusion(f32[4,16,16,144]{3,2,1,0:T(8,128)S(1)} %get-tuple-element.75, f32[3,4,16,16]{3,2,1,0:T(8,128)S(1)} %sub.95, f32[4,16,16,144]{3,2,1,0:T(8,128)S(1)} %get-tuple-element.76, f32[4,1,4,16,144]{4,3,0,2,1:T(8,128)S(1)} %concatenate.107, ...), kind=kLoop, calls=%fused_computation.12 | loop fusion | flops 3827712 | bytes 3399680 | tf_op jit(solution)/shard_map/reduce_sum | solution.py:102
  68.3 4.9 %collective-permute-start.22 = (f32[3,35,128]{2,1,0:T(8,128)S(1)}, f32[3,35,128]{2,1,0:T(8,128)S(1)}, u32[]{:S(2)}, u32[]{:S(2)}) collective-permute-start(f32[3,35,128]{2,1,0:T(8,128)S(1)} %pad_maximum_fusion.38), channel_id=1, source_target_pairs={{1,0},{2,1},{3,2},{4,3},{5,4},{6,5},{7,6},{8,7},{9,8},{10,9},{11,1... | collective-permute-start | bytes 161288 | tf_op jit(solution)/shard_map/ppermute | solution.py:38
  78.3 1.9 %collective-permute-start.3 = (f32[32,6,1,128]{3,0,2,1:T(8,128)S(1)}, f32[32,6,1,128]{3,0,2,1:T(8,128)S(1)}, u32[]{:S(2)}, u32[]{:S(2)}) collective-permute-start(f32[32,6,1,128]{3,0,2,1:T(8,128)S(1)} %get-tuple-element.27), channel_id=1, source_target_pairs={{0,1},{1,2},{2,3},{3,4},{4,5},{5,6},{6,7},{7,8},{8,9},{9,10},{10,1... | collective-permute-start | bytes 294920 | tf_op jit(solution)/shard_map/ppermute | solution.py:26
  80.3 5.8 %collective-permute-start.2 = (f32[32,6,1,128]{3,0,2,1:T(8,128)S(1)}, f32[32,6,1,128]{3,0,2,1:T(8,128)S(1)}, u32[]{:S(2)}, u32[]{:S(2)}) collective-permute-start(f32[32,6,1,128]{3,0,2,1:T(8,128)S(1)} %get-tuple-element.26), channel_id=1, source_target_pairs={{1,0},{2,1},{3,2},{4,3},{5,4},{6,5},{7,6},{8,7},{9,8},{10,9},{11,1... | collective-permute-start | bytes 294920 | tf_op jit(solution)/shard_map/ppermute | solution.py:28
  86.1 2.1 %collective-permute-start.23 = (f32[3,35,128]{2,1,0:T(8,128)S(1)}, f32[3,35,128]{2,1,0:T(8,128)S(1)}, u32[]{:S(2)}, u32[]{:S(2)}) collective-permute-start(f32[3,35,128]{2,1,0:T(8,128)S(1)} %pad_maximum_fusion.39), channel_id=1, source_target_pairs={{0,1},{1,2},{2,3},{3,4},{4,5},{5,6},{6,7},{7,8},{8,9},{9,10},{10,1... | collective-permute-start | bytes 161288 | tf_op jit(solution)/shard_map/ppermute | solution.py:38
  88.3 3.0 %fusion.11 = f32[32,4,16,128]{3,0,2,1:T(8,128)S(1)} fusion(f32[32,4,16,128]{3,0,2,1:T(8,128)S(1)} %copy.92, f32[32,4,16,128]{3,0,2,1:T(8,128)S(1)} %copy-done.3, f32[32,6,16,128]{3,0,2,1:T(8,128)S(1)} %constant_dynamic-update-slice_fusion, f32[32,6,1,128]{3,0,2,1:T(8,128)S(1)} %collective-permute-done.3, f32[32,6,1,128]{3,0,2,1:T(8,128)S(1)} %collective-permute-done.2, ...), kind=kOutput, calls=%fused_computation.48 | convolution fusion | flops 105119744 | bytes 6492288 | tf_op jit(solution)/shard_map/dot_general | solution.py:49
  91.4 1.9 %collective-permute-start.4 = (f32[32,1,16,128]{3,0,2,1:T(8,128)S(1)}, f32[32,1,16,128]{3,0,2,1:T(8,128)S(1)}, u32[]{:S(2)}, u32[]{:S(2)}) collective-permute-start(f32[32,1,16,128]{3,0,2,1:T(8,128)S(1)} %get-tuple-element.33), channel_id=1, source_target_pairs={{16,0},{32,16},{48,32},{64,48},{80,64},{96,80},{112,96},{128,112},... | collective-permute-start | bytes 786440 | tf_op jit(solution)/shard_map/ppermute | solution.py:28
  93.3 7.5 %collective-permute-start.5 = (f32[32,1,16,128]{3,0,2,1:T(8,128)S(1)}, f32[32,1,16,128]{3,0,2,1:T(8,128)S(1)}, u32[]{:S(2)}, u32[]{:S(2)}) collective-permute-start(f32[32,1,16,128]{3,0,2,1:T(8,128)S(1)} %get-tuple-element.32), channel_id=1, source_target_pairs={{0,16},{16,32},{32,48},{48,64},{64,80},{80,96},{96,112},{112,128},... | collective-permute-start | bytes 786440 | tf_op jit(solution)/shard_map/ppermute | solution.py:26
  103.3 3.8 %collective-permute-done.5 = f32[32,1,16,128]{3,0,2,1:T(8,128)S(1)} collective-permute-done((f32[32,1,16,128]{3,0,2,1:T(8,128)S(1)}, f32[32,1,16,128]{3,0,2,1:T(8,128)S(1)}, u32[]{:S(2)}, u32[]{:S(2)}) %collective-permute-start.5) | collective-permute-done | bytes 262176 | tf_op jit(solution)/shard_map/ppermute | solution.py:26
  107.1 1.9 %collective-permute-start.7 = (f32[32,6,1,128]{3,0,2,1:T(8,128)S(1)}, f32[32,6,1,128]{3,0,2,1:T(8,128)S(1)}, u32[]{:S(2)}, u32[]{:S(2)}) collective-permute-start(f32[32,6,1,128]{3,0,2,1:T(8,128)S(1)} %get-tuple-element.25), channel_id=1, source_target_pairs={{0,1},{1,2},{2,3},{3,4},{4,5},{5,6},{6,7},{7,8},{8,9},{9,10},{10,1... | collective-permute-start | bytes 294920 | tf_op jit(solution)/shard_map/ppermute | solution.py:26
  109.1 6.6 %collective-permute-start.6 = (f32[32,6,1,128]{3,0,2,1:T(8,128)S(1)}, f32[32,6,1,128]{3,0,2,1:T(8,128)S(1)}, u32[]{:S(2)}, u32[]{:S(2)}) collective-permute-start(f32[32,6,1,128]{3,0,2,1:T(8,128)S(1)} %get-tuple-element.24), channel_id=1, source_target_pairs={{1,0},{2,1},{3,2},{4,3},{5,4},{6,5},{7,6},{8,7},{9,8},{10,9},{11,1... | collective-permute-start | bytes 294920 | tf_op jit(solution)/shard_map/ppermute | solution.py:28
  119.0 2.3 %collective-permute-start.8 = (f32[32,1,16,128]{3,0,2,1:T(8,128)S(1)}, f32[32,1,16,128]{3,0,2,1:T(8,128)S(1)}, u32[]{:S(2)}, u32[]{:S(2)}) collective-permute-start(f32[32,1,16,128]{3,0,2,1:T(8,128)S(1)} %get-tuple-element.31), channel_id=1, source_target_pairs={{16,0},{32,16},{48,32},{64,48},{80,64},{96,80},{112,96},{128,112},... | collective-permute-start | bytes 786440 | tf_op jit(solution)/shard_map/ppermute | solution.py:28
  121.3 7.1 %collective-permute-start.9 = (f32[32,1,16,128]{3,0,2,1:T(8,128)S(1)}, f32[32,1,16,128]{3,0,2,1:T(8,128)S(1)}, u32[]{:S(2)}, u32[]{:S(2)}) collective-permute-start(f32[32,1,16,128]{3,0,2,1:T(8,128)S(1)} %get-tuple-element.30), channel_id=1, source_target_pairs={{0,16},{16,32},{32,48},{48,64},{64,80},{80,96},{96,112},{112,128},... | collective-permute-start | bytes 786440 | tf_op jit(solution)/shard_map/ppermute | solution.py:26
  129.1 2.0 %collective-permute-done.8 = f32[32,1,16,128]{3,0,2,1:T(8,128)S(1)} collective-permute-done((f32[32,1,16,128]{3,0,2,1:T(8,128)S(1)}, f32[32,1,16,128]{3,0,2,1:T(8,128)S(1)}, u32[]{:S(2)}, u32[]{:S(2)}) %collective-permute-start.8) | collective-permute-done | bytes 262176 | tf_op jit(solution)/shard_map/ppermute | solution.py:28
  131.1 5.3 %collective-permute-done.9 = f32[32,1,16,128]{3,0,2,1:T(8,128)S(1)} collective-permute-done((f32[32,1,16,128]{3,0,2,1:T(8,128)S(1)}, f32[32,1,16,128]{3,0,2,1:T(8,128)S(1)}, u32[]{:S(2)}, u32[]{:S(2)}) %collective-permute-start.9) | collective-permute-done | bytes 262176 | tf_op jit(solution)/shard_map/ppermute | solution.py:26
  138.3 6.1 %collective-permute-start.10 = (f32[32,6,1,128]{3,0,2,1:T(8,128)S(1)}, f32[32,6,1,128]{3,0,2,1:T(8,128)S(1)}, u32[]{:S(2)}, u32[]{:S(2)}) collective-permute-start(f32[32,6,1,128]{3,0,2,1:T(8,128)S(1)} %get-tuple-element.22), channel_id=1, source_target_pairs={{1,0},{2,1},{3,2},{4,3},{5,4},{6,5},{7,6},{8,7},{9,8},{10,9},{11,1... | collective-permute-start | bytes 294920 | tf_op jit(solution)/shard_map/ppermute | solution.py:28
  147.6 2.3 %collective-permute-start.12 = (f32[32,1,16,128]{3,0,2,1:T(8,128)S(1)}, f32[32,1,16,128]{3,0,2,1:T(8,128)S(1)}, u32[]{:S(2)}, u32[]{:S(2)}) collective-permute-start(f32[32,1,16,128]{3,0,2,1:T(8,128)S(1)} %get-tuple-element.29), channel_id=1, source_target_pairs={{16,0},{32,16},{48,32},{64,48},{80,64},{96,80},{112,96},{128,112},... | collective-permute-start | bytes 786440 | tf_op jit(solution)/shard_map/ppermute | solution.py:28
  150.0 7.1 %collective-permute-start.13 = (f32[32,1,16,128]{3,0,2,1:T(8,128)S(1)}, f32[32,1,16,128]{3,0,2,1:T(8,128)S(1)}, u32[]{:S(2)}, u32[]{:S(2)}) collective-permute-start(f32[32,1,16,128]{3,0,2,1:T(8,128)S(1)} %get-tuple-element.28), channel_id=1, source_target_pairs={{0,16},{16,32},{32,48},{48,64},{64,80},{80,96},{96,112},{112,128},... | collective-permute-start | bytes 786440 | tf_op jit(solution)/shard_map/ppermute | solution.py:26
  159.7 5.3 %collective-permute-done.13 = f32[32,1,16,128]{3,0,2,1:T(8,128)S(1)} collective-permute-done((f32[32,1,16,128]{3,0,2,1:T(8,128)S(1)}, f32[32,1,16,128]{3,0,2,1:T(8,128)S(1)}, u32[]{:S(2)}, u32[]{:S(2)}) %collective-permute-start.13) | collective-permute-done | bytes 262176 | tf_op jit(solution)/shard_map/ppermute | solution.py:26
  167.0 6.3 %collective-permute-start.14 = (f32[32,6,1,128]{3,0,2,1:T(8,128)S(1)}, f32[32,6,1,128]{3,0,2,1:T(8,128)S(1)}, u32[]{:S(2)}, u32[]{:S(2)}) collective-permute-start(f32[32,6,1,128]{3,0,2,1:T(8,128)S(1)} %get-tuple-element.20), channel_id=1, source_target_pairs={{1,0},{2,1},{3,2},{4,3},{5,4},{6,5},{7,6},{8,7},{9,8},{10,9},{11,1... | collective-permute-start | bytes 294920 | tf_op jit(solution)/shard_map/ppermute | solution.py:28
  (120 shorter events, 47.1 us)
Async XLA Ops:
  0.6 87.6 %copy-start = (f32[32,32]{1,0:T(8,128)S(1)}, f32[32,32]{1,0:T(8,128)}, u32[]{:S(2)}) copy-start(f32[32,32]{1,0:T(8,128)} %param.12) | copy-start | bytes 12292
  0.6 23.8 %copy-start.9 = (s32[1,4,256]{2,1,0:T(4,128)S(1)}, s32[1,4,256]{2,1,0:T(4,128)}, u32[]{:S(2)}) copy-start(s32[1,4,256]{2,1,0:T(4,128)} %param.16) | copy-start | bytes 12292
  0.7 26.3 %copy-start.6 = (f32[3,1,4,256]{3,2,1,0:T(4,128)S(1)}, f32[3,1,4,256]{3,2,1,0:T(4,128)}, u32[]{:S(2)}) copy-start(f32[3,1,4,256]{3,2,1,0:T(4,128)} %param.14) | copy-start | bytes 36868
  0.7 23.7 %copy-start.8 = (f32[32,1,4,256]{3,2,1,0:T(4,128)S(1)}, f32[32,1,4,256]{3,2,1,0:T(4,128)}, u32[]{:S(2)}) copy-start(f32[32,1,4,256]{3,2,1,0:T(4,128)} %param.13) | copy-start | bytes 393220
  0.7 24.0 %copy-start.11 = (s32[1,4,256]{2,1,0:T(4,128)S(1)}, s32[1,4,256]{2,1,0:T(4,128)}, u32[]{:S(2)}) copy-start(s32[1,4,256]{2,1,0:T(4,128)} %param.17) | copy-start | bytes 12292
  2.2 24.8 %collective-permute-start.17 = (f32[4,1,4,256]{3,2,1,0:T(4,128)S(1)}, f32[4,1,4,256]{3,2,1,0:T(4,128)S(1)}, u32[]{:S(2)}, u32[]{:S(2)}) collective-permute-start(f32[4,1,4,256]{3,2,1,0:T(4,128)S(1)} %pad_maximum_fusion.40), channel_id=1, source_target_pairs={{16,0},{32,16},{48,32},{64,48},{80,64},{96,80},{112,96},{128,112},... | collective-permute-start | bytes 49160 | tf_op jit(solution)/shard_map/ppermute | solution.py:28
  5.3 21.7 %collective-permute-start.16 = (f32[4,1,4,256]{3,2,1,0:T(4,128)S(1)}, f32[4,1,4,256]{3,2,1,0:T(4,128)S(1)}, u32[]{:S(2)}, u32[]{:S(2)}) collective-permute-start(f32[4,1,4,256]{3,2,1,0:T(4,128)S(1)} %pad_maximum_fusion.40), channel_id=1, source_target_pairs={{0,16},{16,32},{32,48},{48,64},{64,80},{80,96},{96,112},{112,128},... | collective-permute-start | bytes 49160 | tf_op jit(solution)/shard_map/ppermute | solution.py:26
  14.4 61.3 %collective-permute-start.1 = (f32[32,1,16,128]{3,0,2,1:T(8,128)}, f32[32,1,16,128]{3,0,2,1:T(8,128)}, u32[]{:S(2)}, u32[]{:S(2)}) collective-permute-start(f32[32,1,16,128]{3,0,2,1:T(8,128)} %get-tuple-element.35), channel_id=1, source_target_pairs={{0,16},{16,32},{32,48},{48,64},{64,80},{80,96},{96,112},{112,128},... | collective-permute-start | bytes 786440 | tf_op jit(solution)/shard_map/ppermute | solution.py:26
  18.0 59.3 %collective-permute-start = (f32[32,1,16,128]{3,0,2,1:T(8,128)}, f32[32,1,16,128]{3,0,2,1:T(8,128)}, u32[]{:S(2)}, u32[]{:S(2)}) collective-permute-start(f32[32,1,16,128]{3,0,2,1:T(8,128)} %get-tuple-element.34), channel_id=1, source_target_pairs={{16,0},{32,16},{48,32},{64,48},{80,64},{96,80},{112,96},{128,112},... | collective-permute-start | bytes 786440 | tf_op jit(solution)/shard_map/ppermute | solution.py:28
  22.5 44.3 %collective-permute-start.20 = (f32[3,35,128]{2,1,0:T(8,128)}, f32[3,35,128]{2,1,0:T(8,128)}, u32[]{:S(2)}, u32[]{:S(2)}) collective-permute-start(f32[3,35,128]{2,1,0:T(8,128)} %get-tuple-element.65), channel_id=1, source_target_pairs={{16,0},{32,16},{48,32},{64,48},{80,64},{96,80},{112,96},{128,112},... | collective-permute-start | bytes 161288 | tf_op jit(solution)/shard_map/ppermute | solution.py:38
  27.0 17.9 %collective-permute-start.19 = (f32[4,3,1,256]{3,2,1,0:T(1,128)S(1)}, f32[4,3,1,256]{3,2,1,0:T(1,128)S(1)}, u32[]{:S(2)}, u32[]{:S(2)}) collective-permute-start(f32[4,3,1,256]{3,2,1,0:T(1,128)S(1)} %get-tuple-element.72), channel_id=1, source_target_pairs={{1,0},{2,1},{3,2},{4,3},{5,4},{6,5},{7,6},{8,7},{9,8},{10,9},{11,1... | collective-permute-start | bytes 36872 | tf_op jit(solution)/shard_map/ppermute | solution.py:28
  30.2 22.6 %collective-permute-start.18 = (f32[4,3,1,256]{3,2,1,0:T(1,128)S(1)}, f32[4,3,1,256]{3,2,1,0:T(1,128)S(1)}, u32[]{:S(2)}, u32[]{:S(2)}) collective-permute-start(f32[4,3,1,256]{3,2,1,0:T(1,128)S(1)} %get-tuple-element.71), channel_id=1, source_target_pairs={{0,1},{1,2},{2,3},{3,4},{4,5},{5,6},{6,7},{7,8},{8,9},{9,10},{10,1... | collective-permute-start | bytes 36872 | tf_op jit(solution)/shard_map/ppermute | solution.py:26
  45.0 21.0 %collective-permute-start.21 = (f32[3,35,128]{2,1,0:T(8,128)}, f32[3,35,128]{2,1,0:T(8,128)}, u32[]{:S(2)}, u32[]{:S(2)}) collective-permute-start(f32[3,35,128]{2,1,0:T(8,128)} %get-tuple-element.66), channel_id=1, source_target_pairs={{0,16},{16,32},{32,48},{48,64},{64,80},{80,96},{96,112},{112,128},... | collective-permute-start | bytes 161288 | tf_op jit(solution)/shard_map/ppermute | solution.py:38
  64.8 23.4 %copy-start.3 = (f32[32,4,16,128]{3,0,2,1:T(8,128)S(1)}, f32[32,4,16,128]{3,0,2,1:T(8,128)}, u32[]{:S(2)}) copy-start(f32[32,4,16,128]{3,0,2,1:T(8,128)} %copy-done.2) | copy-start | bytes 3145732
  64.8 23.4 %copy-start.10 = (f32[32]{0:T(128)S(1)}, f32[32]{0:T(128)}, u32[]{:S(2)}) copy-start(f32[32]{0:T(128)} %param.11) | copy-start | bytes 388
  66.0 22.3 %copy-start.4 = (f32[4,8,64,128]{3,2,1,0:T(8,128)S(1)}, f32[4,8,64,128]{3,2,1,0:T(8,128)}, u32[]{:S(2)}) copy-start(f32[4,8,64,128]{3,2,1,0:T(8,128)} %copy.112) | copy-start | bytes 3145732
  68.3 6.7 %collective-permute-start.22 = (f32[3,35,128]{2,1,0:T(8,128)S(1)}, f32[3,35,128]{2,1,0:T(8,128)S(1)}, u32[]{:S(2)}, u32[]{:S(2)}) collective-permute-start(f32[3,35,128]{2,1,0:T(8,128)S(1)} %pad_maximum_fusion.38), channel_id=1, source_target_pairs={{1,0},{2,1},{3,2},{4,3},{5,4},{6,5},{7,6},{8,7},{9,8},{10,9},{11,1... | collective-permute-start | bytes 161288 | tf_op jit(solution)/shard_map/ppermute | solution.py:38
  78.3 9.9 %collective-permute-start.3 = (f32[32,6,1,128]{3,0,2,1:T(8,128)S(1)}, f32[32,6,1,128]{3,0,2,1:T(8,128)S(1)}, u32[]{:S(2)}, u32[]{:S(2)}) collective-permute-start(f32[32,6,1,128]{3,0,2,1:T(8,128)S(1)} %get-tuple-element.27), channel_id=1, source_target_pairs={{0,1},{1,2},{2,3},{3,4},{4,5},{5,6},{6,7},{7,8},{8,9},{9,10},{10,1... | collective-permute-start | bytes 294920 | tf_op jit(solution)/shard_map/ppermute | solution.py:26
  80.3 8.0 %collective-permute-start.2 = (f32[32,6,1,128]{3,0,2,1:T(8,128)S(1)}, f32[32,6,1,128]{3,0,2,1:T(8,128)S(1)}, u32[]{:S(2)}, u32[]{:S(2)}) collective-permute-start(f32[32,6,1,128]{3,0,2,1:T(8,128)S(1)} %get-tuple-element.26), channel_id=1, source_target_pairs={{1,0},{2,1},{3,2},{4,3},{5,4},{6,5},{7,6},{8,7},{9,8},{10,9},{11,1... | collective-permute-start | bytes 294920 | tf_op jit(solution)/shard_map/ppermute | solution.py:28
  86.1 14.8 %collective-permute-start.23 = (f32[3,35,128]{2,1,0:T(8,128)S(1)}, f32[3,35,128]{2,1,0:T(8,128)S(1)}, u32[]{:S(2)}, u32[]{:S(2)}) collective-permute-start(f32[3,35,128]{2,1,0:T(8,128)S(1)} %pad_maximum_fusion.39), channel_id=1, source_target_pairs={{0,1},{1,2},{2,3},{3,4},{4,5},{5,6},{6,7},{7,8},{8,9},{9,10},{10,1... | collective-permute-start | bytes 161288 | tf_op jit(solution)/shard_map/ppermute | solution.py:38
  91.4 12.0 %collective-permute-start.4 = (f32[32,1,16,128]{3,0,2,1:T(8,128)S(1)}, f32[32,1,16,128]{3,0,2,1:T(8,128)S(1)}, u32[]{:S(2)}, u32[]{:S(2)}) collective-permute-start(f32[32,1,16,128]{3,0,2,1:T(8,128)S(1)} %get-tuple-element.33), channel_id=1, source_target_pairs={{16,0},{32,16},{48,32},{64,48},{80,64},{96,80},{112,96},{128,112},... | collective-permute-start | bytes 786440 | tf_op jit(solution)/shard_map/ppermute | solution.py:28
  93.3 13.8 %collective-permute-start.5 = (f32[32,1,16,128]{3,0,2,1:T(8,128)S(1)}, f32[32,1,16,128]{3,0,2,1:T(8,128)S(1)}, u32[]{:S(2)}, u32[]{:S(2)}) collective-permute-start(f32[32,1,16,128]{3,0,2,1:T(8,128)S(1)} %get-tuple-element.32), channel_id=1, source_target_pairs={{0,16},{16,32},{32,48},{48,64},{64,80},{80,96},{96,112},{112,128},... | collective-permute-start | bytes 786440 | tf_op jit(solution)/shard_map/ppermute | solution.py:26
  107.1 10.4 %collective-permute-start.7 = (f32[32,6,1,128]{3,0,2,1:T(8,128)S(1)}, f32[32,6,1,128]{3,0,2,1:T(8,128)S(1)}, u32[]{:S(2)}, u32[]{:S(2)}) collective-permute-start(f32[32,6,1,128]{3,0,2,1:T(8,128)S(1)} %get-tuple-element.25), channel_id=1, source_target_pairs={{0,1},{1,2},{2,3},{3,4},{4,5},{5,6},{6,7},{7,8},{8,9},{9,10},{10,1... | collective-permute-start | bytes 294920 | tf_op jit(solution)/shard_map/ppermute | solution.py:26
  109.1 8.8 %collective-permute-start.6 = (f32[32,6,1,128]{3,0,2,1:T(8,128)S(1)}, f32[32,6,1,128]{3,0,2,1:T(8,128)S(1)}, u32[]{:S(2)}, u32[]{:S(2)}) collective-permute-start(f32[32,6,1,128]{3,0,2,1:T(8,128)S(1)} %get-tuple-element.24), channel_id=1, source_target_pairs={{1,0},{2,1},{3,2},{4,3},{5,4},{6,5},{7,6},{8,7},{9,8},{10,9},{11,1... | collective-permute-start | bytes 294920 | tf_op jit(solution)/shard_map/ppermute | solution.py:28
  119.0 12.1 %collective-permute-start.8 = (f32[32,1,16,128]{3,0,2,1:T(8,128)S(1)}, f32[32,1,16,128]{3,0,2,1:T(8,128)S(1)}, u32[]{:S(2)}, u32[]{:S(2)}) collective-permute-start(f32[32,1,16,128]{3,0,2,1:T(8,128)S(1)} %get-tuple-element.31), channel_id=1, source_target_pairs={{16,0},{32,16},{48,32},{64,48},{80,64},{96,80},{112,96},{128,112},... | collective-permute-start | bytes 786440 | tf_op jit(solution)/shard_map/ppermute | solution.py:28
  121.3 15.1 %collective-permute-start.9 = (f32[32,1,16,128]{3,0,2,1:T(8,128)S(1)}, f32[32,1,16,128]{3,0,2,1:T(8,128)S(1)}, u32[]{:S(2)}, u32[]{:S(2)}) collective-permute-start(f32[32,1,16,128]{3,0,2,1:T(8,128)S(1)} %get-tuple-element.30), channel_id=1, source_target_pairs={{0,16},{16,32},{32,48},{48,64},{64,80},{80,96},{96,112},{112,128},... | collective-permute-start | bytes 786440 | tf_op jit(solution)/shard_map/ppermute | solution.py:26
  136.4 9.9 %collective-permute-start.11 = (f32[32,6,1,128]{3,0,2,1:T(8,128)S(1)}, f32[32,6,1,128]{3,0,2,1:T(8,128)S(1)}, u32[]{:S(2)}, u32[]{:S(2)}) collective-permute-start(f32[32,6,1,128]{3,0,2,1:T(8,128)S(1)} %get-tuple-element.23), channel_id=1, source_target_pairs={{0,1},{1,2},{2,3},{3,4},{4,5},{5,6},{6,7},{7,8},{8,9},{9,10},{10,1... | collective-permute-start | bytes 294920 | tf_op jit(solution)/shard_map/ppermute | solution.py:26
  138.3 8.3 %collective-permute-start.10 = (f32[32,6,1,128]{3,0,2,1:T(8,128)S(1)}, f32[32,6,1,128]{3,0,2,1:T(8,128)S(1)}, u32[]{:S(2)}, u32[]{:S(2)}) collective-permute-start(f32[32,6,1,128]{3,0,2,1:T(8,128)S(1)} %get-tuple-element.22), channel_id=1, source_target_pairs={{1,0},{2,1},{3,2},{4,3},{5,4},{6,5},{7,6},{8,7},{9,8},{10,9},{11,1... | collective-permute-start | bytes 294920 | tf_op jit(solution)/shard_map/ppermute | solution.py:28
  147.6 12.1 %collective-permute-start.12 = (f32[32,1,16,128]{3,0,2,1:T(8,128)S(1)}, f32[32,1,16,128]{3,0,2,1:T(8,128)S(1)}, u32[]{:S(2)}, u32[]{:S(2)}) collective-permute-start(f32[32,1,16,128]{3,0,2,1:T(8,128)S(1)} %get-tuple-element.29), channel_id=1, source_target_pairs={{16,0},{32,16},{48,32},{64,48},{80,64},{96,80},{112,96},{128,112},... | collective-permute-start | bytes 786440 | tf_op jit(solution)/shard_map/ppermute | solution.py:28
  150.0 15.1 %collective-permute-start.13 = (f32[32,1,16,128]{3,0,2,1:T(8,128)S(1)}, f32[32,1,16,128]{3,0,2,1:T(8,128)S(1)}, u32[]{:S(2)}, u32[]{:S(2)}) collective-permute-start(f32[32,1,16,128]{3,0,2,1:T(8,128)S(1)} %get-tuple-element.28), channel_id=1, source_target_pairs={{0,16},{16,32},{32,48},{48,64},{64,80},{80,96},{96,112},{112,128},... | collective-permute-start | bytes 786440 | tf_op jit(solution)/shard_map/ppermute | solution.py:26
  165.1 10.1 %collective-permute-start.15 = (f32[32,6,1,128]{3,0,2,1:T(8,128)S(1)}, f32[32,6,1,128]{3,0,2,1:T(8,128)S(1)}, u32[]{:S(2)}, u32[]{:S(2)}) collective-permute-start(f32[32,6,1,128]{3,0,2,1:T(8,128)S(1)} %get-tuple-element.21), channel_id=1, source_target_pairs={{0,1},{1,2},{2,3},{3,4},{4,5},{5,6},{6,7},{7,8},{8,9},{9,10},{10,1... | collective-permute-start | bytes 294920 | tf_op jit(solution)/shard_map/ppermute | solution.py:26
  167.0 8.3 %collective-permute-start.14 = (f32[32,6,1,128]{3,0,2,1:T(8,128)S(1)}, f32[32,6,1,128]{3,0,2,1:T(8,128)S(1)}, u32[]{:S(2)}, u32[]{:S(2)}) collective-permute-start(f32[32,6,1,128]{3,0,2,1:T(8,128)S(1)} %get-tuple-element.20), channel_id=1, source_target_pairs={{1,0},{2,1},{3,2},{4,3},{5,4},{6,5},{7,6},{8,7},{9,8},{10,9},{11,1... | collective-permute-start | bytes 294920 | tf_op jit(solution)/shard_map/ppermute | solution.py:28
  (5 other events, 59.3 us)
where the time goes:
time: 181 us; the launch traced here: 178 us
  starting transfers between devices  99.3 us (55%)
  local copies, waits for them, and re-layouts  35.1 us (19%)
  waiting for transfers between devices  20.9 us (12%)
  other arithmetic  11 us (6%)
  matrix products  10.2 us (6%)
    ppermute x10, starting transfers between devices, padded_2(): lax.ppermute(head, axis, [((i + 1) % count, i) for i in range(ends)])  41.3 us
    ppermute x10, starting transfers between devices, padded_2(): lax.ppermute(tail, axis, [(i, (i + 1) % count) for i in range(ends)])  41.3 us
    ppermute x4, starting transfers between devices, shifted(): return lax.ppermute(block, axis, route)  16.7 us
    ppermute x10, waiting for transfers between devices, padded_2(): lax.ppermute(tail, axis, [(i, (i + 1) % count) for i in range(ends)])  14.5 us
    mul x3, local copies, waits for them, and re-layouts, advance(): time_step * source  10.3 us
    unnamed x43, local copies, waits for them, and re-layouts  9.05 us
    dot_general x4, matrix products, advance(): jnp.dot(mixing, center.reshape(species, -1), precision=lax.Precision.HIGH...  8.06 us
    ppermute x10, waiting for transfers between devices, padded_2(): lax.ppermute(head, axis, [((i + 1) % count, i) for i in range(ends)])  5.18 us
  transfers between devices with their start and end apart: 24, of which 11 were waited for; matrix products, arithmetic and copies ran while one was open for 27% of the time, Pallas kernels for 0%

commit v1 on v0

--- a/solution.py
+++ b/solution.py
@@ -30,6 +30,32 @@
             axis=dim,
         )
     return cells
+
+
+def halos(cells, axis, dim):
+    count = lax.axis_size(axis)
+    ends = count - 1
+    head = lax.slice_in_dim(cells, 0, 1, axis=dim)
+    tail = lax.slice_in_dim(cells, cells.shape[dim] - 1, cells.shape[dim], axis=dim)
+    low = lax.ppermute(tail, axis, [(i, (i + 1) % count) for i in range(ends)])
+    high = lax.ppermute(head, axis, [((i + 1) % count, i) for i in range(ends)])
+    return low, high
+
+
+def framed(cells, x_low, x_high, y_low, y_high):
+    species, width, depth, lanes = cells.shape
+    corner = jnp.zeros((species, 1, 1, lanes), cells.dtype)
+    middle = jnp.concatenate([x_low, cells, x_high], axis=1)
+    left = jnp.concatenate([corner, y_low, corner], axis=1)
+    right = jnp.concatenate([corner, y_high, corner], axis=1)
+    return jnp.concatenate([left, middle, right], axis=2)
+
+
+def substep(current, source, rates, mixing):
+    x_low, x_high = halos(current, "gx", 1)
+    y_low, y_high = halos(current, "gy", 2)
+    padded = framed(current, x_low, x_high, y_low, y_high)
+    return advance(padded, source, rates, mixing)
 
 
 def shifted(block, axis, distance):
@@ -134,9 +160,8 @@
     arrived = jnp.stack(moving)
     source = deposit(secretion, occupancy, offsets)
     current = field
-    for substep in range(SUBSTEPS):
-        padded = padded_2(current, (("gx", 1), ("gy", 2)), 1)
-        current = advance(padded, source, rates, mixing)
+    for _ in range(SUBSTEPS):
+        current = substep(current, source, rates, mixing)
     displacement = pair_forces(points, bordered, occupancy)
     return (current, displacement, arrived)
 

time: 181 us -> 169 us (0.934)
  waiting for transfers between devices: 20.9 us -> 13.8 us
  starting transfers between devices: 99.3 us -> 95.9 us
    ppermute x0 -> x16, starting transfers between devices: none -> 67 us  [the longest x8 33.9 us: halos(): low = lax.ppermute(tail, axis, [(i, (i + 1) % count) for i in range(ends)])]
    ppermute x10 -> x2, starting transfers between devices: 41.3 us -> 8.23 us  [padded_2(): lax.ppermute(tail, axis, [(i, (i + 1) % count) for i in range(ends)])]
    ppermute x10 -> x2, starting transfers between devices: 41.3 us -> 9.01 us  [padded_2(): lax.ppermute(head, axis, [((i + 1) % count, i) for i in range(ends)])]
    ppermute x10 -> x2, waiting for transfers between devices: 14.5 us -> 0.01 us  [padded_2(): lax.ppermute(tail, axis, [(i, (i + 1) % count) for i in range(ends)])]
    ppermute x4, waiting for transfers between devices: 1.25 us -> 13.7 us  [shifted(): return lax.ppermute(block, axis, route)]
    ppermute x10 -> x2, waiting for transfers between devices: 5.18 us -> 0.01 us  [padded_2(): lax.ppermute(head, axis, [((i + 1) % count, i) for i in range(ends)])]
    ppermute x4, starting transfers between devices: 16.7 us -> 11.7 us  [shifted(): return lax.ppermute(block, axis, route)]
    unnamed x43 -> x47, local copies, waits for them, and re-layouts: 9.05 us -> 9.06 us
  transfers between devices with their start and end apart: 24 -> 24, of which waited for: 11 -> 3; matrix products, arithmetic and copies ran while one was open for 27% -> 27% of each run, Pallas kernels for 0% -> 0%
where the time goes in v1:
time: 169 us; the launch traced here: 167 us
  starting transfers between devices  95.9 us (57%)
  local copies, waits for them, and re-layouts  34.3 us (20%)
  waiting for transfers between devices  13.8 us (8%)
  other arithmetic  11.3 us (7%)
  matrix products  10.3 us (6%)
    ppermute x8, starting transfers between devices, halos(): low = lax.ppermute(tail, axis, [(i, (i + 1) % count) for i in range(ends)])  33.9 us
    ppermute x8, starting transfers between devices, halos(): high = lax.ppermute(head, axis, [((i + 1) % count, i) for i in range(ends)])  33.1 us
    ppermute x4, waiting for transfers between devices, shifted(): return lax.ppermute(block, axis, route)  13.7 us
    ppermute x4, starting transfers between devices, shifted(): return lax.ppermute(block, axis, route)  11.7 us
    mul x3, local copies, waits for them, and re-layouts, advance(): time_step * source  10.3 us
    unnamed x47, local copies, waits for them, and re-layouts  9.06 us
    ppermute x2, starting transfers between devices, padded_2(): lax.ppermute(head, axis, [((i + 1) % count, i) for i in range(ends)])  9.01 us
    ppermute x2, starting transfers between devices, padded_2(): lax.ppermute(tail, axis, [(i, (i + 1) % count) for i in range(ends)])  8.23 us
  transfers between devices with their start and end apart: 24, of which 3 were waited for; matrix products, arithmetic and copies ran while one was open for 27% of the time, Pallas kernels for 0%

profile of v1, /device:TPU:120, one launch (start us, length us, event | category | flops | bytes accessed | tf_op | source)
XLA Modules:
  0.0 167.1 jit_solution(13157633059957385115)
XLA Ops:
  2.2 3.3 %collective-permute-start.17 = (f32[4,1,4,256]{3,2,1,0:T(4,128)S(1)}, f32[4,1,4,256]{3,2,1,0:T(4,128)S(1)}, u32[]{:S(2)}, u32[]{:S(2)}) collective-permute-start(f32[4,1,4,256]{3,2,1,0:T(4,128)S(1)} %pad_maximum_fusion.39), channel_id=1, source_target_pairs={{16,0},{32,16},{48,32},{64,48},{80,64},{96,80},{112,96},{128,112},... | collective-permute-start | bytes 49160 | tf_op jit(solution)/shard_map/ppermute | solution.py:28
  5.5 6.3 %collective-permute-start.16 = (f32[4,1,4,256]{3,2,1,0:T(4,128)S(1)}, f32[4,1,4,256]{3,2,1,0:T(4,128)S(1)}, u32[]{:S(2)}, u32[]{:S(2)}) collective-permute-start(f32[4,1,4,256]{3,2,1,0:T(4,128)S(1)} %pad_maximum_fusion.39), channel_id=1, source_target_pairs={{0,16},{16,32},{32,48},{48,64},{64,80},{80,96},{96,112},{112,128},... | collective-permute-start | bytes 49160 | tf_op jit(solution)/shard_map/ppermute | solution.py:26
  14.6 3.6 %collective-permute-start.1 = (f32[32,1,16,128]{3,0,2,1:T(8,128)}, f32[32,1,16,128]{3,0,2,1:T(8,128)}, u32[]{:S(2)}, u32[]{:S(2)}) collective-permute-start(f32[32,1,16,128]{3,0,2,1:T(8,128)} %get-tuple-element.35), channel_id=1, source_target_pairs={{0,16},{16,32},{32,48},{48,64},{64,80},{80,96},{96,112},{112,128},... | collective-permute-start | bytes 786440 | tf_op jit(solution)/shard_map/ppermute | solution.py:40
  18.1 3.7 %collective-permute-start = (f32[32,1,16,128]{3,0,2,1:T(8,128)}, f32[32,1,16,128]{3,0,2,1:T(8,128)}, u32[]{:S(2)}, u32[]{:S(2)}) collective-permute-start(f32[32,1,16,128]{3,0,2,1:T(8,128)} %get-tuple-element.34), channel_id=1, source_target_pairs={{16,0},{32,16},{48,32},{64,48},{80,64},{96,80},{112,96},{128,112},... | collective-permute-start | bytes 786440 | tf_op jit(solution)/shard_map/ppermute | solution.py:41
  22.6 1.9 %collective-permute-start.3 = (f32[32,4,1,128]{3,0,2,1:T(8,128)}, f32[32,4,1,128]{3,0,2,1:T(8,128)}, u32[]{:S(2)}, u32[]{:S(2)}) collective-permute-start(f32[32,4,1,128]{3,0,2,1:T(8,128)} %get-tuple-element.33), channel_id=1, source_target_pairs={{0,1},{1,2},{2,3},{3,4},{4,5},{5,6},{6,7},{7,8},{8,9},{9,10},{10,1... | collective-permute-start | bytes 196616 | tf_op jit(solution)/shard_map/ppermute | solution.py:40
  25.0 2.1 %fusion.9 = f32[32,64,128]{2,0,1:T(8,128)S(1)} fusion(f32[32,64,16]{0,2,1:T(8,128)S(1)} %bitcast.97, f32[64,16]{1,0:T(8,128)S(1)} %convert_element_type.30, s32[64,16]{1,0:T(8,128)S(1)} %eq.10), kind=kOutput, calls=%fused_computation.61 | convolution fusion | flops 50855936 | bytes 1187840 | tf_op jit(solution)/shard_map/snk,nkc->snc/dot_general | solution.py:96
  27.8 5.8 %collective-permute-start.19 = (f32[4,3,1,256]{3,2,1,0:T(1,128)S(1)}, f32[4,3,1,256]{3,2,1,0:T(1,128)S(1)}, u32[]{:S(2)}, u32[]{:S(2)}) collective-permute-start(f32[4,3,1,256]{3,2,1,0:T(1,128)S(1)} %get-tuple-element.72), channel_id=1, source_target_pairs={{1,0},{2,1},{3,2},{4,3},{5,4},{6,5},{7,6},{8,7},{9,8},{10,9},{11,1... | collective-permute-start | bytes 36872 | tf_op jit(solution)/shard_map/ppermute | solution.py:28
  33.6 1.9 %collective-permute-start.18 = (f32[4,3,1,256]{3,2,1,0:T(1,128)S(1)}, f32[4,3,1,256]{3,2,1,0:T(1,128)S(1)}, u32[]{:S(2)}, u32[]{:S(2)}) collective-permute-start(f32[4,3,1,256]{3,2,1,0:T(1,128)S(1)} %get-tuple-element.71), channel_id=1, source_target_pairs={{0,1},{1,2},{2,3},{3,4},{4,5},{5,6},{6,7},{7,8},{8,9},{9,10},{10,1... | collective-permute-start | bytes 36872 | tf_op jit(solution)/shard_map/ppermute | solution.py:26
  36.2 2.7 %copy.98 = f32[32,64,128]{0,2,1:T(8,128)} copy(f32[32,64,128]{2,0,1:T(8,128)S(1)} %fusion.9) | data formatting | bytes 2097152 | tf_op jit(solution)/shard_map/mul | solution.py:82
  38.9 4.8 %copy.99 = f32[32,1,4,4,4,16,8]{0,6,5,4,3,2,1:T(8,128)} copy(f32[32,1,4,4,4,16,8]{0,6,4,2,5,3,1:T(8,128)} %bitcast.88) | data formatting | bytes 2097152 | tf_op jit(solution)/shard_map/mul | solution.py:82
  43.7 2.9 %copy.100 = f32[32,4,16,128]{3,0,2,1:T(8,128)S(1)} copy(f32[32,4,16,128]{0,3,2,1:T(8,128)} %bitcast.89) | data formatting | bytes 2097152 | tf_op jit(solution)/shard_map/mul | solution.py:82
  48.4 5.7 %collective-permute-start.2 = (f32[32,4,1,128]{3,0,2,1:T(8,128)}, f32[32,4,1,128]{3,0,2,1:T(8,128)}, u32[]{:S(2)}, u32[]{:S(2)}) collective-permute-start(f32[32,4,1,128]{3,0,2,1:T(8,128)} %get-tuple-element.32), channel_id=1, source_target_pairs={{1,0},{2,1},{3,2},{4,3},{5,4},{6,5},{7,6},{8,7},{9,8},{10,9},{11,1... | collective-permute-start | bytes 196616 | tf_op jit(solution)/shard_map/ppermute | solution.py:41
  54.1 5.7 %collective-permute-start.21 = (f32[3,35,128]{2,1,0:T(8,128)}, f32[3,35,128]{2,1,0:T(8,128)}, u32[]{:S(2)}, u32[]{:S(2)}) collective-permute-start(f32[3,35,128]{2,1,0:T(8,128)} %get-tuple-element.66), channel_id=1, source_target_pairs={{0,16},{16,32},{32,48},{48,64},{64,80},{80,96},{96,112},{112,128},... | collective-permute-start | bytes 161288 | tf_op jit(solution)/shard_map/ppermute | solution.py:64
  69.7 2.0 %fusion.3 = (f32[3,4,16,16]{3,2,1,0:T(8,128)S(1)}, f32[4,16,16,144]{3,2,1,0:T(8,128)S(1)}, f32[3,4,16,16]{3,2,1,0:T(8,128)S(1)}) fusion(f32[4,16,16,144]{3,2,1,0:T(8,128)S(1)} %get-tuple-element.75, f32[3,4,16,16]{3,2,1,0:T(8,128)S(1)} %sub.95, f32[4,16,16,144]{3,2,1,0:T(8,128)S(1)} %get-tuple-element.76, f32[4,1,4,16,144]{4,3,0,2,1:T(8,128)S(1)} %concatenate.139, ...), kind=kLoop, calls=%fused_computation.12 | loop fusion | flops 3827712 | bytes 3399680 | tf_op jit(solution)/shard_map/reduce_sum | solution.py:128
  72.9 1.9 %collective-permute-start.20 = (f32[3,35,128]{2,1,0:T(8,128)S(1)}, f32[3,35,128]{2,1,0:T(8,128)S(1)}, u32[]{:S(2)}, u32[]{:S(2)}) collective-permute-start(f32[3,35,128]{2,1,0:T(8,128)S(1)} %copy-done.10), channel_id=1, source_target_pairs={{16,0},{32,16},{48,32},{64,48},{80,64},{96,80},{112,96},{128,112},... | collective-permute-start | bytes 161288 | tf_op jit(solution)/shard_map/ppermute | solution.py:64
  75.6 7.0 %collective-permute-done.20 = f32[3,35,128]{2,1,0:T(8,128)S(1)} collective-permute-done((f32[3,35,128]{2,1,0:T(8,128)S(1)}, f32[3,35,128]{2,1,0:T(8,128)S(1)}, u32[]{:S(2)}, u32[]{:S(2)}) %collective-permute-start.20) | collective-permute-done | bytes 53792 | tf_op jit(solution)/shard_map/ppermute | solution.py:64
  82.6 1.9 %collective-permute-start.22 = (f32[3,35,128]{2,1,0:T(8,128)S(1)}, f32[3,35,128]{2,1,0:T(8,128)S(1)}, u32[]{:S(2)}, u32[]{:S(2)}) collective-permute-start(f32[3,35,128]{2,1,0:T(8,128)S(1)} %pad_maximum_fusion.37), channel_id=1, source_target_pairs={{1,0},{2,1},{3,2},{4,3},{5,4},{6,5},{7,6},{8,7},{9,8},{10,9},{11,1... | collective-permute-start | bytes 161288 | tf_op jit(solution)/shard_map/ppermute | solution.py:64
  86.4 2.1 %collective-permute-start.23 = (f32[3,35,128]{2,1,0:T(8,128)S(1)}, f32[3,35,128]{2,1,0:T(8,128)S(1)}, u32[]{:S(2)}, u32[]{:S(2)}) collective-permute-start(f32[3,35,128]{2,1,0:T(8,128)S(1)} %pad_maximum_fusion.38), channel_id=1, source_target_pairs={{0,1},{1,2},{2,3},{3,4},{4,5},{5,6},{6,7},{7,8},{8,9},{9,10},{10,1... | collective-permute-start | bytes 161288 | tf_op jit(solution)/shard_map/ppermute | solution.py:64
  89.1 5.0 %collective-permute-done.23 = f32[3,35,128]{2,1,0:T(8,128)S(1)} collective-permute-done((f32[3,35,128]{2,1,0:T(8,128)S(1)}, f32[3,35,128]{2,1,0:T(8,128)S(1)}, u32[]{:S(2)}, u32[]{:S(2)}) %collective-permute-start.23) | collective-permute-done | bytes 53792 | tf_op jit(solution)/shard_map/ppermute | solution.py:64
  98.2 3.2 %fusion.11 = f32[32,4,16,128]{3,0,2,1:T(8,128)S(1)} fusion(f32[32,4,16,128]{3,0,2,1:T(8,128)S(1)} %copy.100, f32[32,4,16,128]{3,0,2,1:T(8,128)S(1)} %copy-done.3, f32[32,1,1,128]{3,0,2,1:T(8,128)S(1)} %broadcast.209, f32[32,6,16,128]{3,0,2,1:T(8,128)S(1)} %constant_dynamic-update-slice_fusion, f32[32,4,1,128]{3,0,2,1:T(8,128)} %collective-permute-done.3, ...), kind=kOutput, calls=%fused_computation.64 | convolution fusion | flops 106168320 | bytes 6443136 | tf_op jit(solution)/shard_map/dot_general | solution.py:75
  101.4 1.9 %collective-permute-start.4 = (f32[32,1,16,128]{3,0,2,1:T(8,128)S(1)}, f32[32,1,16,128]{3,0,2,1:T(8,128)S(1)}, u32[]{:S(2)}, u32[]{:S(2)}) collective-permute-start(f32[32,1,16,128]{3,0,2,1:T(8,128)S(1)} %get-tuple-element.31), channel_id=1, source_target_pairs={{16,0},{32,16},{48,32},{64,48},{80,64},{96,80},{112,96},{128,112},... | collective-permute-start | bytes 786440 | tf_op jit(solution)/shard_map/ppermute | solution.py:41
  103.3 7.5 %collective-permute-start.5 = (f32[32,1,16,128]{3,0,2,1:T(8,128)S(1)}, f32[32,1,16,128]{3,0,2,1:T(8,128)S(1)}, u32[]{:S(2)}, u32[]{:S(2)}) collective-permute-start(f32[32,1,16,128]{3,0,2,1:T(8,128)S(1)} %get-tuple-element.30), channel_id=1, source_target_pairs={{0,16},{16,32},{32,48},{48,64},{64,80},{80,96},{96,112},{112,128},... | collective-permute-start | bytes 786440 | tf_op jit(solution)/shard_map/ppermute | solution.py:40
  111.5 1.9 %collective-permute-start.7 = (f32[32,4,1,128]{3,0,2,1:T(8,128)S(1)}, f32[32,4,1,128]{3,0,2,1:T(8,128)S(1)}, u32[]{:S(2)}, u32[]{:S(2)}) collective-permute-start(f32[32,4,1,128]{3,0,2,1:T(8,128)S(1)} %get-tuple-element.29), channel_id=1, source_target_pairs={{0,1},{1,2},{2,3},{3,4},{4,5},{5,6},{6,7},{7,8},{8,9},{9,10},{10,1... | collective-permute-start | bytes 196616 | tf_op jit(solution)/shard_map/ppermute | solution.py:40
  113.5 5.8 %collective-permute-start.6 = (f32[32,4,1,128]{3,0,2,1:T(8,128)S(1)}, f32[32,4,1,128]{3,0,2,1:T(8,128)S(1)}, u32[]{:S(2)}, u32[]{:S(2)}) collective-permute-start(f32[32,4,1,128]{3,0,2,1:T(8,128)S(1)} %get-tuple-element.28), channel_id=1, source_target_pairs={{1,0},{2,1},{3,2},{4,3},{5,4},{6,5},{7,6},{8,7},{9,8},{10,9},{11,1... | collective-permute-start | bytes 196616 | tf_op jit(solution)/shard_map/ppermute | solution.py:41
  122.6 1.9 %collective-permute-start.8 = (f32[32,1,16,128]{3,0,2,1:T(8,128)S(1)}, f32[32,1,16,128]{3,0,2,1:T(8,128)S(1)}, u32[]{:S(2)}, u32[]{:S(2)}) collective-permute-start(f32[32,1,16,128]{3,0,2,1:T(8,128)S(1)} %get-tuple-element.27), channel_id=1, source_target_pairs={{16,0},{32,16},{48,32},{64,48},{80,64},{96,80},{112,96},{128,112},... | collective-permute-start | bytes 786440 | tf_op jit(solution)/shard_map/ppermute | solution.py:41
  124.5 7.5 %collective-permute-start.9 = (f32[32,1,16,128]{3,0,2,1:T(8,128)S(1)}, f32[32,1,16,128]{3,0,2,1:T(8,128)S(1)}, u32[]{:S(2)}, u32[]{:S(2)}) collective-permute-start(f32[32,1,16,128]{3,0,2,1:T(8,128)S(1)} %get-tuple-element.26), channel_id=1, source_target_pairs={{0,16},{16,32},{32,48},{48,64},{64,80},{80,96},{96,112},{112,128},... | collective-permute-start | bytes 786440 | tf_op jit(solution)/shard_map/ppermute | solution.py:40
  132.7 1.9 %collective-permute-start.11 = (f32[32,4,1,128]{3,0,2,1:T(8,128)S(1)}, f32[32,4,1,128]{3,0,2,1:T(8,128)S(1)}, u32[]{:S(2)}, u32[]{:S(2)}) collective-permute-start(f32[32,4,1,128]{3,0,2,1:T(8,128)S(1)} %get-tuple-element.25), channel_id=1, source_target_pairs={{0,1},{1,2},{2,3},{3,4},{4,5},{5,6},{6,7},{7,8},{8,9},{9,10},{10,1... | collective-permute-start | bytes 196616 | tf_op jit(solution)/shard_map/ppermute | solution.py:40
  134.6 5.9 %collective-permute-start.10 = (f32[32,4,1,128]{3,0,2,1:T(8,128)S(1)}, f32[32,4,1,128]{3,0,2,1:T(8,128)S(1)}, u32[]{:S(2)}, u32[]{:S(2)}) collective-permute-start(f32[32,4,1,128]{3,0,2,1:T(8,128)S(1)} %get-tuple-element.24), channel_id=1, source_target_pairs={{1,0},{2,1},{3,2},{4,3},{5,4},{6,5},{7,6},{8,7},{9,8},{10,9},{11,1... | collective-permute-start | bytes 196616 | tf_op jit(solution)/shard_map/ppermute | solution.py:41
  144.0 1.9 %collective-permute-start.12 = (f32[32,1,16,128]{3,0,2,1:T(8,128)S(1)}, f32[32,1,16,128]{3,0,2,1:T(8,128)S(1)}, u32[]{:S(2)}, u32[]{:S(2)}) collective-permute-start(f32[32,1,16,128]{3,0,2,1:T(8,128)S(1)} %get-tuple-element.23), channel_id=1, source_target_pairs={{16,0},{32,16},{48,32},{64,48},{80,64},{96,80},{112,96},{128,112},... | collective-permute-start | bytes 786440 | tf_op jit(solution)/shard_map/ppermute | solution.py:41
  145.9 7.5 %collective-permute-start.13 = (f32[32,1,16,128]{3,0,2,1:T(8,128)S(1)}, f32[32,1,16,128]{3,0,2,1:T(8,128)S(1)}, u32[]{:S(2)}, u32[]{:S(2)}) collective-permute-start(f32[32,1,16,128]{3,0,2,1:T(8,128)S(1)} %get-tuple-element.22), channel_id=1, source_target_pairs={{0,16},{16,32},{32,48},{48,64},{64,80},{80,96},{96,112},{112,128},... | collective-permute-start | bytes 786440 | tf_op jit(solution)/shard_map/ppermute | solution.py:40
  154.1 1.9 %collective-permute-start.15 = (f32[32,4,1,128]{3,0,2,1:T(8,128)S(1)}, f32[32,4,1,128]{3,0,2,1:T(8,128)S(1)}, u32[]{:S(2)}, u32[]{:S(2)}) collective-permute-start(f32[32,4,1,128]{3,0,2,1:T(8,128)S(1)} %get-tuple-element.21), channel_id=1, source_target_pairs={{0,1},{1,2},{2,3},{3,4},{4,5},{5,6},{6,7},{7,8},{8,9},{9,10},{10,1... | collective-permute-start | bytes 196616 | tf_op jit(solution)/shard_map/ppermute | solution.py:40
  156.0 6.2 %collective-permute-start.14 = (f32[32,4,1,128]{3,0,2,1:T(8,128)S(1)}, f32[32,4,1,128]{3,0,2,1:T(8,128)S(1)}, u32[]{:S(2)}, u32[]{:S(2)}) collective-permute-start(f32[32,4,1,128]{3,0,2,1:T(8,128)S(1)} %get-tuple-element.20), channel_id=1, source_target_pairs={{1,0},{2,1},{3,2},{4,3},{5,4},{6,5},{7,6},{8,7},{9,8},{10,9},{11,1... | collective-permute-start | bytes 196616 | tf_op jit(solution)/shard_map/ppermute | solution.py:41
  (125 shorter events, 40.1 us)
Async XLA Ops:
  0.6 97.5 %copy-start = (f32[32,32]{1,0:T(8,128)S(1)}, f32[32,32]{1,0:T(8,128)}, u32[]{:S(2)}) copy-start(f32[32,32]{1,0:T(8,128)} %param.12) | copy-start | bytes 12292
  0.7 23.9 %copy-start.8 = (f32[32,1,4,256]{3,2,1,0:T(4,128)S(1)}, f32[32,1,4,256]{3,2,1,0:T(4,128)}, u32[]{:S(2)}) copy-start(f32[32,1,4,256]{3,2,1,0:T(4,128)} %param.13) | copy-start | bytes 393220
  0.7 24.1 %copy-start.13 = (s32[1,4,256]{2,1,0:T(4,128)S(1)}, s32[1,4,256]{2,1,0:T(4,128)}, u32[]{:S(2)}) copy-start(s32[1,4,256]{2,1,0:T(4,128)} %param.17) | copy-start | bytes 12292
  0.7 24.2 %copy-start.14 = (s32[8,1,128]{2,1,0:T(1,128)S(1)}, s32[8,1,128]{2,1,0:T(1,128)}, u32[]{:S(2)}) copy-start(s32[8,1,128]{2,1,0:T(1,128)} %param.19) | copy-start | bytes 12292
  0.7 24.2 %copy-start.7 = (f32[8,35,128]{2,0,1:T(8,128)S(1)}, f32[8,35,128]{2,0,1:T(8,128)}, u32[]{:S(2)}) copy-start(f32[8,35,128]{2,0,1:T(8,128)} %param.18) | copy-start | bytes 430084
  2.2 25.6 %copy-start.6 = (f32[3,1,4,256]{3,2,1,0:T(4,128)S(1)}, f32[3,1,4,256]{3,2,1,0:T(4,128)}, u32[]{:S(2)}) copy-start(f32[3,1,4,256]{3,2,1,0:T(4,128)} %param.14) | copy-start | bytes 36868
  2.2 25.6 %collective-permute-start.17 = (f32[4,1,4,256]{3,2,1,0:T(4,128)S(1)}, f32[4,1,4,256]{3,2,1,0:T(4,128)S(1)}, u32[]{:S(2)}, u32[]{:S(2)}) collective-permute-start(f32[4,1,4,256]{3,2,1,0:T(4,128)S(1)} %pad_maximum_fusion.39), channel_id=1, source_target_pairs={{16,0},{32,16},{48,32},{64,48},{80,64},{96,80},{112,96},{128,112},... | collective-permute-start | bytes 49160 | tf_op jit(solution)/shard_map/ppermute | solution.py:28
  5.5 22.3 %collective-permute-start.16 = (f32[4,1,4,256]{3,2,1,0:T(4,128)S(1)}, f32[4,1,4,256]{3,2,1,0:T(4,128)S(1)}, u32[]{:S(2)}, u32[]{:S(2)}) collective-permute-start(f32[4,1,4,256]{3,2,1,0:T(4,128)S(1)} %pad_maximum_fusion.39), channel_id=1, source_target_pairs={{0,16},{16,32},{32,48},{48,64},{64,80},{80,96},{96,112},{112,128},... | collective-permute-start | bytes 49160 | tf_op jit(solution)/shard_map/ppermute | solution.py:26
  14.6 81.0 %collective-permute-start.1 = (f32[32,1,16,128]{3,0,2,1:T(8,128)}, f32[32,1,16,128]{3,0,2,1:T(8,128)}, u32[]{:S(2)}, u32[]{:S(2)}) collective-permute-start(f32[32,1,16,128]{3,0,2,1:T(8,128)} %get-tuple-element.35), channel_id=1, source_target_pairs={{0,16},{16,32},{32,48},{48,64},{64,80},{80,96},{96,112},{112,128},... | collective-permute-start | bytes 786440 | tf_op jit(solution)/shard_map/ppermute | solution.py:40
  18.1 79.0 %collective-permute-start = (f32[32,1,16,128]{3,0,2,1:T(8,128)}, f32[32,1,16,128]{3,0,2,1:T(8,128)}, u32[]{:S(2)}, u32[]{:S(2)}) collective-permute-start(f32[32,1,16,128]{3,0,2,1:T(8,128)} %get-tuple-element.34), channel_id=1, source_target_pairs={{16,0},{32,16},{48,32},{64,48},{80,64},{96,80},{112,96},{128,112},... | collective-permute-start | bytes 786440 | tf_op jit(solution)/shard_map/ppermute | solution.py:41
  22.6 75.6 %collective-permute-start.3 = (f32[32,4,1,128]{3,0,2,1:T(8,128)}, f32[32,4,1,128]{3,0,2,1:T(8,128)}, u32[]{:S(2)}, u32[]{:S(2)}) collective-permute-start(f32[32,4,1,128]{3,0,2,1:T(8,128)} %get-tuple-element.33), channel_id=1, source_target_pairs={{0,1},{1,2},{2,3},{3,4},{4,5},{5,6},{6,7},{7,8},{8,9},{9,10},{10,1... | collective-permute-start | bytes 196616 | tf_op jit(solution)/shard_map/ppermute | solution.py:40
  27.8 20.5 %collective-permute-start.19 = (f32[4,3,1,256]{3,2,1,0:T(1,128)S(1)}, f32[4,3,1,256]{3,2,1,0:T(1,128)S(1)}, u32[]{:S(2)}, u32[]{:S(2)}) collective-permute-start(f32[4,3,1,256]{3,2,1,0:T(1,128)S(1)} %get-tuple-element.72), channel_id=1, source_target_pairs={{1,0},{2,1},{3,2},{4,3},{5,4},{6,5},{7,6},{8,7},{9,8},{10,9},{11,1... | collective-permute-start | bytes 36872 | tf_op jit(solution)/shard_map/ppermute | solution.py:28
  33.6 20.5 %collective-permute-start.18 = (f32[4,3,1,256]{3,2,1,0:T(1,128)S(1)}, f32[4,3,1,256]{3,2,1,0:T(1,128)S(1)}, u32[]{:S(2)}, u32[]{:S(2)}) collective-permute-start(f32[4,3,1,256]{3,2,1,0:T(1,128)S(1)} %get-tuple-element.71), channel_id=1, source_target_pairs={{0,1},{1,2},{2,3},{3,4},{4,5},{5,6},{6,7},{7,8},{8,9},{9,10},{10,1... | collective-permute-start | bytes 36872 | tf_op jit(solution)/shard_map/ppermute | solution.py:26
  48.4 49.8 %collective-permute-start.2 = (f32[32,4,1,128]{3,0,2,1:T(8,128)}, f32[32,4,1,128]{3,0,2,1:T(8,128)}, u32[]{:S(2)}, u32[]{:S(2)}) collective-permute-start(f32[32,4,1,128]{3,0,2,1:T(8,128)} %get-tuple-element.32), channel_id=1, source_target_pairs={{1,0},{2,1},{3,2},{4,3},{5,4},{6,5},{7,6},{8,7},{9,8},{10,9},{11,1... | collective-permute-start | bytes 196616 | tf_op jit(solution)/shard_map/ppermute | solution.py:41
  54.1 18.7 %collective-permute-start.21 = (f32[3,35,128]{2,1,0:T(8,128)}, f32[3,35,128]{2,1,0:T(8,128)}, u32[]{:S(2)}, u32[]{:S(2)}) collective-permute-start(f32[3,35,128]{2,1,0:T(8,128)} %get-tuple-element.66), channel_id=1, source_target_pairs={{0,16},{16,32},{32,48},{48,64},{64,80},{80,96},{96,112},{112,128},... | collective-permute-start | bytes 161288 | tf_op jit(solution)/shard_map/ppermute | solution.py:64
  71.9 26.3 %copy-start.3 = (f32[32,4,16,128]{3,0,2,1:T(8,128)S(1)}, f32[32,4,16,128]{3,0,2,1:T(8,128)}, u32[]{:S(2)}) copy-start(f32[32,4,16,128]{3,0,2,1:T(8,128)} %copy-done.2) | copy-start | bytes 3145732
  71.9 26.3 %copy-start.12 = (f32[32]{0:T(128)S(1)}, f32[32]{0:T(128)}, u32[]{:S(2)}) copy-start(f32[32]{0:T(128)} %param.11) | copy-start | bytes 388
  72.9 9.7 %collective-permute-start.20 = (f32[3,35,128]{2,1,0:T(8,128)S(1)}, f32[3,35,128]{2,1,0:T(8,128)S(1)}, u32[]{:S(2)}, u32[]{:S(2)}) collective-permute-start(f32[3,35,128]{2,1,0:T(8,128)S(1)} %copy-done.10), channel_id=1, source_target_pairs={{16,0},{32,16},{48,32},{64,48},{80,64},{96,80},{112,96},{128,112},... | collective-permute-start | bytes 161288 | tf_op jit(solution)/shard_map/ppermute | solution.py:64
  82.6 3.8 %collective-permute-start.22 = (f32[3,35,128]{2,1,0:T(8,128)S(1)}, f32[3,35,128]{2,1,0:T(8,128)S(1)}, u32[]{:S(2)}, u32[]{:S(2)}) collective-permute-start(f32[3,35,128]{2,1,0:T(8,128)S(1)} %pad_maximum_fusion.37), channel_id=1, source_target_pairs={{1,0},{2,1},{3,2},{4,3},{5,4},{6,5},{7,6},{8,7},{9,8},{10,9},{11,1... | collective-permute-start | bytes 161288 | tf_op jit(solution)/shard_map/ppermute | solution.py:64
  86.4 7.7 %collective-permute-start.23 = (f32[3,35,128]{2,1,0:T(8,128)S(1)}, f32[3,35,128]{2,1,0:T(8,128)S(1)}, u32[]{:S(2)}, u32[]{:S(2)}) collective-permute-start(f32[3,35,128]{2,1,0:T(8,128)S(1)} %pad_maximum_fusion.38), channel_id=1, source_target_pairs={{0,1},{1,2},{2,3},{3,4},{4,5},{5,6},{6,7},{7,8},{8,9},{9,10},{10,1... | collective-permute-start | bytes 161288 | tf_op jit(solution)/shard_map/ppermute | solution.py:64
  101.4 19.7 %collective-permute-start.4 = (f32[32,1,16,128]{3,0,2,1:T(8,128)S(1)}, f32[32,1,16,128]{3,0,2,1:T(8,128)S(1)}, u32[]{:S(2)}, u32[]{:S(2)}) collective-permute-start(f32[32,1,16,128]{3,0,2,1:T(8,128)S(1)} %get-tuple-element.31), channel_id=1, source_target_pairs={{16,0},{32,16},{48,32},{64,48},{80,64},{96,80},{112,96},{128,112},... | collective-permute-start | bytes 786440 | tf_op jit(solution)/shard_map/ppermute | solution.py:41
  103.3 17.8 %collective-permute-start.5 = (f32[32,1,16,128]{3,0,2,1:T(8,128)S(1)}, f32[32,1,16,128]{3,0,2,1:T(8,128)S(1)}, u32[]{:S(2)}, u32[]{:S(2)}) collective-permute-start(f32[32,1,16,128]{3,0,2,1:T(8,128)S(1)} %get-tuple-element.30), channel_id=1, source_target_pairs={{0,16},{16,32},{32,48},{48,64},{64,80},{80,96},{96,112},{112,128},... | collective-permute-start | bytes 786440 | tf_op jit(solution)/shard_map/ppermute | solution.py:40
  111.5 9.6 %collective-permute-start.7 = (f32[32,4,1,128]{3,0,2,1:T(8,128)S(1)}, f32[32,4,1,128]{3,0,2,1:T(8,128)S(1)}, u32[]{:S(2)}, u32[]{:S(2)}) collective-permute-start(f32[32,4,1,128]{3,0,2,1:T(8,128)S(1)} %get-tuple-element.29), channel_id=1, source_target_pairs={{0,1},{1,2},{2,3},{3,4},{4,5},{5,6},{6,7},{7,8},{8,9},{9,10},{10,1... | collective-permute-start | bytes 196616 | tf_op jit(solution)/shard_map/ppermute | solution.py:40
  113.5 7.7 %collective-permute-start.6 = (f32[32,4,1,128]{3,0,2,1:T(8,128)S(1)}, f32[32,4,1,128]{3,0,2,1:T(8,128)S(1)}, u32[]{:S(2)}, u32[]{:S(2)}) collective-permute-start(f32[32,4,1,128]{3,0,2,1:T(8,128)S(1)} %get-tuple-element.28), channel_id=1, source_target_pairs={{1,0},{2,1},{3,2},{4,3},{5,4},{6,5},{7,6},{8,7},{9,8},{10,9},{11,1... | collective-permute-start | bytes 196616 | tf_op jit(solution)/shard_map/ppermute | solution.py:41
  122.6 19.9 %collective-permute-start.8 = (f32[32,1,16,128]{3,0,2,1:T(8,128)S(1)}, f32[32,1,16,128]{3,0,2,1:T(8,128)S(1)}, u32[]{:S(2)}, u32[]{:S(2)}) collective-permute-start(f32[32,1,16,128]{3,0,2,1:T(8,128)S(1)} %get-tuple-element.27), channel_id=1, source_target_pairs={{16,0},{32,16},{48,32},{64,48},{80,64},{96,80},{112,96},{128,112},... | collective-permute-start | bytes 786440 | tf_op jit(solution)/shard_map/ppermute | solution.py:41
  124.5 18.0 %collective-permute-start.9 = (f32[32,1,16,128]{3,0,2,1:T(8,128)S(1)}, f32[32,1,16,128]{3,0,2,1:T(8,128)S(1)}, u32[]{:S(2)}, u32[]{:S(2)}) collective-permute-start(f32[32,1,16,128]{3,0,2,1:T(8,128)S(1)} %get-tuple-element.26), channel_id=1, source_target_pairs={{0,16},{16,32},{32,48},{48,64},{64,80},{80,96},{96,112},{112,128},... | collective-permute-start | bytes 786440 | tf_op jit(solution)/shard_map/ppermute | solution.py:40
  132.7 9.8 %collective-permute-start.11 = (f32[32,4,1,128]{3,0,2,1:T(8,128)S(1)}, f32[32,4,1,128]{3,0,2,1:T(8,128)S(1)}, u32[]{:S(2)}, u32[]{:S(2)}) collective-permute-start(f32[32,4,1,128]{3,0,2,1:T(8,128)S(1)} %get-tuple-element.25), channel_id=1, source_target_pairs={{0,1},{1,2},{2,3},{3,4},{4,5},{5,6},{6,7},{7,8},{8,9},{9,10},{10,1... | collective-permute-start | bytes 196616 | tf_op jit(solution)/shard_map/ppermute | solution.py:40
  134.6 7.8 %collective-permute-start.10 = (f32[32,4,1,128]{3,0,2,1:T(8,128)S(1)}, f32[32,4,1,128]{3,0,2,1:T(8,128)S(1)}, u32[]{:S(2)}, u32[]{:S(2)}) collective-permute-start(f32[32,4,1,128]{3,0,2,1:T(8,128)S(1)} %get-tuple-element.24), channel_id=1, source_target_pairs={{1,0},{2,1},{3,2},{4,3},{5,4},{6,5},{7,6},{8,7},{9,8},{10,9},{11,1... | collective-permute-start | bytes 196616 | tf_op jit(solution)/shard_map/ppermute | solution.py:41
  144.0 20.1 %collective-permute-start.12 = (f32[32,1,16,128]{3,0,2,1:T(8,128)S(1)}, f32[32,1,16,128]{3,0,2,1:T(8,128)S(1)}, u32[]{:S(2)}, u32[]{:S(2)}) collective-permute-start(f32[32,1,16,128]{3,0,2,1:T(8,128)S(1)} %get-tuple-element.23), channel_id=1, source_target_pairs={{16,0},{32,16},{48,32},{64,48},{80,64},{96,80},{112,96},{128,112},... | collective-permute-start | bytes 786440 | tf_op jit(solution)/shard_map/ppermute | solution.py:41
  145.9 18.2 %collective-permute-start.13 = (f32[32,1,16,128]{3,0,2,1:T(8,128)S(1)}, f32[32,1,16,128]{3,0,2,1:T(8,128)S(1)}, u32[]{:S(2)}, u32[]{:S(2)}) collective-permute-start(f32[32,1,16,128]{3,0,2,1:T(8,128)S(1)} %get-tuple-element.22), channel_id=1, source_target_pairs={{0,16},{16,32},{32,48},{48,64},{64,80},{80,96},{96,112},{112,128},... | collective-permute-start | bytes 786440 | tf_op jit(solution)/shard_map/ppermute | solution.py:40
  154.1 10.0 %collective-permute-start.15 = (f32[32,4,1,128]{3,0,2,1:T(8,128)S(1)}, f32[32,4,1,128]{3,0,2,1:T(8,128)S(1)}, u32[]{:S(2)}, u32[]{:S(2)}) collective-permute-start(f32[32,4,1,128]{3,0,2,1:T(8,128)S(1)} %get-tuple-element.21), channel_id=1, source_target_pairs={{0,1},{1,2},{2,3},{3,4},{4,5},{5,6},{6,7},{7,8},{8,9},{9,10},{10,1... | collective-permute-start | bytes 196616 | tf_op jit(solution)/shard_map/ppermute | solution.py:40
  156.0 8.1 %collective-permute-start.14 = (f32[32,4,1,128]{3,0,2,1:T(8,128)S(1)}, f32[32,4,1,128]{3,0,2,1:T(8,128)S(1)}, u32[]{:S(2)}, u32[]{:S(2)}) collective-permute-start(f32[32,4,1,128]{3,0,2,1:T(8,128)S(1)} %get-tuple-element.20), channel_id=1, source_target_pairs={{1,0},{2,1},{3,2},{4,3},{5,4},{6,5},{7,6},{8,7},{9,8},{10,9},{11,1... | collective-permute-start | bytes 196616 | tf_op jit(solution)/shard_map/ppermute | solution.py:41
  (7 other events, 70.6 us)

commit v2 on v1

--- a/solution.py
+++ b/solution.py
@@ -130,6 +130,29 @@
     return (move_step * active * force).reshape(3, bins_x, bins_y, lanes)
 
 
+def pack(pieces):
+    return jnp.concatenate([piece.reshape(-1, 128) for piece in pieces], axis=0)
+
+
+def unpack(flat, pieces):
+    out = []
+    row = 0
+    for piece in pieces:
+        rows = piece.size // 128
+        out.append(flat[row : row + rows].reshape(piece.shape))
+        row += rows
+    return out
+
+
+def send_pair(axis, upward, downward):
+    count = lax.axis_size(axis)
+    up = [(i, i + 1) for i in range(count - 1)]
+    down = [(i + 1, i) for i in range(count - 1)]
+    from_below = unpack(lax.ppermute(pack(upward), axis, up), upward)
+    from_above = unpack(lax.ppermute(pack(downward), axis, down), downward)
+    return from_below, from_above
+
+
 def on_device(
     field,
     rates,
@@ -144,23 +167,45 @@
 ):
     weight = stiffness * occupancy.astype(jnp.float32)
     points = jnp.concatenate([positions, weight[None]], axis=0)
-    bordered = padded_2(points, (("gx", 1), ("gy", 2)), 1)
     payload = migrant_state * migrant_live.astype(jnp.float32)
-    moving = [payload[index] for index in range(8)]
-    for stride in (1, -1):
-        picked = [index for index in range(8) if shifts[index][0] == stride]
-        landed = shifted(jnp.stack([moving[index] for index in picked]), "gx", stride)
-        for place, index in enumerate(picked):
-            moving[index] = landed[place]
-    for stride in (1, -1):
-        picked = [index for index in range(8) if shifts[index][1] == stride]
-        landed = shifted(jnp.stack([moving[index] for index in picked]), "gy", stride)
-        for place, index in enumerate(picked):
-            moving[index] = landed[place]
-    arrived = jnp.stack(moving)
     source = deposit(secretion, occupancy, offsets)
     current = field
-    for _ in range(SUBSTEPS):
+
+    (x_low, points_low, moved_up), (x_high, points_high, moved_down) = send_pair(
+        "gx",
+        [current[:, -1:], points, payload[5:8]],
+        [current[:, :1], points, payload[0:3]],
+    )
+    (y_low, beside_up), (y_high, beside_down) = send_pair(
+        "gy",
+        [current[:, :, -1:], payload[4:5]],
+        [current[:, :, :1], payload[3:4]],
+    )
+    current = advance(framed(current, x_low, x_high, y_low, y_high), source, rates, mixing)
+
+    row_points = jnp.concatenate([points_low, points, points_high], axis=1)
+    x_low, x_high = halos(current, "gx", 1)
+    (y_low, points_low, corner_up), (y_high, points_high, corner_down) = send_pair(
+        "gy",
+        [current[:, :, -1:], row_points[:, :, -1:], jnp.stack([moved_down[2], moved_up[2]])],
+        [current[:, :, :1], row_points[:, :, :1], jnp.stack([moved_down[0], moved_up[0]])],
+    )
+    current = advance(framed(current, x_low, x_high, y_low, y_high), source, rates, mixing)
+    bordered = jnp.concatenate([points_low, row_points, points_high], axis=2)
+    arrived = jnp.stack(
+        [
+            corner_down[0],
+            moved_down[1],
+            corner_up[0],
+            beside_down[0],
+            beside_up[0],
+            corner_down[1],
+            moved_up[1],
+            corner_up[1],
+        ]
+    )
+
+    for _ in range(SUBSTEPS - 2):
         current = substep(current, source, rates, mixing)
     displacement = pair_forces(points, bordered, occupancy)
     return (current, displacement, arrived)

time: 169 us -> 169 us (level)
  the two profiles are of different devices: /device:TPU:120 before, /device:TPU:119 now
where the time goes in v2:
time: 169 us; the launch traced here: 166 us
  local copies, waits for them, and re-layouts  61.5 us (36%)
  starting transfers between devices  56.9 us (34%)
  other arithmetic  25.5 us (15%)
  waiting for transfers between devices  11.8 us (7%)
  matrix products  9.23 us (5%)
    ppermute x5, starting transfers between devices, halos(): low = lax.ppermute(tail, axis, [(i, (i + 1) % count) for i in range(ends)])  24.7 us
    ppermute x3, starting transfers between devices, send_pair(): from_below = unpack(lax.ppermute(pack(upward), axis, up), upward)  15 us
    unnamed x60, local copies, waits for them, and re-layouts  11 us
    ppermute x5, starting transfers between devices, halos(): high = lax.ppermute(head, axis, [((i + 1) % count, i) for i in range(ends)])  10.8 us
    mul x3, local copies, waits for them, and re-layouts, advance(): time_step * source  10.2 us
    ppermute x5, waiting for transfers between devices, halos(): high = lax.ppermute(head, axis, [((i + 1) % count, i) for i in range(ends)])  7.57 us
    dot_general x4, matrix products, advance(): jnp.dot(mixing, center.reshape(species, -1), precision=lax.Precision.HIGH...  7.08 us
    slice x11, local copies, waits for them, and re-layouts, unpack(): out.append(flat[row:row + rows].reshape(piece.shape))  6.92 us
  transfers between devices with their start and end apart: 16, of which 3 were waited for; matrix products, arithmetic and copies ran while one was open for 44% of the time, Pallas kernels for 0%

profile of v2, /device:TPU:119, one launch (start us, length us, event | category | flops | bytes accessed | tf_op | source)
XLA Modules:
  0.0 166.3 jit_solution(6507961410188506012)
XLA Ops:
  6.4 4.5 %collective-permute-start.1 = (f32[649,128]{1,0:T(8,128)S(1)}, f32[649,128]{1,0:T(8,128)S(1)}, u32[]{:S(2)}, u32[]{:S(2)}) collective-permute-start(f32[649,128]{1,0:T(8,128)S(1)} %get-tuple-element.75), channel_id=1, source_target_pairs={{0,16},{16,32},{32,48},{48,64},{64,80},{80,96},{96,112},{112,128},... | collective-permute-start | bytes 996872 | tf_op jit(solution)/shard_map/ppermute | solution.py:151
  10.9 2.3 %collective-permute-start = (f32[649,128]{1,0:T(8,128)}, f32[649,128]{1,0:T(8,128)}, u32[]{:S(2)}, u32[]{:S(2)}) collective-permute-start(f32[649,128]{1,0:T(8,128)} %get-tuple-element.74), channel_id=1, source_target_pairs={{16,0},{32,16},{48,32},{64,48},{80,64},{96,80},{112,96},{128,112},... | collective-permute-start | bytes 996872 | tf_op jit(solution)/shard_map/ppermute | solution.py:152
  13.9 4.2 %collective-permute-start.3 = (f32[163,128]{1,0:T(8,128)}, f32[163,128]{1,0:T(8,128)}, u32[]{:S(2)}, u32[]{:S(2)}) collective-permute-start(f32[163,128]{1,0:T(8,128)} %pad_maximum_fusion.54), channel_id=1, source_target_pairs={{0,1},{1,2},{2,3},{3,4},{4,5},{5,6},{6,7},{7,8},{8,9},{9,10},{10,1... | collective-permute-start | bytes 250376 | tf_op jit(solution)/shard_map/ppermute | solution.py:151
  18.8 1.9 %collective-permute-start.2 = (f32[163,128]{1,0:T(8,128)}, f32[163,128]{1,0:T(8,128)}, u32[]{:S(2)}, u32[]{:S(2)}) collective-permute-start(f32[163,128]{1,0:T(8,128)} %pad_maximum_fusion.53), channel_id=1, source_target_pairs={{1,0},{2,1},{3,2},{4,3},{5,4},{6,5},{7,6},{8,7},{9,8},{10,9},{11,1... | collective-permute-start | bytes 250376 | tf_op jit(solution)/shard_map/ppermute | solution.py:152
  21.1 2.2 %fusion.9 = f32[32,64,128]{2,0,1:T(8,128)S(1)} fusion(f32[32,64,16]{0,2,1:T(8,128)S(1)} %bitcast.165, f32[64,16]{1,0:T(8,128)S(1)} %convert_element_type.31, s32[64,16]{1,0:T(8,128)S(1)} %eq.10), kind=kOutput, calls=%fused_computation.43 | convolution fusion | flops 50855936 | bytes 1187840 | tf_op jit(solution)/shard_map/snk,nkc->snc/dot_general | solution.py:96
  24.2 2.7 %copy.88 = f32[32,64,128]{0,2,1:T(8,128)} copy(f32[32,64,128]{2,0,1:T(8,128)S(1)} %fusion.9) | data formatting | bytes 2097152 | tf_op jit(solution)/shard_map/mul | solution.py:82
  26.8 4.8 %copy.89 = f32[32,1,4,4,4,16,8]{0,6,5,4,3,2,1:T(8,128)} copy(f32[32,1,4,4,4,16,8]{0,6,4,2,5,3,1:T(8,128)} %bitcast.148) | data formatting | bytes 2097152 | tf_op jit(solution)/shard_map/mul | solution.py:82
  31.6 2.8 %copy.90 = f32[32,4,16,128]{3,0,2,1:T(8,128)S(1)} copy(f32[32,4,16,128]{0,3,2,1:T(8,128)} %bitcast.149) | data formatting | bytes 2097152 | tf_op jit(solution)/shard_map/mul | solution.py:82
  39.4 2.1 %fusion.11 = f32[32,4,16,128]{3,0,2,1:T(8,128)S(1)} fusion(f32[32,4,16,128]{3,0,2,1:T(8,128)S(1)} %copy.90, f32[32,4,16,128]{3,0,2,1:T(8,128)S(1)} %get-tuple-element.34, f32[32,1,1,128]{3,0,2,1:T(8,128)S(1)} %broadcast.209, f32[32,6,16,128]{3,0,2,1:T(8,128)S(1)} %get-tuple-element.64, f32[32,4,1,128]{3,0,2,1:T(8,128)S(1)} %copy.82, ...), kind=kOutput, calls=%fused_computation.46 | convolution fusion | flops 106168320 | bytes 6443136 | tf_op jit(solution)/shard_map/dot_general | solution.py:75
  47.8 2.9 %collective-permute-start.4 = (f32[32,1,16,128]{3,0,2,1:T(8,128)}, f32[32,1,16,128]{3,0,2,1:T(8,128)}, u32[]{:S(2)}, u32[]{:S(2)}) collective-permute-start(f32[32,1,16,128]{3,0,2,1:T(8,128)} %get-tuple-element.28), channel_id=1, source_target_pairs={{16,0},{32,16},{48,32},{64,48},{80,64},{96,80},{112,96},{128,112},... | collective-permute-start | bytes 786440 | tf_op jit(solution)/shard_map/ppermute | solution.py:41
  50.7 6.0 %collective-permute-start.5 = (f32[32,1,16,128]{3,0,2,1:T(8,128)}, f32[32,1,16,128]{3,0,2,1:T(8,128)}, u32[]{:S(2)}, u32[]{:S(2)}) collective-permute-start(f32[32,1,16,128]{3,0,2,1:T(8,128)} %get-tuple-element.27), channel_id=1, source_target_pairs={{0,16},{16,32},{32,48},{48,64},{64,80},{80,96},{96,112},{112,128},... | collective-permute-start | bytes 786440 | tf_op jit(solution)/shard_map/ppermute | solution.py:40
  64.0 6.3 %collective-permute-start.7 = (f32[222,128]{1,0:T(8,128)}, f32[222,128]{1,0:T(8,128)}, u32[]{:S(2)}, u32[]{:S(2)}) collective-permute-start(f32[222,128]{1,0:T(8,128)} %pad_maximum_fusion.52), channel_id=1, source_target_pairs={{0,1},{1,2},{2,3},{3,4},{4,5},{5,6},{6,7},{7,8},{8,9},{9,10},{10,1... | collective-permute-start | bytes 341000 | tf_op jit(solution)/shard_map/ppermute | solution.py:151
  73.4 2.1 %collective-permute-start.6 = (f32[222,128]{1,0:T(8,128)S(1)}, f32[222,128]{1,0:T(8,128)S(1)}, u32[]{:S(2)}, u32[]{:S(2)}) collective-permute-start(f32[222,128]{1,0:T(8,128)S(1)} %pad_maximum_fusion.51), channel_id=1, source_target_pairs={{1,0},{2,1},{3,2},{4,3},{5,4},{6,5},{7,6},{8,7},{9,8},{10,9},{11,1... | collective-permute-start | bytes 341000 | tf_op jit(solution)/shard_map/ppermute | solution.py:152
  77.3 4.2 %collective-permute-done.6 = f32[222,128]{1,0:T(8,128)S(1)} collective-permute-done((f32[222,128]{1,0:T(8,128)S(1)}, f32[222,128]{1,0:T(8,128)S(1)}, u32[]{:S(2)}, u32[]{:S(2)}) %collective-permute-start.6) | collective-permute-done | bytes 113696 | tf_op jit(solution)/shard_map/ppermute | solution.py:152
  92.7 2.3 %concatenate.201 = f32[4,1,4,16,144]{4,3,2,1,0:T(8,128)} concatenate(f32[4,1,4,16,16]{4,3,2,1,0:T(8,128)} %get-tuple-element.46, f32[4,1,4,16,16]{4,3,2,1,0:T(8,128)} %get-tuple-element.58, f32[4,1,4,16,16]{4,3,2,1,0:T(8,128)} %get-tuple-element.45, f32[4,1,4,16,16]{4,3,2,1,0:T(8,128)} %get-tuple-element.44, f32[4,1,4,16,16]{4,3,2,1,0:T(8,128)} %get-tuple-element.71, ...), dimensions={4} | concatenate | bytes 294912 | tf_op jit(solution)/shard_map/concatenate | solution.py:110
  98.1 2.3 %concatenate.200 = f32[4,1,4,16,144]{4,3,2,1,0:T(8,128)} concatenate(f32[4,1,4,16,16]{4,3,2,1,0:T(8,128)} %get-tuple-element.52, f32[4,1,4,16,16]{4,3,2,1,0:T(8,128)S(1)} %copy-done.4, f32[4,1,4,16,16]{4,3,2,1,0:T(8,128)} %get-tuple-element.51, f32[4,1,4,16,16]{4,3,2,1,0:T(8,128)} %get-tuple-element.50, f32[4,1,4,16,16]{4,3,2,1,0:T(8,128)S(1)} %bitcast.164, ...), dimensions={4} | concatenate | bytes 294912 | tf_op jit(solution)/shard_map/concatenate | solution.py:110
  102.8 2.3 %concatenate.202 = f32[4,1,4,16,144]{4,3,2,1,0:T(8,128)} concatenate(f32[4,1,4,16,16]{4,3,2,1,0:T(8,128)} %get-tuple-element.40, f32[4,1,4,16,16]{4,3,2,1,0:T(8,128)} %get-tuple-element.56, f32[4,1,4,16,16]{4,3,2,1,0:T(8,128)} %get-tuple-element.39, f32[4,1,4,16,16]{4,3,2,1,0:T(8,128)} %get-tuple-element.38, f32[4,1,4,16,16]{4,3,2,1,0:T(8,128)S(1)} %bitcast.160, ...), dimensions={4} | concatenate | bytes 294912 | tf_op jit(solution)/shard_map/concatenate | solution.py:110
  106.9 2.0 %fusion.2 = (f32[4,16,16,144]{3,2,1,0:T(8,128)S(1)}, f32[4,16,16,144]{3,2,1,0:T(8,128)S(1)}) fusion(f32[3,4,16,144]{3,2,1,0:T(8,128)} %slice_bitcast_fusion.1, f32[3,4,16,16]{3,2,1,0:T(8,128)} %sub.95, f32[3,4,16,144]{3,2,1,0:T(8,128)S(1)} %slice_bitcast_fusion.2), kind=kLoop, calls=%fused_computation.11 | loop fusion | flops 2359296 | bytes 1413120 | tf_op jit(solution)/shard_map/reduce_sum | solution.py:126
  109.4 1.8 %fusion.3 = (f32[3,4,16,16]{3,2,1,0:T(8,128)S(1)}, f32[4,16,16,144]{3,2,1,0:T(8,128)S(1)}, f32[3,4,16,16]{3,2,1,0:T(8,128)S(1)}) fusion(f32[4,16,16,144]{3,2,1,0:T(8,128)S(1)} %exponential_multiply_fusion.1, f32[3,4,16,144]{3,2,1,0:T(8,128)S(1)} %copy-done.2, f32[3,4,16,16]{3,2,1,0:T(8,128)S(1)} %copy-done.3, f32[3,4,16,144]{3,2,1,0:T(8,128)S(1)} %slice_bitcast_fusion, ...), kind=kLoop, calls=%fused_computation.12 | loop fusion | flops 3827712 | bytes 2138112 | tf_op jit(solution)/shard_map/reduce_sum | solution.py:128
  120.2 2.4 %fusion.31 = f32[32,4,16,128]{3,0,2,1:T(8,128)S(1)} fusion(f32[32,4,16,128]{3,0,2,1:T(8,128)S(1)} %copy.90, f32[32,4,16,128]{3,0,2,1:T(8,128)S(1)} %fusion.11, f32[32,1,1,128]{3,0,2,1:T(8,128)S(1)} %copy-done.7, f32[32,1,16,128]{3,0,2,1:T(8,128)} %collective-permute-done.4, f32[32,1,16,128]{3,0,2,1:T(8,128)} %collective-permute-done.5, ...), kind=kLoop, calls=%fused_computation.68 | loop fusion | flops 6291456 | bytes 4866176 | tf_op jit(solution)/shard_map/add | solution.py:79
  122.6 1.9 %collective-permute-start.8 = (f32[32,1,16,128]{3,0,2,1:T(8,128)S(1)}, f32[32,1,16,128]{3,0,2,1:T(8,128)S(1)}, u32[]{:S(2)}, u32[]{:S(2)}) collective-permute-start(f32[32,1,16,128]{3,0,2,1:T(8,128)S(1)} %get-tuple-element.24), channel_id=1, source_target_pairs={{16,0},{32,16},{48,32},{64,48},{80,64},{96,80},{112,96},{128,112},... | collective-permute-start | bytes 786440 | tf_op jit(solution)/shard_map/ppermute | solution.py:41
  124.5 7.0 %collective-permute-start.9 = (f32[32,1,16,128]{3,0,2,1:T(8,128)S(1)}, f32[32,1,16,128]{3,0,2,1:T(8,128)S(1)}, u32[]{:S(2)}, u32[]{:S(2)}) collective-permute-start(f32[32,1,16,128]{3,0,2,1:T(8,128)S(1)} %get-tuple-element.23), channel_id=1, source_target_pairs={{0,16},{16,32},{32,48},{48,64},{64,80},{80,96},{96,112},{112,128},... | collective-permute-start | bytes 786440 | tf_op jit(solution)/shard_map/ppermute | solution.py:40
  132.1 2.4 %collective-permute-start.11 = (f32[32,4,1,128]{3,0,2,1:T(8,128)S(1)}, f32[32,4,1,128]{3,0,2,1:T(8,128)S(1)}, u32[]{:S(2)}, u32[]{:S(2)}) collective-permute-start(f32[32,4,1,128]{3,0,2,1:T(8,128)S(1)} %get-tuple-element.22), channel_id=1, source_target_pairs={{0,1},{1,2},{2,3},{3,4},{4,5},{5,6},{6,7},{7,8},{8,9},{9,10},{10,1... | collective-permute-start | bytes 196616 | tf_op jit(solution)/shard_map/ppermute | solution.py:40
  134.5 2.0 %collective-permute-start.10 = (f32[32,4,1,128]{3,0,2,1:T(8,128)S(1)}, f32[32,4,1,128]{3,0,2,1:T(8,128)S(1)}, u32[]{:S(2)}, u32[]{:S(2)}) collective-permute-start(f32[32,4,1,128]{3,0,2,1:T(8,128)S(1)} %get-tuple-element.21), channel_id=1, source_target_pairs={{1,0},{2,1},{3,2},{4,3},{5,4},{6,5},{7,6},{8,7},{9,8},{10,9},{11,1... | collective-permute-start | bytes 196616 | tf_op jit(solution)/shard_map/ppermute | solution.py:41
  136.5 1.7 %fusion.7 = f32[4,8,64,128]{3,1,2,0:T(8,128)S(1)} fusion(f32[32,32]{1,0:T(8,128)S(1)} %copy-done, f32[4,8,64,128]{3,2,1,0:T(8,128)S(1)} %bitcast.155), kind=kOutput, calls=%fused_computation.40 | convolution fusion | flops 100925440 | bytes 2101248 | tf_op jit(solution)/shard_map/dot_general | solution.py:75
  138.4 3.9 %collective-permute-done.10 = f32[32,4,1,128]{3,0,2,1:T(8,128)S(1)} collective-permute-done((f32[32,4,1,128]{3,0,2,1:T(8,128)S(1)}, f32[32,4,1,128]{3,0,2,1:T(8,128)S(1)}, u32[]{:S(2)}, u32[]{:S(2)}) %collective-permute-start.10) | collective-permute-done | bytes 65568 | tf_op jit(solution)/shard_map/ppermute | solution.py:41
  143.7 1.9 %collective-permute-start.12 = (f32[32,1,16,128]{3,0,2,1:T(8,128)S(1)}, f32[32,1,16,128]{3,0,2,1:T(8,128)S(1)}, u32[]{:S(2)}, u32[]{:S(2)}) collective-permute-start(f32[32,1,16,128]{3,0,2,1:T(8,128)S(1)} %get-tuple-element.20), channel_id=1, source_target_pairs={{16,0},{32,16},{48,32},{64,48},{80,64},{96,80},{112,96},{128,112},... | collective-permute-start | bytes 786440 | tf_op jit(solution)/shard_map/ppermute | solution.py:41
  145.7 7.0 %collective-permute-start.13 = (f32[32,1,16,128]{3,0,2,1:T(8,128)S(1)}, f32[32,1,16,128]{3,0,2,1:T(8,128)S(1)}, u32[]{:S(2)}, u32[]{:S(2)}) collective-permute-start(f32[32,1,16,128]{3,0,2,1:T(8,128)S(1)} %get-tuple-element.19), channel_id=1, source_target_pairs={{0,16},{16,32},{32,48},{48,64},{64,80},{80,96},{96,112},{112,128},... | collective-permute-start | bytes 786440 | tf_op jit(solution)/shard_map/ppermute | solution.py:40
  153.3 2.4 %collective-permute-start.15 = (f32[32,4,1,128]{3,0,2,1:T(8,128)S(1)}, f32[32,4,1,128]{3,0,2,1:T(8,128)S(1)}, u32[]{:S(2)}, u32[]{:S(2)}) collective-permute-start(f32[32,4,1,128]{3,0,2,1:T(8,128)S(1)} %get-tuple-element.18), channel_id=1, source_target_pairs={{0,1},{1,2},{2,3},{3,4},{4,5},{5,6},{6,7},{7,8},{8,9},{9,10},{10,1... | collective-permute-start | bytes 196616 | tf_op jit(solution)/shard_map/ppermute | solution.py:40
  155.7 2.2 %collective-permute-start.14 = (f32[32,4,1,128]{3,0,2,1:T(8,128)S(1)}, f32[32,4,1,128]{3,0,2,1:T(8,128)S(1)}, u32[]{:S(2)}, u32[]{:S(2)}) collective-permute-start(f32[32,4,1,128]{3,0,2,1:T(8,128)S(1)} %get-tuple-element.17), channel_id=1, source_target_pairs={{1,0},{2,1},{3,2},{4,3},{5,4},{6,5},{7,6},{8,7},{9,8},{10,9},{11,1... | collective-permute-start | bytes 196616 | tf_op jit(solution)/shard_map/ppermute | solution.py:41
  157.8 1.7 %fusion.8 = f32[4,8,64,128]{3,1,2,0:T(8,128)S(1)} fusion(f32[32,32]{1,0:T(8,128)S(1)} %copy-done, f32[4,8,64,128]{3,2,1,0:T(8,128)S(1)} %bitcast.156), kind=kOutput, calls=%fused_computation.41 | convolution fusion | flops 100925440 | bytes 2101248 | tf_op jit(solution)/shard_map/dot_general | solution.py:75
  159.7 3.6 %collective-permute-done.14 = f32[32,4,1,128]{3,0,2,1:T(8,128)S(1)} collective-permute-done((f32[32,4,1,128]{3,0,2,1:T(8,128)S(1)}, f32[32,4,1,128]{3,0,2,1:T(8,128)S(1)}, u32[]{:S(2)}, u32[]{:S(2)}) %collective-permute-start.14) | collective-permute-done | bytes 65568 | tf_op jit(solution)/shard_map/ppermute | solution.py:41
  (157 shorter events, 65.3 us)
Async XLA Ops:
  0.6 38.8 %copy-start = (f32[32,32]{1,0:T(8,128)S(1)}, f32[32,32]{1,0:T(8,128)}, u32[]{:S(2)}) copy-start(f32[32,32]{1,0:T(8,128)} %param.12) | copy-start | bytes 12292
  0.6 20.1 %copy-start.18 = (s32[1,4,256]{2,1,0:T(4,128)S(1)}, s32[1,4,256]{2,1,0:T(4,128)}, u32[]{:S(2)}) copy-start(s32[1,4,256]{2,1,0:T(4,128)} %param.16) | copy-start | bytes 12292
  0.7 12.5 %copy-start.1 = (f32[32,4,16,128]{3,2,1,0:T(8,128)S(1)}, f32[32,4,16,128]{3,2,1,0:T(8,128)}, u32[]{:S(2)}) copy-start(f32[32,4,16,128]{3,2,1,0:T(8,128)} %param.10) | copy-start | bytes 3145732
  0.7 20.1 %copy-start.15 = (f32[32,1,4,256]{3,2,1,0:T(4,128)S(1)}, f32[32,1,4,256]{3,2,1,0:T(4,128)}, u32[]{:S(2)}) copy-start(f32[32,1,4,256]{3,2,1,0:T(4,128)} %param.13) | copy-start | bytes 393220
  0.7 20.3 %copy-start.21 = (s32[1,4,256]{2,1,0:T(4,128)S(1)}, s32[1,4,256]{2,1,0:T(4,128)}, u32[]{:S(2)}) copy-start(s32[1,4,256]{2,1,0:T(4,128)} %param.17) | copy-start | bytes 12292
  2.1 21.2 %copy-start.16 = (f32[1,4,256]{2,1,0:T(4,128)}, f32[1,4,256]{2,1,0:T(4,128)S(1)}, u32[]{:S(2)}) copy-start(f32[1,4,256]{2,1,0:T(4,128)S(1)} %get-tuple-element.77) | copy-start | bytes 12292
  3.5 19.9 %copy-start.13 = (f32[3,1,4,256]{3,2,1,0:T(4,128)S(1)}, f32[3,1,4,256]{3,2,1,0:T(4,128)}, u32[]{:S(2)}) copy-start(f32[3,1,4,256]{3,2,1,0:T(4,128)} %param.14) | copy-start | bytes 36868
  6.4 30.6 %collective-permute-start.1 = (f32[649,128]{1,0:T(8,128)S(1)}, f32[649,128]{1,0:T(8,128)S(1)}, u32[]{:S(2)}, u32[]{:S(2)}) collective-permute-start(f32[649,128]{1,0:T(8,128)S(1)} %get-tuple-element.75), channel_id=1, source_target_pairs={{0,16},{16,32},{32,48},{48,64},{64,80},{80,96},{96,112},{112,128},... | collective-permute-start | bytes 996872 | tf_op jit(solution)/shard_map/ppermute | solution.py:151
  10.9 27.4 %collective-permute-start = (f32[649,128]{1,0:T(8,128)}, f32[649,128]{1,0:T(8,128)}, u32[]{:S(2)}, u32[]{:S(2)}) collective-permute-start(f32[649,128]{1,0:T(8,128)} %get-tuple-element.74), channel_id=1, source_target_pairs={{16,0},{32,16},{48,32},{64,48},{80,64},{96,80},{112,96},{128,112},... | collective-permute-start | bytes 996872 | tf_op jit(solution)/shard_map/ppermute | solution.py:152
  13.9 21.3 %collective-permute-start.3 = (f32[163,128]{1,0:T(8,128)}, f32[163,128]{1,0:T(8,128)}, u32[]{:S(2)}, u32[]{:S(2)}) collective-permute-start(f32[163,128]{1,0:T(8,128)} %pad_maximum_fusion.54), channel_id=1, source_target_pairs={{0,1},{1,2},{2,3},{3,4},{4,5},{5,6},{6,7},{7,8},{8,9},{9,10},{10,1... | collective-permute-start | bytes 250376 | tf_op jit(solution)/shard_map/ppermute | solution.py:151
  18.8 17.3 %collective-permute-start.2 = (f32[163,128]{1,0:T(8,128)}, f32[163,128]{1,0:T(8,128)}, u32[]{:S(2)}, u32[]{:S(2)}) collective-permute-start(f32[163,128]{1,0:T(8,128)} %pad_maximum_fusion.53), channel_id=1, source_target_pairs={{1,0},{2,1},{3,2},{4,3},{5,4},{6,5},{7,6},{8,7},{9,8},{10,9},{11,1... | collective-permute-start | bytes 250376 | tf_op jit(solution)/shard_map/ppermute | solution.py:152
  35.2 4.2 %copy-start.19 = (f32[32]{0:T(128)S(1)}, f32[32]{0:T(128)}, u32[]{:S(2)}) copy-start(f32[32]{0:T(128)} %param.11) | copy-start | bytes 388
  47.8 72.4 %collective-permute-start.4 = (f32[32,1,16,128]{3,0,2,1:T(8,128)}, f32[32,1,16,128]{3,0,2,1:T(8,128)}, u32[]{:S(2)}, u32[]{:S(2)}) collective-permute-start(f32[32,1,16,128]{3,0,2,1:T(8,128)} %get-tuple-element.28), channel_id=1, source_target_pairs={{16,0},{32,16},{48,32},{64,48},{80,64},{96,80},{112,96},{128,112},... | collective-permute-start | bytes 786440 | tf_op jit(solution)/shard_map/ppermute | solution.py:41
  50.7 69.5 %collective-permute-start.5 = (f32[32,1,16,128]{3,0,2,1:T(8,128)}, f32[32,1,16,128]{3,0,2,1:T(8,128)}, u32[]{:S(2)}, u32[]{:S(2)}) collective-permute-start(f32[32,1,16,128]{3,0,2,1:T(8,128)} %get-tuple-element.27), channel_id=1, source_target_pairs={{0,16},{16,32},{32,48},{48,64},{64,80},{80,96},{96,112},{112,128},... | collective-permute-start | bytes 786440 | tf_op jit(solution)/shard_map/ppermute | solution.py:40
  64.0 20.3 %collective-permute-start.7 = (f32[222,128]{1,0:T(8,128)}, f32[222,128]{1,0:T(8,128)}, u32[]{:S(2)}, u32[]{:S(2)}) collective-permute-start(f32[222,128]{1,0:T(8,128)} %pad_maximum_fusion.52), channel_id=1, source_target_pairs={{0,1},{1,2},{2,3},{3,4},{4,5},{5,6},{6,7},{7,8},{8,9},{9,10},{10,1... | collective-permute-start | bytes 341000 | tf_op jit(solution)/shard_map/ppermute | solution.py:151
  73.4 8.2 %collective-permute-start.6 = (f32[222,128]{1,0:T(8,128)S(1)}, f32[222,128]{1,0:T(8,128)S(1)}, u32[]{:S(2)}, u32[]{:S(2)}) collective-permute-start(f32[222,128]{1,0:T(8,128)S(1)} %pad_maximum_fusion.51), channel_id=1, source_target_pairs={{1,0},{2,1},{3,2},{4,3},{5,4},{6,5},{7,6},{8,7},{9,8},{10,9},{11,1... | collective-permute-start | bytes 341000 | tf_op jit(solution)/shard_map/ppermute | solution.py:152
  91.3 6.8 %copy-start.4 = (f32[4,1,4,16,16]{4,3,2,1,0:T(8,128)S(1)}, f32[4,1,4,16,16]{4,3,2,1,0:T(8,128)}, u32[]{:S(2)}) copy-start(f32[4,1,4,16,16]{4,3,2,1,0:T(8,128)} %get-tuple-element.57) | copy-start | bytes 49156
  100.4 8.6 %copy-start.8 = (f32[4,16,144]{2,1,0:T(8,128)S(1)}, f32[4,16,144]{2,1,0:T(8,128)}, u32[]{:S(2)}) copy-start(f32[4,16,144]{2,1,0:T(8,128)} %slice_bitcast_fusion.4) | copy-start | bytes 110596
  105.1 4.1 %copy-start.9 = (f32[4,16,144]{2,1,0:T(8,128)S(1)}, f32[4,16,144]{2,1,0:T(8,128)}, u32[]{:S(2)}) copy-start(f32[4,16,144]{2,1,0:T(8,128)} %slice_bitcast_fusion.5) | copy-start | bytes 110596
  109.4 3.1 %copy-start.11 = (f32[222,128]{1,0:T(8,128)S(1)}, f32[222,128]{1,0:T(8,128)}, u32[]{:S(2)}) copy-start(f32[222,128]{1,0:T(8,128)} %copy-done.10) | copy-start | bytes 340996
  111.2 6.6 %slice-start = ((f32[222,128]{1,0:T(8,128)}), f32[128,128]{1,0:T(8,128)S(1)}, s32[]{:S(2)}) async-start(f32[222,128]{1,0:T(8,128)} %copy-done.10), calls=%async_computation | async-start | bytes 131072 | tf_op jit(solution)/shard_map/slice | solution.py:142
  111.2 8.3 %copy-start.17 = (f32[4,256]{1,0:T(4,128)S(1)}, f32[4,256]{1,0:T(4,128)}, u32[]{:S(2)}) copy-start(f32[4,256]{1,0:T(4,128)} %get-tuple-element.76) | copy-start | bytes 12292
  111.3 8.9 %copy-start.7 = (f32[32,1,1,128]{3,0,2,1:T(8,128)S(1)}, f32[32,1,1,128]{3,0,2,1:T(8,128)}, u32[]{:S(2)}) copy-start(f32[32,1,1,128]{3,0,2,1:T(8,128)} %copy-done.6) | copy-start | bytes 49156
  111.3 8.9 %copy-start.20 = (f32[32]{0:T(128)S(1)}, f32[32]{0:T(128)}, u32[]{:S(2)}) copy-start(f32[32]{0:T(128)} %param.11) | copy-start | bytes 388
  122.6 19.7 %collective-permute-start.8 = (f32[32,1,16,128]{3,0,2,1:T(8,128)S(1)}, f32[32,1,16,128]{3,0,2,1:T(8,128)S(1)}, u32[]{:S(2)}, u32[]{:S(2)}) collective-permute-start(f32[32,1,16,128]{3,0,2,1:T(8,128)S(1)} %get-tuple-element.24), channel_id=1, source_target_pairs={{16,0},{32,16},{48,32},{64,48},{80,64},{96,80},{112,96},{128,112},... | collective-permute-start | bytes 786440 | tf_op jit(solution)/shard_map/ppermute | solution.py:41
  124.5 17.8 %collective-permute-start.9 = (f32[32,1,16,128]{3,0,2,1:T(8,128)S(1)}, f32[32,1,16,128]{3,0,2,1:T(8,128)S(1)}, u32[]{:S(2)}, u32[]{:S(2)}) collective-permute-start(f32[32,1,16,128]{3,0,2,1:T(8,128)S(1)} %get-tuple-element.23), channel_id=1, source_target_pairs={{0,16},{16,32},{32,48},{48,64},{64,80},{80,96},{96,112},{112,128},... | collective-permute-start | bytes 786440 | tf_op jit(solution)/shard_map/ppermute | solution.py:40
  132.1 6.2 %collective-permute-start.11 = (f32[32,4,1,128]{3,0,2,1:T(8,128)S(1)}, f32[32,4,1,128]{3,0,2,1:T(8,128)S(1)}, u32[]{:S(2)}, u32[]{:S(2)}) collective-permute-start(f32[32,4,1,128]{3,0,2,1:T(8,128)S(1)} %get-tuple-element.22), channel_id=1, source_target_pairs={{0,1},{1,2},{2,3},{3,4},{4,5},{5,6},{6,7},{7,8},{8,9},{9,10},{10,1... | collective-permute-start | bytes 196616 | tf_op jit(solution)/shard_map/ppermute | solution.py:40
  134.5 7.8 %collective-permute-start.10 = (f32[32,4,1,128]{3,0,2,1:T(8,128)S(1)}, f32[32,4,1,128]{3,0,2,1:T(8,128)S(1)}, u32[]{:S(2)}, u32[]{:S(2)}) collective-permute-start(f32[32,4,1,128]{3,0,2,1:T(8,128)S(1)} %get-tuple-element.21), channel_id=1, source_target_pairs={{1,0},{2,1},{3,2},{4,3},{5,4},{6,5},{7,6},{8,7},{9,8},{10,9},{11,1... | collective-permute-start | bytes 196616 | tf_op jit(solution)/shard_map/ppermute | solution.py:41
  143.7 19.6 %collective-permute-start.12 = (f32[32,1,16,128]{3,0,2,1:T(8,128)S(1)}, f32[32,1,16,128]{3,0,2,1:T(8,128)S(1)}, u32[]{:S(2)}, u32[]{:S(2)}) collective-permute-start(f32[32,1,16,128]{3,0,2,1:T(8,128)S(1)} %get-tuple-element.20), channel_id=1, source_target_pairs={{16,0},{32,16},{48,32},{64,48},{80,64},{96,80},{112,96},{128,112},... | collective-permute-start | bytes 786440 | tf_op jit(solution)/shard_map/ppermute | solution.py:41
  145.7 17.7 %collective-permute-start.13 = (f32[32,1,16,128]{3,0,2,1:T(8,128)S(1)}, f32[32,1,16,128]{3,0,2,1:T(8,128)S(1)}, u32[]{:S(2)}, u32[]{:S(2)}) collective-permute-start(f32[32,1,16,128]{3,0,2,1:T(8,128)S(1)} %get-tuple-element.19), channel_id=1, source_target_pairs={{0,16},{16,32},{32,48},{48,64},{64,80},{80,96},{96,112},{112,128},... | collective-permute-start | bytes 786440 | tf_op jit(solution)/shard_map/ppermute | solution.py:40
  153.3 6.4 %collective-permute-start.15 = (f32[32,4,1,128]{3,0,2,1:T(8,128)S(1)}, f32[32,4,1,128]{3,0,2,1:T(8,128)S(1)}, u32[]{:S(2)}, u32[]{:S(2)}) collective-permute-start(f32[32,4,1,128]{3,0,2,1:T(8,128)S(1)} %get-tuple-element.18), channel_id=1, source_target_pairs={{0,1},{1,2},{2,3},{3,4},{4,5},{5,6},{6,7},{7,8},{8,9},{9,10},{10,1... | collective-permute-start | bytes 196616 | tf_op jit(solution)/shard_map/ppermute | solution.py:40
  155.7 7.7 %collective-permute-start.14 = (f32[32,4,1,128]{3,0,2,1:T(8,128)S(1)}, f32[32,4,1,128]{3,0,2,1:T(8,128)S(1)}, u32[]{:S(2)}, u32[]{:S(2)}) collective-permute-start(f32[32,4,1,128]{3,0,2,1:T(8,128)S(1)} %get-tuple-element.17), channel_id=1, source_target_pairs={{1,0},{2,1},{3,2},{4,3},{5,4},{6,5},{7,6},{8,7},{9,8},{10,9},{11,1... | collective-permute-start | bytes 196616 | tf_op jit(solution)/shard_map/ppermute | solution.py:41
  (7 other events, 9.8 us)

commit v3 on v2

--- a/solution.py
+++ b/solution.py
@@ -1,6 +1,8 @@
 import jax
 import jax.numpy as jnp
 from jax import lax
+from jax.experimental import pallas as pl
+from jax.experimental.pallas import tpu as pltpu
 from jax.sharding import PartitionSpec as P
 
 BIN_XY = 4
@@ -153,6 +155,66 @@
     return from_below, from_above
 
 
+def forces_kernel(own_ref, near_ref, occ_ref, out_ref):
+    rows = own_ref.shape[1]
+    lanes = own_ref.shape[-1]
+    layers = lanes // SLOTS
+    px = own_ref[0]
+    py = own_ref[1]
+    pz = own_ref[2]
+    lane = lax.broadcasted_iota(jnp.int32, px.shape, 1)
+    slot = lane % SLOTS
+    layer = lane // SLOTS
+
+    def body(offset_x, carry):
+        fx, fy, fz = carry
+        for offset_y in range(3):
+            row = [near_ref[plane, offset_x, offset_y : offset_y + rows, :] for plane in range(4)]
+            for offset_z in (-1, 0, 1):
+                if offset_z == 0:
+                    base = row
+                else:
+                    inside = (layer + offset_z >= 0) & (layer + offset_z < layers)
+                    base = [
+                        jnp.where(inside, pltpu.roll(part, (-offset_z * SLOTS) % lanes, 1), 0.0)
+                        for part in row
+                    ]
+                for turn in range(SLOTS):
+                    if turn == 0:
+                        other = base
+                    else:
+                        keep = slot + turn < SLOTS
+                        other = [
+                            jnp.where(keep, pltpu.roll(part, lanes - turn, 1), pltpu.roll(part, SLOTS - turn, 1))
+                            for part in base
+                        ]
+                    dx = px - other[0]
+                    dy = py - other[1]
+                    dz = pz - other[2]
+                    strength = other[3] * jnp.exp(-(dx * dx + dy * dy + dz * dz) / spread_sq)
+                    fx = fx + dx * strength
+                    fy = fy + dy * strength
+                    fz = fz + dz * strength
+        return fx, fy, fz
+
+    zero = jnp.zeros_like(px)
+    fx, fy, fz = lax.fori_loop(0, 3, body, (zero, zero, zero))
+    active = move_step * occ_ref[...]
+    out_ref[0] = active * fx
+    out_ref[1] = active * fy
+    out_ref[2] = active * fz
+
+
+def pallas_forces(points, bordered, occupancy):
+    planes, _, rows, lanes = points.shape
+    out = pl.pallas_call(
+        forces_kernel,
+        out_shape=jax.ShapeDtypeStruct((3, rows, lanes), jnp.float32),
+        cost_estimate=pl.CostEstimate(flops=9_000_000, transcendentals=450_000, bytes_accessed=120_000),
+    )(points[:, 0], bordered, occupancy[0].astype(jnp.float32))
+    return out.reshape(3, 1, rows, lanes)
+
+
 def on_device(
     field,
     rates,
@@ -207,7 +269,7 @@
 
     for _ in range(SUBSTEPS - 2):
         current = substep(current, source, rates, mixing)
-    displacement = pair_forces(points, bordered, occupancy)
+    displacement = pallas_forces(points, bordered, occupancy)
     return (current, displacement, arrived)
 
 

time: 169 us -> 146 us (0.86)
  local copies, waits for them, and re-layouts: 61.5 us -> 38 us
  Pallas kernels: 0 us -> 10.4 us
  other arithmetic: 25.5 us -> 16.5 us
    concatenate x9 -> x0, local copies, waits for them, and re-layouts: 10.8 us -> none  [the longest x3 6.88 us: pair_forces(): jnp.concatenate([boxed[:, offset_x:offset_x + bins_x, offset_y:offset_y +...]
    pallas_call x0 -> x1, Pallas kernels: none -> 10.4 us  [pallas_forces(): pl.pallas_call(forces_kernel, out_shape=jax.ShapeDtypeStruct((3, rows, la...]
    reduce_sum x3 -> x0, other arithmetic: 4.8 us -> none  [the longest x2 2.76 us: pair_forces(): force = force + jnp.sum(apart * strength[None], axis=-1)]
    sub x4 -> x0, local copies, waits for them, and re-layouts: 4.3 us -> none  [pair_forces(): apart = owned - nearby[:3, :, :, :, None, :]]
    mul x3 -> x0, local copies, waits for them, and re-layouts: 3.76 us -> none  [pair_forces(): nearby[3][:, :, :, None, :]]
    concatenate x3 -> x1, other arithmetic: 4.28 us -> 0.66 us  [on_device(): bordered = jnp.concatenate([points_low, row_points, points_high], axis=2)]
    unnamed x60 -> x40, local copies, waits for them, and re-layouts: 11 us -> 7.46 us
    reshape x8, local copies, waits for them, and re-layouts: 1.43 us -> 4.09 us  [unpack(): out.append(flat[row:row + rows].reshape(piece.shape))]
  transfers between devices with their start and end apart: 16 -> 16, of which waited for: 3 -> 3; matrix products, arithmetic and copies ran while one was open for 44% -> 32% of each run, Pallas kernels for 0% -> 7%
where the time goes in v3:
time: 146 us; the launch traced here: 144 us
  starting transfers between devices  58.1 us (40%)
  local copies, waits for them, and re-layouts  38 us (26%)
  other arithmetic  16.5 us (11%)
  Pallas kernels  10.4 us (7%)
  waiting for transfers between devices  10.3 us (7%)
  matrix products  9.34 us (6%)
    ppermute x5, starting transfers between devices, halos(): low = lax.ppermute(tail, axis, [(i, (i + 1) % count) for i in range(ends)])  26 us
    ppermute x3, starting transfers between devices, send_pair(): from_below = unpack(lax.ppermute(pack(upward), axis, up), upward)  15 us
    ppermute x5, starting transfers between devices, halos(): high = lax.ppermute(head, axis, [((i + 1) % count, i) for i in range(ends)])  10.8 us
    pallas_call x1, Pallas kernels, pallas_forces(): pl.pallas_call(forces_kernel, out_shape=jax.ShapeDtypeStruct((3, rows, la...  10.4 us
    mul x3, local copies, waits for them, and re-layouts, advance(): time_step * source  10.2 us
    ppermute x5, waiting for transfers between devices, halos(): high = lax.ppermute(head, axis, [((i + 1) % count, i) for i in range(ends)])  7.61 us
    unnamed x40, local copies, waits for them, and re-layouts  7.46 us
    dot_general x4, matrix products, advance(): jnp.dot(mixing, center.reshape(species, -1), precision=lax.Precision.HIGH...  7.18 us
  transfers between devices with their start and end apart: 16, of which 3 were waited for; matrix products, arithmetic and copies ran while one was open for 32% of the time, Pallas kernels for 7%

profile of v3, /device:TPU:119, one launch (start us, length us, event | category | flops | bytes accessed | tf_op | source)
XLA Modules:
  0.0 144.0 jit_solution(13865273186055855611)
XLA Ops:
  6.5 4.5 %collective-permute-start.1 = (f32[649,128]{1,0:T(8,128)}, f32[649,128]{1,0:T(8,128)S(1)}, u32[]{:S(2)}, u32[]{:S(2)}) collective-permute-start(f32[649,128]{1,0:T(8,128)} %get-tuple-element.44), channel_id=1, source_target_pairs={{0,16},{16,32},{32,48},{48,64},{64,80},{80,96},{96,112},{112,128},... | collective-permute-start | bytes 996872 | tf_op jit(solution)/shard_map/ppermute | solution.py:153
  11.0 2.3 %collective-permute-start = (f32[649,128]{1,0:T(8,128)}, f32[649,128]{1,0:T(8,128)}, u32[]{:S(2)}, u32[]{:S(2)}) collective-permute-start(f32[649,128]{1,0:T(8,128)} %get-tuple-element.43), channel_id=1, source_target_pairs={{16,0},{32,16},{48,32},{64,48},{80,64},{96,80},{112,96},{128,112},... | collective-permute-start | bytes 996872 | tf_op jit(solution)/shard_map/ppermute | solution.py:154
  14.1 4.2 %collective-permute-start.3 = (f32[163,128]{1,0:T(8,128)}, f32[163,128]{1,0:T(8,128)}, u32[]{:S(2)}, u32[]{:S(2)}) collective-permute-start(f32[163,128]{1,0:T(8,128)} %pad_maximum_fusion.42), channel_id=1, source_target_pairs={{0,1},{1,2},{2,3},{3,4},{4,5},{5,6},{6,7},{7,8},{8,9},{9,10},{10,1... | collective-permute-start | bytes 250376 | tf_op jit(solution)/shard_map/ppermute | solution.py:153
  18.9 1.9 %collective-permute-start.2 = (f32[163,128]{1,0:T(8,128)}, f32[163,128]{1,0:T(8,128)}, u32[]{:S(2)}, u32[]{:S(2)}) collective-permute-start(f32[163,128]{1,0:T(8,128)} %pad_maximum_fusion.41), channel_id=1, source_target_pairs={{1,0},{2,1},{3,2},{4,3},{5,4},{6,5},{7,6},{8,7},{9,8},{10,9},{11,1... | collective-permute-start | bytes 250376 | tf_op jit(solution)/shard_map/ppermute | solution.py:154
  21.8 2.2 %fusion.3 = f32[32,64,128]{2,0,1:T(8,128)S(1)} fusion(f32[32,64,16]{0,2,1:T(8,128)S(1)} %bitcast.138, f32[64,16]{1,0:T(8,128)S(1)} %convert_element_type.25, s32[64,16]{1,0:T(8,128)S(1)} %eq.10), kind=kOutput, calls=%fused_computation.31 | convolution fusion | flops 50855936 | bytes 1187840 | tf_op jit(solution)/shard_map/snk,nkc->snc/dot_general | solution.py:98
  24.0 2.7 %copy.42 = f32[32,64,128]{0,2,1:T(8,128)} copy(f32[32,64,128]{2,0,1:T(8,128)S(1)} %fusion.3) | data formatting | bytes 2097152 | tf_op jit(solution)/shard_map/mul | solution.py:84
  26.6 4.8 %copy.43 = f32[32,1,4,4,4,16,8]{0,6,5,4,3,2,1:T(8,128)} copy(f32[32,1,4,4,4,16,8]{0,6,4,2,5,3,1:T(8,128)} %bitcast.129) | data formatting | bytes 2097152 | tf_op jit(solution)/shard_map/mul | solution.py:84
  31.4 2.8 %copy.44 = f32[32,4,16,128]{3,0,2,1:T(8,128)S(1)} copy(f32[32,4,16,128]{0,3,2,1:T(8,128)} %bitcast.130) | data formatting | bytes 2097152 | tf_op jit(solution)/shard_map/mul | solution.py:84
  38.6 2.1 %fusion.5 = f32[32,4,16,128]{3,0,2,1:T(8,128)S(1)} fusion(f32[32,4,16,128]{3,0,2,1:T(8,128)S(1)} %copy.44, f32[32,4,16,128]{3,0,2,1:T(8,128)S(1)} %get-tuple-element.26, f32[32,1,1,128]{3,0,2,1:T(8,128)S(1)} %broadcast.42, f32[32,6,16,128]{3,0,2,1:T(8,128)S(1)} %get-tuple-element.32, f32[32,4,1,128]{3,0,2,1:T(8,128)S(1)} %copy.36, ...), kind=kOutput, calls=%fused_computation.34 | convolution fusion | flops 106168320 | bytes 6443136 | tf_op jit(solution)/shard_map/dot_general | solution.py:77
  42.9 2.9 %collective-permute-start.4 = (f32[32,1,16,128]{3,0,2,1:T(8,128)}, f32[32,1,16,128]{3,0,2,1:T(8,128)}, u32[]{:S(2)}, u32[]{:S(2)}) collective-permute-start(f32[32,1,16,128]{3,0,2,1:T(8,128)} %get-tuple-element.20), channel_id=1, source_target_pairs={{16,0},{32,16},{48,32},{64,48},{80,64},{96,80},{112,96},{128,112},... | collective-permute-start | bytes 786440 | tf_op jit(solution)/shard_map/ppermute | solution.py:43
  45.8 6.0 %collective-permute-start.5 = (f32[32,1,16,128]{3,0,2,1:T(8,128)}, f32[32,1,16,128]{3,0,2,1:T(8,128)}, u32[]{:S(2)}, u32[]{:S(2)}) collective-permute-start(f32[32,1,16,128]{3,0,2,1:T(8,128)} %get-tuple-element.19), channel_id=1, source_target_pairs={{0,16},{16,32},{32,48},{48,64},{64,80},{80,96},{96,112},{112,128},... | collective-permute-start | bytes 786440 | tf_op jit(solution)/shard_map/ppermute | solution.py:42
  60.0 1.4 pad_maximum_fusion.49
  61.5 1.4 pad_maximum_fusion.39
  62.9 6.3 %collective-permute-start.7 = (f32[222,128]{1,0:T(8,128)}, f32[222,128]{1,0:T(8,128)}, u32[]{:S(2)}, u32[]{:S(2)}) collective-permute-start(f32[222,128]{1,0:T(8,128)} %pad_maximum_fusion.39), channel_id=1, source_target_pairs={{0,1},{1,2},{2,3},{3,4},{4,5},{5,6},{6,7},{7,8},{8,9},{9,10},{10,1... | collective-permute-start | bytes 341000 | tf_op jit(solution)/shard_map/ppermute | solution.py:153
  71.5 2.1 %collective-permute-start.6 = (f32[222,128]{1,0:T(8,128)S(1)}, f32[222,128]{1,0:T(8,128)S(1)}, u32[]{:S(2)}, u32[]{:S(2)}) collective-permute-start(f32[222,128]{1,0:T(8,128)S(1)} %pad_maximum_fusion.38), channel_id=1, source_target_pairs={{1,0},{2,1},{3,2},{4,3},{5,4},{6,5},{7,6},{8,7},{9,8},{10,9},{11,1... | collective-permute-start | bytes 341000 | tf_op jit(solution)/shard_map/ppermute | solution.py:154
  73.6 1.7 %fusion = f32[4,8,64,128]{3,1,2,0:T(8,128)S(1)} fusion(f32[32,32]{1,0:T(8,128)S(1)} %copy-done, f32[4,8,64,128]{3,2,1,0:T(8,128)S(1)} %bitcast.135), kind=kOutput, calls=%fused_computation.27 | convolution fusion | flops 100925440 | bytes 2101248 | tf_op jit(solution)/shard_map/dot_general | solution.py:77
  77.0 2.7 %collective-permute-done.6 = f32[222,128]{1,0:T(8,128)S(1)} collective-permute-done((f32[222,128]{1,0:T(8,128)S(1)}, f32[222,128]{1,0:T(8,128)S(1)}, u32[]{:S(2)}, u32[]{:S(2)}) %collective-permute-start.6) | collective-permute-done | bytes 113696 | tf_op jit(solution)/shard_map/ppermute | solution.py:154
  86.1 10.4 %shard_map.121 = f32[3,4,256]{2,1,0:T(4,128)} custom-call(f32[4,4,256]{2,1,0:T(4,128)} %get-tuple-element.41.own_ref, f32[4,3,6,256]{3,2,1,0:T(8,128)} %pad_maximum_fusion.40.near_ref, f32[4,256]{1,0:T(4,128)} %get-tuple-element.45.occ_ref), custom_call_target="tpu_custom_call" | custom-call | flops 9000000 | bytes 120000 | tf_op jit(solution)/shard_map/pallas_call | solution.py:210
  96.5 2.4 %fusion.25 = f32[32,4,16,128]{3,0,2,1:T(8,128)S(1)} fusion(f32[32,4,16,128]{3,0,2,1:T(8,128)S(1)} %copy.44, f32[32,4,16,128]{3,0,2,1:T(8,128)S(1)} %fusion.5, f32[32,1,1,128]{3,0,2,1:T(8,128)S(1)} %broadcast.42, f32[32,1,16,128]{3,0,2,1:T(8,128)} %collective-permute-done.4, f32[32,1,16,128]{3,0,2,1:T(8,128)} %collective-permute-done.5, ...), kind=kLoop, calls=%fused_computation.54 | loop fusion | flops 6291456 | bytes 4866176 | tf_op jit(solution)/shard_map/add | solution.py:81
  99.0 1.9 %collective-permute-start.8 = (f32[32,1,16,128]{3,0,2,1:T(8,128)S(1)}, f32[32,1,16,128]{3,0,2,1:T(8,128)S(1)}, u32[]{:S(2)}, u32[]{:S(2)}) collective-permute-start(f32[32,1,16,128]{3,0,2,1:T(8,128)S(1)} %get-tuple-element.16), channel_id=1, source_target_pairs={{16,0},{32,16},{48,32},{64,48},{80,64},{96,80},{112,96},{128,112},... | collective-permute-start | bytes 786440 | tf_op jit(solution)/shard_map/ppermute | solution.py:43
  100.9 7.0 %collective-permute-start.9 = (f32[32,1,16,128]{3,0,2,1:T(8,128)S(1)}, f32[32,1,16,128]{3,0,2,1:T(8,128)S(1)}, u32[]{:S(2)}, u32[]{:S(2)}) collective-permute-start(f32[32,1,16,128]{3,0,2,1:T(8,128)S(1)} %get-tuple-element.15), channel_id=1, source_target_pairs={{0,16},{16,32},{32,48},{48,64},{64,80},{80,96},{96,112},{112,128},... | collective-permute-start | bytes 786440 | tf_op jit(solution)/shard_map/ppermute | solution.py:42
  108.5 3.6 %collective-permute-start.11 = (f32[32,4,1,128]{3,0,2,1:T(8,128)S(1)}, f32[32,4,1,128]{3,0,2,1:T(8,128)S(1)}, u32[]{:S(2)}, u32[]{:S(2)}) collective-permute-start(f32[32,4,1,128]{3,0,2,1:T(8,128)S(1)} %get-tuple-element.14), channel_id=1, source_target_pairs={{0,1},{1,2},{2,3},{3,4},{4,5},{5,6},{6,7},{7,8},{8,9},{9,10},{10,1... | collective-permute-start | bytes 196616 | tf_op jit(solution)/shard_map/ppermute | solution.py:42
  112.2 1.9 %collective-permute-start.10 = (f32[32,4,1,128]{3,0,2,1:T(8,128)S(1)}, f32[32,4,1,128]{3,0,2,1:T(8,128)S(1)}, u32[]{:S(2)}, u32[]{:S(2)}) collective-permute-start(f32[32,4,1,128]{3,0,2,1:T(8,128)S(1)} %get-tuple-element.13), channel_id=1, source_target_pairs={{1,0},{2,1},{3,2},{4,3},{5,4},{6,5},{7,6},{8,7},{9,8},{10,9},{11,1... | collective-permute-start | bytes 196616 | tf_op jit(solution)/shard_map/ppermute | solution.py:43
  114.1 1.7 %fusion.1 = f32[4,8,64,128]{3,1,2,0:T(8,128)S(1)} fusion(f32[32,32]{1,0:T(8,128)S(1)} %copy-done, f32[4,8,64,128]{3,2,1,0:T(8,128)S(1)} %bitcast.136), kind=kOutput, calls=%fused_computation.28 | convolution fusion | flops 100925440 | bytes 2101248 | tf_op jit(solution)/shard_map/dot_general | solution.py:77
  116.0 4.0 %collective-permute-done.10 = f32[32,4,1,128]{3,0,2,1:T(8,128)S(1)} collective-permute-done((f32[32,4,1,128]{3,0,2,1:T(8,128)S(1)}, f32[32,4,1,128]{3,0,2,1:T(8,128)S(1)}, u32[]{:S(2)}, u32[]{:S(2)}) %collective-permute-start.10) | collective-permute-done | bytes 65568 | tf_op jit(solution)/shard_map/ppermute | solution.py:43
  121.4 1.9 %collective-permute-start.12 = (f32[32,1,16,128]{3,0,2,1:T(8,128)S(1)}, f32[32,1,16,128]{3,0,2,1:T(8,128)S(1)}, u32[]{:S(2)}, u32[]{:S(2)}) collective-permute-start(f32[32,1,16,128]{3,0,2,1:T(8,128)S(1)} %get-tuple-element.12), channel_id=1, source_target_pairs={{16,0},{32,16},{48,32},{64,48},{80,64},{96,80},{112,96},{128,112},... | collective-permute-start | bytes 786440 | tf_op jit(solution)/shard_map/ppermute | solution.py:43
  123.3 7.0 %collective-permute-start.13 = (f32[32,1,16,128]{3,0,2,1:T(8,128)S(1)}, f32[32,1,16,128]{3,0,2,1:T(8,128)S(1)}, u32[]{:S(2)}, u32[]{:S(2)}) collective-permute-start(f32[32,1,16,128]{3,0,2,1:T(8,128)S(1)} %get-tuple-element.11), channel_id=1, source_target_pairs={{0,16},{16,32},{32,48},{48,64},{64,80},{80,96},{96,112},{112,128},... | collective-permute-start | bytes 786440 | tf_op jit(solution)/shard_map/ppermute | solution.py:42
  130.9 2.4 %collective-permute-start.15 = (f32[32,4,1,128]{3,0,2,1:T(8,128)S(1)}, f32[32,4,1,128]{3,0,2,1:T(8,128)S(1)}, u32[]{:S(2)}, u32[]{:S(2)}) collective-permute-start(f32[32,4,1,128]{3,0,2,1:T(8,128)S(1)} %get-tuple-element.10), channel_id=1, source_target_pairs={{0,1},{1,2},{2,3},{3,4},{4,5},{5,6},{6,7},{7,8},{8,9},{9,10},{10,1... | collective-permute-start | bytes 196616 | tf_op jit(solution)/shard_map/ppermute | solution.py:42
  133.3 2.2 %collective-permute-start.14 = (f32[32,4,1,128]{3,0,2,1:T(8,128)S(1)}, f32[32,4,1,128]{3,0,2,1:T(8,128)S(1)}, u32[]{:S(2)}, u32[]{:S(2)}) collective-permute-start(f32[32,4,1,128]{3,0,2,1:T(8,128)S(1)} %get-tuple-element.9), channel_id=1, source_target_pairs={{1,0},{2,1},{3,2},{4,3},{5,4},{6,5},{7,6},{8,7},{9,8},{10,9},{11,1... | collective-permute-start | bytes 196616 | tf_op jit(solution)/shard_map/ppermute | solution.py:43
  135.5 1.7 %fusion.2 = f32[4,8,64,128]{3,1,2,0:T(8,128)S(1)} fusion(f32[32,32]{1,0:T(8,128)S(1)} %copy-done, f32[4,8,64,128]{3,2,1,0:T(8,128)S(1)} %bitcast.137), kind=kOutput, calls=%fused_computation.29 | convolution fusion | flops 100925440 | bytes 2101248 | tf_op jit(solution)/shard_map/dot_general | solution.py:77
  137.4 3.6 %collective-permute-done.14 = f32[32,4,1,128]{3,0,2,1:T(8,128)S(1)} collective-permute-done((f32[32,4,1,128]{3,0,2,1:T(8,128)S(1)}, f32[32,4,1,128]{3,0,2,1:T(8,128)S(1)}, u32[]{:S(2)}, u32[]{:S(2)}) %collective-permute-start.14) | collective-permute-done | bytes 65568 | tf_op jit(solution)/shard_map/ppermute | solution.py:43
  142.4 1.6 %copy.58 = f32[32,4,16,128]{3,2,1,0:T(8,128)} copy(f32[32,4,16,128]{3,0,2,1:T(8,128)S(1)} %fusion.47) | data formatting | bytes 2097152
  (109 shorter events, 37.6 us)
Async XLA Ops:
  0.6 38.0 %copy-start = (f32[32,32]{1,0:T(8,128)S(1)}, f32[32,32]{1,0:T(8,128)}, u32[]{:S(2)}) copy-start(f32[32,32]{1,0:T(8,128)} %param.12) | copy-start | bytes 12292
  1.4 2.0 %copy-start.6 = (f32[1,1,4,256]{3,2,1,0:T(4,128)}, f32[1,1,4,256]{3,2,1,0:T(4,128)S(1)}, u32[]{:S(2)}) copy-start(f32[1,1,4,256]{3,2,1,0:T(4,128)S(1)} %multiply_bitcast_fusion) | copy-start | bytes 12292
  3.4 9.9 %copy-start.1 = (f32[32,4,16,128]{3,2,1,0:T(8,128)S(1)}, f32[32,4,16,128]{3,2,1,0:T(8,128)}, u32[]{:S(2)}) copy-start(f32[32,4,16,128]{3,2,1,0:T(8,128)} %param.10) | copy-start | bytes 3145732
  4.4 16.4 %copy-start.8 = (s32[1,4,256]{2,1,0:T(4,128)S(1)}, s32[1,4,256]{2,1,0:T(4,128)}, u32[]{:S(2)}) copy-start(s32[1,4,256]{2,1,0:T(4,128)} %param.16) | copy-start | bytes 12292
  4.5 17.0 %copy-start.4 = (f32[32,1,4,256]{3,2,1,0:T(4,128)S(1)}, f32[32,1,4,256]{3,2,1,0:T(4,128)}, u32[]{:S(2)}) copy-start(f32[32,1,4,256]{3,2,1,0:T(4,128)} %param.13) | copy-start | bytes 393220
  5.6 16.1 %copy-start.11 = (s32[1,4,256]{2,1,0:T(4,128)S(1)}, s32[1,4,256]{2,1,0:T(4,128)}, u32[]{:S(2)}) copy-start(s32[1,4,256]{2,1,0:T(4,128)} %param.17) | copy-start | bytes 12292
  6.5 30.3 %collective-permute-start.1 = (f32[649,128]{1,0:T(8,128)}, f32[649,128]{1,0:T(8,128)S(1)}, u32[]{:S(2)}, u32[]{:S(2)}) collective-permute-start(f32[649,128]{1,0:T(8,128)} %get-tuple-element.44), channel_id=1, source_target_pairs={{0,16},{16,32},{32,48},{48,64},{64,80},{80,96},{96,112},{112,128},... | collective-permute-start | bytes 996872 | tf_op jit(solution)/shard_map/ppermute | solution.py:153
  11.0 26.5 %collective-permute-start = (f32[649,128]{1,0:T(8,128)}, f32[649,128]{1,0:T(8,128)}, u32[]{:S(2)}, u32[]{:S(2)}) collective-permute-start(f32[649,128]{1,0:T(8,128)} %get-tuple-element.43), channel_id=1, source_target_pairs={{16,0},{32,16},{48,32},{64,48},{80,64},{96,80},{112,96},{128,112},... | collective-permute-start | bytes 996872 | tf_op jit(solution)/shard_map/ppermute | solution.py:154
  14.1 21.0 %collective-permute-start.3 = (f32[163,128]{1,0:T(8,128)}, f32[163,128]{1,0:T(8,128)}, u32[]{:S(2)}, u32[]{:S(2)}) collective-permute-start(f32[163,128]{1,0:T(8,128)} %pad_maximum_fusion.42), channel_id=1, source_target_pairs={{0,1},{1,2},{2,3},{3,4},{4,5},{5,6},{6,7},{7,8},{8,9},{9,10},{10,1... | collective-permute-start | bytes 250376 | tf_op jit(solution)/shard_map/ppermute | solution.py:153
  18.9 17.0 %collective-permute-start.2 = (f32[163,128]{1,0:T(8,128)}, f32[163,128]{1,0:T(8,128)}, u32[]{:S(2)}, u32[]{:S(2)}) collective-permute-start(f32[163,128]{1,0:T(8,128)} %pad_maximum_fusion.41), channel_id=1, source_target_pairs={{1,0},{2,1},{3,2},{4,3},{5,4},{6,5},{7,6},{8,7},{9,8},{10,9},{11,1... | collective-permute-start | bytes 250376 | tf_op jit(solution)/shard_map/ppermute | solution.py:154
  36.9 1.7 %copy-start.9 = (f32[32]{0:T(128)S(1)}, f32[32]{0:T(128)}, u32[]{:S(2)}) copy-start(f32[32]{0:T(128)} %param.11) | copy-start | bytes 388
  42.9 53.6 %collective-permute-start.4 = (f32[32,1,16,128]{3,0,2,1:T(8,128)}, f32[32,1,16,128]{3,0,2,1:T(8,128)}, u32[]{:S(2)}, u32[]{:S(2)}) collective-permute-start(f32[32,1,16,128]{3,0,2,1:T(8,128)} %get-tuple-element.20), channel_id=1, source_target_pairs={{16,0},{32,16},{48,32},{64,48},{80,64},{96,80},{112,96},{128,112},... | collective-permute-start | bytes 786440 | tf_op jit(solution)/shard_map/ppermute | solution.py:43
  45.8 50.7 %collective-permute-start.5 = (f32[32,1,16,128]{3,0,2,1:T(8,128)}, f32[32,1,16,128]{3,0,2,1:T(8,128)}, u32[]{:S(2)}, u32[]{:S(2)}) collective-permute-start(f32[32,1,16,128]{3,0,2,1:T(8,128)} %get-tuple-element.19), channel_id=1, source_target_pairs={{0,16},{16,32},{32,48},{48,64},{64,80},{80,96},{96,112},{112,128},... | collective-permute-start | bytes 786440 | tf_op jit(solution)/shard_map/ppermute | solution.py:42
  62.9 12.6 %collective-permute-start.7 = (f32[222,128]{1,0:T(8,128)}, f32[222,128]{1,0:T(8,128)}, u32[]{:S(2)}, u32[]{:S(2)}) collective-permute-start(f32[222,128]{1,0:T(8,128)} %pad_maximum_fusion.39), channel_id=1, source_target_pairs={{0,1},{1,2},{2,3},{3,4},{4,5},{5,6},{6,7},{7,8},{8,9},{9,10},{10,1... | collective-permute-start | bytes 341000 | tf_op jit(solution)/shard_map/ppermute | solution.py:153
  71.5 8.2 %collective-permute-start.6 = (f32[222,128]{1,0:T(8,128)S(1)}, f32[222,128]{1,0:T(8,128)S(1)}, u32[]{:S(2)}, u32[]{:S(2)}) collective-permute-start(f32[222,128]{1,0:T(8,128)S(1)} %pad_maximum_fusion.38), channel_id=1, source_target_pairs={{1,0},{2,1},{3,2},{4,3},{5,4},{6,5},{7,6},{8,7},{9,8},{10,9},{11,1... | collective-permute-start | bytes 341000 | tf_op jit(solution)/shard_map/ppermute | solution.py:154
  75.3 10.1 %copy-start.2 = (f32[4,1,4,256]{3,2,1,0:T(4,128)S(1)}, f32[4,1,4,256]{3,2,1,0:T(4,128)}, u32[]{:S(2)}) copy-start(f32[4,1,4,256]{3,2,1,0:T(4,128)} %reshape.158) | copy-start | bytes 49156
  75.3 10.1 %copy-start.3 = (f32[4,1,4,256]{3,2,1,0:T(4,128)S(1)}, f32[4,1,4,256]{3,2,1,0:T(4,128)}, u32[]{:S(2)}) copy-start(f32[4,1,4,256]{3,2,1,0:T(4,128)} %reshape.157) | copy-start | bytes 49156
  75.3 10.1 %copy-start.5 = (f32[3,1,4,256]{3,2,1,0:T(4,128)S(1)}, f32[3,1,4,256]{3,2,1,0:T(4,128)}, u32[]{:S(2)}) copy-start(f32[3,1,4,256]{3,2,1,0:T(4,128)} %param.14) | copy-start | bytes 36868
  75.3 10.1 %copy-start.7 = (f32[1,1,4,256]{3,2,1,0:T(4,128)S(1)}, f32[1,1,4,256]{3,2,1,0:T(4,128)}, u32[]{:S(2)}) copy-start(f32[1,1,4,256]{3,2,1,0:T(4,128)} %copy-done.6) | copy-start | bytes 12292
  75.5 21.0 %copy-start.10 = (f32[32]{0:T(128)S(1)}, f32[32]{0:T(128)}, u32[]{:S(2)}) copy-start(f32[32]{0:T(128)} %param.11) | copy-start | bytes 388
  99.0 21.0 %collective-permute-start.8 = (f32[32,1,16,128]{3,0,2,1:T(8,128)S(1)}, f32[32,1,16,128]{3,0,2,1:T(8,128)S(1)}, u32[]{:S(2)}, u32[]{:S(2)}) collective-permute-start(f32[32,1,16,128]{3,0,2,1:T(8,128)S(1)} %get-tuple-element.16), channel_id=1, source_target_pairs={{16,0},{32,16},{48,32},{64,48},{80,64},{96,80},{112,96},{128,112},... | collective-permute-start | bytes 786440 | tf_op jit(solution)/shard_map/ppermute | solution.py:43
  100.9 19.1 %collective-permute-start.9 = (f32[32,1,16,128]{3,0,2,1:T(8,128)S(1)}, f32[32,1,16,128]{3,0,2,1:T(8,128)S(1)}, u32[]{:S(2)}, u32[]{:S(2)}) collective-permute-start(f32[32,1,16,128]{3,0,2,1:T(8,128)S(1)} %get-tuple-element.15), channel_id=1, source_target_pairs={{0,16},{16,32},{32,48},{48,64},{64,80},{80,96},{96,112},{112,128},... | collective-permute-start | bytes 786440 | tf_op jit(solution)/shard_map/ppermute | solution.py:42
  108.5 7.5 %collective-permute-start.11 = (f32[32,4,1,128]{3,0,2,1:T(8,128)S(1)}, f32[32,4,1,128]{3,0,2,1:T(8,128)S(1)}, u32[]{:S(2)}, u32[]{:S(2)}) collective-permute-start(f32[32,4,1,128]{3,0,2,1:T(8,128)S(1)} %get-tuple-element.14), channel_id=1, source_target_pairs={{0,1},{1,2},{2,3},{3,4},{4,5},{5,6},{6,7},{7,8},{8,9},{9,10},{10,1... | collective-permute-start | bytes 196616 | tf_op jit(solution)/shard_map/ppermute | solution.py:42
  112.2 7.8 %collective-permute-start.10 = (f32[32,4,1,128]{3,0,2,1:T(8,128)S(1)}, f32[32,4,1,128]{3,0,2,1:T(8,128)S(1)}, u32[]{:S(2)}, u32[]{:S(2)}) collective-permute-start(f32[32,4,1,128]{3,0,2,1:T(8,128)S(1)} %get-tuple-element.13), channel_id=1, source_target_pairs={{1,0},{2,1},{3,2},{4,3},{5,4},{6,5},{7,6},{8,7},{9,8},{10,9},{11,1... | collective-permute-start | bytes 196616 | tf_op jit(solution)/shard_map/ppermute | solution.py:43
  121.4 19.6 %collective-permute-start.12 = (f32[32,1,16,128]{3,0,2,1:T(8,128)S(1)}, f32[32,1,16,128]{3,0,2,1:T(8,128)S(1)}, u32[]{:S(2)}, u32[]{:S(2)}) collective-permute-start(f32[32,1,16,128]{3,0,2,1:T(8,128)S(1)} %get-tuple-element.12), channel_id=1, source_target_pairs={{16,0},{32,16},{48,32},{64,48},{80,64},{96,80},{112,96},{128,112},... | collective-permute-start | bytes 786440 | tf_op jit(solution)/shard_map/ppermute | solution.py:43
  123.3 17.7 %collective-permute-start.13 = (f32[32,1,16,128]{3,0,2,1:T(8,128)S(1)}, f32[32,1,16,128]{3,0,2,1:T(8,128)S(1)}, u32[]{:S(2)}, u32[]{:S(2)}) collective-permute-start(f32[32,1,16,128]{3,0,2,1:T(8,128)S(1)} %get-tuple-element.11), channel_id=1, source_target_pairs={{0,16},{16,32},{32,48},{48,64},{64,80},{80,96},{96,112},{112,128},... | collective-permute-start | bytes 786440 | tf_op jit(solution)/shard_map/ppermute | solution.py:42
  130.9 6.4 %collective-permute-start.15 = (f32[32,4,1,128]{3,0,2,1:T(8,128)S(1)}, f32[32,4,1,128]{3,0,2,1:T(8,128)S(1)}, u32[]{:S(2)}, u32[]{:S(2)}) collective-permute-start(f32[32,4,1,128]{3,0,2,1:T(8,128)S(1)} %get-tuple-element.10), channel_id=1, source_target_pairs={{0,1},{1,2},{2,3},{3,4},{4,5},{5,6},{6,7},{7,8},{8,9},{9,10},{10,1... | collective-permute-start | bytes 196616 | tf_op jit(solution)/shard_map/ppermute | solution.py:42
  133.3 7.7 %collective-permute-start.14 = (f32[32,4,1,128]{3,0,2,1:T(8,128)S(1)}, f32[32,4,1,128]{3,0,2,1:T(8,128)S(1)}, u32[]{:S(2)}, u32[]{:S(2)}) collective-permute-start(f32[32,4,1,128]{3,0,2,1:T(8,128)S(1)} %get-tuple-element.9), channel_id=1, source_target_pairs={{1,0},{2,1},{3,2},{4,3},{5,4},{6,5},{7,6},{8,7},{9,8},{10,9},{11,1... | collective-permute-start | bytes 196616 | tf_op jit(solution)/shard_map/ppermute | solution.py:43

commit v4 on v3

--- a/solution.py
+++ b/solution.py
@@ -1,3 +1,5 @@
+import functools
+
 import jax
 import jax.numpy as jnp
 from jax import lax
@@ -132,8 +134,16 @@
     return (move_step * active * force).reshape(3, bins_x, bins_y, lanes)
 
 
+def storage_order(piece):
+    if piece.ndim == 4 and piece.shape[0] > 4:
+        return (1, 2, 0, 3)
+    return tuple(range(piece.ndim))
+
+
 def pack(pieces):
-    return jnp.concatenate([piece.reshape(-1, 128) for piece in pieces], axis=0)
+    return jnp.concatenate(
+        [jnp.transpose(piece, storage_order(piece)).reshape(-1, 128) for piece in pieces], axis=0
+    )
 
 
 def unpack(flat, pieces):
@@ -141,7 +151,9 @@
     row = 0
     for piece in pieces:
         rows = piece.size // 128
-        out.append(flat[row : row + rows].reshape(piece.shape))
+        order = storage_order(piece)
+        stored = flat[row : row + rows].reshape(tuple(piece.shape[axis] for axis in order))
+        out.append(jnp.transpose(stored, tuple(order.index(axis) for axis in range(piece.ndim))))
         row += rows
     return out
 
@@ -150,9 +162,9 @@
     count = lax.axis_size(axis)
     up = [(i, i + 1) for i in range(count - 1)]
     down = [(i + 1, i) for i in range(count - 1)]
-    from_below = unpack(lax.ppermute(pack(upward), axis, up), upward)
-    from_above = unpack(lax.ppermute(pack(downward), axis, down), downward)
-    return from_below, from_above
+    below = lax.ppermute(pack(upward), axis, up)
+    above = lax.ppermute(pack(downward), axis, down)
+    return unpack(below, upward), unpack(above, downward), below, above
 
 
 def forces_kernel(own_ref, near_ref, occ_ref, out_ref):
@@ -215,6 +227,32 @@
     return out.reshape(3, 1, rows, lanes)
 
 
+def arrived_kernel(starts, state, x_below, x_above, side_below, side_above, corner_below, corner_above, out_ref):
+    along_x, beside, corner = starts
+    span = state
+
+    def rows(ref, first):
+        return ref[first : first + span, :]
+
+    out_ref[0] = rows(corner_above, corner)
+    out_ref[1] = rows(x_above, along_x + span)
+    out_ref[2] = rows(corner_below, corner)
+    out_ref[3] = rows(side_above, beside)
+    out_ref[4] = rows(side_below, beside)
+    out_ref[5] = rows(corner_above, corner + span)
+    out_ref[6] = rows(x_below, along_x + span)
+    out_ref[7] = rows(corner_below, corner + span)
+
+
+def gather_arrived(x_flats, side_flats, corner_flats, along_x, beside, corner, shape):
+    state, lanes = shape
+    return pl.pallas_call(
+        functools.partial(arrived_kernel, (along_x, beside, corner), state),
+        out_shape=jax.ShapeDtypeStruct((8, state, lanes), jnp.float32),
+        cost_estimate=pl.CostEstimate(flops=0, transcendentals=0, bytes_accessed=300_000),
+    )(*x_flats, *side_flats, *corner_flats)
+
+
 def on_device(
     field,
     rates,
@@ -233,12 +271,12 @@
     source = deposit(secretion, occupancy, offsets)
     current = field
 
-    (x_low, points_low, moved_up), (x_high, points_high, moved_down) = send_pair(
+    (x_low, points_low, moved_up), (x_high, points_high, moved_down), *x_flats = send_pair(
         "gx",
         [current[:, -1:], points, payload[5:8]],
         [current[:, :1], points, payload[0:3]],
     )
-    (y_low, beside_up), (y_high, beside_down) = send_pair(
+    (y_low, beside_up), (y_high, beside_down), *side_flats = send_pair(
         "gy",
         [current[:, :, -1:], payload[4:5]],
         [current[:, :, :1], payload[3:4]],
@@ -247,24 +285,23 @@
 
     row_points = jnp.concatenate([points_low, points, points_high], axis=1)
     x_low, x_high = halos(current, "gx", 1)
-    (y_low, points_low, corner_up), (y_high, points_high, corner_down) = send_pair(
+    (y_low, points_low, corner_up), (y_high, points_high, corner_down), *corner_flats = send_pair(
         "gy",
         [current[:, :, -1:], row_points[:, :, -1:], jnp.stack([moved_down[2], moved_up[2]])],
         [current[:, :, :1], row_points[:, :, :1], jnp.stack([moved_down[0], moved_up[0]])],
     )
     current = advance(framed(current, x_low, x_high, y_low, y_high), source, rates, mixing)
     bordered = jnp.concatenate([points_low, row_points, points_high], axis=2)
-    arrived = jnp.stack(
-        [
-            corner_down[0],
-            moved_down[1],
-            corner_up[0],
-            beside_down[0],
-            beside_up[0],
-            corner_down[1],
-            moved_up[1],
-            corner_up[1],
-        ]
+    field_rows = x_low.size // 128
+    side_rows = y_low.size // 128
+    arrived = gather_arrived(
+        x_flats,
+        side_flats,
+        corner_flats,
+        field_rows + points.size // 128,
+        side_rows,
+        side_rows + points_low.size // 128,
+        payload.shape[1:],
     )
 
     for _ in range(SUBSTEPS - 2):

time: 146 us -> 144 us (0.986)
  the two profiles are of different devices: /device:TPU:119 before, /device:TPU:120 now
where the time goes in v4:
time: 144 us; the launch traced here: 142 us
  starting transfers between devices  68.9 us (48%)
  local copies, waits for them, and re-layouts  33.5 us (23%)
  other arithmetic  16.2 us (11%)
  Pallas kernels  12.3 us (9%)
  matrix products  9.31 us (6%)
    ppermute x5, starting transfers between devices, halos(): low = lax.ppermute(tail, axis, [(i, (i + 1) % count) for i in range(ends)])  26.4 us
    ppermute x5, starting transfers between devices, halos(): high = lax.ppermute(head, axis, [((i + 1) % count, i) for i in range(ends)])  17.5 us
    ppermute x3, starting transfers between devices, send_pair(): above = lax.ppermute(pack(downward), axis, down)  14.8 us
    pallas_call x1, Pallas kernels, pallas_forces(): pl.pallas_call(forces_kernel, out_shape=jax.ShapeDtypeStruct((3, rows, la...  10.4 us
    mul x3, local copies, waits for them, and re-layouts, advance(): time_step * source  10.2 us
    ppermute x3, starting transfers between devices, send_pair(): below = lax.ppermute(pack(upward), axis, up)  10.1 us
    unnamed x37, local copies, waits for them, and re-layouts  8.05 us
    slice x10, local copies, waits for them, and re-layouts, unpack(): flat[row:row + rows].reshape(tuple((piece.shape[axis] for axis in order)))  7.31 us
  transfers between devices with their start and end apart: 16, of which 1 were waited for; matrix products, arithmetic and copies ran while one was open for 28% of the time, Pallas kernels for 9%

profile of v4, /device:TPU:120, one launch (start us, length us, event | category | flops | bytes accessed | tf_op | source)
XLA Modules:
  0.0 141.7 jit_solution(2417422332554438246)
XLA Ops:
  7.3 3.1 %collective-permute-start = (f32[649,128]{1,0:T(8,128)}, f32[649,128]{1,0:T(8,128)S(1)}, u32[]{:S(2)}, u32[]{:S(2)}) collective-permute-start(f32[649,128]{1,0:T(8,128)} %get-tuple-element.38), channel_id=1, source_target_pairs={{16,0},{32,16},{48,32},{64,48},{80,64},{96,80},{112,96},{128,112},... | collective-permute-start | bytes 996872 | tf_op jit(solution)/shard_map/ppermute | solution.py:166
  10.4 6.3 %collective-permute-start.1 = (f32[649,128]{1,0:T(8,128)}, f32[649,128]{1,0:T(8,128)}, u32[]{:S(2)}, u32[]{:S(2)}) collective-permute-start(f32[649,128]{1,0:T(8,128)} %get-tuple-element.37), channel_id=1, source_target_pairs={{0,16},{16,32},{32,48},{48,64},{64,80},{80,96},{96,112},{112,128},... | collective-permute-start | bytes 996872 | tf_op jit(solution)/shard_map/ppermute | solution.py:165
  17.5 1.9 %collective-permute-start.3 = (f32[163,128]{1,0:T(8,128)}, f32[163,128]{1,0:T(8,128)}, u32[]{:S(2)}, u32[]{:S(2)}) collective-permute-start(f32[163,128]{1,0:T(8,128)} %pad_maximum_fusion.46), channel_id=1, source_target_pairs={{0,1},{1,2},{2,3},{3,4},{4,5},{5,6},{6,7},{7,8},{8,9},{9,10},{10,1... | collective-permute-start | bytes 250376 | tf_op jit(solution)/shard_map/ppermute | solution.py:165
  20.1 5.7 %collective-permute-start.2 = (f32[163,128]{1,0:T(8,128)}, f32[163,128]{1,0:T(8,128)}, u32[]{:S(2)}, u32[]{:S(2)}) collective-permute-start(f32[163,128]{1,0:T(8,128)} %pad_maximum_fusion.45), channel_id=1, source_target_pairs={{1,0},{2,1},{3,2},{4,3},{5,4},{6,5},{7,6},{8,7},{9,8},{10,9},{11,1... | collective-permute-start | bytes 250376 | tf_op jit(solution)/shard_map/ppermute | solution.py:166
  26.9 2.2 %fusion.3 = f32[32,64,128]{2,0,1:T(8,128)S(1)} fusion(f32[32,64,16]{0,2,1:T(8,128)S(1)} %bitcast.140, f32[64,16]{1,0:T(8,128)S(1)} %convert_element_type.25, s32[64,16]{1,0:T(8,128)S(1)} %eq.10), kind=kOutput, calls=%fused_computation.31 | convolution fusion | flops 50855936 | bytes 1187840 | tf_op jit(solution)/shard_map/snk,nkc->snc/dot_general | solution.py:100
  29.0 1.6 %copy.49 = f32[32,4,16,128]{3,0,2,1:T(8,128)} copy(f32[32,4,16,128]{3,2,1,0:T(8,128)S(1)} %copy-done.1) | data formatting | bytes 2097152 | tf_op args[0]
  30.6 2.7 %copy.52 = f32[32,64,128]{0,2,1:T(8,128)} copy(f32[32,64,128]{2,0,1:T(8,128)S(1)} %fusion.3) | data formatting | bytes 2097152 | tf_op jit(solution)/shard_map/mul | solution.py:86
  33.2 4.8 %copy.53 = f32[32,1,4,4,4,16,8]{0,6,5,4,3,2,1:T(8,128)} copy(f32[32,1,4,4,4,16,8]{0,6,4,2,5,3,1:T(8,128)} %bitcast.131) | data formatting | bytes 2097152 | tf_op jit(solution)/shard_map/mul | solution.py:86
  38.0 2.8 %copy.54 = f32[32,4,16,128]{3,0,2,1:T(8,128)S(1)} copy(f32[32,4,16,128]{0,3,2,1:T(8,128)} %bitcast.132) | data formatting | bytes 2097152 | tf_op jit(solution)/shard_map/mul | solution.py:86
  44.6 2.1 %fusion.5 = f32[32,4,16,128]{3,0,2,1:T(8,128)S(1)} fusion(f32[32,4,16,128]{3,0,2,1:T(8,128)S(1)} %copy.54, f32[32,4,16,128]{3,0,2,1:T(8,128)S(1)} %copy-done.3, f32[32,1,1,128]{3,0,2,1:T(8,128)S(1)} %broadcast.42, f32[32,1,16,128]{3,0,2,1:T(8,128)S(1)} %bitcast.146, f32[32,1,16,128]{3,0,2,1:T(8,128)S(1)} %bitcast.147, f32[32,4,1,128]{3,0,2,1:T(8,128)S(1)} %bitcast.156, ...), kind=kOutput, calls=%fused_computation.34 | convolution fusion | flops 107216896 | bytes 4870272 | tf_op jit(solution)/shard_map/dot_general | solution.py:79
  48.8 1.9 %collective-permute-start.4 = (f32[32,1,16,128]{3,0,2,1:T(8,128)}, f32[32,1,16,128]{3,0,2,1:T(8,128)}, u32[]{:S(2)}, u32[]{:S(2)}) collective-permute-start(f32[32,1,16,128]{3,0,2,1:T(8,128)} %get-tuple-element.20), channel_id=1, source_target_pairs={{16,0},{32,16},{48,32},{64,48},{80,64},{96,80},{112,96},{128,112},... | collective-permute-start | bytes 786440 | tf_op jit(solution)/shard_map/ppermute | solution.py:45
  50.8 7.5 %collective-permute-start.5 = (f32[32,1,16,128]{3,0,2,1:T(8,128)}, f32[32,1,16,128]{3,0,2,1:T(8,128)}, u32[]{:S(2)}, u32[]{:S(2)}) collective-permute-start(f32[32,1,16,128]{3,0,2,1:T(8,128)} %get-tuple-element.19), channel_id=1, source_target_pairs={{0,16},{16,32},{32,48},{48,64},{64,80},{80,96},{96,112},{112,128},... | collective-permute-start | bytes 786440 | tf_op jit(solution)/shard_map/ppermute | solution.py:44
  64.0 1.5 %pad_maximum_fusion.43 = f32[222,128]{1,0:T(8,128)} fusion(f32[70,128]{1,0:T(8,128)} %reshape.156, f32[24,128]{1,0:T(8,128)S(1)} %bitcast.159, f32[128,128]{1,0:T(8,128)} %bitcast.149), kind=kLoop, calls=%fused_computation.130 | loop fusion | flops 56832 | bytes 227328 | tf_op jit(solution)/shard_map/concatenate | solution.py:144
  65.5 1.9 %collective-permute-start.7 = (f32[222,128]{1,0:T(8,128)}, f32[222,128]{1,0:T(8,128)S(1)}, u32[]{:S(2)}, u32[]{:S(2)}) collective-permute-start(f32[222,128]{1,0:T(8,128)} %pad_maximum_fusion.43), channel_id=1, source_target_pairs={{0,1},{1,2},{2,3},{3,4},{4,5},{5,6},{6,7},{7,8},{8,9},{9,10},{10,1... | collective-permute-start | bytes 341000 | tf_op jit(solution)/shard_map/ppermute | solution.py:165
  68.3 5.9 %collective-permute-start.6 = (f32[222,128]{1,0:T(8,128)S(1)}, f32[222,128]{1,0:T(8,128)S(1)}, u32[]{:S(2)}, u32[]{:S(2)}) collective-permute-start(f32[222,128]{1,0:T(8,128)S(1)} %pad_maximum_fusion.42), channel_id=1, source_target_pairs={{1,0},{2,1},{3,2},{4,3},{5,4},{6,5},{7,6},{8,7},{9,8},{10,9},{11,1... | collective-permute-start | bytes 341000 | tf_op jit(solution)/shard_map/ppermute | solution.py:166
  74.2 1.7 %fusion = f32[4,8,64,128]{3,1,2,0:T(8,128)S(1)} fusion(f32[32,32]{1,0:T(8,128)S(1)} %copy-done, f32[4,8,64,128]{3,2,1,0:T(8,128)S(1)} %bitcast.137), kind=kOutput, calls=%fused_computation.27 | convolution fusion | flops 100925440 | bytes 2101248 | tf_op jit(solution)/shard_map/dot_general | solution.py:79
  77.4 1.9 %shard_map.122 = f32[8,35,128]{2,1,0:T(8,128)} custom-call(f32[649,128]{1,0:T(8,128)} %collective-permute-done.1.x_below, f32[649,128]{1,0:T(8,128)} %copy-done.2, f32[163,128]{1,0:T(8,128)} %collective-permute-done.3.side_below, f32[163,128]{1,0:T(8,128)} %collective-permute-done.2.side_above, f32[222,128]{1,0:T(8,128)} %copy-done.4, f32[222,128]{1,0:T(8,128)} %copy-done.5), custom_call_target="tpu_custom_call" | custom-call | bytes 300000 | tf_op jit(solution)/shard_map/pallas_call | solution.py:249
  79.3 1.6 %copy.72 = f32[8,35,128]{2,0,1:T(8,128)} copy(f32[8,35,128]{2,1,0:T(8,128)} %shard_map.122) | data formatting | bytes 286720
  84.7 10.4 %shard_map.121 = f32[3,4,256]{2,1,0:T(4,128)} custom-call(f32[4,4,256]{2,1,0:T(4,128)} %get-tuple-element.35.own_ref, f32[4,3,6,256]{3,2,1,0:T(8,128)} %pad_maximum_fusion.44.near_ref, f32[4,256]{1,0:T(4,128)} %get-tuple-element.39.occ_ref), custom_call_target="tpu_custom_call" | custom-call | flops 9000000 | bytes 120000 | tf_op jit(solution)/shard_map/pallas_call | solution.py:222
  95.1 2.4 %fusion.25 = f32[32,4,16,128]{3,0,2,1:T(8,128)S(1)} fusion(f32[32,4,16,128]{3,0,2,1:T(8,128)S(1)} %copy.54, f32[32,4,16,128]{3,0,2,1:T(8,128)S(1)} %fusion.5, f32[32,1,1,128]{3,0,2,1:T(8,128)S(1)} %broadcast.42, f32[32,1,16,128]{3,0,2,1:T(8,128)} %collective-permute-done.4, f32[32,1,16,128]{3,0,2,1:T(8,128)} %collective-permute-done.5, ...), kind=kLoop, calls=%fused_computation.54 | loop fusion | flops 6291456 | bytes 4866176 | tf_op jit(solution)/shard_map/add | solution.py:83
  97.6 1.9 %collective-permute-start.8 = (f32[32,1,16,128]{3,0,2,1:T(8,128)S(1)}, f32[32,1,16,128]{3,0,2,1:T(8,128)S(1)}, u32[]{:S(2)}, u32[]{:S(2)}) collective-permute-start(f32[32,1,16,128]{3,0,2,1:T(8,128)S(1)} %get-tuple-element.16), channel_id=1, source_target_pairs={{16,0},{32,16},{48,32},{64,48},{80,64},{96,80},{112,96},{128,112},... | collective-permute-start | bytes 786440 | tf_op jit(solution)/shard_map/ppermute | solution.py:45
  99.5 7.5 %collective-permute-start.9 = (f32[32,1,16,128]{3,0,2,1:T(8,128)S(1)}, f32[32,1,16,128]{3,0,2,1:T(8,128)S(1)}, u32[]{:S(2)}, u32[]{:S(2)}) collective-permute-start(f32[32,1,16,128]{3,0,2,1:T(8,128)S(1)} %get-tuple-element.15), channel_id=1, source_target_pairs={{0,16},{16,32},{32,48},{48,64},{64,80},{80,96},{96,112},{112,128},... | collective-permute-start | bytes 786440 | tf_op jit(solution)/shard_map/ppermute | solution.py:44
  107.7 1.9 %collective-permute-start.11 = (f32[32,4,1,128]{3,0,2,1:T(8,128)S(1)}, f32[32,4,1,128]{3,0,2,1:T(8,128)S(1)}, u32[]{:S(2)}, u32[]{:S(2)}) collective-permute-start(f32[32,4,1,128]{3,0,2,1:T(8,128)S(1)} %get-tuple-element.14), channel_id=1, source_target_pairs={{0,1},{1,2},{2,3},{3,4},{4,5},{5,6},{6,7},{7,8},{8,9},{9,10},{10,1... | collective-permute-start | bytes 196616 | tf_op jit(solution)/shard_map/ppermute | solution.py:44
  109.6 5.8 %collective-permute-start.10 = (f32[32,4,1,128]{3,0,2,1:T(8,128)S(1)}, f32[32,4,1,128]{3,0,2,1:T(8,128)S(1)}, u32[]{:S(2)}, u32[]{:S(2)}) collective-permute-start(f32[32,4,1,128]{3,0,2,1:T(8,128)S(1)} %get-tuple-element.13), channel_id=1, source_target_pairs={{1,0},{2,1},{3,2},{4,3},{5,4},{6,5},{7,6},{8,7},{9,8},{10,9},{11,1... | collective-permute-start | bytes 196616 | tf_op jit(solution)/shard_map/ppermute | solution.py:45
  115.4 1.7 %fusion.1 = f32[4,8,64,128]{3,1,2,0:T(8,128)S(1)} fusion(f32[32,32]{1,0:T(8,128)S(1)} %copy-done, f32[4,8,64,128]{3,2,1,0:T(8,128)S(1)} %bitcast.138), kind=kOutput, calls=%fused_computation.28 | convolution fusion | flops 100925440 | bytes 2101248 | tf_op jit(solution)/shard_map/dot_general | solution.py:79
  117.3 1.4 fusion.36
  118.8 1.9 %collective-permute-start.12 = (f32[32,1,16,128]{3,0,2,1:T(8,128)S(1)}, f32[32,1,16,128]{3,0,2,1:T(8,128)S(1)}, u32[]{:S(2)}, u32[]{:S(2)}) collective-permute-start(f32[32,1,16,128]{3,0,2,1:T(8,128)S(1)} %get-tuple-element.12), channel_id=1, source_target_pairs={{16,0},{32,16},{48,32},{64,48},{80,64},{96,80},{112,96},{128,112},... | collective-permute-start | bytes 786440 | tf_op jit(solution)/shard_map/ppermute | solution.py:45
  120.7 7.5 %collective-permute-start.13 = (f32[32,1,16,128]{3,0,2,1:T(8,128)S(1)}, f32[32,1,16,128]{3,0,2,1:T(8,128)S(1)}, u32[]{:S(2)}, u32[]{:S(2)}) collective-permute-start(f32[32,1,16,128]{3,0,2,1:T(8,128)S(1)} %get-tuple-element.11), channel_id=1, source_target_pairs={{0,16},{16,32},{32,48},{48,64},{64,80},{80,96},{96,112},{112,128},... | collective-permute-start | bytes 786440 | tf_op jit(solution)/shard_map/ppermute | solution.py:44
  128.9 1.9 %collective-permute-start.15 = (f32[32,4,1,128]{3,0,2,1:T(8,128)S(1)}, f32[32,4,1,128]{3,0,2,1:T(8,128)S(1)}, u32[]{:S(2)}, u32[]{:S(2)}) collective-permute-start(f32[32,4,1,128]{3,0,2,1:T(8,128)S(1)} %get-tuple-element.10), channel_id=1, source_target_pairs={{0,1},{1,2},{2,3},{3,4},{4,5},{5,6},{6,7},{7,8},{8,9},{9,10},{10,1... | collective-permute-start | bytes 196616 | tf_op jit(solution)/shard_map/ppermute | solution.py:44
  130.8 6.0 %collective-permute-start.14 = (f32[32,4,1,128]{3,0,2,1:T(8,128)S(1)}, f32[32,4,1,128]{3,0,2,1:T(8,128)S(1)}, u32[]{:S(2)}, u32[]{:S(2)}) collective-permute-start(f32[32,4,1,128]{3,0,2,1:T(8,128)S(1)} %get-tuple-element.9), channel_id=1, source_target_pairs={{1,0},{2,1},{3,2},{4,3},{5,4},{6,5},{7,6},{8,7},{9,8},{10,9},{11,1... | collective-permute-start | bytes 196616 | tf_op jit(solution)/shard_map/ppermute | solution.py:45
  136.8 1.7 %fusion.2 = f32[4,8,64,128]{3,1,2,0:T(8,128)S(1)} fusion(f32[32,32]{1,0:T(8,128)S(1)} %copy-done, f32[4,8,64,128]{3,2,1,0:T(8,128)S(1)} %bitcast.139), kind=kOutput, calls=%fused_computation.29 | convolution fusion | flops 100925440 | bytes 2101248 | tf_op jit(solution)/shard_map/dot_general | solution.py:79
  140.1 1.6 %copy.70 = f32[32,4,16,128]{3,2,1,0:T(8,128)} copy(f32[32,4,16,128]{3,0,2,1:T(8,128)S(1)} %fusion.47) | data formatting | bytes 2097152
  (102 shorter events, 29.7 us)
Async XLA Ops:
  0.6 44.0 %copy-start = (f32[32,32]{1,0:T(8,128)S(1)}, f32[32,32]{1,0:T(8,128)}, u32[]{:S(2)}) copy-start(f32[32,32]{1,0:T(8,128)} %param.12) | copy-start | bytes 12292
  1.4 0.6 copy-start.8
  4.0 12.8 %copy-start.1 = (f32[32,4,16,128]{3,2,1,0:T(8,128)S(1)}, f32[32,4,16,128]{3,2,1,0:T(8,128)}, u32[]{:S(2)}) copy-start(f32[32,4,16,128]{3,2,1,0:T(8,128)} %param.10) | copy-start | bytes 3145732
  5.0 20.8 %copy-start.10 = (s32[1,4,256]{2,1,0:T(4,128)S(1)}, s32[1,4,256]{2,1,0:T(4,128)}, u32[]{:S(2)}) copy-start(s32[1,4,256]{2,1,0:T(4,128)} %param.16) | copy-start | bytes 12292
  5.0 21.4 %copy-start.6 = (f32[32,1,4,256]{3,2,1,0:T(4,128)S(1)}, f32[32,1,4,256]{3,2,1,0:T(4,128)}, u32[]{:S(2)}) copy-start(f32[32,1,4,256]{3,2,1,0:T(4,128)} %param.13) | copy-start | bytes 393220
  6.2 20.6 %copy-start.13 = (s32[1,4,256]{2,1,0:T(4,128)S(1)}, s32[1,4,256]{2,1,0:T(4,128)}, u32[]{:S(2)}) copy-start(s32[1,4,256]{2,1,0:T(4,128)} %param.17) | copy-start | bytes 12292
  7.3 36.2 %collective-permute-start = (f32[649,128]{1,0:T(8,128)}, f32[649,128]{1,0:T(8,128)S(1)}, u32[]{:S(2)}, u32[]{:S(2)}) collective-permute-start(f32[649,128]{1,0:T(8,128)} %get-tuple-element.38), channel_id=1, source_target_pairs={{16,0},{32,16},{48,32},{64,48},{80,64},{96,80},{112,96},{128,112},... | collective-permute-start | bytes 996872 | tf_op jit(solution)/shard_map/ppermute | solution.py:166
  10.4 33.1 %collective-permute-start.1 = (f32[649,128]{1,0:T(8,128)}, f32[649,128]{1,0:T(8,128)}, u32[]{:S(2)}, u32[]{:S(2)}) collective-permute-start(f32[649,128]{1,0:T(8,128)} %get-tuple-element.37), channel_id=1, source_target_pairs={{0,16},{16,32},{32,48},{48,64},{64,80},{80,96},{96,112},{112,128},... | collective-permute-start | bytes 996872 | tf_op jit(solution)/shard_map/ppermute | solution.py:165
  17.5 24.1 %collective-permute-start.3 = (f32[163,128]{1,0:T(8,128)}, f32[163,128]{1,0:T(8,128)}, u32[]{:S(2)}, u32[]{:S(2)}) collective-permute-start(f32[163,128]{1,0:T(8,128)} %pad_maximum_fusion.46), channel_id=1, source_target_pairs={{0,1},{1,2},{2,3},{3,4},{4,5},{5,6},{6,7},{7,8},{8,9},{9,10},{10,1... | collective-permute-start | bytes 250376 | tf_op jit(solution)/shard_map/ppermute | solution.py:165
  20.1 22.5 %collective-permute-start.2 = (f32[163,128]{1,0:T(8,128)}, f32[163,128]{1,0:T(8,128)}, u32[]{:S(2)}, u32[]{:S(2)}) collective-permute-start(f32[163,128]{1,0:T(8,128)} %pad_maximum_fusion.45), channel_id=1, source_target_pairs={{1,0},{2,1},{3,2},{4,3},{5,4},{6,5},{7,6},{8,7},{9,8},{10,9},{11,1... | collective-permute-start | bytes 250376 | tf_op jit(solution)/shard_map/ppermute | solution.py:166
  41.4 3.2 %copy-start.3 = (f32[32,4,16,128]{3,0,2,1:T(8,128)S(1)}, f32[32,4,16,128]{3,0,2,1:T(8,128)}, u32[]{:S(2)}) copy-start(f32[32,4,16,128]{3,0,2,1:T(8,128)} %copy.49) | copy-start | bytes 3145732
  41.4 3.2 %copy-start.11 = (f32[32]{0:T(128)S(1)}, f32[32]{0:T(128)}, u32[]{:S(2)}) copy-start(f32[32]{0:T(128)} %param.11) | copy-start | bytes 388
  43.5 17.6 %copy-start.2 = (f32[649,128]{1,0:T(8,128)}, f32[649,128]{1,0:T(8,128)S(1)}, u32[]{:S(2)}) copy-start(f32[649,128]{1,0:T(8,128)S(1)} %collective-permute-done.x_above) | copy-start | bytes 996868
  48.8 46.3 %collective-permute-start.4 = (f32[32,1,16,128]{3,0,2,1:T(8,128)}, f32[32,1,16,128]{3,0,2,1:T(8,128)}, u32[]{:S(2)}, u32[]{:S(2)}) collective-permute-start(f32[32,1,16,128]{3,0,2,1:T(8,128)} %get-tuple-element.20), channel_id=1, source_target_pairs={{16,0},{32,16},{48,32},{64,48},{80,64},{96,80},{112,96},{128,112},... | collective-permute-start | bytes 786440 | tf_op jit(solution)/shard_map/ppermute | solution.py:45
  50.8 44.4 %collective-permute-start.5 = (f32[32,1,16,128]{3,0,2,1:T(8,128)}, f32[32,1,16,128]{3,0,2,1:T(8,128)}, u32[]{:S(2)}, u32[]{:S(2)}) collective-permute-start(f32[32,1,16,128]{3,0,2,1:T(8,128)} %get-tuple-element.19), channel_id=1, source_target_pairs={{0,16},{16,32},{32,48},{48,64},{64,80},{80,96},{96,112},{112,128},... | collective-permute-start | bytes 786440 | tf_op jit(solution)/shard_map/ppermute | solution.py:44
  65.5 10.6 %collective-permute-start.7 = (f32[222,128]{1,0:T(8,128)}, f32[222,128]{1,0:T(8,128)S(1)}, u32[]{:S(2)}, u32[]{:S(2)}) collective-permute-start(f32[222,128]{1,0:T(8,128)} %pad_maximum_fusion.43), channel_id=1, source_target_pairs={{0,1},{1,2},{2,3},{3,4},{4,5},{5,6},{6,7},{7,8},{8,9},{9,10},{10,1... | collective-permute-start | bytes 341000 | tf_op jit(solution)/shard_map/ppermute | solution.py:165
  68.3 8.1 %collective-permute-start.6 = (f32[222,128]{1,0:T(8,128)S(1)}, f32[222,128]{1,0:T(8,128)S(1)}, u32[]{:S(2)}, u32[]{:S(2)}) collective-permute-start(f32[222,128]{1,0:T(8,128)S(1)} %pad_maximum_fusion.42), channel_id=1, source_target_pairs={{1,0},{2,1},{3,2},{4,3},{5,4},{6,5},{7,6},{8,7},{9,8},{10,9},{11,1... | collective-permute-start | bytes 341000 | tf_op jit(solution)/shard_map/ppermute | solution.py:166
  75.9 8.1 %copy-start.7 = (f32[3,1,4,256]{3,2,1,0:T(4,128)S(1)}, f32[3,1,4,256]{3,2,1,0:T(4,128)}, u32[]{:S(2)}) copy-start(f32[3,1,4,256]{3,2,1,0:T(4,128)} %param.14) | copy-start | bytes 36868
  75.9 8.1 %copy-start.9 = (f32[1,1,4,256]{3,2,1,0:T(4,128)S(1)}, f32[1,1,4,256]{3,2,1,0:T(4,128)}, u32[]{:S(2)}) copy-start(f32[1,1,4,256]{3,2,1,0:T(4,128)} %copy-done.8) | copy-start | bytes 12292
  75.9 19.2 %copy-start.12 = (f32[32]{0:T(128)S(1)}, f32[32]{0:T(128)}, u32[]{:S(2)}) copy-start(f32[32]{0:T(128)} %param.11) | copy-start | bytes 388
  76.1 0.7 copy-start.4
  76.8 0.6 copy-start.5
  97.6 19.7 %collective-permute-start.8 = (f32[32,1,16,128]{3,0,2,1:T(8,128)S(1)}, f32[32,1,16,128]{3,0,2,1:T(8,128)S(1)}, u32[]{:S(2)}, u32[]{:S(2)}) collective-permute-start(f32[32,1,16,128]{3,0,2,1:T(8,128)S(1)} %get-tuple-element.16), channel_id=1, source_target_pairs={{16,0},{32,16},{48,32},{64,48},{80,64},{96,80},{112,96},{128,112},... | collective-permute-start | bytes 786440 | tf_op jit(solution)/shard_map/ppermute | solution.py:45
  99.5 17.8 %collective-permute-start.9 = (f32[32,1,16,128]{3,0,2,1:T(8,128)S(1)}, f32[32,1,16,128]{3,0,2,1:T(8,128)S(1)}, u32[]{:S(2)}, u32[]{:S(2)}) collective-permute-start(f32[32,1,16,128]{3,0,2,1:T(8,128)S(1)} %get-tuple-element.15), channel_id=1, source_target_pairs={{0,16},{16,32},{32,48},{48,64},{64,80},{80,96},{96,112},{112,128},... | collective-permute-start | bytes 786440 | tf_op jit(solution)/shard_map/ppermute | solution.py:44
  107.7 9.6 %collective-permute-start.11 = (f32[32,4,1,128]{3,0,2,1:T(8,128)S(1)}, f32[32,4,1,128]{3,0,2,1:T(8,128)S(1)}, u32[]{:S(2)}, u32[]{:S(2)}) collective-permute-start(f32[32,4,1,128]{3,0,2,1:T(8,128)S(1)} %get-tuple-element.14), channel_id=1, source_target_pairs={{0,1},{1,2},{2,3},{3,4},{4,5},{5,6},{6,7},{7,8},{8,9},{9,10},{10,1... | collective-permute-start | bytes 196616 | tf_op jit(solution)/shard_map/ppermute | solution.py:44
  109.6 7.7 %collective-permute-start.10 = (f32[32,4,1,128]{3,0,2,1:T(8,128)S(1)}, f32[32,4,1,128]{3,0,2,1:T(8,128)S(1)}, u32[]{:S(2)}, u32[]{:S(2)}) collective-permute-start(f32[32,4,1,128]{3,0,2,1:T(8,128)S(1)} %get-tuple-element.13), channel_id=1, source_target_pairs={{1,0},{2,1},{3,2},{4,3},{5,4},{6,5},{7,6},{8,7},{9,8},{10,9},{11,1... | collective-permute-start | bytes 196616 | tf_op jit(solution)/shard_map/ppermute | solution.py:45
  118.8 19.9 %collective-permute-start.12 = (f32[32,1,16,128]{3,0,2,1:T(8,128)S(1)}, f32[32,1,16,128]{3,0,2,1:T(8,128)S(1)}, u32[]{:S(2)}, u32[]{:S(2)}) collective-permute-start(f32[32,1,16,128]{3,0,2,1:T(8,128)S(1)} %get-tuple-element.12), channel_id=1, source_target_pairs={{16,0},{32,16},{48,32},{64,48},{80,64},{96,80},{112,96},{128,112},... | collective-permute-start | bytes 786440 | tf_op jit(solution)/shard_map/ppermute | solution.py:45
  120.7 18.0 %collective-permute-start.13 = (f32[32,1,16,128]{3,0,2,1:T(8,128)S(1)}, f32[32,1,16,128]{3,0,2,1:T(8,128)S(1)}, u32[]{:S(2)}, u32[]{:S(2)}) collective-permute-start(f32[32,1,16,128]{3,0,2,1:T(8,128)S(1)} %get-tuple-element.11), channel_id=1, source_target_pairs={{0,16},{16,32},{32,48},{48,64},{64,80},{80,96},{96,112},{112,128},... | collective-permute-start | bytes 786440 | tf_op jit(solution)/shard_map/ppermute | solution.py:44
  128.9 9.8 %collective-permute-start.15 = (f32[32,4,1,128]{3,0,2,1:T(8,128)S(1)}, f32[32,4,1,128]{3,0,2,1:T(8,128)S(1)}, u32[]{:S(2)}, u32[]{:S(2)}) collective-permute-start(f32[32,4,1,128]{3,0,2,1:T(8,128)S(1)} %get-tuple-element.10), channel_id=1, source_target_pairs={{0,1},{1,2},{2,3},{3,4},{4,5},{5,6},{6,7},{7,8},{8,9},{9,10},{10,1... | collective-permute-start | bytes 196616 | tf_op jit(solution)/shard_map/ppermute | solution.py:44
  130.8 7.9 %collective-permute-start.14 = (f32[32,4,1,128]{3,0,2,1:T(8,128)S(1)}, f32[32,4,1,128]{3,0,2,1:T(8,128)S(1)}, u32[]{:S(2)}, u32[]{:S(2)}) collective-permute-start(f32[32,4,1,128]{3,0,2,1:T(8,128)S(1)} %get-tuple-element.9), channel_id=1, source_target_pairs={{1,0},{2,1},{3,2},{4,3},{5,4},{6,5},{7,6},{8,7},{9,8},{10,9},{11,1... | collective-permute-start | bytes 196616 | tf_op jit(solution)/shard_map/ppermute | solution.py:45

commit v5 on v4

--- a/solution.py
+++ b/solution.py
@@ -87,21 +87,52 @@
     )
 
 
+def deposit_kernel(rates_ref, code_ref, out_ref, spread_ref, place_ref):
+    slots, rows, layers = rates_ref.shape
+    bins_y = code_ref.shape[1]
+    species = rows // bins_y
+    lanes = layers * BIN_Z
+    layer_of = lax.broadcasted_iota(jnp.int32, (layers, lanes), 1) // BIN_Z
+    expand = (lax.broadcasted_iota(jnp.int32, (layers, lanes), 0) == layer_of).astype(jnp.float32)
+    for slot in range(slots):
+        spread_ref[slot] = jnp.dot(rates_ref[slot], expand, precision=lax.Precision.HIGHEST, preferred_element_type=jnp.float32)
+        place_ref[slot] = jnp.dot(code_ref[slot], expand, precision=lax.Precision.HIGHEST, preferred_element_type=jnp.float32)
+    depth = lax.broadcasted_iota(jnp.int32, (1, lanes), 1) % BIN_Z
+
+    def body(index, carry):
+        cell_x = index // (bins_y * BIN_XY)
+        row_y = index % (bins_y * BIN_XY)
+        bin_y = row_y // BIN_XY
+        cell_y = row_y % BIN_XY
+        target = (depth + (cell_x * (BIN_XY * BIN_Z) + cell_y * BIN_Z)).astype(jnp.float32)
+        first = pl.multiple_of(bin_y * species, species)
+        total = jnp.zeros((species, lanes), jnp.float32)
+        for slot in range(slots):
+            hit = place_ref[slot, pl.ds(bin_y, 1), :] == target
+            total = total + jnp.where(hit, spread_ref[slot, pl.ds(first, species), :], 0.0)
+        out_ref[cell_x, row_y] = total
+        return carry
+
+    lax.fori_loop(0, BIN_XY * bins_y * BIN_XY, body, 0)
+
+
 def deposit(secretion, occupancy, offsets):
     species, bins_x, bins_y, lanes = secretion.shape
     layers = lanes // SLOTS
-    cells = BIN_XY * BIN_XY * BIN_Z
-    count = bins_x * bins_y * layers
-    rates_slot = secretion.reshape(species, count, SLOTS)
-    place = offsets.reshape(count, SLOTS)
-    alive = occupancy.reshape(count, SLOTS).astype(jnp.float32)
-    voxel_ids = lax.broadcasted_iota(jnp.int32, (count, SLOTS, cells), 2)
-    onehot = (place[:, :, None] == voxel_ids).astype(jnp.float32) * alive[:, :, None]
-    filled = jnp.einsum("snk,nkc->snc", rates_slot, onehot, precision=lax.Precision.HIGHEST)
-    filled = filled.reshape(species, bins_x, bins_y, layers, BIN_XY, BIN_XY, BIN_Z)
-    filled = jnp.transpose(filled, (0, 1, 4, 2, 5, 3, 6))
-    return filled.reshape(species, bins_x * BIN_XY, bins_y * BIN_XY, layers * BIN_Z)
-
+    rates_slot = secretion.reshape(species, bins_y, layers, SLOTS)
+    rates_slot = jnp.transpose(rates_slot, (3, 1, 0, 2)).reshape(SLOTS, bins_y * species, layers)
+    code = jnp.where(occupancy != 0, offsets, -1).astype(jnp.float32).reshape(bins_y, layers, SLOTS)
+    code = jnp.transpose(code, (2, 0, 1))
+    out = pl.pallas_call(
+        deposit_kernel,
+        out_shape=jax.ShapeDtypeStruct((BIN_XY, bins_y * BIN_XY, species, layers * BIN_Z), jnp.float32),
+        scratch_shapes=[
+            pltpu.VMEM((SLOTS, bins_y * species, layers * BIN_Z), jnp.float32),
+            pltpu.VMEM((SLOTS, bins_y, layers * BIN_Z), jnp.float32),
+        ],
+        cost_estimate=pl.CostEstimate(flops=10_000_000, transcendentals=0, bytes_accessed=1_300_000),
+    )(rates_slot, code)
+    return jnp.transpose(out, (2, 0, 1, 3))
 
 def pair_forces(points, padded, occupancy):
     planes, bins_x, bins_y, lanes = points.shape

time: 144 us -> 138 us (0.958)
  local copies, waits for them, and re-layouts: 33.5 us -> 22.3 us
  waiting for transfers between devices: 0.26 us -> 7.4 us
  starting transfers between devices: 68.9 us -> 62.2 us
  Pallas kernels: 12.3 us -> 18.6 us
    mul x3 -> x0, local copies, waits for them, and re-layouts: 10.2 us -> none  [advance(): time_step * source]
    ppermute x5, waiting for transfers between devices: 0.01 us -> 7.37 us  [halos(): low = lax.ppermute(tail, axis, [(i, (i + 1) % count) for i in range(ends)])]
    pallas_call x0 -> x1, Pallas kernels: none -> 6.34 us  [deposit(): pl.pallas_call(deposit_kernel, out_shape=jax.ShapeDtypeStruct((BIN_XY, bi...]
    slice x10 -> x13, local copies, waits for them, and re-layouts: 7.31 us -> 2.09 us  [unpack(): flat[row:row + rows].reshape(tuple((piece.shape[axis] for axis in order)))]
    ppermute x5, starting transfers between devices: 17.5 us -> 12.5 us  [halos(): high = lax.ppermute(head, axis, [((i + 1) % count, i) for i in range(ends)])]
    unnamed x37, local copies, waits for them, and re-layouts: 8.05 us -> 10.3 us
    ppermute x3, starting transfers between devices: 14.8 us -> 12.6 us  [send_pair(): above = lax.ppermute(pack(downward), axis, down)]
    dot_general x1 -> x0, matrix products: 2.15 us -> none  [deposit(): jnp.einsum('snk,nkc->snc', rates_slot, onehot, precision=lax.Precision.HI...]
  transfers between devices with their start and end apart: 16 -> 16, of which waited for: 1 -> 2; matrix products, arithmetic and copies ran while one was open for 28% -> 15% of each run, Pallas kernels for 9% -> 14%
where the time goes in v5:
time: 138 us; the launch traced here: 136 us
  starting transfers between devices  62.2 us (45%)
  local copies, waits for them, and re-layouts  22.3 us (16%)
  Pallas kernels  18.6 us (13%)
  other arithmetic  16.1 us (12%)
  matrix products  8.58 us (6%)
  waiting for transfers between devices  7.4 us (5%)
    ppermute x5, starting transfers between devices, halos(): low = lax.ppermute(tail, axis, [(i, (i + 1) % count) for i in range(ends)])  26.9 us
    ppermute x3, starting transfers between devices, send_pair(): above = lax.ppermute(pack(downward), axis, down)  12.6 us
    ppermute x5, starting transfers between devices, halos(): high = lax.ppermute(head, axis, [((i + 1) % count, i) for i in range(ends)])  12.5 us
    pallas_call x1, Pallas kernels, pallas_forces(): pl.pallas_call(forces_kernel, out_shape=jax.ShapeDtypeStruct((3, rows, la...  10.4 us
    unnamed x37, local copies, waits for them, and re-layouts  10.3 us
    ppermute x3, starting transfers between devices, send_pair(): below = lax.ppermute(pack(upward), axis, up)  10.1 us
    dot_general x4, matrix products, advance(): jnp.dot(mixing, center.reshape(species, -1), precision=lax.Precision.HIGH...  8.58 us
    ppermute x5, waiting for transfers between devices, halos(): low = lax.ppermute(tail, axis, [(i, (i + 1) % count) for i in range(ends)])  7.37 us
  transfers between devices with their start and end apart: 16, of which 2 were waited for; matrix products, arithmetic and copies ran while one was open for 15% of the time, Pallas kernels for 14%

profile of v5, /device:TPU:120, one launch (start us, length us, event | category | flops | bytes accessed | tf_op | source)
XLA Modules:
  0.0 136.4 jit_solution(16514660925557494002)
XLA Ops:
  6.5 3.1 %collective-permute-start = (f32[649,128]{1,0:T(8,128)}, f32[649,128]{1,0:T(8,128)S(1)}, u32[]{:S(2)}, u32[]{:S(2)}) collective-permute-start(f32[649,128]{1,0:T(8,128)} %get-tuple-element.38), channel_id=1, source_target_pairs={{16,0},{32,16},{48,32},{64,48},{80,64},{96,80},{112,96},{128,112},... | collective-permute-start | bytes 996872 | tf_op jit(solution)/shard_map/ppermute | solution.py:197
  9.7 6.3 %collective-permute-start.1 = (f32[649,128]{1,0:T(8,128)}, f32[649,128]{1,0:T(8,128)S(1)}, u32[]{:S(2)}, u32[]{:S(2)}) collective-permute-start(f32[649,128]{1,0:T(8,128)} %get-tuple-element.37), channel_id=1, source_target_pairs={{0,16},{16,32},{32,48},{48,64},{64,80},{80,96},{96,112},{112,128},... | collective-permute-start | bytes 996872 | tf_op jit(solution)/shard_map/ppermute | solution.py:196
  16.8 3.7 %collective-permute-start.2 = (f32[163,128]{1,0:T(8,128)}, f32[163,128]{1,0:T(8,128)S(1)}, u32[]{:S(2)}, u32[]{:S(2)}) collective-permute-start(f32[163,128]{1,0:T(8,128)} %pad_maximum_fusion.45), channel_id=1, source_target_pairs={{1,0},{2,1},{3,2},{4,3},{5,4},{6,5},{7,6},{8,7},{9,8},{10,9},{11,1... | collective-permute-start | bytes 250376 | tf_op jit(solution)/shard_map/ppermute | solution.py:197
  21.2 1.9 %collective-permute-start.3 = (f32[163,128]{1,0:T(8,128)}, f32[163,128]{1,0:T(8,128)S(1)}, u32[]{:S(2)}, u32[]{:S(2)}) collective-permute-start(f32[163,128]{1,0:T(8,128)} %pad_maximum_fusion.46), channel_id=1, source_target_pairs={{0,1},{1,2},{2,3},{3,4},{4,5},{5,6},{6,7},{7,8},{8,9},{9,10},{10,1... | collective-permute-start | bytes 250376 | tf_op jit(solution)/shard_map/ppermute | solution.py:196
  29.3 6.3 %shard_map.121 = f32[4,16,32,128]{3,2,1,0:T(8,128)} custom-call(f32[16,128,16]{2,1,0:T(8,128)} %bitcast.140, f32[16,4,16]{2,1,0:T(4,128)} %bitcast.157), custom_call_target="tpu_custom_call" | custom-call | flops 10000000 | bytes 1300000 | tf_op jit(solution)/shard_map/pallas_call | solution.py:126
  37.2 3.5 %fusion.4 = f32[32,4,16,128]{3,0,2,1:T(8,128)S(1)} fusion(f32[32,4,16,128]{3,0,2,1:T(8,128)S(1)} %copy.48, f32[32,1,1,128]{3,0,2,1:T(8,128)S(1)} %broadcast.33, f32[32,1,16,128]{3,0,2,1:T(8,128)S(1)} %bitcast.147, f32[32,1,16,128]{3,0,2,1:T(8,128)S(1)} %bitcast.148, f32[32,4,1,128]{3,0,2,1:T(8,128)S(1)} %bitcast.159, f32[32,4,1,128]{3,0,2,1:T(8,128)S(1)} %bitcast.158, ...), kind=kOutput, calls=%fused_computation.32 | convolution fusion | flops 107479040 | bytes 4870272 | tf_op jit(solution)/shard_map/dot_general | solution.py:79
  43.9 1.4 %reshape.146 = f32[70,128]{1,0:T(8,128)} reshape(f32[2,35,128]{2,1,0:T(8,128)} %get-tuple-element.41) | data formatting | bytes 71680 | tf_op jit(solution)/shard_map/reshape | solution.py:176
  47.4 1.5 %pad_maximum_fusion.42 = f32[222,128]{1,0:T(8,128)} fusion(f32[70,128]{1,0:T(8,128)} %reshape.146, f32[24,128]{1,0:T(8,128)S(1)} %bitcast.161, f32[128,128]{1,0:T(8,128)} %bitcast.150), kind=kLoop, calls=%fused_computation.122 | loop fusion | flops 56832 | bytes 227328 | tf_op jit(solution)/shard_map/concatenate | solution.py:175
  48.9 5.7 %collective-permute-start.6 = (f32[222,128]{1,0:T(8,128)}, f32[222,128]{1,0:T(8,128)S(1)}, u32[]{:S(2)}, u32[]{:S(2)}) collective-permute-start(f32[222,128]{1,0:T(8,128)} %pad_maximum_fusion.42), channel_id=1, source_target_pairs={{1,0},{2,1},{3,2},{4,3},{5,4},{6,5},{7,6},{8,7},{9,8},{10,9},{11,1... | collective-permute-start | bytes 341000 | tf_op jit(solution)/shard_map/ppermute | solution.py:197
  56.3 1.9 %collective-permute-start.7 = (f32[222,128]{1,0:T(8,128)S(1)}, f32[222,128]{1,0:T(8,128)S(1)}, u32[]{:S(2)}, u32[]{:S(2)}) collective-permute-start(f32[222,128]{1,0:T(8,128)S(1)} %pad_maximum_fusion.43), channel_id=1, source_target_pairs={{0,1},{1,2},{2,3},{3,4},{4,5},{5,6},{6,7},{7,8},{8,9},{9,10},{10,1... | collective-permute-start | bytes 341000 | tf_op jit(solution)/shard_map/ppermute | solution.py:196
  58.3 1.9 %collective-permute-start.4 = (f32[32,1,16,128]{3,0,2,1:T(8,128)}, f32[32,1,16,128]{3,0,2,1:T(8,128)}, u32[]{:S(2)}, u32[]{:S(2)}) collective-permute-start(f32[32,1,16,128]{3,0,2,1:T(8,128)} %get-tuple-element.20), channel_id=1, source_target_pairs={{16,0},{32,16},{48,32},{64,48},{80,64},{96,80},{112,96},{128,112},... | collective-permute-start | bytes 786440 | tf_op jit(solution)/shard_map/ppermute | solution.py:45
  60.2 7.5 %collective-permute-start.5 = (f32[32,1,16,128]{3,0,2,1:T(8,128)}, f32[32,1,16,128]{3,0,2,1:T(8,128)}, u32[]{:S(2)}, u32[]{:S(2)}) collective-permute-start(f32[32,1,16,128]{3,0,2,1:T(8,128)} %get-tuple-element.19), channel_id=1, source_target_pairs={{0,16},{16,32},{32,48},{48,64},{64,80},{80,96},{96,112},{112,128},... | collective-permute-start | bytes 786440 | tf_op jit(solution)/shard_map/ppermute | solution.py:44
  67.7 1.7 %fusion = f32[4,8,64,128]{3,1,2,0:T(8,128)S(1)} fusion(f32[32,32]{1,0:T(8,128)S(1)} %copy-done, f32[4,8,64,128]{3,2,1,0:T(8,128)S(1)} %bitcast.137), kind=kOutput, calls=%fused_computation.27 | convolution fusion | flops 100925440 | bytes 2101248 | tf_op jit(solution)/shard_map/dot_general | solution.py:79
  70.9 1.9 %shard_map.123 = f32[8,35,128]{2,1,0:T(8,128)} custom-call(f32[649,128]{1,0:T(8,128)} %copy-done.4, f32[649,128]{1,0:T(8,128)} %copy-done.3, f32[163,128]{1,0:T(8,128)} %copy-done.9, f32[163,128]{1,0:T(8,128)} %copy-done.8, f32[222,128]{1,0:T(8,128)} %copy-done.7, f32[222,128]{1,0:T(8,128)} %copy-done.6), custom_call_target="tpu_custom_call" | custom-call | bytes 300000 | tf_op jit(solution)/shard_map/pallas_call | solution.py:280
  72.8 1.6 %copy.67 = f32[8,35,128]{2,0,1:T(8,128)} copy(f32[8,35,128]{2,1,0:T(8,128)} %shard_map.123) | data formatting | bytes 286720
  76.5 10.4 %shard_map.122 = f32[3,4,256]{2,1,0:T(4,128)} custom-call(f32[4,4,256]{2,1,0:T(4,128)} %get-tuple-element.35.own_ref, f32[4,3,6,256]{3,2,1,0:T(8,128)} %pad_maximum_fusion.44.near_ref, f32[4,256]{1,0:T(4,128)} %get-tuple-element.39.occ_ref), custom_call_target="tpu_custom_call" | custom-call | flops 9000000 | bytes 120000 | tf_op jit(solution)/shard_map/pallas_call | solution.py:253
  87.0 2.4 %fusion.24 = f32[32,4,16,128]{3,0,2,1:T(8,128)S(1)} fusion(f32[32,4,16,128]{3,0,2,1:T(8,128)S(1)} %fusion.4, f32[32,1,1,128]{3,0,2,1:T(8,128)S(1)} %broadcast.33, f32[32,1,16,128]{3,0,2,1:T(8,128)} %collective-permute-done.4, f32[32,1,16,128]{3,0,2,1:T(8,128)} %collective-permute-done.5, f32[32,4,1,128]{3,0,2,1:T(8,128)S(1)} %bitcast.146, ...), kind=kLoop, calls=%fused_computation.52 | loop fusion | flops 6553600 | bytes 4866176 | tf_op jit(solution)/shard_map/add | solution.py:83
  89.5 2.1 %collective-permute-start.8 = (f32[32,1,16,128]{3,0,2,1:T(8,128)S(1)}, f32[32,1,16,128]{3,0,2,1:T(8,128)S(1)}, u32[]{:S(2)}, u32[]{:S(2)}) collective-permute-start(f32[32,1,16,128]{3,0,2,1:T(8,128)S(1)} %get-tuple-element.16), channel_id=1, source_target_pairs={{16,0},{32,16},{48,32},{64,48},{80,64},{96,80},{112,96},{128,112},... | collective-permute-start | bytes 786440 | tf_op jit(solution)/shard_map/ppermute | solution.py:45
  91.6 7.5 %collective-permute-start.9 = (f32[32,1,16,128]{3,0,2,1:T(8,128)S(1)}, f32[32,1,16,128]{3,0,2,1:T(8,128)S(1)}, u32[]{:S(2)}, u32[]{:S(2)}) collective-permute-start(f32[32,1,16,128]{3,0,2,1:T(8,128)S(1)} %get-tuple-element.15), channel_id=1, source_target_pairs={{0,16},{16,32},{32,48},{48,64},{64,80},{80,96},{96,112},{112,128},... | collective-permute-start | bytes 786440 | tf_op jit(solution)/shard_map/ppermute | solution.py:44
  99.7 4.6 %collective-permute-start.10 = (f32[32,4,1,128]{3,0,2,1:T(8,128)S(1)}, f32[32,4,1,128]{3,0,2,1:T(8,128)S(1)}, u32[]{:S(2)}, u32[]{:S(2)}) collective-permute-start(f32[32,4,1,128]{3,0,2,1:T(8,128)S(1)} %get-tuple-element.13), channel_id=1, source_target_pairs={{1,0},{2,1},{3,2},{4,3},{5,4},{6,5},{7,6},{8,7},{9,8},{10,9},{11,1... | collective-permute-start | bytes 196616 | tf_op jit(solution)/shard_map/ppermute | solution.py:45
  104.4 1.9 %collective-permute-start.11 = (f32[32,4,1,128]{3,0,2,1:T(8,128)S(1)}, f32[32,4,1,128]{3,0,2,1:T(8,128)S(1)}, u32[]{:S(2)}, u32[]{:S(2)}) collective-permute-start(f32[32,4,1,128]{3,0,2,1:T(8,128)S(1)} %get-tuple-element.14), channel_id=1, source_target_pairs={{0,1},{1,2},{2,3},{3,4},{4,5},{5,6},{6,7},{7,8},{8,9},{9,10},{10,1... | collective-permute-start | bytes 196616 | tf_op jit(solution)/shard_map/ppermute | solution.py:44
  106.3 1.7 %fusion.1 = f32[4,8,64,128]{3,1,2,0:T(8,128)S(1)} fusion(f32[32,32]{1,0:T(8,128)S(1)} %copy-done, f32[4,8,64,128]{3,2,1,0:T(8,128)S(1)} %bitcast.138), kind=kOutput, calls=%fused_computation.28 | convolution fusion | flops 100925440 | bytes 2101248 | tf_op jit(solution)/shard_map/dot_general | solution.py:79
  108.2 4.0 %collective-permute-done.11 = f32[32,4,1,128]{3,0,2,1:T(8,128)S(1)} collective-permute-done((f32[32,4,1,128]{3,0,2,1:T(8,128)S(1)}, f32[32,4,1,128]{3,0,2,1:T(8,128)S(1)}, u32[]{:S(2)}, u32[]{:S(2)}) %collective-permute-start.11) | collective-permute-done | bytes 65568 | tf_op jit(solution)/shard_map/ppermute | solution.py:44
  112.2 1.4 %fusion.35 = f32[32,4,16,128]{3,0,2,1:T(8,128)S(1)} fusion(f32[32,4,16,128]{3,0,2,1:T(8,128)S(1)} %fusion.24, f32[32,1,1,128]{3,0,2,1:T(8,128)S(1)} %broadcast.33, f32[32,1,16,128]{3,0,2,1:T(8,128)S(1)} %collective-permute-done.8, f32[32,1,16,128]{3,0,2,1:T(8,128)S(1)} %collective-permute-done.9, f32[32,4,1,128]{3,0,2,1:T(8,128)S(1)} %collective-permute-done.11, ...), kind=kLoop, calls=%fused_computation.63 | loop fusion | flops 6553600 | bytes 4866176 | tf_op jit(solution)/shard_map/add | solution.py:83
  113.6 1.9 %collective-permute-start.12 = (f32[32,1,16,128]{3,0,2,1:T(8,128)S(1)}, f32[32,1,16,128]{3,0,2,1:T(8,128)S(1)}, u32[]{:S(2)}, u32[]{:S(2)}) collective-permute-start(f32[32,1,16,128]{3,0,2,1:T(8,128)S(1)} %get-tuple-element.12), channel_id=1, source_target_pairs={{16,0},{32,16},{48,32},{64,48},{80,64},{96,80},{112,96},{128,112},... | collective-permute-start | bytes 786440 | tf_op jit(solution)/shard_map/ppermute | solution.py:45
  115.6 7.5 %collective-permute-start.13 = (f32[32,1,16,128]{3,0,2,1:T(8,128)S(1)}, f32[32,1,16,128]{3,0,2,1:T(8,128)S(1)}, u32[]{:S(2)}, u32[]{:S(2)}) collective-permute-start(f32[32,1,16,128]{3,0,2,1:T(8,128)S(1)} %get-tuple-element.11), channel_id=1, source_target_pairs={{0,16},{16,32},{32,48},{48,64},{64,80},{80,96},{96,112},{112,128},... | collective-permute-start | bytes 786440 | tf_op jit(solution)/shard_map/ppermute | solution.py:44
  123.8 1.9 %collective-permute-start.14 = (f32[32,4,1,128]{3,0,2,1:T(8,128)S(1)}, f32[32,4,1,128]{3,0,2,1:T(8,128)S(1)}, u32[]{:S(2)}, u32[]{:S(2)}) collective-permute-start(f32[32,4,1,128]{3,0,2,1:T(8,128)S(1)} %get-tuple-element.9), channel_id=1, source_target_pairs={{1,0},{2,1},{3,2},{4,3},{5,4},{6,5},{7,6},{8,7},{9,8},{10,9},{11,1... | collective-permute-start | bytes 196616 | tf_op jit(solution)/shard_map/ppermute | solution.py:45
  125.7 2.4 %collective-permute-start.15 = (f32[32,4,1,128]{3,0,2,1:T(8,128)S(1)}, f32[32,4,1,128]{3,0,2,1:T(8,128)S(1)}, u32[]{:S(2)}, u32[]{:S(2)}) collective-permute-start(f32[32,4,1,128]{3,0,2,1:T(8,128)S(1)} %get-tuple-element.10), channel_id=1, source_target_pairs={{0,1},{1,2},{2,3},{3,4},{4,5},{5,6},{6,7},{7,8},{8,9},{9,10},{10,1... | collective-permute-start | bytes 196616 | tf_op jit(solution)/shard_map/ppermute | solution.py:44
  128.1 1.7 %fusion.2 = f32[4,8,64,128]{3,1,2,0:T(8,128)S(1)} fusion(f32[32,32]{1,0:T(8,128)S(1)} %copy-done, f32[4,8,64,128]{3,2,1,0:T(8,128)S(1)} %bitcast.139), kind=kOutput, calls=%fused_computation.29 | convolution fusion | flops 100925440 | bytes 2101248 | tf_op jit(solution)/shard_map/dot_general | solution.py:79
  130.0 3.4 %collective-permute-done.15 = f32[32,4,1,128]{3,0,2,1:T(8,128)S(1)} collective-permute-done((f32[32,4,1,128]{3,0,2,1:T(8,128)S(1)}, f32[32,4,1,128]{3,0,2,1:T(8,128)S(1)}, u32[]{:S(2)}, u32[]{:S(2)}) %collective-permute-start.15) | collective-permute-done | bytes 65568 | tf_op jit(solution)/shard_map/ppermute | solution.py:44
  133.4 1.4 %fusion.46 = f32[32,4,16,128]{3,0,2,1:T(8,128)S(1)} fusion(f32[32,4,16,128]{3,0,2,1:T(8,128)S(1)} %fusion.35, f32[32,1,1,128]{3,0,2,1:T(8,128)S(1)} %broadcast.33, f32[32,1,16,128]{3,0,2,1:T(8,128)S(1)} %collective-permute-done.12, f32[32,1,16,128]{3,0,2,1:T(8,128)S(1)} %collective-permute-done.13, f32[32,4,1,128]{3,0,2,1:T(8,128)S(1)} %collective-permute-done.15, ...), kind=kLoop, calls=%fused_computation.74 | loop fusion | flops 6553600 | bytes 4866176 | tf_op jit(solution)/shard_map/add | solution.py:83
  134.8 1.6 %copy.65 = f32[32,4,16,128]{3,2,1,0:T(8,128)} copy(f32[32,4,16,128]{3,0,2,1:T(8,128)S(1)} %fusion.46) | data formatting | bytes 2097152
  (103 shorter events, 27.0 us)
Async XLA Ops:
  0.6 35.9 %copy-start = (f32[32,32]{1,0:T(8,128)S(1)}, f32[32,32]{1,0:T(8,128)}, u32[]{:S(2)}) copy-start(f32[32,32]{1,0:T(8,128)} %param.12) | copy-start | bytes 12292
  5.5 10.5 %copy-start.2 = (f32[32,4,16,128]{3,2,1,0:T(8,128)S(1)}, f32[32,4,16,128]{3,2,1,0:T(8,128)}, u32[]{:S(2)}) copy-start(f32[32,4,16,128]{3,2,1,0:T(8,128)} %param.10) | copy-start | bytes 3145732
  5.6 17.4 %copy-start.11 = (s32[1,4,256]{2,1,0:T(4,128)S(1)}, s32[1,4,256]{2,1,0:T(4,128)}, u32[]{:S(2)}) copy-start(s32[1,4,256]{2,1,0:T(4,128)} %param.16) | copy-start | bytes 12292
  5.7 17.4 %copy-start.13 = (s32[1,4,256]{2,1,0:T(4,128)S(1)}, s32[1,4,256]{2,1,0:T(4,128)}, u32[]{:S(2)}) copy-start(s32[1,4,256]{2,1,0:T(4,128)} %param.17) | copy-start | bytes 12292
  6.5 29.2 %collective-permute-start = (f32[649,128]{1,0:T(8,128)}, f32[649,128]{1,0:T(8,128)S(1)}, u32[]{:S(2)}, u32[]{:S(2)}) collective-permute-start(f32[649,128]{1,0:T(8,128)} %get-tuple-element.38), channel_id=1, source_target_pairs={{16,0},{32,16},{48,32},{64,48},{80,64},{96,80},{112,96},{128,112},... | collective-permute-start | bytes 996872 | tf_op jit(solution)/shard_map/ppermute | solution.py:197
  9.7 26.1 %collective-permute-start.1 = (f32[649,128]{1,0:T(8,128)}, f32[649,128]{1,0:T(8,128)S(1)}, u32[]{:S(2)}, u32[]{:S(2)}) collective-permute-start(f32[649,128]{1,0:T(8,128)} %get-tuple-element.37), channel_id=1, source_target_pairs={{0,16},{16,32},{32,48},{48,64},{64,80},{80,96},{96,112},{112,128},... | collective-permute-start | bytes 996872 | tf_op jit(solution)/shard_map/ppermute | solution.py:196
  16.8 18.9 %collective-permute-start.2 = (f32[163,128]{1,0:T(8,128)}, f32[163,128]{1,0:T(8,128)S(1)}, u32[]{:S(2)}, u32[]{:S(2)}) collective-permute-start(f32[163,128]{1,0:T(8,128)} %pad_maximum_fusion.45), channel_id=1, source_target_pairs={{1,0},{2,1},{3,2},{4,3},{5,4},{6,5},{7,6},{8,7},{9,8},{10,9},{11,1... | collective-permute-start | bytes 250376 | tf_op jit(solution)/shard_map/ppermute | solution.py:197
  21.2 14.6 %collective-permute-start.3 = (f32[163,128]{1,0:T(8,128)}, f32[163,128]{1,0:T(8,128)S(1)}, u32[]{:S(2)}, u32[]{:S(2)}) collective-permute-start(f32[163,128]{1,0:T(8,128)} %pad_maximum_fusion.46), channel_id=1, source_target_pairs={{0,1},{1,2},{2,3},{3,4},{4,5},{5,6},{6,7},{7,8},{8,9},{9,10},{10,1... | collective-permute-start | bytes 250376 | tf_op jit(solution)/shard_map/ppermute | solution.py:196
  35.7 1.5 %copy-start.1 = (f32[4,16,32,128]{3,2,1,0:T(8,128)S(1)}, f32[4,16,32,128]{3,2,1,0:T(8,128)}, u32[]{:S(2)}) copy-start(f32[4,16,32,128]{3,2,1,0:T(8,128)} %shard_map.121) | copy-start | bytes 3145732
  35.7 1.5 %copy-start.12 = (f32[32]{0:T(128)S(1)}, f32[32]{0:T(128)}, u32[]{:S(2)}) copy-start(f32[32]{0:T(128)} %param.11) | copy-start | bytes 388
  35.7 0.6 copy-start.9
  35.8 9.5 %copy-start.3 = (f32[649,128]{1,0:T(8,128)}, f32[649,128]{1,0:T(8,128)S(1)}, u32[]{:S(2)}) copy-start(f32[649,128]{1,0:T(8,128)S(1)} %collective-permute-done.x_above) | copy-start | bytes 996868
  35.8 0.7 copy-start.4
  42.2 1.0 copy-start.5
  42.2 3.0 %slice-start = ((f32[649,128]{1,0:T(8,128)}), f32[32,128]{1,0:T(8,128)S(1)}, s32[]{:S(2)}) async-start(f32[649,128]{1,0:T(8,128)} %copy-done.4), calls=%async_computation | async-start | bytes 32768 | tf_op jit(solution)/shard_map/slice | solution.py:186
  48.9 20.7 %collective-permute-start.6 = (f32[222,128]{1,0:T(8,128)}, f32[222,128]{1,0:T(8,128)S(1)}, u32[]{:S(2)}, u32[]{:S(2)}) collective-permute-start(f32[222,128]{1,0:T(8,128)} %pad_maximum_fusion.42), channel_id=1, source_target_pairs={{1,0},{2,1},{3,2},{4,3},{5,4},{6,5},{7,6},{8,7},{9,8},{10,9},{11,1... | collective-permute-start | bytes 341000 | tf_op jit(solution)/shard_map/ppermute | solution.py:197
  56.3 13.3 %collective-permute-start.7 = (f32[222,128]{1,0:T(8,128)S(1)}, f32[222,128]{1,0:T(8,128)S(1)}, u32[]{:S(2)}, u32[]{:S(2)}) collective-permute-start(f32[222,128]{1,0:T(8,128)S(1)} %pad_maximum_fusion.43), channel_id=1, source_target_pairs={{0,1},{1,2},{2,3},{3,4},{4,5},{5,6},{6,7},{7,8},{8,9},{9,10},{10,1... | collective-permute-start | bytes 341000 | tf_op jit(solution)/shard_map/ppermute | solution.py:196
  58.3 28.7 %collective-permute-start.4 = (f32[32,1,16,128]{3,0,2,1:T(8,128)}, f32[32,1,16,128]{3,0,2,1:T(8,128)}, u32[]{:S(2)}, u32[]{:S(2)}) collective-permute-start(f32[32,1,16,128]{3,0,2,1:T(8,128)} %get-tuple-element.20), channel_id=1, source_target_pairs={{16,0},{32,16},{48,32},{64,48},{80,64},{96,80},{112,96},{128,112},... | collective-permute-start | bytes 786440 | tf_op jit(solution)/shard_map/ppermute | solution.py:45
  60.2 26.8 %collective-permute-start.5 = (f32[32,1,16,128]{3,0,2,1:T(8,128)}, f32[32,1,16,128]{3,0,2,1:T(8,128)}, u32[]{:S(2)}, u32[]{:S(2)}) collective-permute-start(f32[32,1,16,128]{3,0,2,1:T(8,128)} %get-tuple-element.19), channel_id=1, source_target_pairs={{0,16},{16,32},{32,48},{48,64},{64,80},{80,96},{96,112},{112,128},... | collective-permute-start | bytes 786440 | tf_op jit(solution)/shard_map/ppermute | solution.py:44
  69.6 6.3 %copy-start.10 = (f32[3,1,4,256]{3,2,1,0:T(4,128)S(1)}, f32[3,1,4,256]{3,2,1,0:T(4,128)}, u32[]{:S(2)}) copy-start(f32[3,1,4,256]{3,2,1,0:T(4,128)} %param.14) | copy-start | bytes 36868
  69.6 0.7 copy-start.6
  70.3 0.6 copy-start.7
  72.8 14.2 %slice-start.1 = ((f32[222,128]{1,0:T(8,128)}), f32[128,128]{1,0:T(8,128)S(1)}, s32[]{:S(2)}) async-start(f32[222,128]{1,0:T(8,128)} %copy-done.6), calls=%async_computation.1 | async-start | bytes 131072 | tf_op jit(solution)/shard_map/slice | solution.py:186
  72.8 14.2 %slice-start.2 = ((f32[222,128]{1,0:T(8,128)}), f32[128,128]{1,0:T(8,128)S(1)}, s32[]{:S(2)}) async-start(f32[222,128]{1,0:T(8,128)} %copy-done.7), calls=%async_computation.2 | async-start | bytes 131072 | tf_op jit(solution)/shard_map/slice | solution.py:186
  89.5 22.7 %collective-permute-start.8 = (f32[32,1,16,128]{3,0,2,1:T(8,128)S(1)}, f32[32,1,16,128]{3,0,2,1:T(8,128)S(1)}, u32[]{:S(2)}, u32[]{:S(2)}) collective-permute-start(f32[32,1,16,128]{3,0,2,1:T(8,128)S(1)} %get-tuple-element.16), channel_id=1, source_target_pairs={{16,0},{32,16},{48,32},{64,48},{80,64},{96,80},{112,96},{128,112},... | collective-permute-start | bytes 786440 | tf_op jit(solution)/shard_map/ppermute | solution.py:45
  91.6 20.6 %collective-permute-start.9 = (f32[32,1,16,128]{3,0,2,1:T(8,128)S(1)}, f32[32,1,16,128]{3,0,2,1:T(8,128)S(1)}, u32[]{:S(2)}, u32[]{:S(2)}) collective-permute-start(f32[32,1,16,128]{3,0,2,1:T(8,128)S(1)} %get-tuple-element.15), channel_id=1, source_target_pairs={{0,16},{16,32},{32,48},{48,64},{64,80},{80,96},{96,112},{112,128},... | collective-permute-start | bytes 786440 | tf_op jit(solution)/shard_map/ppermute | solution.py:44
  99.7 8.5 %collective-permute-start.10 = (f32[32,4,1,128]{3,0,2,1:T(8,128)S(1)}, f32[32,4,1,128]{3,0,2,1:T(8,128)S(1)}, u32[]{:S(2)}, u32[]{:S(2)}) collective-permute-start(f32[32,4,1,128]{3,0,2,1:T(8,128)S(1)} %get-tuple-element.13), channel_id=1, source_target_pairs={{1,0},{2,1},{3,2},{4,3},{5,4},{6,5},{7,6},{8,7},{9,8},{10,9},{11,1... | collective-permute-start | bytes 196616 | tf_op jit(solution)/shard_map/ppermute | solution.py:45
  104.4 7.8 %collective-permute-start.11 = (f32[32,4,1,128]{3,0,2,1:T(8,128)S(1)}, f32[32,4,1,128]{3,0,2,1:T(8,128)S(1)}, u32[]{:S(2)}, u32[]{:S(2)}) collective-permute-start(f32[32,4,1,128]{3,0,2,1:T(8,128)S(1)} %get-tuple-element.14), channel_id=1, source_target_pairs={{0,1},{1,2},{2,3},{3,4},{4,5},{5,6},{6,7},{7,8},{8,9},{9,10},{10,1... | collective-permute-start | bytes 196616 | tf_op jit(solution)/shard_map/ppermute | solution.py:44
  113.6 19.7 %collective-permute-start.12 = (f32[32,1,16,128]{3,0,2,1:T(8,128)S(1)}, f32[32,1,16,128]{3,0,2,1:T(8,128)S(1)}, u32[]{:S(2)}, u32[]{:S(2)}) collective-permute-start(f32[32,1,16,128]{3,0,2,1:T(8,128)S(1)} %get-tuple-element.12), channel_id=1, source_target_pairs={{16,0},{32,16},{48,32},{64,48},{80,64},{96,80},{112,96},{128,112},... | collective-permute-start | bytes 786440 | tf_op jit(solution)/shard_map/ppermute | solution.py:45
  115.6 17.8 %collective-permute-start.13 = (f32[32,1,16,128]{3,0,2,1:T(8,128)S(1)}, f32[32,1,16,128]{3,0,2,1:T(8,128)S(1)}, u32[]{:S(2)}, u32[]{:S(2)}) collective-permute-start(f32[32,1,16,128]{3,0,2,1:T(8,128)S(1)} %get-tuple-element.11), channel_id=1, source_target_pairs={{0,16},{16,32},{32,48},{48,64},{64,80},{80,96},{96,112},{112,128},... | collective-permute-start | bytes 786440 | tf_op jit(solution)/shard_map/ppermute | solution.py:44
  123.8 6.2 %collective-permute-start.14 = (f32[32,4,1,128]{3,0,2,1:T(8,128)S(1)}, f32[32,4,1,128]{3,0,2,1:T(8,128)S(1)}, u32[]{:S(2)}, u32[]{:S(2)}) collective-permute-start(f32[32,4,1,128]{3,0,2,1:T(8,128)S(1)} %get-tuple-element.9), channel_id=1, source_target_pairs={{1,0},{2,1},{3,2},{4,3},{5,4},{6,5},{7,6},{8,7},{9,8},{10,9},{11,1... | collective-permute-start | bytes 196616 | tf_op jit(solution)/shard_map/ppermute | solution.py:45
  125.7 7.7 %collective-permute-start.15 = (f32[32,4,1,128]{3,0,2,1:T(8,128)S(1)}, f32[32,4,1,128]{3,0,2,1:T(8,128)S(1)}, u32[]{:S(2)}, u32[]{:S(2)}) collective-permute-start(f32[32,4,1,128]{3,0,2,1:T(8,128)S(1)} %get-tuple-element.10), channel_id=1, source_target_pairs={{0,1},{1,2},{2,3},{3,4},{4,5},{5,6},{6,7},{7,8},{8,9},{9,10},{10,1... | collective-permute-start | bytes 196616 | tf_op jit(solution)/shard_map/ppermute | solution.py:44
  (1 other events, 0.6 us)

commit v6 on v5

--- a/solution.py
+++ b/solution.py
@@ -53,6 +53,15 @@
     left = jnp.concatenate([corner, y_low, corner], axis=1)
     right = jnp.concatenate([corner, y_high, corner], axis=1)
     return jnp.concatenate([left, middle, right], axis=2)
+
+
+def substep_beside(current, source, rates, mixing, work):
+    x_low, x_high = halos(current, "gx", 1)
+    y_low, y_high = halos(current, "gy", 2)
+    done = work()
+    current, done = lax.optimization_barrier((current, done))
+    padded = framed(current, x_low, x_high, y_low, y_high)
+    return advance(padded, source, rates, mixing), done
 
 
 def substep(current, source, rates, mixing):
@@ -198,7 +207,7 @@
     return unpack(below, upward), unpack(above, downward), below, above
 
 
-def forces_kernel(own_ref, near_ref, occ_ref, out_ref):
+def forces_kernel(span, scale, own_ref, near_ref, occ_ref, start_ref, out_ref):
     rows = own_ref.shape[1]
     lanes = own_ref.shape[-1]
     layers = lanes // SLOTS
@@ -240,22 +249,27 @@
                     fz = fz + dz * strength
         return fx, fy, fz
 
-    zero = jnp.zeros_like(px)
-    fx, fy, fz = lax.fori_loop(0, 3, body, (zero, zero, zero))
-    active = move_step * occ_ref[...]
-    out_ref[0] = active * fx
-    out_ref[1] = active * fy
-    out_ref[2] = active * fz
-
-
-def pallas_forces(points, bordered, occupancy):
+    fx, fy, fz = lax.fori_loop(span[0], span[1], body, (start_ref[0], start_ref[1], start_ref[2]))
+    if scale:
+        active = move_step * occ_ref[...]
+        fx = active * fx
+        fy = active * fy
+        fz = active * fz
+    out_ref[0] = fx
+    out_ref[1] = fy
+    out_ref[2] = fz
+
+
+def pallas_forces(points, bordered, occupancy, partial, span, scale):
     planes, _, rows, lanes = points.shape
-    out = pl.pallas_call(
-        forces_kernel,
+    share = span[1] - span[0]
+    return pl.pallas_call(
+        functools.partial(forces_kernel, span, scale),
         out_shape=jax.ShapeDtypeStruct((3, rows, lanes), jnp.float32),
-        cost_estimate=pl.CostEstimate(flops=9_000_000, transcendentals=450_000, bytes_accessed=120_000),
-    )(points[:, 0], bordered, occupancy[0].astype(jnp.float32))
-    return out.reshape(3, 1, rows, lanes)
+        cost_estimate=pl.CostEstimate(
+            flops=3_000_000 * share, transcendentals=150_000 * share, bytes_accessed=120_000
+        ),
+    )(points[:, 0], bordered, occupancy[0].astype(jnp.float32), partial)
 
 
 def arrived_kernel(starts, state, x_below, x_above, side_below, side_above, corner_below, corner_above, out_ref):
@@ -325,19 +339,25 @@
     bordered = jnp.concatenate([points_low, row_points, points_high], axis=2)
     field_rows = x_low.size // 128
     side_rows = y_low.size // 128
-    arrived = gather_arrived(
-        x_flats,
-        side_flats,
-        corner_flats,
-        field_rows + points.size // 128,
-        side_rows,
-        side_rows + points_low.size // 128,
-        payload.shape[1:],
-    )
-
-    for _ in range(SUBSTEPS - 2):
-        current = substep(current, source, rates, mixing)
-    displacement = pallas_forces(points, bordered, occupancy)
+    starts = (field_rows + points.size // 128, side_rows, side_rows + points_low.size // 128)
+    current, bordered, x_flats, side_flats, corner_flats = lax.optimization_barrier(
+        (current, bordered, x_flats, side_flats, corner_flats)
+    )
+    rows = points.shape[2]
+    zero = jnp.zeros((3, rows, points.shape[3]), jnp.float32)
+
+    def first_work():
+        arrived = gather_arrived(x_flats, side_flats, corner_flats, *starts, payload.shape[1:])
+        return arrived, pallas_forces(points, bordered, occupancy, zero, (0, 2), False)
+
+    current, (arrived, partial) = substep_beside(current, source, rates, mixing, first_work)
+    current, partial = lax.optimization_barrier((current, partial))
+
+    def second_work():
+        return pallas_forces(points, bordered, occupancy, partial, (2, 3), True)
+
+    current, force = substep_beside(current, source, rates, mixing, second_work)
+    displacement = force.reshape(3, 1, rows, points.shape[3])
     return (current, displacement, arrived)
 
 

time: 138 us -> 136 us (0.986)
  the two profiles are of different devices: /device:TPU:120 before, /device:TPU:136 now
where the time goes in v6:
time: 136 us; the launch traced here: 135 us
  starting transfers between devices  58.4 us (43%)
  Pallas kernels  20.2 us (15%)
  local copies, waits for them, and re-layouts  19.5 us (14%)
  waiting for transfers between devices  17.2 us (13%)
  other arithmetic  9.32 us (7%)
  matrix products  8.59 us (6%)
  between operations  1.53 us (1%)
    ppermute x5, starting transfers between devices, halos(): high = lax.ppermute(head, axis, [((i + 1) % count, i) for i in range(ends)])  26.4 us
    ppermute x5, waiting for transfers between devices, halos(): low = lax.ppermute(tail, axis, [(i, (i + 1) % count) for i in range(ends)])  17.1 us
    ppermute x3, starting transfers between devices, send_pair(): above = lax.ppermute(pack(downward), axis, down)  12.9 us
    pallas_call x2, Pallas kernels, pallas_forces(): pl.pallas_call(functools.partial(forces_kernel, span, scale), out_shape=j...  11.9 us
    ppermute x5, starting transfers between devices, halos(): low = lax.ppermute(tail, axis, [(i, (i + 1) % count) for i in range(ends)])  11.5 us
    unnamed x71, local copies, waits for them, and re-layouts  9.42 us
    dot_general x4, matrix products, advance(): jnp.dot(mixing, center.reshape(species, -1), precision=lax.Precision.HIGH...  8.59 us
    ppermute x3, starting transfers between devices, send_pair(): below = lax.ppermute(pack(upward), axis, up)  7.56 us
  transfers between devices with their start and end apart: 16, of which 3 were waited for; matrix products, arithmetic and copies ran while one was open for 13% of the time, Pallas kernels for 15%

profile of v6, /device:TPU:136, one launch (start us, length us, event | category | flops | bytes accessed | tf_op | source)
XLA Modules:
  0.0 134.7 jit_solution(1880904604580759660)
XLA Ops:
  1.4 1.3 fusion.65
  5.8 3.7 %collective-permute-start = (f32[649,128]{1,0:T(8,128)S(1)}, f32[649,128]{1,0:T(8,128)S(1)}, u32[]{:S(2)}, u32[]{:S(2)}) collective-permute-start(f32[649,128]{1,0:T(8,128)S(1)} %get-tuple-element.68), channel_id=1, source_target_pairs={{16,0},{32,16},{48,32},{64,48},{80,64},{96,80},{112,96},{128,112},... | collective-permute-start | bytes 996872 | tf_op jit(solution)/shard_map/ppermute | solution.py:206
  9.6 3.7 %collective-permute-start.1 = (f32[649,128]{1,0:T(8,128)S(1)}, f32[649,128]{1,0:T(8,128)S(1)}, u32[]{:S(2)}, u32[]{:S(2)}) collective-permute-start(f32[649,128]{1,0:T(8,128)S(1)} %get-tuple-element.67), channel_id=1, source_target_pairs={{0,16},{16,32},{32,48},{48,64},{64,80},{80,96},{96,112},{112,128},... | collective-permute-start | bytes 996872 | tf_op jit(solution)/shard_map/ppermute | solution.py:205
  13.5 3.4 %collective-permute-start.2 = (f32[163,128]{1,0:T(8,128)S(1)}, f32[163,128]{1,0:T(8,128)S(1)}, u32[]{:S(2)}, u32[]{:S(2)}) collective-permute-start(f32[163,128]{1,0:T(8,128)S(1)} %pad_maximum_fusion.37), channel_id=1, source_target_pairs={{1,0},{2,1},{3,2},{4,3},{5,4},{6,5},{7,6},{8,7},{9,8},{10,9},{11,1... | collective-permute-start | bytes 250376 | tf_op jit(solution)/shard_map/ppermute | solution.py:206
  17.6 1.9 %collective-permute-start.3 = (f32[163,128]{1,0:T(8,128)}, f32[163,128]{1,0:T(8,128)S(1)}, u32[]{:S(2)}, u32[]{:S(2)}) collective-permute-start(f32[163,128]{1,0:T(8,128)} %pad_maximum_fusion.38), channel_id=1, source_target_pairs={{0,1},{1,2},{2,3},{3,4},{4,5},{5,6},{6,7},{7,8},{8,9},{9,10},{10,1... | collective-permute-start | bytes 250376 | tf_op jit(solution)/shard_map/ppermute | solution.py:205
  20.1 1.6 %copy.44 = f32[32,4,16,128]{3,0,2,1:T(8,128)} copy(f32[32,4,16,128]{3,2,1,0:T(8,128)S(1)} %copy-done.2) | data formatting | bytes 2097152 | tf_op args[0]
  22.7 1.4 %copy.47 = f32[16,4,32,16]{3,2,1,0:T(8,128)} copy(f32[16,4,32,16]{2,0,3,1:T(8,128)S(1)} %bitcast.139) | data formatting | bytes 262144 | tf_op jit(solution)/shard_map/transpose | solution.py:132
  25.8 6.5 %shard_map.121 = f32[4,16,32,128]{3,2,1,0:T(8,128)} custom-call(f32[16,128,16]{2,1,0:T(8,128)} %bitcast.136, f32[16,4,16]{2,1,0:T(4,128)} %bitcast.151), custom_call_target="tpu_custom_call" | custom-call | flops 10000000 | bytes 1300000 | tf_op jit(solution)/shard_map/pallas_call | solution.py:135
  33.0 3.6 %fusion.4 = f32[32,4,16,128]{3,0,2,1:T(8,128)S(1)} fusion(f32[32,4,16,128]{3,0,2,1:T(8,128)S(1)} %copy-done.5, f32[32,1,1,128]{3,0,2,1:T(8,128)S(1)} %broadcast.33, f32[32,1,16,128]{3,0,2,1:T(8,128)S(1)} %bitcast.145, f32[32,1,16,128]{3,0,2,1:T(8,128)S(1)} %bitcast.146, f32[32,4,1,128]{3,0,2,1:T(8,128)S(1)} %bitcast.153, ...), kind=kOutput, calls=%fused_computation.32 | convolution fusion | flops 107479040 | bytes 4870272 | tf_op jit(solution)/shard_map/dot_general | solution.py:88
  38.8 5.8 %collective-permute-start.6 = (f32[222,128]{1,0:T(8,128)S(1)}, f32[222,128]{1,0:T(8,128)S(1)}, u32[]{:S(2)}, u32[]{:S(2)}) collective-permute-start(f32[222,128]{1,0:T(8,128)S(1)} %pad_maximum_fusion.34), channel_id=1, source_target_pairs={{1,0},{2,1},{3,2},{4,3},{5,4},{6,5},{7,6},{8,7},{9,8},{10,9},{11,1... | collective-permute-start | bytes 341000 | tf_op jit(solution)/shard_map/ppermute | solution.py:206
  44.6 1.9 %collective-permute-start.7 = (f32[222,128]{1,0:T(8,128)S(1)}, f32[222,128]{1,0:T(8,128)S(1)}, u32[]{:S(2)}, u32[]{:S(2)}) collective-permute-start(f32[222,128]{1,0:T(8,128)S(1)} %pad_maximum_fusion.35), channel_id=1, source_target_pairs={{0,1},{1,2},{2,3},{3,4},{4,5},{5,6},{6,7},{7,8},{8,9},{9,10},{10,1... | collective-permute-start | bytes 341000 | tf_op jit(solution)/shard_map/ppermute | solution.py:205
  46.5 6.2 %collective-permute-start.4 = (f32[32,1,16,128]{3,0,2,1:T(8,128)}, f32[32,1,16,128]{3,0,2,1:T(8,128)S(1)}, u32[]{:S(2)}, u32[]{:S(2)}) collective-permute-start(f32[32,1,16,128]{3,0,2,1:T(8,128)} %get-tuple-element.50), channel_id=1, source_target_pairs={{16,0},{32,16},{48,32},{64,48},{80,64},{96,80},{112,96},{128,112},... | collective-permute-start | bytes 786440 | tf_op jit(solution)/shard_map/ppermute | solution.py:45
  52.7 1.9 %collective-permute-start.5 = (f32[32,1,16,128]{3,0,2,1:T(8,128)}, f32[32,1,16,128]{3,0,2,1:T(8,128)S(1)}, u32[]{:S(2)}, u32[]{:S(2)}) collective-permute-start(f32[32,1,16,128]{3,0,2,1:T(8,128)} %get-tuple-element.49), channel_id=1, source_target_pairs={{0,16},{16,32},{32,48},{48,64},{64,80},{80,96},{96,112},{112,128},... | collective-permute-start | bytes 786440 | tf_op jit(solution)/shard_map/ppermute | solution.py:44
  54.6 1.7 %fusion = f32[4,8,64,128]{3,1,2,0:T(8,128)S(1)} fusion(f32[32,32]{1,0:T(8,128)S(1)} %copy-done, f32[4,8,64,128]{3,2,1,0:T(8,128)S(1)} %bitcast.135), kind=kOutput, calls=%fused_computation.27 | convolution fusion | flops 100925440 | bytes 2101248 | tf_op jit(solution)/shard_map/dot_general | solution.py:88
  57.7 7.1 %collective-permute-done.5 = f32[32,1,16,128]{3,0,2,1:T(8,128)S(1)} collective-permute-done((f32[32,1,16,128]{3,0,2,1:T(8,128)}, f32[32,1,16,128]{3,0,2,1:T(8,128)S(1)}, u32[]{:S(2)}, u32[]{:S(2)}) %collective-permute-start.5) | collective-permute-done | bytes 262176 | tf_op jit(solution)/shard_map/ppermute | solution.py:44
  64.8 1.4 %fusion.24 = f32[32,4,16,128]{3,0,2,1:T(8,128)S(1)} fusion(f32[32,4,16,128]{3,0,2,1:T(8,128)S(1)} %fusion.4, f32[32,1,1,128]{3,0,2,1:T(8,128)S(1)} %broadcast.33, f32[32,1,16,128]{3,0,2,1:T(8,128)S(1)} %collective-permute-done.4, f32[32,1,16,128]{3,0,2,1:T(8,128)S(1)} %collective-permute-done.5, f32[32,4,1,128]{3,0,2,1:T(8,128)S(1)} %bitcast.144, ...), kind=kLoop, calls=%fused_computation.52 | loop fusion | flops 6553600 | bytes 4866176 | tf_op jit(solution)/shard_map/add | solution.py:92
  67.0 3.3 %collective-permute-start.9 = (f32[32,1,16,128]{3,0,2,1:T(8,128)}, f32[32,1,16,128]{3,0,2,1:T(8,128)S(1)}, u32[]{:S(2)}, u32[]{:S(2)}) collective-permute-start(f32[32,1,16,128]{3,0,2,1:T(8,128)} %get-tuple-element.46), channel_id=1, source_target_pairs={{0,16},{16,32},{32,48},{48,64},{64,80},{80,96},{96,112},{112,128},... | collective-permute-start | bytes 786440 | tf_op jit(solution)/shard_map/ppermute | solution.py:44
  71.0 1.9 %shard_map.122 = f32[8,35,128]{2,1,0:T(8,128)} custom-call(f32[649,128]{1,0:T(8,128)} %copy-done.4, f32[649,128]{1,0:T(8,128)} %copy-done.3, f32[163,128]{1,0:T(8,128)} %copy-done.10, f32[163,128]{1,0:T(8,128)} %copy-done.9, f32[222,128]{1,0:T(8,128)} %copy-done.8, f32[222,128]{1,0:T(8,128)} %copy-done.7), custom_call_target="tpu_custom_call" | custom-call | bytes 300000 | tf_op jit(solution)/shard_map/pallas_call | solution.py:294
  73.5 7.4 %shard_map.123.start_ref = f32[3,4,256]{2,1,0:T(4,128)} custom-call(f32[4,4,256]{2,1,0:T(4,128)} %get-tuple-element.65.own_ref, f32[4,3,6,256]{3,2,1,0:T(8,128)} %pad_maximum_fusion.36.near_ref, f32[4,256]{1,0:T(4,128)} %get-tuple-element.69.occ_ref, f32[3,4,256]{2,1,0:T(4,128)} %broadcast_in_dim.16.start_ref), custom_call_target="tpu_custom_call" | custom-call | flops 6000000 | bytes 120000 | tf_op jit(solution)/shard_map/pallas_call | solution.py:266
  81.0 6.3 %collective-permute-start.8 = (f32[32,1,16,128]{3,0,2,1:T(8,128)}, f32[32,1,16,128]{3,0,2,1:T(8,128)S(1)}, u32[]{:S(2)}, u32[]{:S(2)}) collective-permute-start(f32[32,1,16,128]{3,0,2,1:T(8,128)} %get-tuple-element.45), channel_id=1, source_target_pairs={{16,0},{32,16},{48,32},{64,48},{80,64},{96,80},{112,96},{128,112},... | collective-permute-start | bytes 786440 | tf_op jit(solution)/shard_map/ppermute | solution.py:45
  87.9 1.7 %fusion.1 = f32[4,8,64,128]{3,1,2,0:T(8,128)S(1)} fusion(f32[32,32]{1,0:T(8,128)S(1)} %copy-done, f32[4,8,64,128]{3,2,1,0:T(8,128)S(1)} %bitcast.137), kind=kOutput, calls=%fused_computation.28 | convolution fusion | flops 100925440 | bytes 2101248 | tf_op jit(solution)/shard_map/dot_general | solution.py:88
  90.4 4.6 %collective-permute-start.10 = (f32[32,4,1,128]{3,0,2,1:T(8,128)S(1)}, f32[32,4,1,128]{3,0,2,1:T(8,128)S(1)}, u32[]{:S(2)}, u32[]{:S(2)}) collective-permute-start(f32[32,4,1,128]{3,0,2,1:T(8,128)S(1)} %copy-done.21), channel_id=1, source_target_pairs={{1,0},{2,1},{3,2},{4,3},{5,4},{6,5},{7,6},{8,7},{9,8},{10,9},{11,1... | collective-permute-start | bytes 196616 | tf_op jit(solution)/shard_map/ppermute | solution.py:45
  95.0 1.9 %collective-permute-start.11 = (f32[32,4,1,128]{3,0,2,1:T(8,128)S(1)}, f32[32,4,1,128]{3,0,2,1:T(8,128)S(1)}, u32[]{:S(2)}, u32[]{:S(2)}) collective-permute-start(f32[32,4,1,128]{3,0,2,1:T(8,128)S(1)} %copy-done.20), channel_id=1, source_target_pairs={{0,1},{1,2},{2,3},{3,4},{4,5},{5,6},{6,7},{7,8},{8,9},{9,10},{10,1... | collective-permute-start | bytes 196616 | tf_op jit(solution)/shard_map/ppermute | solution.py:44
  97.8 5.0 %collective-permute-done.11 = f32[32,4,1,128]{3,0,2,1:T(8,128)S(1)} collective-permute-done((f32[32,4,1,128]{3,0,2,1:T(8,128)S(1)}, f32[32,4,1,128]{3,0,2,1:T(8,128)S(1)}, u32[]{:S(2)}, u32[]{:S(2)}) %collective-permute-start.11) | collective-permute-done | bytes 65568 | tf_op jit(solution)/shard_map/ppermute | solution.py:44
  104.7 1.9 %collective-permute-start.13 = (f32[32,1,16,128]{3,0,2,1:T(8,128)}, f32[32,1,16,128]{3,0,2,1:T(8,128)S(1)}, u32[]{:S(2)}, u32[]{:S(2)}) collective-permute-start(f32[32,1,16,128]{3,0,2,1:T(8,128)} %get-tuple-element.42), channel_id=1, source_target_pairs={{0,16},{16,32},{32,48},{48,64},{64,80},{80,96},{96,112},{112,128},... | collective-permute-start | bytes 786440 | tf_op jit(solution)/shard_map/ppermute | solution.py:44
  107.3 4.5 %shard_map.124 = f32[3,4,256]{2,1,0:T(4,128)} custom-call(f32[4,4,256]{2,1,0:T(4,128)} %get-tuple-element.65.own_ref, f32[4,3,6,256]{3,2,1,0:T(8,128)} %pad_maximum_fusion.36.near_ref, f32[4,256]{1,0:T(4,128)} %get-tuple-element.69.occ_ref, f32[3,4,256]{2,1,0:T(4,128)} %shard_map.123.start_ref), custom_call_target="tpu_custom_call" | custom-call | flops 3000000 | bytes 120000 | tf_op jit(solution)/shard_map/pallas_call | solution.py:266
  111.8 7.5 %collective-permute-start.12 = (f32[32,1,16,128]{3,0,2,1:T(8,128)}, f32[32,1,16,128]{3,0,2,1:T(8,128)S(1)}, u32[]{:S(2)}, u32[]{:S(2)}) collective-permute-start(f32[32,1,16,128]{3,0,2,1:T(8,128)} %get-tuple-element.41), channel_id=1, source_target_pairs={{16,0},{32,16},{48,32},{64,48},{80,64},{96,80},{112,96},{128,112},... | collective-permute-start | bytes 786440 | tf_op jit(solution)/shard_map/ppermute | solution.py:45
  119.9 1.7 %fusion.2 = f32[4,8,64,128]{3,1,2,0:T(8,128)S(1)} fusion(f32[32,32]{1,0:T(8,128)S(1)} %copy-done, f32[4,8,64,128]{3,2,1,0:T(8,128)S(1)} %bitcast.138), kind=kOutput, calls=%fused_computation.29 | convolution fusion | flops 100925440 | bytes 2101248 | tf_op jit(solution)/shard_map/dot_general | solution.py:88
  122.5 1.9 %collective-permute-start.14 = (f32[32,4,1,128]{3,0,2,1:T(8,128)S(1)}, f32[32,4,1,128]{3,0,2,1:T(8,128)S(1)}, u32[]{:S(2)}, u32[]{:S(2)}) collective-permute-start(f32[32,4,1,128]{3,0,2,1:T(8,128)S(1)} %copy-done.23), channel_id=1, source_target_pairs={{1,0},{2,1},{3,2},{4,3},{5,4},{6,5},{7,6},{8,7},{9,8},{10,9},{11,1... | collective-permute-start | bytes 196616 | tf_op jit(solution)/shard_map/ppermute | solution.py:45
  124.4 2.4 %collective-permute-start.15 = (f32[32,4,1,128]{3,0,2,1:T(8,128)S(1)}, f32[32,4,1,128]{3,0,2,1:T(8,128)S(1)}, u32[]{:S(2)}, u32[]{:S(2)}) collective-permute-start(f32[32,4,1,128]{3,0,2,1:T(8,128)S(1)} %copy-done.22), channel_id=1, source_target_pairs={{0,1},{1,2},{2,3},{3,4},{4,5},{5,6},{6,7},{7,8},{8,9},{9,10},{10,1... | collective-permute-start | bytes 196616 | tf_op jit(solution)/shard_map/ppermute | solution.py:44
  127.0 5.1 %collective-permute-done.15 = f32[32,4,1,128]{3,0,2,1:T(8,128)S(1)} collective-permute-done((f32[32,4,1,128]{3,0,2,1:T(8,128)S(1)}, f32[32,4,1,128]{3,0,2,1:T(8,128)S(1)}, u32[]{:S(2)}, u32[]{:S(2)}) %collective-permute-start.15) | collective-permute-done | bytes 65568 | tf_op jit(solution)/shard_map/ppermute | solution.py:44
  133.2 1.6 %copy.57 = f32[32,4,16,128]{3,2,1,0:T(8,128)} copy(f32[32,4,16,128]{3,0,2,1:T(8,128)S(1)} %fusion.46) | data formatting | bytes 2097152
  (138 shorter events, 21.6 us)
Async XLA Ops:
  0.6 32.3 %copy-start = (f32[32,32]{1,0:T(8,128)S(1)}, f32[32,32]{1,0:T(8,128)}, u32[]{:S(2)}) copy-start(f32[32,32]{1,0:T(8,128)} %param.12) | copy-start | bytes 12292
  1.4 36.8 %copy-start.18 = (f32[1,1,4,256]{3,2,1,0:T(4,128)}, f32[1,1,4,256]{3,2,1,0:T(4,128)S(1)}, u32[]{:S(2)}) copy-start(f32[1,1,4,256]{3,2,1,0:T(4,128)S(1)} %multiply_bitcast_fusion) | copy-start | bytes 12292
  4.4 9.0 %copy-start.2 = (f32[32,4,16,128]{3,2,1,0:T(8,128)S(1)}, f32[32,4,16,128]{3,2,1,0:T(8,128)}, u32[]{:S(2)}) copy-start(f32[32,4,16,128]{3,2,1,0:T(8,128)} %param.10) | copy-start | bytes 3145732
  5.5 13.9 %copy-start.24 = (s32[1,4,256]{2,1,0:T(4,128)S(1)}, s32[1,4,256]{2,1,0:T(4,128)}, u32[]{:S(2)}) copy-start(s32[1,4,256]{2,1,0:T(4,128)} %param.16) | copy-start | bytes 12292
  5.6 13.9 %copy-start.28 = (s32[1,4,256]{2,1,0:T(4,128)S(1)}, s32[1,4,256]{2,1,0:T(4,128)}, u32[]{:S(2)}) copy-start(s32[1,4,256]{2,1,0:T(4,128)} %param.17) | copy-start | bytes 12292
  5.8 26.5 %collective-permute-start = (f32[649,128]{1,0:T(8,128)S(1)}, f32[649,128]{1,0:T(8,128)S(1)}, u32[]{:S(2)}, u32[]{:S(2)}) collective-permute-start(f32[649,128]{1,0:T(8,128)S(1)} %get-tuple-element.68), channel_id=1, source_target_pairs={{16,0},{32,16},{48,32},{64,48},{80,64},{96,80},{112,96},{128,112},... | collective-permute-start | bytes 996872 | tf_op jit(solution)/shard_map/ppermute | solution.py:206
  9.6 12.9 %copy-start.15 = (f32[32,1,4,256]{3,2,1,0:T(4,128)S(1)}, f32[32,1,4,256]{3,2,1,0:T(4,128)}, u32[]{:S(2)}) copy-start(f32[32,1,4,256]{3,2,1,0:T(4,128)} %param.13) | copy-start | bytes 393220
  9.6 22.8 %collective-permute-start.1 = (f32[649,128]{1,0:T(8,128)S(1)}, f32[649,128]{1,0:T(8,128)S(1)}, u32[]{:S(2)}, u32[]{:S(2)}) collective-permute-start(f32[649,128]{1,0:T(8,128)S(1)} %get-tuple-element.67), channel_id=1, source_target_pairs={{0,16},{16,32},{32,48},{48,64},{64,80},{80,96},{96,112},{112,128},... | collective-permute-start | bytes 996872 | tf_op jit(solution)/shard_map/ppermute | solution.py:205
  13.5 18.8 %collective-permute-start.2 = (f32[163,128]{1,0:T(8,128)S(1)}, f32[163,128]{1,0:T(8,128)S(1)}, u32[]{:S(2)}, u32[]{:S(2)}) collective-permute-start(f32[163,128]{1,0:T(8,128)S(1)} %pad_maximum_fusion.37), channel_id=1, source_target_pairs={{1,0},{2,1},{3,2},{4,3},{5,4},{6,5},{7,6},{8,7},{9,8},{10,9},{11,1... | collective-permute-start | bytes 250376 | tf_op jit(solution)/shard_map/ppermute | solution.py:206
  17.6 14.7 %collective-permute-start.3 = (f32[163,128]{1,0:T(8,128)}, f32[163,128]{1,0:T(8,128)S(1)}, u32[]{:S(2)}, u32[]{:S(2)}) collective-permute-start(f32[163,128]{1,0:T(8,128)} %pad_maximum_fusion.38), channel_id=1, source_target_pairs={{0,1},{1,2},{2,3},{3,4},{4,5},{5,6},{6,7},{7,8},{8,9},{9,10},{10,1... | collective-permute-start | bytes 250376 | tf_op jit(solution)/shard_map/ppermute | solution.py:205
  25.8 7.1 %copy-start.5 = (f32[32,4,16,128]{3,0,2,1:T(8,128)S(1)}, f32[32,4,16,128]{3,0,2,1:T(8,128)}, u32[]{:S(2)}) copy-start(f32[32,4,16,128]{3,0,2,1:T(8,128)} %copy.44) | copy-start | bytes 3145732
  25.8 7.1 %copy-start.25 = (f32[32]{0:T(128)S(1)}, f32[32]{0:T(128)}, u32[]{:S(2)}) copy-start(f32[32]{0:T(128)} %param.11) | copy-start | bytes 388
  32.3 5.8 %copy-start.3 = (f32[649,128]{1,0:T(8,128)}, f32[649,128]{1,0:T(8,128)S(1)}, u32[]{:S(2)}) copy-start(f32[649,128]{1,0:T(8,128)S(1)} %collective-permute-done.x_above) | copy-start | bytes 996868
  32.4 5.7 %copy-start.4 = (f32[649,128]{1,0:T(8,128)}, f32[649,128]{1,0:T(8,128)S(1)}, u32[]{:S(2)}) copy-start(f32[649,128]{1,0:T(8,128)S(1)} %collective-permute-done.1.x_below) | copy-start | bytes 996868
  38.8 17.8 %collective-permute-start.6 = (f32[222,128]{1,0:T(8,128)S(1)}, f32[222,128]{1,0:T(8,128)S(1)}, u32[]{:S(2)}, u32[]{:S(2)}) collective-permute-start(f32[222,128]{1,0:T(8,128)S(1)} %pad_maximum_fusion.34), channel_id=1, source_target_pairs={{1,0},{2,1},{3,2},{4,3},{5,4},{6,5},{7,6},{8,7},{9,8},{10,9},{11,1... | collective-permute-start | bytes 341000 | tf_op jit(solution)/shard_map/ppermute | solution.py:206
  44.6 12.0 %collective-permute-start.7 = (f32[222,128]{1,0:T(8,128)S(1)}, f32[222,128]{1,0:T(8,128)S(1)}, u32[]{:S(2)}, u32[]{:S(2)}) collective-permute-start(f32[222,128]{1,0:T(8,128)S(1)} %pad_maximum_fusion.35), channel_id=1, source_target_pairs={{0,1},{1,2},{2,3},{3,4},{4,5},{5,6},{6,7},{7,8},{8,9},{9,10},{10,1... | collective-permute-start | bytes 341000 | tf_op jit(solution)/shard_map/ppermute | solution.py:205
  46.5 11.2 %collective-permute-start.4 = (f32[32,1,16,128]{3,0,2,1:T(8,128)}, f32[32,1,16,128]{3,0,2,1:T(8,128)S(1)}, u32[]{:S(2)}, u32[]{:S(2)}) collective-permute-start(f32[32,1,16,128]{3,0,2,1:T(8,128)} %get-tuple-element.50), channel_id=1, source_target_pairs={{16,0},{32,16},{48,32},{64,48},{80,64},{96,80},{112,96},{128,112},... | collective-permute-start | bytes 786440 | tf_op jit(solution)/shard_map/ppermute | solution.py:45
  52.7 12.1 %collective-permute-start.5 = (f32[32,1,16,128]{3,0,2,1:T(8,128)}, f32[32,1,16,128]{3,0,2,1:T(8,128)S(1)}, u32[]{:S(2)}, u32[]{:S(2)}) collective-permute-start(f32[32,1,16,128]{3,0,2,1:T(8,128)} %get-tuple-element.49), channel_id=1, source_target_pairs={{0,16},{16,32},{32,48},{48,64},{64,80},{80,96},{96,112},{112,128},... | collective-permute-start | bytes 786440 | tf_op jit(solution)/shard_map/ppermute | solution.py:44
  56.3 8.4 %copy-start.1 = (f32[4,16,32,128]{3,2,1,0:T(8,128)S(1)}, f32[4,16,32,128]{3,2,1,0:T(8,128)}, u32[]{:S(2)}) copy-start(f32[4,16,32,128]{3,2,1,0:T(8,128)} %shard_map.121) | copy-start | bytes 3145732
  56.3 8.4 %copy-start.26 = (f32[32]{0:T(128)S(1)}, f32[32]{0:T(128)}, u32[]{:S(2)}) copy-start(f32[32]{0:T(128)} %param.11) | copy-start | bytes 388
  56.6 9.6 %copy-start.7 = (f32[222,128]{1,0:T(8,128)}, f32[222,128]{1,0:T(8,128)S(1)}, u32[]{:S(2)}) copy-start(f32[222,128]{1,0:T(8,128)S(1)} %collective-permute-done.6.corner_above) | copy-start | bytes 340996
  56.6 9.6 %copy-start.8 = (f32[222,128]{1,0:T(8,128)}, f32[222,128]{1,0:T(8,128)S(1)}, u32[]{:S(2)}) copy-start(f32[222,128]{1,0:T(8,128)S(1)} %collective-permute-done.7.corner_below) | copy-start | bytes 340996
  67.0 30.6 %collective-permute-start.9 = (f32[32,1,16,128]{3,0,2,1:T(8,128)}, f32[32,1,16,128]{3,0,2,1:T(8,128)S(1)}, u32[]{:S(2)}, u32[]{:S(2)}) collective-permute-start(f32[32,1,16,128]{3,0,2,1:T(8,128)} %get-tuple-element.46), channel_id=1, source_target_pairs={{0,16},{16,32},{32,48},{48,64},{64,80},{80,96},{96,112},{112,128},... | collective-permute-start | bytes 786440 | tf_op jit(solution)/shard_map/ppermute | solution.py:44
  81.0 16.8 %collective-permute-start.8 = (f32[32,1,16,128]{3,0,2,1:T(8,128)}, f32[32,1,16,128]{3,0,2,1:T(8,128)S(1)}, u32[]{:S(2)}, u32[]{:S(2)}) collective-permute-start(f32[32,1,16,128]{3,0,2,1:T(8,128)} %get-tuple-element.45), channel_id=1, source_target_pairs={{16,0},{32,16},{48,32},{64,48},{80,64},{96,80},{112,96},{128,112},... | collective-permute-start | bytes 786440 | tf_op jit(solution)/shard_map/ppermute | solution.py:45
  89.6 5.4 %copy-start.20 = (f32[32,4,1,128]{3,0,2,1:T(8,128)S(1)}, f32[32,4,1,128]{3,0,2,1:T(8,128)}, u32[]{:S(2)}) copy-start(f32[32,4,1,128]{3,0,2,1:T(8,128)} %get-tuple-element.44) | copy-start | bytes 196612
  89.6 7.3 %copy-start.6 = (f32[8,35,128]{2,1,0:T(8,128)S(1)}, f32[8,35,128]{2,1,0:T(8,128)}, u32[]{:S(2)}) copy-start(f32[8,35,128]{2,1,0:T(8,128)} %shard_map.122) | copy-start | bytes 430084
  90.4 7.4 %collective-permute-start.10 = (f32[32,4,1,128]{3,0,2,1:T(8,128)S(1)}, f32[32,4,1,128]{3,0,2,1:T(8,128)S(1)}, u32[]{:S(2)}, u32[]{:S(2)}) collective-permute-start(f32[32,4,1,128]{3,0,2,1:T(8,128)S(1)} %copy-done.21), channel_id=1, source_target_pairs={{1,0},{2,1},{3,2},{4,3},{5,4},{6,5},{7,6},{8,7},{9,8},{10,9},{11,1... | collective-permute-start | bytes 196616 | tf_op jit(solution)/shard_map/ppermute | solution.py:45
  95.0 7.7 %collective-permute-start.11 = (f32[32,4,1,128]{3,0,2,1:T(8,128)S(1)}, f32[32,4,1,128]{3,0,2,1:T(8,128)S(1)}, u32[]{:S(2)}, u32[]{:S(2)}) collective-permute-start(f32[32,4,1,128]{3,0,2,1:T(8,128)S(1)} %copy-done.20), channel_id=1, source_target_pairs={{0,1},{1,2},{2,3},{3,4},{4,5},{5,6},{6,7},{7,8},{8,9},{9,10},{10,1... | collective-permute-start | bytes 196616 | tf_op jit(solution)/shard_map/ppermute | solution.py:44
  104.7 22.1 %collective-permute-start.13 = (f32[32,1,16,128]{3,0,2,1:T(8,128)}, f32[32,1,16,128]{3,0,2,1:T(8,128)S(1)}, u32[]{:S(2)}, u32[]{:S(2)}) collective-permute-start(f32[32,1,16,128]{3,0,2,1:T(8,128)} %get-tuple-element.42), channel_id=1, source_target_pairs={{0,16},{16,32},{32,48},{48,64},{64,80},{80,96},{96,112},{112,128},... | collective-permute-start | bytes 786440 | tf_op jit(solution)/shard_map/ppermute | solution.py:44
  111.8 15.1 %collective-permute-start.12 = (f32[32,1,16,128]{3,0,2,1:T(8,128)}, f32[32,1,16,128]{3,0,2,1:T(8,128)S(1)}, u32[]{:S(2)}, u32[]{:S(2)}) collective-permute-start(f32[32,1,16,128]{3,0,2,1:T(8,128)} %get-tuple-element.41), channel_id=1, source_target_pairs={{16,0},{32,16},{48,32},{64,48},{80,64},{96,80},{112,96},{128,112},... | collective-permute-start | bytes 786440 | tf_op jit(solution)/shard_map/ppermute | solution.py:45
  122.5 4.5 %collective-permute-start.14 = (f32[32,4,1,128]{3,0,2,1:T(8,128)S(1)}, f32[32,4,1,128]{3,0,2,1:T(8,128)S(1)}, u32[]{:S(2)}, u32[]{:S(2)}) collective-permute-start(f32[32,4,1,128]{3,0,2,1:T(8,128)S(1)} %copy-done.23), channel_id=1, source_target_pairs={{1,0},{2,1},{3,2},{4,3},{5,4},{6,5},{7,6},{8,7},{9,8},{10,9},{11,1... | collective-permute-start | bytes 196616 | tf_op jit(solution)/shard_map/ppermute | solution.py:45
  124.4 7.7 %collective-permute-start.15 = (f32[32,4,1,128]{3,0,2,1:T(8,128)S(1)}, f32[32,4,1,128]{3,0,2,1:T(8,128)S(1)}, u32[]{:S(2)}, u32[]{:S(2)}) collective-permute-start(f32[32,4,1,128]{3,0,2,1:T(8,128)S(1)} %copy-done.22), channel_id=1, source_target_pairs={{0,1},{1,2},{2,3},{3,4},{4,5},{5,6},{6,7},{7,8},{8,9},{9,10},{10,1... | collective-permute-start | bytes 196616 | tf_op jit(solution)/shard_map/ppermute | solution.py:44
  (13 other events, 19.3 us)

commit v7 on v6

--- a/solution.py
+++ b/solution.py
@@ -335,28 +335,23 @@
         [current[:, :, -1:], row_points[:, :, -1:], jnp.stack([moved_down[2], moved_up[2]])],
         [current[:, :, :1], row_points[:, :, :1], jnp.stack([moved_down[0], moved_up[0]])],
     )
-    current = advance(framed(current, x_low, x_high, y_low, y_high), source, rates, mixing)
     bordered = jnp.concatenate([points_low, row_points, points_high], axis=2)
     field_rows = x_low.size // 128
     side_rows = y_low.size // 128
     starts = (field_rows + points.size // 128, side_rows, side_rows + points_low.size // 128)
-    current, bordered, x_flats, side_flats, corner_flats = lax.optimization_barrier(
-        (current, bordered, x_flats, side_flats, corner_flats)
-    )
     rows = points.shape[2]
     zero = jnp.zeros((3, rows, points.shape[3]), jnp.float32)
-
-    def first_work():
-        arrived = gather_arrived(x_flats, side_flats, corner_flats, *starts, payload.shape[1:])
-        return arrived, pallas_forces(points, bordered, occupancy, zero, (0, 2), False)
-
-    current, (arrived, partial) = substep_beside(current, source, rates, mixing, first_work)
-    current, partial = lax.optimization_barrier((current, partial))
-
-    def second_work():
+    arrived = gather_arrived(x_flats, side_flats, corner_flats, *starts, payload.shape[1:])
+    partial = pallas_forces(points, bordered, occupancy, zero, (0, 2), False)
+    current, arrived, partial = lax.optimization_barrier((current, arrived, partial))
+    current = advance(framed(current, x_low, x_high, y_low, y_high), source, rates, mixing)
+    current, bordered, partial = lax.optimization_barrier((current, bordered, partial))
+
+    def later_work():
         return pallas_forces(points, bordered, occupancy, partial, (2, 3), True)
 
-    current, force = substep_beside(current, source, rates, mixing, second_work)
+    current, force = substep_beside(current, source, rates, mixing, later_work)
+    current = substep(current, source, rates, mixing)
     displacement = force.reshape(3, 1, rows, points.shape[3])
     return (current, displacement, arrived)
 

time: 136 us -> 130 us (0.956)
  the two profiles are of different devices: /device:TPU:136 before, /device:TPU:120 now
where the time goes in v7:
time: 130 us; the launch traced here: 127 us
  starting transfers between devices  64.9 us (50%)
  local copies, waits for them, and re-layouts  21.4 us (16%)
  Pallas kernels  20.2 us (16%)
  other arithmetic  10.5 us (8%)
  matrix products  8.58 us (7%)
  between operations  1.51 us (1%)
    ppermute x5, starting transfers between devices, halos(): high = lax.ppermute(head, axis, [((i + 1) % count, i) for i in range(ends)])  20.1 us
    ppermute x5, starting transfers between devices, halos(): low = lax.ppermute(tail, axis, [(i, (i + 1) % count) for i in range(ends)])  20 us
    ppermute x3, starting transfers between devices, send_pair(): above = lax.ppermute(pack(downward), axis, down)  14.6 us
    pallas_call x2, Pallas kernels, pallas_forces(): pl.pallas_call(functools.partial(forces_kernel, span, scale), out_shape=j...  11.9 us
    ppermute x3, starting transfers between devices, send_pair(): below = lax.ppermute(pack(upward), axis, up)  10.2 us
    unnamed x63, local copies, waits for them, and re-layouts  8.74 us
    dot_general x4, matrix products, advance(): jnp.dot(mixing, center.reshape(species, -1), precision=lax.Precision.HIGH...  8.58 us
    pallas_call x1, Pallas kernels, deposit(): pl.pallas_call(deposit_kernel, out_shape=jax.ShapeDtypeStruct((BIN_XY, bi...  6.42 us
  transfers between devices with their start and end apart: 16, of which 0 were waited for; matrix products, arithmetic and copies ran while one was open for 15% of the time, Pallas kernels for 16%

profile of v7, /device:TPU:120, one launch (start us, length us, event | category | flops | bytes accessed | tf_op | source)
XLA Modules:
  0.0 127.1 jit_solution(3210251731484997062)
XLA Ops:
  1.4 1.3 %fusion.65 = (f32[4,4,256]{2,1,0:T(4,128)}, f32[4,1,4,256]{3,2,1,0:T(4,128)S(1)}) fusion(f32[1,1,4,256]{3,2,1,0:T(4,128)S(1)} %multiply_bitcast_fusion, f32[3,1,4,256]{3,2,1,0:T(4,128)} %param.14), kind=kLoop, calls=%fused_computation.144 | loop fusion | flops 4096 | bytes 49152 | tf_op jit(solution)/shard_map/squeeze | solution.py:272
  6.5 3.1 %collective-permute-start = (f32[649,128]{1,0:T(8,128)S(1)}, f32[649,128]{1,0:T(8,128)S(1)}, u32[]{:S(2)}, u32[]{:S(2)}) collective-permute-start(f32[649,128]{1,0:T(8,128)S(1)} %get-tuple-element.54), channel_id=1, source_target_pairs={{16,0},{32,16},{48,32},{64,48},{80,64},{96,80},{112,96},{128,112},... | collective-permute-start | bytes 996872 | tf_op jit(solution)/shard_map/ppermute | solution.py:206
  9.7 6.3 %collective-permute-start.1 = (f32[649,128]{1,0:T(8,128)}, f32[649,128]{1,0:T(8,128)S(1)}, u32[]{:S(2)}, u32[]{:S(2)}) collective-permute-start(f32[649,128]{1,0:T(8,128)} %get-tuple-element.53), channel_id=1, source_target_pairs={{0,16},{16,32},{32,48},{48,64},{64,80},{80,96},{96,112},{112,128},... | collective-permute-start | bytes 996872 | tf_op jit(solution)/shard_map/ppermute | solution.py:205
  16.1 1.9 %collective-permute-start.3 = (f32[163,128]{1,0:T(8,128)S(1)}, f32[163,128]{1,0:T(8,128)S(1)}, u32[]{:S(2)}, u32[]{:S(2)}) collective-permute-start(f32[163,128]{1,0:T(8,128)S(1)} %pad_maximum_fusion.38), channel_id=1, source_target_pairs={{0,1},{1,2},{2,3},{3,4},{4,5},{5,6},{6,7},{7,8},{8,9},{9,10},{10,1... | collective-permute-start | bytes 250376 | tf_op jit(solution)/shard_map/ppermute | solution.py:205
  18.1 5.8 %collective-permute-start.2 = (f32[163,128]{1,0:T(8,128)S(1)}, f32[163,128]{1,0:T(8,128)S(1)}, u32[]{:S(2)}, u32[]{:S(2)}) collective-permute-start(f32[163,128]{1,0:T(8,128)S(1)} %pad_maximum_fusion.37), channel_id=1, source_target_pairs={{1,0},{2,1},{3,2},{4,3},{5,4},{6,5},{7,6},{8,7},{9,8},{10,9},{11,1... | collective-permute-start | bytes 250376 | tf_op jit(solution)/shard_map/ppermute | solution.py:206
  24.5 1.6 %copy.44 = f32[32,4,16,128]{3,0,2,1:T(8,128)} copy(f32[32,4,16,128]{3,2,1,0:T(8,128)S(1)} %copy-done.2) | data formatting | bytes 2097152 | tf_op args[0]
  26.7 1.2 copy.62
  28.1 1.4 %copy.47 = f32[16,4,32,16]{3,2,1,0:T(8,128)} copy(f32[16,4,32,16]{2,0,3,1:T(8,128)S(1)} %bitcast.139) | data formatting | bytes 262144 | tf_op jit(solution)/shard_map/transpose | solution.py:132
  30.3 6.4 %shard_map.121 = f32[4,16,32,128]{3,2,1,0:T(8,128)} custom-call(f32[16,128,16]{2,1,0:T(8,128)} %bitcast.136, f32[16,4,16]{2,1,0:T(4,128)} %bitcast.151), custom_call_target="tpu_custom_call" | custom-call | flops 10000000 | bytes 1300000 | tf_op jit(solution)/shard_map/pallas_call | solution.py:135
  40.1 3.5 %fusion.4 = f32[32,4,16,128]{3,0,2,1:T(8,128)S(1)} fusion(f32[32,4,16,128]{3,0,2,1:T(8,128)S(1)} %copy-done.5, f32[32,1,1,128]{3,0,2,1:T(8,128)S(1)} %broadcast.33, f32[32,1,16,128]{3,0,2,1:T(8,128)S(1)} %bitcast.145, f32[32,1,16,128]{3,0,2,1:T(8,128)S(1)} %bitcast.146, f32[32,4,1,128]{3,0,2,1:T(8,128)} %bitcast.152, f32[32,4,1,128]{3,0,2,1:T(8,128)} %bitcast.153, ...), kind=kOutput, calls=%fused_computation.32 | convolution fusion | flops 107479040 | bytes 4870272 | tf_op jit(solution)/shard_map/dot_general | solution.py:88
  43.9 1.9 %collective-permute-start.4 = (f32[222,128]{1,0:T(8,128)S(1)}, f32[222,128]{1,0:T(8,128)S(1)}, u32[]{:S(2)}, u32[]{:S(2)}) collective-permute-start(f32[222,128]{1,0:T(8,128)S(1)} %pad_maximum_fusion.34), channel_id=1, source_target_pairs={{0,1},{1,2},{2,3},{3,4},{4,5},{5,6},{6,7},{7,8},{8,9},{9,10},{10,1... | collective-permute-start | bytes 341000 | tf_op jit(solution)/shard_map/ppermute | solution.py:205
  45.8 5.8 %collective-permute-start.5 = (f32[222,128]{1,0:T(8,128)S(1)}, f32[222,128]{1,0:T(8,128)S(1)}, u32[]{:S(2)}, u32[]{:S(2)}) collective-permute-start(f32[222,128]{1,0:T(8,128)S(1)} %pad_maximum_fusion.35), channel_id=1, source_target_pairs={{1,0},{2,1},{3,2},{4,3},{5,4},{6,5},{7,6},{8,7},{9,8},{10,9},{11,1... | collective-permute-start | bytes 341000 | tf_op jit(solution)/shard_map/ppermute | solution.py:206
  51.6 3.6 %collective-permute-start.7 = (f32[32,1,16,128]{3,0,2,1:T(8,128)S(1)}, f32[32,1,16,128]{3,0,2,1:T(8,128)S(1)}, u32[]{:S(2)}, u32[]{:S(2)}) collective-permute-start(f32[32,1,16,128]{3,0,2,1:T(8,128)S(1)} %get-tuple-element.34), channel_id=1, source_target_pairs={{0,16},{16,32},{32,48},{48,64},{64,80},{80,96},{96,112},{112,128},... | collective-permute-start | bytes 786440 | tf_op jit(solution)/shard_map/ppermute | solution.py:44
  55.2 3.9 %collective-permute-start.6 = (f32[32,1,16,128]{3,0,2,1:T(8,128)S(1)}, f32[32,1,16,128]{3,0,2,1:T(8,128)}, u32[]{:S(2)}, u32[]{:S(2)}) collective-permute-start(f32[32,1,16,128]{3,0,2,1:T(8,128)S(1)} %get-tuple-element.33), channel_id=1, source_target_pairs={{16,0},{32,16},{48,32},{64,48},{80,64},{96,80},{112,96},{128,112},... | collective-permute-start | bytes 786440 | tf_op jit(solution)/shard_map/ppermute | solution.py:45
  60.5 1.9 %shard_map.122 = f32[8,35,128]{2,1,0:T(8,128)} custom-call(f32[649,128]{1,0:T(8,128)} %copy-done.4, f32[649,128]{1,0:T(8,128)} %copy-done.3, f32[163,128]{1,0:T(8,128)} %copy-done.9, f32[163,128]{1,0:T(8,128)} %copy-done.10, f32[222,128]{1,0:T(8,128)} %copy-done.7, f32[222,128]{1,0:T(8,128)} %copy-done.8), custom_call_target="tpu_custom_call" | custom-call | bytes 300000 | tf_op jit(solution)/shard_map/pallas_call | solution.py:294
  64.4 7.4 %shard_map.123.start_ref = f32[3,4,256]{2,1,0:T(4,128)} custom-call(f32[4,4,256]{2,1,0:T(4,128)} %get-tuple-element.51.own_ref, f32[4,3,6,256]{3,2,1,0:T(8,128)} %pad_maximum_fusion.36.near_ref, f32[4,256]{1,0:T(4,128)} %get-tuple-element.55.occ_ref, f32[3,4,256]{2,1,0:T(4,128)} %broadcast_in_dim.16.start_ref), custom_call_target="tpu_custom_call" | custom-call | flops 6000000 | bytes 120000 | tf_op jit(solution)/shard_map/pallas_call | solution.py:266
  72.4 1.7 %fusion = f32[4,8,64,128]{3,1,2,0:T(8,128)S(1)} fusion(f32[32,32]{1,0:T(8,128)S(1)} %copy-done, f32[4,8,64,128]{3,2,1,0:T(8,128)S(1)} %bitcast.137), kind=kOutput, calls=%fused_computation.27 | convolution fusion | flops 100925440 | bytes 2101248 | tf_op jit(solution)/shard_map/dot_general | solution.py:88
  76.8 2.1 %fusion.24 = f32[32,4,16,128]{3,0,2,1:T(8,128)S(1)} fusion(f32[32,4,16,128]{3,0,2,1:T(8,128)S(1)} %fusion.4, f32[32,1,1,128]{3,0,2,1:T(8,128)S(1)} %broadcast.33, f32[32,6,16,128]{3,0,2,1:T(8,128)S(1)} %constant_dynamic-update-slice_fusion, f32[32,4,1,128]{3,0,2,1:T(8,128)S(1)} %bitcast.143, f32[32,4,1,128]{3,0,2,1:T(8,128)S(1)} %bitcast.144, ...), kind=kLoop, calls=%fused_computation.52 | loop fusion | flops 5505024 | bytes 6439040 | tf_op jit(solution)/shard_map/add | solution.py:92
  79.8 5.7 %collective-permute-start.9 = (f32[32,1,16,128]{3,0,2,1:T(8,128)}, f32[32,1,16,128]{3,0,2,1:T(8,128)S(1)}, u32[]{:S(2)}, u32[]{:S(2)}) collective-permute-start(f32[32,1,16,128]{3,0,2,1:T(8,128)} %get-tuple-element.32), channel_id=1, source_target_pairs={{0,16},{16,32},{32,48},{48,64},{64,80},{80,96},{96,112},{112,128},... | collective-permute-start | bytes 786440 | tf_op jit(solution)/shard_map/ppermute | solution.py:44
  86.2 4.5 %shard_map.124 = f32[3,4,256]{2,1,0:T(4,128)} custom-call(f32[4,4,256]{2,1,0:T(4,128)} %get-tuple-element.51.own_ref, f32[4,3,6,256]{3,2,1,0:T(8,128)} %pad_maximum_fusion.36.near_ref, f32[4,256]{1,0:T(4,128)} %get-tuple-element.55.occ_ref, f32[3,4,256]{2,1,0:T(4,128)} %shard_map.123.start_ref), custom_call_target="tpu_custom_call" | custom-call | flops 3000000 | bytes 120000 | tf_op jit(solution)/shard_map/pallas_call | solution.py:266
  90.6 1.9 %collective-permute-start.8 = (f32[32,1,16,128]{3,0,2,1:T(8,128)}, f32[32,1,16,128]{3,0,2,1:T(8,128)S(1)}, u32[]{:S(2)}, u32[]{:S(2)}) collective-permute-start(f32[32,1,16,128]{3,0,2,1:T(8,128)} %get-tuple-element.31), channel_id=1, source_target_pairs={{16,0},{32,16},{48,32},{64,48},{80,64},{96,80},{112,96},{128,112},... | collective-permute-start | bytes 786440 | tf_op jit(solution)/shard_map/ppermute | solution.py:45
  92.6 1.9 %collective-permute-start.11 = (f32[32,4,1,128]{3,0,2,1:T(8,128)}, f32[32,4,1,128]{3,0,2,1:T(8,128)S(1)}, u32[]{:S(2)}, u32[]{:S(2)}) collective-permute-start(f32[32,4,1,128]{3,0,2,1:T(8,128)} %get-tuple-element.30), channel_id=1, source_target_pairs={{0,1},{1,2},{2,3},{3,4},{4,5},{5,6},{6,7},{7,8},{8,9},{9,10},{10,1... | collective-permute-start | bytes 196616 | tf_op jit(solution)/shard_map/ppermute | solution.py:44
  94.5 6.0 %collective-permute-start.10 = (f32[32,4,1,128]{3,0,2,1:T(8,128)}, f32[32,4,1,128]{3,0,2,1:T(8,128)S(1)}, u32[]{:S(2)}, u32[]{:S(2)}) collective-permute-start(f32[32,4,1,128]{3,0,2,1:T(8,128)} %get-tuple-element.29), channel_id=1, source_target_pairs={{1,0},{2,1},{3,2},{4,3},{5,4},{6,5},{7,6},{8,7},{9,8},{10,9},{11,1... | collective-permute-start | bytes 196616 | tf_op jit(solution)/shard_map/ppermute | solution.py:45
  101.1 1.7 %fusion.1 = f32[4,8,64,128]{3,1,2,0:T(8,128)S(1)} fusion(f32[32,32]{1,0:T(8,128)S(1)} %copy-done, f32[4,8,64,128]{3,2,1,0:T(8,128)S(1)} %bitcast.138), kind=kOutput, calls=%fused_computation.28 | convolution fusion | flops 100925440 | bytes 2101248 | tf_op jit(solution)/shard_map/dot_general | solution.py:88
  103.2 1.2 fusion.35
  104.4 2.6 %collective-permute-start.12 = (f32[32,1,16,128]{3,0,2,1:T(8,128)S(1)}, f32[32,1,16,128]{3,0,2,1:T(8,128)S(1)}, u32[]{:S(2)}, u32[]{:S(2)}) collective-permute-start(f32[32,1,16,128]{3,0,2,1:T(8,128)S(1)} %get-tuple-element.28), channel_id=1, source_target_pairs={{16,0},{32,16},{48,32},{64,48},{80,64},{96,80},{112,96},{128,112},... | collective-permute-start | bytes 786440 | tf_op jit(solution)/shard_map/ppermute | solution.py:45
  106.9 6.9 %collective-permute-start.13 = (f32[32,1,16,128]{3,0,2,1:T(8,128)S(1)}, f32[32,1,16,128]{3,0,2,1:T(8,128)S(1)}, u32[]{:S(2)}, u32[]{:S(2)}) collective-permute-start(f32[32,1,16,128]{3,0,2,1:T(8,128)S(1)} %get-tuple-element.27), channel_id=1, source_target_pairs={{0,16},{16,32},{32,48},{48,64},{64,80},{80,96},{96,112},{112,128},... | collective-permute-start | bytes 786440 | tf_op jit(solution)/shard_map/ppermute | solution.py:44
  114.5 1.9 %collective-permute-start.15 = (f32[32,4,1,128]{3,0,2,1:T(8,128)S(1)}, f32[32,4,1,128]{3,0,2,1:T(8,128)S(1)}, u32[]{:S(2)}, u32[]{:S(2)}) collective-permute-start(f32[32,4,1,128]{3,0,2,1:T(8,128)S(1)} %get-tuple-element.26), channel_id=1, source_target_pairs={{0,1},{1,2},{2,3},{3,4},{4,5},{5,6},{6,7},{7,8},{8,9},{9,10},{10,1... | collective-permute-start | bytes 196616 | tf_op jit(solution)/shard_map/ppermute | solution.py:44
  116.4 5.8 %collective-permute-start.14 = (f32[32,4,1,128]{3,0,2,1:T(8,128)S(1)}, f32[32,4,1,128]{3,0,2,1:T(8,128)S(1)}, u32[]{:S(2)}, u32[]{:S(2)}) collective-permute-start(f32[32,4,1,128]{3,0,2,1:T(8,128)S(1)} %get-tuple-element.25), channel_id=1, source_target_pairs={{1,0},{2,1},{3,2},{4,3},{5,4},{6,5},{7,6},{8,7},{9,8},{10,9},{11,1... | collective-permute-start | bytes 196616 | tf_op jit(solution)/shard_map/ppermute | solution.py:45
  122.2 1.7 %fusion.2 = f32[4,8,64,128]{3,1,2,0:T(8,128)S(1)} fusion(f32[32,32]{1,0:T(8,128)S(1)} %copy-done, f32[4,8,64,128]{3,2,1,0:T(8,128)S(1)} %bitcast.135), kind=kOutput, calls=%fused_computation.29 | convolution fusion | flops 100925440 | bytes 2101248 | tf_op jit(solution)/shard_map/dot_general | solution.py:88
  124.1 1.4 %fusion.46 = f32[32,4,16,128]{3,0,2,1:T(8,128)S(1)} fusion(f32[32,4,16,128]{3,0,2,1:T(8,128)S(1)} %fusion.35, f32[32,1,1,128]{3,0,2,1:T(8,128)S(1)} %broadcast.33, f32[32,1,16,128]{3,0,2,1:T(8,128)S(1)} %collective-permute-done.12, f32[32,1,16,128]{3,0,2,1:T(8,128)S(1)} %collective-permute-done.13, f32[32,4,1,128]{3,0,2,1:T(8,128)S(1)} %collective-permute-done.15, ...), kind=kLoop, calls=%fused_computation.74 | loop fusion | flops 6553600 | bytes 4866176 | tf_op jit(solution)/shard_map/add | solution.py:92
  125.5 1.6 %copy.57 = f32[32,4,16,128]{3,2,1,0:T(8,128)} copy(f32[32,4,16,128]{3,0,2,1:T(8,128)S(1)} %fusion.46) | data formatting | bytes 2097152
  (132 shorter events, 20.1 us)
Async XLA Ops:
  0.6 39.4 %copy-start = (f32[32,32]{1,0:T(8,128)S(1)}, f32[32,32]{1,0:T(8,128)}, u32[]{:S(2)}) copy-start(f32[32,32]{1,0:T(8,128)} %param.12) | copy-start | bytes 12292
  4.4 11.6 %copy-start.2 = (f32[32,4,16,128]{3,2,1,0:T(8,128)S(1)}, f32[32,4,16,128]{3,2,1,0:T(8,128)}, u32[]{:S(2)}) copy-start(f32[32,4,16,128]{3,2,1,0:T(8,128)} %param.10) | copy-start | bytes 3145732
  5.6 18.2 %copy-start.22 = (s32[1,4,256]{2,1,0:T(4,128)S(1)}, s32[1,4,256]{2,1,0:T(4,128)}, u32[]{:S(2)}) copy-start(s32[1,4,256]{2,1,0:T(4,128)} %param.16) | copy-start | bytes 12292
  5.6 18.2 %copy-start.24 = (s32[1,4,256]{2,1,0:T(4,128)S(1)}, s32[1,4,256]{2,1,0:T(4,128)}, u32[]{:S(2)}) copy-start(s32[1,4,256]{2,1,0:T(4,128)} %param.17) | copy-start | bytes 12292
  6.5 31.5 %collective-permute-start = (f32[649,128]{1,0:T(8,128)S(1)}, f32[649,128]{1,0:T(8,128)S(1)}, u32[]{:S(2)}, u32[]{:S(2)}) collective-permute-start(f32[649,128]{1,0:T(8,128)S(1)} %get-tuple-element.54), channel_id=1, source_target_pairs={{16,0},{32,16},{48,32},{64,48},{80,64},{96,80},{112,96},{128,112},... | collective-permute-start | bytes 996872 | tf_op jit(solution)/shard_map/ppermute | solution.py:206
  9.7 28.3 %collective-permute-start.1 = (f32[649,128]{1,0:T(8,128)}, f32[649,128]{1,0:T(8,128)S(1)}, u32[]{:S(2)}, u32[]{:S(2)}) collective-permute-start(f32[649,128]{1,0:T(8,128)} %get-tuple-element.53), channel_id=1, source_target_pairs={{0,16},{16,32},{32,48},{48,64},{64,80},{80,96},{96,112},{112,128},... | collective-permute-start | bytes 996872 | tf_op jit(solution)/shard_map/ppermute | solution.py:205
  16.1 20.5 %collective-permute-start.3 = (f32[163,128]{1,0:T(8,128)S(1)}, f32[163,128]{1,0:T(8,128)S(1)}, u32[]{:S(2)}, u32[]{:S(2)}) collective-permute-start(f32[163,128]{1,0:T(8,128)S(1)} %pad_maximum_fusion.38), channel_id=1, source_target_pairs={{0,1},{1,2},{2,3},{3,4},{4,5},{5,6},{6,7},{7,8},{8,9},{9,10},{10,1... | collective-permute-start | bytes 250376 | tf_op jit(solution)/shard_map/ppermute | solution.py:205
  18.1 19.2 %collective-permute-start.2 = (f32[163,128]{1,0:T(8,128)S(1)}, f32[163,128]{1,0:T(8,128)S(1)}, u32[]{:S(2)}, u32[]{:S(2)}) collective-permute-start(f32[163,128]{1,0:T(8,128)S(1)} %pad_maximum_fusion.37), channel_id=1, source_target_pairs={{1,0},{2,1},{3,2},{4,3},{5,4},{6,5},{7,6},{8,7},{9,8},{10,9},{11,1... | collective-permute-start | bytes 250376 | tf_op jit(solution)/shard_map/ppermute | solution.py:206
  30.3 9.8 %copy-start.5 = (f32[32,4,16,128]{3,0,2,1:T(8,128)S(1)}, f32[32,4,16,128]{3,0,2,1:T(8,128)}, u32[]{:S(2)}) copy-start(f32[32,4,16,128]{3,0,2,1:T(8,128)} %copy.44) | copy-start | bytes 3145732
  36.7 3.4 %copy-start.1 = (f32[4,16,32,128]{3,2,1,0:T(8,128)S(1)}, f32[4,16,32,128]{3,2,1,0:T(8,128)}, u32[]{:S(2)}) copy-start(f32[4,16,32,128]{3,2,1,0:T(8,128)} %shard_map.121) | copy-start | bytes 3145732
  38.0 5.7 %copy-start.3 = (f32[649,128]{1,0:T(8,128)}, f32[649,128]{1,0:T(8,128)S(1)}, u32[]{:S(2)}) copy-start(f32[649,128]{1,0:T(8,128)S(1)} %collective-permute-done.x_above) | copy-start | bytes 996868
  40.1 3.7 %copy-start.12 = (f32[4,1,4,256]{3,2,1,0:T(4,128)S(1)}, f32[4,1,4,256]{3,2,1,0:T(4,128)}, u32[]{:S(2)}) copy-start(f32[4,1,4,256]{3,2,1,0:T(4,128)} %reshape.144) | copy-start | bytes 49156
  40.1 3.7 %copy-start.14 = (f32[4,1,4,256]{3,2,1,0:T(4,128)S(1)}, f32[4,1,4,256]{3,2,1,0:T(4,128)}, u32[]{:S(2)}) copy-start(f32[4,1,4,256]{3,2,1,0:T(4,128)} %reshape.143) | copy-start | bytes 49156
  40.1 3.7 %copy-start.17 = (f32[3,1,4,256]{3,2,1,0:T(4,128)S(1)}, f32[3,1,4,256]{3,2,1,0:T(4,128)}, u32[]{:S(2)}) copy-start(f32[3,1,4,256]{3,2,1,0:T(4,128)} %param.14) | copy-start | bytes 36868
  40.1 3.7 %copy-start.20 = (f32[1,1,4,256]{3,2,1,0:T(4,128)S(1)}, f32[1,1,4,256]{3,2,1,0:T(4,128)}, u32[]{:S(2)}) copy-start(f32[1,1,4,256]{3,2,1,0:T(4,128)} %copy-done.19) | copy-start | bytes 12292
  40.1 3.7 %copy-start.11 = (f32[70,128]{1,0:T(8,128)S(1)}, f32[70,128]{1,0:T(8,128)}, u32[]{:S(2)}) copy-start(f32[70,128]{1,0:T(8,128)} %reshape.146) | copy-start | bytes 107524
  43.7 19.4 %copy-start.13 = (f32[4,1,4,256]{3,2,1,0:T(4,128)S(1)}, f32[4,1,4,256]{3,2,1,0:T(4,128)}, u32[]{:S(2)}) copy-start(f32[4,1,4,256]{3,2,1,0:T(4,128)} %reshape.144) | copy-start | bytes 49156
  43.7 19.4 %copy-start.15 = (f32[4,1,4,256]{3,2,1,0:T(4,128)S(1)}, f32[4,1,4,256]{3,2,1,0:T(4,128)}, u32[]{:S(2)}) copy-start(f32[4,1,4,256]{3,2,1,0:T(4,128)} %reshape.143) | copy-start | bytes 49156
  43.7 19.3 %copy-start.18 = (f32[3,1,4,256]{3,2,1,0:T(4,128)S(1)}, f32[3,1,4,256]{3,2,1,0:T(4,128)}, u32[]{:S(2)}) copy-start(f32[3,1,4,256]{3,2,1,0:T(4,128)} %param.14) | copy-start | bytes 36868
  43.7 19.3 %copy-start.21 = (f32[1,1,4,256]{3,2,1,0:T(4,128)S(1)}, f32[1,1,4,256]{3,2,1,0:T(4,128)}, u32[]{:S(2)}) copy-start(f32[1,1,4,256]{3,2,1,0:T(4,128)} %copy-done.19) | copy-start | bytes 12292
  43.9 15.3 %collective-permute-start.4 = (f32[222,128]{1,0:T(8,128)S(1)}, f32[222,128]{1,0:T(8,128)S(1)}, u32[]{:S(2)}, u32[]{:S(2)}) collective-permute-start(f32[222,128]{1,0:T(8,128)S(1)} %pad_maximum_fusion.34), channel_id=1, source_target_pairs={{0,1},{1,2},{2,3},{3,4},{4,5},{5,6},{6,7},{7,8},{8,9},{9,10},{10,1... | collective-permute-start | bytes 341000 | tf_op jit(solution)/shard_map/ppermute | solution.py:205
  45.8 13.4 %collective-permute-start.5 = (f32[222,128]{1,0:T(8,128)S(1)}, f32[222,128]{1,0:T(8,128)S(1)}, u32[]{:S(2)}, u32[]{:S(2)}) collective-permute-start(f32[222,128]{1,0:T(8,128)S(1)} %pad_maximum_fusion.35), channel_id=1, source_target_pairs={{1,0},{2,1},{3,2},{4,3},{5,4},{6,5},{7,6},{8,7},{9,8},{10,9},{11,1... | collective-permute-start | bytes 341000 | tf_op jit(solution)/shard_map/ppermute | solution.py:206
  51.6 24.1 %collective-permute-start.7 = (f32[32,1,16,128]{3,0,2,1:T(8,128)S(1)}, f32[32,1,16,128]{3,0,2,1:T(8,128)S(1)}, u32[]{:S(2)}, u32[]{:S(2)}) collective-permute-start(f32[32,1,16,128]{3,0,2,1:T(8,128)S(1)} %get-tuple-element.34), channel_id=1, source_target_pairs={{0,16},{16,32},{32,48},{48,64},{64,80},{80,96},{96,112},{112,128},... | collective-permute-start | bytes 786440 | tf_op jit(solution)/shard_map/ppermute | solution.py:44
  55.2 20.6 %collective-permute-start.6 = (f32[32,1,16,128]{3,0,2,1:T(8,128)S(1)}, f32[32,1,16,128]{3,0,2,1:T(8,128)}, u32[]{:S(2)}, u32[]{:S(2)}) collective-permute-start(f32[32,1,16,128]{3,0,2,1:T(8,128)S(1)} %get-tuple-element.33), channel_id=1, source_target_pairs={{16,0},{32,16},{48,32},{64,48},{80,64},{96,80},{112,96},{128,112},... | collective-permute-start | bytes 786440 | tf_op jit(solution)/shard_map/ppermute | solution.py:45
  79.8 23.2 %collective-permute-start.9 = (f32[32,1,16,128]{3,0,2,1:T(8,128)}, f32[32,1,16,128]{3,0,2,1:T(8,128)S(1)}, u32[]{:S(2)}, u32[]{:S(2)}) collective-permute-start(f32[32,1,16,128]{3,0,2,1:T(8,128)} %get-tuple-element.32), channel_id=1, source_target_pairs={{0,16},{16,32},{32,48},{48,64},{64,80},{80,96},{96,112},{112,128},... | collective-permute-start | bytes 786440 | tf_op jit(solution)/shard_map/ppermute | solution.py:44
  90.6 12.5 %collective-permute-start.8 = (f32[32,1,16,128]{3,0,2,1:T(8,128)}, f32[32,1,16,128]{3,0,2,1:T(8,128)S(1)}, u32[]{:S(2)}, u32[]{:S(2)}) collective-permute-start(f32[32,1,16,128]{3,0,2,1:T(8,128)} %get-tuple-element.31), channel_id=1, source_target_pairs={{16,0},{32,16},{48,32},{64,48},{80,64},{96,80},{112,96},{128,112},... | collective-permute-start | bytes 786440 | tf_op jit(solution)/shard_map/ppermute | solution.py:45
  92.6 10.6 %collective-permute-start.11 = (f32[32,4,1,128]{3,0,2,1:T(8,128)}, f32[32,4,1,128]{3,0,2,1:T(8,128)S(1)}, u32[]{:S(2)}, u32[]{:S(2)}) collective-permute-start(f32[32,4,1,128]{3,0,2,1:T(8,128)} %get-tuple-element.30), channel_id=1, source_target_pairs={{0,1},{1,2},{2,3},{3,4},{4,5},{5,6},{6,7},{7,8},{8,9},{9,10},{10,1... | collective-permute-start | bytes 196616 | tf_op jit(solution)/shard_map/ppermute | solution.py:44
  94.5 8.7 %collective-permute-start.10 = (f32[32,4,1,128]{3,0,2,1:T(8,128)}, f32[32,4,1,128]{3,0,2,1:T(8,128)S(1)}, u32[]{:S(2)}, u32[]{:S(2)}) collective-permute-start(f32[32,4,1,128]{3,0,2,1:T(8,128)} %get-tuple-element.29), channel_id=1, source_target_pairs={{1,0},{2,1},{3,2},{4,3},{5,4},{6,5},{7,6},{8,7},{9,8},{10,9},{11,1... | collective-permute-start | bytes 196616 | tf_op jit(solution)/shard_map/ppermute | solution.py:45
  104.4 19.7 %collective-permute-start.12 = (f32[32,1,16,128]{3,0,2,1:T(8,128)S(1)}, f32[32,1,16,128]{3,0,2,1:T(8,128)S(1)}, u32[]{:S(2)}, u32[]{:S(2)}) collective-permute-start(f32[32,1,16,128]{3,0,2,1:T(8,128)S(1)} %get-tuple-element.28), channel_id=1, source_target_pairs={{16,0},{32,16},{48,32},{64,48},{80,64},{96,80},{112,96},{128,112},... | collective-permute-start | bytes 786440 | tf_op jit(solution)/shard_map/ppermute | solution.py:45
  106.9 17.2 %collective-permute-start.13 = (f32[32,1,16,128]{3,0,2,1:T(8,128)S(1)}, f32[32,1,16,128]{3,0,2,1:T(8,128)S(1)}, u32[]{:S(2)}, u32[]{:S(2)}) collective-permute-start(f32[32,1,16,128]{3,0,2,1:T(8,128)S(1)} %get-tuple-element.27), channel_id=1, source_target_pairs={{0,16},{16,32},{32,48},{48,64},{64,80},{80,96},{96,112},{112,128},... | collective-permute-start | bytes 786440 | tf_op jit(solution)/shard_map/ppermute | solution.py:44
  114.5 9.6 %collective-permute-start.15 = (f32[32,4,1,128]{3,0,2,1:T(8,128)S(1)}, f32[32,4,1,128]{3,0,2,1:T(8,128)S(1)}, u32[]{:S(2)}, u32[]{:S(2)}) collective-permute-start(f32[32,4,1,128]{3,0,2,1:T(8,128)S(1)} %get-tuple-element.26), channel_id=1, source_target_pairs={{0,1},{1,2},{2,3},{3,4},{4,5},{5,6},{6,7},{7,8},{8,9},{9,10},{10,1... | collective-permute-start | bytes 196616 | tf_op jit(solution)/shard_map/ppermute | solution.py:44
  116.4 7.7 %collective-permute-start.14 = (f32[32,4,1,128]{3,0,2,1:T(8,128)S(1)}, f32[32,4,1,128]{3,0,2,1:T(8,128)S(1)}, u32[]{:S(2)}, u32[]{:S(2)}) collective-permute-start(f32[32,4,1,128]{3,0,2,1:T(8,128)S(1)} %get-tuple-element.25), channel_id=1, source_target_pairs={{1,0},{2,1},{3,2},{4,3},{5,4},{6,5},{7,6},{8,7},{9,8},{10,9},{11,1... | collective-permute-start | bytes 196616 | tf_op jit(solution)/shard_map/ppermute | solution.py:45
  (11 other events, 17.9 us)

commit v8 on v7

--- a/solution.py
+++ b/solution.py
@@ -298,6 +298,55 @@
     )(*x_flats, *side_flats, *corner_flats)
 
 
+def diagonal(block, step_x, step_y):
+    count_x = lax.axis_size("gx")
+    count_y = lax.axis_size("gy")
+    pairs = []
+    for i in range(count_x):
+        for j in range(count_y):
+            if 0 <= i + step_x < count_x and 0 <= j + step_y < count_y:
+                pairs.append((i * count_y + j, (i + step_x) * count_y + j + step_y))
+    return lax.ppermute(block, ("gx", "gy"), pairs)
+
+
+def two_substeps(current, source, source_halos, rates, mixing, work):
+    species, width, depth, lanes = current.shape
+    (x_low,), (x_high,), *_ = send_pair("gx", [current[:, -2:]], [current[:, :2]])
+    (y_low,), (y_high,), *_ = send_pair("gy", [current[:, :, -2:]], [current[:, :, :2]])
+    low_low = diagonal(current[:, -1:, -1:], 1, 1)
+    low_high = diagonal(current[:, -1:, :1], 1, -1)
+    high_low = diagonal(current[:, :1, -1:], -1, 1)
+    high_high = diagonal(current[:, :1, :1], -1, -1)
+    done = work()
+    current, done = lax.optimization_barrier((current, done))
+    gap = jnp.zeros((species, 2, 2, lanes), current.dtype)
+    left = jnp.concatenate([gap, y_low, gap], axis=1)
+    right = jnp.concatenate([gap, y_high, gap], axis=1)
+    padded = jnp.concatenate([left, jnp.concatenate([x_low, current, x_high], axis=1), right], axis=2)
+    padded = padded.at[:, 1:2, 1:2].set(low_low)
+    padded = padded.at[:, 1:2, depth + 2 : depth + 3].set(low_high)
+    padded = padded.at[:, width + 2 : width + 3, 1:2].set(high_low)
+    padded = padded.at[:, width + 2 : width + 3, depth + 2 : depth + 3].set(high_high)
+    s_x_low, s_x_high, s_y_low, s_y_high = source_halos
+    corner = jnp.zeros((species, 1, 1, lanes), current.dtype)
+    s_left = jnp.concatenate([corner, s_y_low, corner], axis=1)
+    s_right = jnp.concatenate([corner, s_y_high, corner], axis=1)
+    wide_source = jnp.concatenate(
+        [s_left, jnp.concatenate([s_x_low, source, s_x_high], axis=1), s_right], axis=2
+    )
+    wide = advance(padded, wide_source, rates, mixing)
+    row = lax.broadcasted_iota(jnp.int32, (1, width + 2, depth + 2, 1), 1)
+    col = lax.broadcasted_iota(jnp.int32, (1, width + 2, depth + 2, 1), 2)
+    edge_x = lax.axis_size("gx") - 1
+    edge_y = lax.axis_size("gy") - 1
+    outside = (row == 0) & (lax.axis_index("gx") == 0)
+    outside = outside | ((row == width + 1) & (lax.axis_index("gx") == edge_x))
+    outside = outside | ((col == 0) & (lax.axis_index("gy") == 0))
+    outside = outside | ((col == depth + 1) & (lax.axis_index("gy") == edge_y))
+    wide = jnp.where(outside, 0.0, wide)
+    return advance(wide, source, rates, mixing), done
+
+
 def on_device(
     field,
     rates,
@@ -329,11 +378,13 @@
     current = advance(framed(current, x_low, x_high, y_low, y_high), source, rates, mixing)
 
     row_points = jnp.concatenate([points_low, points, points_high], axis=1)
-    x_low, x_high = halos(current, "gx", 1)
-    (y_low, points_low, corner_up), (y_high, points_high, corner_down), *corner_flats = send_pair(
+    (x_low, s_x_low), (x_high, s_x_high), *_ = send_pair(
+        "gx", [current[:, -1:], source[:, -1:]], [current[:, :1], source[:, :1]]
+    )
+    (y_low, points_low, corner_up, s_y_low), (y_high, points_high, corner_down, s_y_high), *corner_flats = send_pair(
         "gy",
-        [current[:, :, -1:], row_points[:, :, -1:], jnp.stack([moved_down[2], moved_up[2]])],
-        [current[:, :, :1], row_points[:, :, :1], jnp.stack([moved_down[0], moved_up[0]])],
+        [current[:, :, -1:], row_points[:, :, -1:], jnp.stack([moved_down[2], moved_up[2]]), source[:, :, -1:]],
+        [current[:, :, :1], row_points[:, :, :1], jnp.stack([moved_down[0], moved_up[0]]), source[:, :, :1]],
     )
     bordered = jnp.concatenate([points_low, row_points, points_high], axis=2)
     field_rows = x_low.size // 128
@@ -350,8 +401,8 @@
     def later_work():
         return pallas_forces(points, bordered, occupancy, partial, (2, 3), True)
 
-    current, force = substep_beside(current, source, rates, mixing, later_work)
-    current = substep(current, source, rates, mixing)
+    source_halos = (s_x_low, s_x_high, s_y_low, s_y_high)
+    current, force = two_substeps(current, source, source_halos, rates, mixing, later_work)
     displacement = force.reshape(3, 1, rows, points.shape[3])
     return (current, displacement, arrived)
 

time: 130 us -> 155 us (1.19)
  local copies, waits for them, and re-layouts: 21.4 us -> 32.4 us
  other arithmetic: 10.5 us -> 20.1 us
  waiting for transfers between devices: 0.04 us -> 7.04 us
  starting transfers between devices: 64.9 us -> 62.4 us
    ppermute x10 -> x4, starting transfers between devices: 40.2 us -> 15 us  [diagonal(): return lax.ppermute(block, ('gx', 'gy'), pairs)]
    ppermute x3 -> x6, starting transfers between devices: 10.2 us -> 24.3 us  [send_pair(): below = lax.ppermute(pack(upward), axis, up)]
    ppermute x3 -> x6, starting transfers between devices: 14.6 us -> 23.1 us  [send_pair(): above = lax.ppermute(pack(downward), axis, down)]
    slice x5 -> x10, local copies, waits for them, and re-layouts: 1.57 us -> 7 us  [the longest x4 3.35 us: advance(): center = padded[:, 1:-1, 1:-1, :]]
    select_n x0 -> x1, other arithmetic: none -> 5.07 us  [two_substeps(): wide = jnp.where(outside, 0.0, wide)]
    concatenate x5 -> x7, other arithmetic: 0.8 us -> 5.64 us  [pack(): jnp.concatenate([jnp.transpose(piece, storage_order(piece)).reshape(-1, 1...]
    ppermute x10 -> x4, waiting for transfers between devices: 0.03 us -> 3.58 us  [diagonal(): return lax.ppermute(block, ('gx', 'gy'), pairs)]
    ppermute x3 -> x6, waiting for transfers between devices: 0.01 us -> 3.45 us  [send_pair(): below = lax.ppermute(pack(upward), axis, up)]
  transfers between devices with their start and end apart: 16 -> 16, of which waited for: 0 -> 3; matrix products, arithmetic and copies ran while one was open for 15% -> 15% of each run, Pallas kernels for 16% -> 13%
where the time goes in v8:
time: 155 us; the launch traced here: 154 us
  starting transfers between devices  62.4 us (40%)
  local copies, waits for them, and re-layouts  32.4 us (21%)
  Pallas kernels  20.2 us (13%)
  other arithmetic  20.1 us (13%)
  matrix products  9.84 us (6%)
  waiting for transfers between devices  7.04 us (5%)
  between operations  1.58 us (1%)
    ppermute x6, starting transfers between devices, send_pair(): below = lax.ppermute(pack(upward), axis, up)  24.3 us
    ppermute x6, starting transfers between devices, send_pair(): above = lax.ppermute(pack(downward), axis, down)  23.1 us
    ppermute x4, starting transfers between devices, diagonal(): return lax.ppermute(block, ('gx', 'gy'), pairs)  15 us
    pallas_call x2, Pallas kernels, pallas_forces(): pl.pallas_call(functools.partial(forces_kernel, span, scale), out_shape=j...  11.9 us
    dot_general x4, matrix products, advance(): jnp.dot(mixing, center.reshape(species, -1), precision=lax.Precision.HIGH...  9.84 us
    unnamed x78, local copies, waits for them, and re-layouts  9.14 us
    pallas_call x1, Pallas kernels, deposit(): pl.pallas_call(deposit_kernel, out_shape=jax.ShapeDtypeStruct((BIN_XY, bi...  6.34 us
    concatenate x7, other arithmetic, pack(): jnp.concatenate([jnp.transpose(piece, storage_order(piece)).reshape(-1, 1...  5.64 us
  transfers between devices with their start and end apart: 16, of which 3 were waited for; matrix products, arithmetic and copies ran while one was open for 15% of the time, Pallas kernels for 13%

profile of v8, /device:TPU:120, one launch (start us, length us, event | category | flops | bytes accessed | tf_op | source)
XLA Modules:
  0.0 153.5 jit_solution(7488796669151097362)
XLA Ops:
  4.4 1.9 %collective-permute-start.3 = (f32[163,128]{1,0:T(8,128)}, f32[163,128]{1,0:T(8,128)}, u32[]{:S(2)}, u32[]{:S(2)}) collective-permute-start(f32[163,128]{1,0:T(8,128)} %pad_maximum_fusion.28), channel_id=1, source_target_pairs={{0,1},{1,2},{2,3},{3,4},{4,5},{5,6},{6,7},{7,8},{8,9},{9,10},{10,1... | collective-permute-start | bytes 250376 | tf_op jit(solution)/shard_map/ppermute | solution.py:205
  7.0 5.7 %collective-permute-start.2 = (f32[163,128]{1,0:T(8,128)}, f32[163,128]{1,0:T(8,128)}, u32[]{:S(2)}, u32[]{:S(2)}) collective-permute-start(f32[163,128]{1,0:T(8,128)} %pad_maximum_fusion.27), channel_id=1, source_target_pairs={{1,0},{2,1},{3,2},{4,3},{5,4},{6,5},{7,6},{8,7},{9,8},{10,9},{11,1... | collective-permute-start | bytes 250376 | tf_op jit(solution)/shard_map/ppermute | solution.py:206
  13.7 5.7 %collective-permute-start.1 = (f32[649,128]{1,0:T(8,128)S(1)}, f32[649,128]{1,0:T(8,128)S(1)}, u32[]{:S(2)}, u32[]{:S(2)}) collective-permute-start(f32[649,128]{1,0:T(8,128)S(1)} %get-tuple-element.113), channel_id=1, source_target_pairs={{0,16},{16,32},{32,48},{48,64},{64,80},{80,96},{96,112},{112,128},... | collective-permute-start | bytes 996872 | tf_op jit(solution)/shard_map/ppermute | solution.py:205
  19.5 1.9 %collective-permute-start = (f32[649,128]{1,0:T(8,128)S(1)}, f32[649,128]{1,0:T(8,128)S(1)}, u32[]{:S(2)}, u32[]{:S(2)}) collective-permute-start(f32[649,128]{1,0:T(8,128)S(1)} %get-tuple-element.114), channel_id=1, source_target_pairs={{16,0},{32,16},{48,32},{64,48},{80,64},{96,80},{112,96},{128,112},... | collective-permute-start | bytes 996872 | tf_op jit(solution)/shard_map/ppermute | solution.py:206
  25.9 6.3 %shard_map.121 = f32[4,16,32,128]{3,2,1,0:T(8,128)} custom-call(f32[16,128,16]{2,1,0:T(8,128)} %bitcast.194, f32[16,4,16]{2,1,0:T(4,128)} %bitcast.223), custom_call_target="tpu_custom_call" | custom-call | flops 10000000 | bytes 1300000 | tf_op jit(solution)/shard_map/pallas_call | solution.py:135
  32.3 1.9 %fusion.59 = (f32[32,1,16,128]{3,0,2,1:T(8,128)}, f32[32,1,16,128]{3,0,2,1:T(8,128)}) fusion(f32[32,4,16,128]{3,0,2,1:T(8,128)} %bitcast.187), kind=kLoop, calls=%fused_computation.138 | loop fusion | bytes 1048576 | tf_op jit(solution)/shard_map/slice | solution.py:382
  38.7 2.1 %fusion.13 = f32[32,4,16,128]{3,0,2,1:T(8,128)S(1)} fusion(f32[32,4,16,128]{3,0,2,1:T(8,128)S(1)} %copy-done.10, f32[32,1,1,128]{3,0,2,1:T(8,128)S(1)} %broadcast.171, f32[32,1,16,128]{3,0,2,1:T(8,128)S(1)} %bitcast.216, f32[32,1,16,128]{3,0,2,1:T(8,128)S(1)} %bitcast.215, f32[32,4,1,128]{3,0,2,1:T(8,128)S(1)} %bitcast.228, ...), kind=kOutput, calls=%fused_computation.38 | convolution fusion | flops 107479040 | bytes 4870272 | tf_op jit(solution)/shard_map/dot_general | solution.py:88
  43.4 1.9 %collective-permute-start.4 = (f32[350,128]{1,0:T(8,128)S(1)}, f32[350,128]{1,0:T(8,128)S(1)}, u32[]{:S(2)}, u32[]{:S(2)}) collective-permute-start(f32[350,128]{1,0:T(8,128)S(1)} %pad_maximum_fusion.24), channel_id=1, source_target_pairs={{0,1},{1,2},{2,3},{3,4},{4,5},{5,6},{6,7},{7,8},{8,9},{9,10},{10,1... | collective-permute-start | bytes 537608 | tf_op jit(solution)/shard_map/ppermute | solution.py:205
  46.2 5.8 %collective-permute-start.5 = (f32[350,128]{1,0:T(8,128)S(1)}, f32[350,128]{1,0:T(8,128)S(1)}, u32[]{:S(2)}, u32[]{:S(2)}) collective-permute-start(f32[350,128]{1,0:T(8,128)S(1)} %pad_maximum_fusion.25), channel_id=1, source_target_pairs={{1,0},{2,1},{3,2},{4,3},{5,4},{6,5},{7,6},{8,7},{9,8},{10,9},{11,1... | collective-permute-start | bytes 537608 | tf_op jit(solution)/shard_map/ppermute | solution.py:206
  52.0 1.8 %pad_maximum_fusion.20 = f32[1024,128]{1,0:T(8,128)} fusion(f32[512,128]{1,0:T(8,128)S(1)} %bitcast.205, f32[512,128]{1,0:T(8,128)} %bitcast.207), kind=kLoop, calls=%fused_computation.92 | loop fusion | flops 131072 | bytes 1048576 | tf_op jit(solution)/shard_map/concatenate | solution.py:184
  53.7 3.7 %collective-permute-start.6 = (f32[1024,128]{1,0:T(8,128)}, f32[1024,128]{1,0:T(8,128)}, u32[]{:S(2)}, u32[]{:S(2)}) collective-permute-start(f32[1024,128]{1,0:T(8,128)} %pad_maximum_fusion.20), channel_id=1, source_target_pairs={{16,0},{32,16},{48,32},{64,48},{80,64},{96,80},{112,96},{128,112},... | collective-permute-start | bytes 1572872 | tf_op jit(solution)/shard_map/ppermute | solution.py:206
  58.3 5.9 %collective-permute-start.7 = (f32[1024,128]{1,0:T(8,128)}, f32[1024,128]{1,0:T(8,128)}, u32[]{:S(2)}, u32[]{:S(2)}) collective-permute-start(f32[1024,128]{1,0:T(8,128)} %pad_maximum_fusion.21), channel_id=1, source_target_pairs={{0,16},{16,32},{32,48},{48,64},{64,80},{80,96},{96,112},{112,128},... | collective-permute-start | bytes 1572872 | tf_op jit(solution)/shard_map/ppermute | solution.py:205
  66.2 7.4 %shard_map.123.start_ref = f32[3,4,256]{2,1,0:T(4,128)} custom-call(f32[4,4,256]{2,1,0:T(4,128)} %get-tuple-element.111.own_ref, f32[4,3,6,256]{3,2,1,0:T(8,128)} %pad_maximum_fusion.26.near_ref, f32[4,256]{1,0:T(4,128)} %get-tuple-element.115.occ_ref, f32[3,4,256]{2,1,0:T(4,128)} %broadcast_in_dim.34.start_ref), custom_call_target="tpu_custom_call" | custom-call | flops 6000000 | bytes 120000 | tf_op jit(solution)/shard_map/pallas_call | solution.py:266
  73.7 1.9 %shard_map.122 = f32[8,35,128]{2,1,0:T(8,128)} custom-call(f32[649,128]{1,0:T(8,128)} %copy-done.6, f32[649,128]{1,0:T(8,128)} %copy-done.7, f32[163,128]{1,0:T(8,128)} %collective-permute-done.3.side_below, f32[163,128]{1,0:T(8,128)} %collective-permute-done.2.side_above, f32[350,128]{1,0:T(8,128)} %copy-done.15, f32[350,128]{1,0:T(8,128)} %copy-done.17), custom_call_target="tpu_custom_call" | custom-call | bytes 300000 | tf_op jit(solution)/shard_map/pallas_call | solution.py:294
  79.5 2.0 %collective-permute-done.7 = f32[1024,128]{1,0:T(8,128)} collective-permute-done((f32[1024,128]{1,0:T(8,128)}, f32[1024,128]{1,0:T(8,128)}, u32[]{:S(2)}, u32[]{:S(2)}) %collective-permute-start.7) | collective-permute-done | bytes 524320 | tf_op jit(solution)/shard_map/ppermute | solution.py:205
  81.5 1.8 %fusion.62 = (f32[512,128]{1,0:T(8,128)}, f32[512,128]{1,0:T(8,128)S(1)}) fusion(f32[1024,128]{1,0:T(8,128)} %collective-permute-done.7), kind=kLoop, calls=%fused_computation.141 | loop fusion | bytes 1048576 | tf_op jit(solution)/shard_map/slice | solution.py:195
  85.7 2.4 %collective-permute-start.10 = (f32[1024,128]{1,0:T(8,128)}, f32[1024,128]{1,0:T(8,128)S(1)}, u32[]{:S(2)}, u32[]{:S(2)}) collective-permute-start(f32[1024,128]{1,0:T(8,128)} %bitcast.80), channel_id=1, source_target_pairs={{16,0},{32,16},{48,32},{64,48},{80,64},{96,80},{112,96},{128,112},... | collective-permute-start | bytes 1572872 | tf_op jit(solution)/shard_map/ppermute | solution.py:206
  88.1 7.0 %collective-permute-start.9 = (f32[1024,128]{1,0:T(8,128)S(1)}, f32[1024,128]{1,0:T(8,128)S(1)}, u32[]{:S(2)}, u32[]{:S(2)}) collective-permute-start(f32[1024,128]{1,0:T(8,128)S(1)} %bitcast.210), channel_id=1, source_target_pairs={{0,16},{16,32},{32,48},{48,64},{64,80},{80,96},{96,112},{112,128},... | collective-permute-start | bytes 1572872 | tf_op jit(solution)/shard_map/ppermute | solution.py:205
  96.5 4.5 %shard_map.124 = f32[3,4,256]{2,1,0:T(4,128)} custom-call(f32[4,4,256]{2,1,0:T(4,128)} %get-tuple-element.111.own_ref, f32[4,3,6,256]{3,2,1,0:T(8,128)} %pad_maximum_fusion.26.near_ref, f32[4,256]{1,0:T(4,128)} %get-tuple-element.115.occ_ref, f32[3,4,256]{2,1,0:T(4,128)} %shard_map.123.start_ref), custom_call_target="tpu_custom_call" | custom-call | flops 3000000 | bytes 120000 | tf_op jit(solution)/shard_map/pallas_call | solution.py:266
  101.0 3.5 %collective-permute-start.11 = (f32[256,128]{1,0:T(8,128)S(1)}, f32[256,128]{1,0:T(8,128)S(1)}, u32[]{:S(2)}, u32[]{:S(2)}) collective-permute-start(f32[256,128]{1,0:T(8,128)S(1)} %bitcast.227), channel_id=1, source_target_pairs={{1,0},{2,1},{3,2},{4,3},{5,4},{6,5},{7,6},{8,7},{9,8},{10,9},{11,1... | collective-permute-start | bytes 393224 | tf_op jit(solution)/shard_map/ppermute | solution.py:206
  104.4 1.9 %collective-permute-start.8 = (f32[256,128]{1,0:T(8,128)S(1)}, f32[256,128]{1,0:T(8,128)S(1)}, u32[]{:S(2)}, u32[]{:S(2)}) collective-permute-start(f32[256,128]{1,0:T(8,128)S(1)} %bitcast.226), channel_id=1, source_target_pairs={{0,1},{1,2},{2,3},{3,4},{4,5},{5,6},{6,7},{7,8},{8,9},{9,10},{10,1... | collective-permute-start | bytes 393224 | tf_op jit(solution)/shard_map/ppermute | solution.py:205
  106.4 3.1 %collective-permute-start.15 = (f32[32,1,1,128]{3,0,2,1:T(8,128)S(1)}, f32[32,1,1,128]{3,0,2,1:T(8,128)S(1)}, u32[]{:S(2)}, u32[]{:S(2)}) collective-permute-start(f32[32,1,1,128]{3,0,2,1:T(8,128)S(1)} %get-tuple-element.73), channel_id=1, source_target_pairs={{17,0},{18,1},{19,2},{20,3},{21,4},{22,5},{23,6},{24,7},{25,8},{26... | collective-permute-start | bytes 49160 | tf_op jit(solution)/shard_map/ppermute | solution.py:309
  109.5 1.9 %collective-permute-start.14 = (f32[32,1,1,128]{3,0,2,1:T(8,128)S(1)}, f32[32,1,1,128]{3,0,2,1:T(8,128)S(1)}, u32[]{:S(2)}, u32[]{:S(2)}) collective-permute-start(f32[32,1,1,128]{3,0,2,1:T(8,128)S(1)} %get-tuple-element.74), channel_id=1, source_target_pairs={{16,1},{17,2},{18,3},{19,4},{20,5},{21,6},{22,7},{23,8},{24,9},{25... | collective-permute-start | bytes 49160 | tf_op jit(solution)/shard_map/ppermute | solution.py:309
  112.8 7.7 %collective-permute-start.13 = (f32[32,1,1,128]{3,0,2,1:T(8,128)S(1)}, f32[32,1,1,128]{3,0,2,1:T(8,128)S(1)}, u32[]{:S(2)}, u32[]{:S(2)}) collective-permute-start(f32[32,1,1,128]{3,0,2,1:T(8,128)S(1)} %get-tuple-element.75), channel_id=1, source_target_pairs={{1,16},{2,17},{3,18},{4,19},{5,20},{6,21},{7,22},{8,23},{9,24},{10... | collective-permute-start | bytes 49160 | tf_op jit(solution)/shard_map/ppermute | solution.py:309
  120.5 2.4 %collective-permute-start.12 = (f32[32,1,1,128]{3,0,2,1:T(8,128)S(1)}, f32[32,1,1,128]{3,0,2,1:T(8,128)S(1)}, u32[]{:S(2)}, u32[]{:S(2)}) collective-permute-start(f32[32,1,1,128]{3,0,2,1:T(8,128)S(1)} %get-tuple-element.76), channel_id=1, source_target_pairs={{0,17},{1,18},{2,19},{3,20},{4,21},{5,22},{6,23},{7,24},{8,25},{9,... | collective-permute-start | bytes 49160 | tf_op jit(solution)/shard_map/ppermute | solution.py:309
  125.3 3.6 %collective-permute-done.12 = f32[32,1,1,128]{3,0,2,1:T(8,128)S(1)} collective-permute-done((f32[32,1,1,128]{3,0,2,1:T(8,128)S(1)}, f32[32,1,1,128]{3,0,2,1:T(8,128)S(1)}, u32[]{:S(2)}, u32[]{:S(2)}) %collective-permute-start.12) | collective-permute-done | bytes 16416 | tf_op jit(solution)/shard_map/ppermute | solution.py:309
  130.3 2.5 %copy.55 = f32[32,6,18,128]{3,2,1,0:T(8,128)} copy(f32[32,6,18,128]{3,0,2,1:T(8,128)S(1)} %slice.478) | data formatting | bytes 3538944 | tf_op jit(solution)/shard_map/slice | solution.py:81
  132.8 2.9 %reshape.440 = f32[32,13824]{1,0:T(8,128)} reshape(f32[32,6,18,128]{3,2,1,0:T(8,128)} %copy.55) | data formatting | bytes 3538944 | tf_op jit(solution)/shard_map/reshape | solution.py:88
  135.7 4.4 %fusion = f32[32,13824]{1,0:T(8,128)} fusion(f32[32,13824]{1,0:T(8,128)} %reshape.440, f32[32,32]{1,0:T(8,128)S(1)} %copy-done), kind=kOutput, calls=%fused_computation.1 | convolution fusion | flops 170311680 | bytes 3543040 | tf_op jit(solution)/shard_map/dot_general | solution.py:88
  140.1 3.0 %mul.129 = f32[32,6,18,128]{3,2,1,0:T(8,128)} reshape(f32[32,13824]{1,0:T(8,128)} %fusion) | data formatting | bytes 3538944 | tf_op jit(solution)/shard_map/mul | solution.py:94
  143.2 5.1 %fusion.9 = f32[32,6,18,128]{3,0,2,1:T(8,128)S(1)} fusion(f32[32,6,18,128]{3,0,2,1:T(8,128)} %copy-done.3, f32[32,8,20,128]{3,0,2,1:T(8,128)S(1)} %constant_dynamic-update-slice_fusion.3, f32[32,1,1,128]{3,0,2,1:T(8,128)S(1)} %copy-done.22, f32[32,4,1,128]{3,0,2,1:T(8,128)S(1)} %bitcast.212, f32[32,1,16,128]{3,0,2,1:T(8,128)S(1)} %bitcast.197, ...), kind=kLoop, calls=%fused_computation.21 | loop fusion | flops 9732096 | bytes 14106860 | tf_op jit(solution)/shard_map/jit(_where)/select_n | solution.py:346
  149.0 1.7 %fusion.11 = f32[4,8,64,128]{3,1,2,0:T(8,128)S(1)} fusion(f32[32,32]{1,0:T(8,128)S(1)} %copy-done, f32[4,8,64,128]{3,2,1,0:T(8,128)S(1)} %bitcast.195), kind=kOutput, calls=%fused_computation.35 | convolution fusion | flops 100925440 | bytes 2101248 | tf_op jit(solution)/shard_map/dot_general | solution.py:88
  (162 shorter events, 36.6 us)
Async XLA Ops:
  0.6 38.0 %copy-start = (f32[32,32]{1,0:T(8,128)S(1)}, f32[32,32]{1,0:T(8,128)}, u32[]{:S(2)}) copy-start(f32[32,32]{1,0:T(8,128)} %param.20) | copy-start | bytes 12292
  0.6 12.1 %copy-start.5 = (f32[32,4,16,128]{3,2,1,0:T(8,128)S(1)}, f32[32,4,16,128]{3,2,1,0:T(8,128)}, u32[]{:S(2)}) copy-start(f32[32,4,16,128]{3,2,1,0:T(8,128)} %param.18) | copy-start | bytes 3145732
  0.7 12.1 %copy-start.25 = (s32[1,4,256]{2,1,0:T(4,128)S(1)}, s32[1,4,256]{2,1,0:T(4,128)}, u32[]{:S(2)}) copy-start(s32[1,4,256]{2,1,0:T(4,128)} %param.24) | copy-start | bytes 12292
  0.7 12.1 %copy-start.29 = (f32[1,4,256]{2,1,0:T(4,128)S(1)}, f32[1,4,256]{2,1,0:T(4,128)}, u32[]{:S(2)}) copy-start(f32[1,4,256]{2,1,0:T(4,128)} %param.23) | copy-start | bytes 12292
  0.7 12.1 %copy-start.24 = (f32[3,1,4,256]{3,2,1,0:T(4,128)S(1)}, f32[3,1,4,256]{3,2,1,0:T(4,128)}, u32[]{:S(2)}) copy-start(f32[3,1,4,256]{3,2,1,0:T(4,128)} %param.22) | copy-start | bytes 36868
  4.4 31.7 %collective-permute-start.3 = (f32[163,128]{1,0:T(8,128)}, f32[163,128]{1,0:T(8,128)}, u32[]{:S(2)}, u32[]{:S(2)}) collective-permute-start(f32[163,128]{1,0:T(8,128)} %pad_maximum_fusion.28), channel_id=1, source_target_pairs={{0,1},{1,2},{2,3},{3,4},{4,5},{5,6},{6,7},{7,8},{8,9},{9,10},{10,1... | collective-permute-start | bytes 250376 | tf_op jit(solution)/shard_map/ppermute | solution.py:205
  7.0 30.0 %collective-permute-start.2 = (f32[163,128]{1,0:T(8,128)}, f32[163,128]{1,0:T(8,128)}, u32[]{:S(2)}, u32[]{:S(2)}) collective-permute-start(f32[163,128]{1,0:T(8,128)} %pad_maximum_fusion.27), channel_id=1, source_target_pairs={{1,0},{2,1},{3,2},{4,3},{5,4},{6,5},{7,6},{8,7},{9,8},{10,9},{11,1... | collective-permute-start | bytes 250376 | tf_op jit(solution)/shard_map/ppermute | solution.py:206
  13.7 9.3 %copy-start.30 = (s32[1,4,256]{2,1,0:T(4,128)S(1)}, s32[1,4,256]{2,1,0:T(4,128)}, u32[]{:S(2)}) copy-start(s32[1,4,256]{2,1,0:T(4,128)} %param.25) | copy-start | bytes 12292
  13.7 10.7 %copy-start.23 = (f32[32,1,4,256]{3,2,1,0:T(4,128)S(1)}, f32[32,1,4,256]{3,2,1,0:T(4,128)}, u32[]{:S(2)}) copy-start(f32[32,1,4,256]{3,2,1,0:T(4,128)} %param.21) | copy-start | bytes 393220
  13.7 24.1 %collective-permute-start.1 = (f32[649,128]{1,0:T(8,128)S(1)}, f32[649,128]{1,0:T(8,128)S(1)}, u32[]{:S(2)}, u32[]{:S(2)}) collective-permute-start(f32[649,128]{1,0:T(8,128)S(1)} %get-tuple-element.113), channel_id=1, source_target_pairs={{0,16},{16,32},{32,48},{48,64},{64,80},{80,96},{96,112},{112,128},... | collective-permute-start | bytes 996872 | tf_op jit(solution)/shard_map/ppermute | solution.py:205
  19.5 18.4 %collective-permute-start = (f32[649,128]{1,0:T(8,128)S(1)}, f32[649,128]{1,0:T(8,128)S(1)}, u32[]{:S(2)}, u32[]{:S(2)}) collective-permute-start(f32[649,128]{1,0:T(8,128)S(1)} %get-tuple-element.114), channel_id=1, source_target_pairs={{16,0},{32,16},{48,32},{64,48},{80,64},{96,80},{112,96},{128,112},... | collective-permute-start | bytes 996872 | tf_op jit(solution)/shard_map/ppermute | solution.py:206
  40.8 11.1 %copy-start.12 = (f32[32,1,16,128]{3,0,2,1:T(8,128)S(1)}, f32[32,1,16,128]{3,0,2,1:T(8,128)}, u32[]{:S(2)}) copy-start(f32[32,1,16,128]{3,0,2,1:T(8,128)} %get-tuple-element.84) | copy-start | bytes 786436
  41.5 16.0 %copy-start.11 = (f32[32,1,16,128]{3,0,2,1:T(8,128)S(1)}, f32[32,1,16,128]{3,0,2,1:T(8,128)}, u32[]{:S(2)}) copy-start(f32[32,1,16,128]{3,0,2,1:T(8,128)} %get-tuple-element.83) | copy-start | bytes 786436
  42.4 15.1 %copy-start.13 = (f32[32,1,16,128]{3,0,2,1:T(8,128)S(1)}, f32[32,1,16,128]{3,0,2,1:T(8,128)}, u32[]{:S(2)}) copy-start(f32[32,1,16,128]{3,0,2,1:T(8,128)} %get-tuple-element.81) | copy-start | bytes 786436
  43.4 20.8 %collective-permute-start.4 = (f32[350,128]{1,0:T(8,128)S(1)}, f32[350,128]{1,0:T(8,128)S(1)}, u32[]{:S(2)}, u32[]{:S(2)}) collective-permute-start(f32[350,128]{1,0:T(8,128)S(1)} %pad_maximum_fusion.24), channel_id=1, source_target_pairs={{0,1},{1,2},{2,3},{3,4},{4,5},{5,6},{6,7},{7,8},{8,9},{9,10},{10,1... | collective-permute-start | bytes 537608 | tf_op jit(solution)/shard_map/ppermute | solution.py:205
  46.2 18.1 %collective-permute-start.5 = (f32[350,128]{1,0:T(8,128)S(1)}, f32[350,128]{1,0:T(8,128)S(1)}, u32[]{:S(2)}, u32[]{:S(2)}) collective-permute-start(f32[350,128]{1,0:T(8,128)S(1)} %pad_maximum_fusion.25), channel_id=1, source_target_pairs={{1,0},{2,1},{3,2},{4,3},{5,4},{6,5},{7,6},{8,7},{9,8},{10,9},{11,1... | collective-permute-start | bytes 537608 | tf_op jit(solution)/shard_map/ppermute | solution.py:206
  53.7 24.7 %collective-permute-start.6 = (f32[1024,128]{1,0:T(8,128)}, f32[1024,128]{1,0:T(8,128)}, u32[]{:S(2)}, u32[]{:S(2)}) collective-permute-start(f32[1024,128]{1,0:T(8,128)} %pad_maximum_fusion.20), channel_id=1, source_target_pairs={{16,0},{32,16},{48,32},{64,48},{80,64},{96,80},{112,96},{128,112},... | collective-permute-start | bytes 1572872 | tf_op jit(solution)/shard_map/ppermute | solution.py:206
  58.3 23.2 %collective-permute-start.7 = (f32[1024,128]{1,0:T(8,128)}, f32[1024,128]{1,0:T(8,128)}, u32[]{:S(2)}, u32[]{:S(2)}) collective-permute-start(f32[1024,128]{1,0:T(8,128)} %pad_maximum_fusion.21), channel_id=1, source_target_pairs={{0,16},{16,32},{32,48},{48,64},{64,80},{80,96},{96,112},{112,128},... | collective-permute-start | bytes 1572872 | tf_op jit(solution)/shard_map/ppermute | solution.py:205
  64.2 9.4 %copy-start.15 = (f32[350,128]{1,0:T(8,128)}, f32[350,128]{1,0:T(8,128)S(1)}, u32[]{:S(2)}) copy-start(f32[350,128]{1,0:T(8,128)S(1)} %collective-permute-done.4.corner_below) | copy-start | bytes 537604
  84.7 38.2 %copy-start.4 = (f32[32,4,16,128]{3,0,2,1:T(8,128)}, f32[32,4,16,128]{3,0,2,1:T(8,128)S(1)}, u32[]{:S(2)}) copy-start(f32[32,4,16,128]{3,0,2,1:T(8,128)S(1)} %fusion.33) | copy-start | bytes 3145732
  84.7 10.4 %copy-start.32 = (pred[18]{0:T(512)(128)(4,1)S(1)}, pred[18]{0:T(512)(128)(4,1)}, u32[]{:S(2)}) copy-start(pred[18]{0:T(512)(128)(4,1)} %get-tuple-element.119) | copy-start | bytes 58
  84.8 10.4 %copy-start.33 = (pred[18]{0:T(512)(128)(4,1)S(1)}, pred[18]{0:T(512)(128)(4,1)}, u32[]{:S(2)}) copy-start(pred[18]{0:T(512)(128)(4,1)} %get-tuple-element.120) | copy-start | bytes 58
  84.8 10.4 %copy-start.34 = (pred[6]{0:T(512)(128)(4,1)S(1)}, pred[6]{0:T(512)(128)(4,1)}, u32[]{:S(2)}) copy-start(pred[6]{0:T(512)(128)(4,1)} %and_or_fusion) | copy-start | bytes 22
  84.8 11.0 %copy-start.14 = (f32[8,35,128]{2,1,0:T(8,128)S(1)}, f32[8,35,128]{2,1,0:T(8,128)}, u32[]{:S(2)}) copy-start(f32[8,35,128]{2,1,0:T(8,128)} %shard_map.122) | copy-start | bytes 430084
  85.7 34.8 %collective-permute-start.10 = (f32[1024,128]{1,0:T(8,128)}, f32[1024,128]{1,0:T(8,128)S(1)}, u32[]{:S(2)}, u32[]{:S(2)}) collective-permute-start(f32[1024,128]{1,0:T(8,128)} %bitcast.80), channel_id=1, source_target_pairs={{16,0},{32,16},{48,32},{64,48},{80,64},{96,80},{112,96},{128,112},... | collective-permute-start | bytes 1572872 | tf_op jit(solution)/shard_map/ppermute | solution.py:206
  88.1 34.8 %collective-permute-start.9 = (f32[1024,128]{1,0:T(8,128)S(1)}, f32[1024,128]{1,0:T(8,128)S(1)}, u32[]{:S(2)}, u32[]{:S(2)}) collective-permute-start(f32[1024,128]{1,0:T(8,128)S(1)} %bitcast.210), channel_id=1, source_target_pairs={{0,16},{16,32},{32,48},{48,64},{64,80},{80,96},{96,112},{112,128},... | collective-permute-start | bytes 1572872 | tf_op jit(solution)/shard_map/ppermute | solution.py:205
  101.0 8.5 %collective-permute-start.11 = (f32[256,128]{1,0:T(8,128)S(1)}, f32[256,128]{1,0:T(8,128)S(1)}, u32[]{:S(2)}, u32[]{:S(2)}) collective-permute-start(f32[256,128]{1,0:T(8,128)S(1)} %bitcast.227), channel_id=1, source_target_pairs={{1,0},{2,1},{3,2},{4,3},{5,4},{6,5},{7,6},{8,7},{9,8},{10,9},{11,1... | collective-permute-start | bytes 393224 | tf_op jit(solution)/shard_map/ppermute | solution.py:206
  104.4 8.4 %collective-permute-start.8 = (f32[256,128]{1,0:T(8,128)S(1)}, f32[256,128]{1,0:T(8,128)S(1)}, u32[]{:S(2)}, u32[]{:S(2)}) collective-permute-start(f32[256,128]{1,0:T(8,128)S(1)} %bitcast.226), channel_id=1, source_target_pairs={{0,1},{1,2},{2,3},{3,4},{4,5},{5,6},{6,7},{7,8},{8,9},{9,10},{10,1... | collective-permute-start | bytes 393224 | tf_op jit(solution)/shard_map/ppermute | solution.py:205
  106.4 22.5 %collective-permute-start.15 = (f32[32,1,1,128]{3,0,2,1:T(8,128)S(1)}, f32[32,1,1,128]{3,0,2,1:T(8,128)S(1)}, u32[]{:S(2)}, u32[]{:S(2)}) collective-permute-start(f32[32,1,1,128]{3,0,2,1:T(8,128)S(1)} %get-tuple-element.73), channel_id=1, source_target_pairs={{17,0},{18,1},{19,2},{20,3},{21,4},{22,5},{23,6},{24,7},{25,8},{26... | collective-permute-start | bytes 49160 | tf_op jit(solution)/shard_map/ppermute | solution.py:309
  109.5 19.4 %collective-permute-start.14 = (f32[32,1,1,128]{3,0,2,1:T(8,128)S(1)}, f32[32,1,1,128]{3,0,2,1:T(8,128)S(1)}, u32[]{:S(2)}, u32[]{:S(2)}) collective-permute-start(f32[32,1,1,128]{3,0,2,1:T(8,128)S(1)} %get-tuple-element.74), channel_id=1, source_target_pairs={{16,1},{17,2},{18,3},{19,4},{20,5},{21,6},{22,7},{23,8},{24,9},{25... | collective-permute-start | bytes 49160 | tf_op jit(solution)/shard_map/ppermute | solution.py:309
  112.8 16.1 %collective-permute-start.13 = (f32[32,1,1,128]{3,0,2,1:T(8,128)S(1)}, f32[32,1,1,128]{3,0,2,1:T(8,128)S(1)}, u32[]{:S(2)}, u32[]{:S(2)}) collective-permute-start(f32[32,1,1,128]{3,0,2,1:T(8,128)S(1)} %get-tuple-element.75), channel_id=1, source_target_pairs={{1,16},{2,17},{3,18},{4,19},{5,20},{6,21},{7,22},{8,23},{9,24},{10... | collective-permute-start | bytes 49160 | tf_op jit(solution)/shard_map/ppermute | solution.py:309
  120.5 8.4 %collective-permute-start.12 = (f32[32,1,1,128]{3,0,2,1:T(8,128)S(1)}, f32[32,1,1,128]{3,0,2,1:T(8,128)S(1)}, u32[]{:S(2)}, u32[]{:S(2)}) collective-permute-start(f32[32,1,1,128]{3,0,2,1:T(8,128)S(1)} %get-tuple-element.76), channel_id=1, source_target_pairs={{0,17},{1,18},{2,19},{3,20},{4,21},{5,22},{6,23},{7,24},{8,25},{9,... | collective-permute-start | bytes 49160 | tf_op jit(solution)/shard_map/ppermute | solution.py:309
  (20 other events, 54.0 us)

commit v9 on v7

--- a/solution.py
+++ b/solution.py
@@ -207,67 +207,78 @@
     return unpack(below, upward), unpack(above, downward), below, above
 
 
-def forces_kernel(span, scale, own_ref, near_ref, occ_ref, start_ref, out_ref):
+def forces_kernel(shifts, scale, own_ref, near_ref, occ_ref, start_ref, out_ref, mine_ref, other_ref):
     rows = own_ref.shape[1]
     lanes = own_ref.shape[-1]
     layers = lanes // SLOTS
-    px = own_ref[0]
-    py = own_ref[1]
-    pz = own_ref[2]
-    lane = lax.broadcasted_iota(jnp.int32, px.shape, 1)
+    stacked = mine_ref.shape[1]
+    groups = 9
+    mine_ref[...] = jnp.zeros_like(mine_ref)
+    other_ref[...] = jnp.zeros_like(other_ref)
+    for plane in range(4):
+        for offset_x in range(3):
+            for offset_y in range(3):
+                group = (offset_x * 3 + offset_y) * rows
+                other_ref[plane, group : group + rows, :] = near_ref[plane, offset_x, offset_y : offset_y + rows, :]
+                if plane < 3:
+                    mine_ref[plane, group : group + rows, :] = own_ref[plane]
+    px = mine_ref[0]
+    py = mine_ref[1]
+    pz = mine_ref[2]
+    lane = lax.broadcasted_iota(jnp.int32, (stacked, lanes), 1)
     slot = lane % SLOTS
     layer = lane // SLOTS
-
-    def body(offset_x, carry):
-        fx, fy, fz = carry
-        for offset_y in range(3):
-            row = [near_ref[plane, offset_x, offset_y : offset_y + rows, :] for plane in range(4)]
-            for offset_z in (-1, 0, 1):
-                if offset_z == 0:
-                    base = row
-                else:
-                    inside = (layer + offset_z >= 0) & (layer + offset_z < layers)
-                    base = [
-                        jnp.where(inside, pltpu.roll(part, (-offset_z * SLOTS) % lanes, 1), 0.0)
-                        for part in row
-                    ]
-                for turn in range(SLOTS):
-                    if turn == 0:
-                        other = base
-                    else:
-                        keep = slot + turn < SLOTS
-                        other = [
-                            jnp.where(keep, pltpu.roll(part, lanes - turn, 1), pltpu.roll(part, SLOTS - turn, 1))
-                            for part in base
-                        ]
-                    dx = px - other[0]
-                    dy = py - other[1]
-                    dz = pz - other[2]
-                    strength = other[3] * jnp.exp(-(dx * dx + dy * dy + dz * dz) / spread_sq)
-                    fx = fx + dx * strength
-                    fy = fy + dy * strength
-                    fz = fz + dz * strength
-        return fx, fy, fz
-
-    fx, fy, fz = lax.fori_loop(span[0], span[1], body, (start_ref[0], start_ref[1], start_ref[2]))
+    fx = start_ref[0]
+    fy = start_ref[1]
+    fz = start_ref[2]
+    row = [other_ref[plane] for plane in range(4)]
+    for offset_z in shifts:
+        if offset_z == 0:
+            base = row
+        else:
+            inside = (layer + offset_z >= 0) & (layer + offset_z < layers)
+            base = [jnp.where(inside, pltpu.roll(part, (-offset_z * SLOTS) % lanes, 1), 0.0) for part in row]
+        for turn in range(SLOTS):
+            if turn == 0:
+                other = base
+            else:
+                keep = slot + turn < SLOTS
+                other = [
+                    jnp.where(keep, pltpu.roll(part, lanes - turn, 1), pltpu.roll(part, SLOTS - turn, 1))
+                    for part in base
+                ]
+            dx = px - other[0]
+            dy = py - other[1]
+            dz = pz - other[2]
+            strength = other[3] * jnp.exp(-(dx * dx + dy * dy + dz * dz) / spread_sq)
+            fx = fx + dx * strength
+            fy = fy + dy * strength
+            fz = fz + dz * strength
     if scale:
         active = move_step * occ_ref[...]
-        fx = active * fx
-        fy = active * fy
-        fz = active * fz
-    out_ref[0] = fx
-    out_ref[1] = fy
-    out_ref[2] = fz
-
-
-def pallas_forces(points, bordered, occupancy, partial, span, scale):
+        for plane, total in enumerate((fx, fy, fz)):
+            summed = total[0:rows]
+            for group in range(1, groups):
+                summed = summed + total[group * rows : (group + 1) * rows]
+            out_ref[plane, 0:rows, :] = active * summed
+    else:
+        out_ref[0] = fx
+        out_ref[1] = fy
+        out_ref[2] = fz
+
+
+def pallas_forces(points, bordered, occupancy, partial, shifts, scale):
     planes, _, rows, lanes = points.shape
-    share = span[1] - span[0]
+    stacked = -(-9 * rows // 8) * 8
+    if partial is None:
+        partial = jnp.zeros((3, stacked, lanes), jnp.float32)
+    out_rows = rows if scale else stacked
     return pl.pallas_call(
-        functools.partial(forces_kernel, span, scale),
-        out_shape=jax.ShapeDtypeStruct((3, rows, lanes), jnp.float32),
+        functools.partial(forces_kernel, shifts, scale),
+        out_shape=jax.ShapeDtypeStruct((3, out_rows, lanes), jnp.float32),
+        scratch_shapes=[pltpu.VMEM((3, stacked, lanes), jnp.float32), pltpu.VMEM((4, stacked, lanes), jnp.float32)],
         cost_estimate=pl.CostEstimate(
-            flops=3_000_000 * share, transcendentals=150_000 * share, bytes_accessed=120_000
+            flops=3_000_000 * len(shifts), transcendentals=150_000 * len(shifts), bytes_accessed=150_000
         ),
     )(points[:, 0], bordered, occupancy[0].astype(jnp.float32), partial)
 
@@ -340,15 +351,14 @@
     side_rows = y_low.size // 128
     starts = (field_rows + points.size // 128, side_rows, side_rows + points_low.size // 128)
     rows = points.shape[2]
-    zero = jnp.zeros((3, rows, points.shape[3]), jnp.float32)
     arrived = gather_arrived(x_flats, side_flats, corner_flats, *starts, payload.shape[1:])
-    partial = pallas_forces(points, bordered, occupancy, zero, (0, 2), False)
+    partial = pallas_forces(points, bordered, occupancy, None, (-1, 0), False)
     current, arrived, partial = lax.optimization_barrier((current, arrived, partial))
     current = advance(framed(current, x_low, x_high, y_low, y_high), source, rates, mixing)
     current, bordered, partial = lax.optimization_barrier((current, bordered, partial))
 
     def later_work():
-        return pallas_forces(points, bordered, occupancy, partial, (2, 3), True)
+        return pallas_forces(points, bordered, occupancy, partial, (1,), True)
 
     current, force = substep_beside(current, source, rates, mixing, later_work)
     current = substep(current, source, rates, mixing)

time: 130 us -> 125 us (0.962)
  Pallas kernels: 20.2 us -> 16 us
    pallas_call x2, Pallas kernels: 11.9 us -> 7.7 us  [pallas_forces(): pl.pallas_call(functools.partial(forces_kernel, shifts, scale), out_shape...]
  transfers between devices with their start and end apart: 16 -> 16, of which waited for: 0 -> 0; matrix products, arithmetic and copies ran while one was open for 15% -> 15% of each run, Pallas kernels for 16% -> 13%
where the time goes in v9:
time: 125 us; the launch traced here: 123 us
  starting transfers between devices  64.9 us (52%)
  local copies, waits for them, and re-layouts  21.4 us (17%)
  Pallas kernels  16 us (13%)
  other arithmetic  10.5 us (8%)
  matrix products  8.57 us (7%)
  between operations  1.51 us (1%)
    ppermute x5, starting transfers between devices, halos(): high = lax.ppermute(head, axis, [((i + 1) % count, i) for i in range(ends)])  20.1 us
    ppermute x5, starting transfers between devices, halos(): low = lax.ppermute(tail, axis, [(i, (i + 1) % count) for i in range(ends)])  20 us
    ppermute x3, starting transfers between devices, send_pair(): above = lax.ppermute(pack(downward), axis, down)  14.6 us
    ppermute x3, starting transfers between devices, send_pair(): below = lax.ppermute(pack(upward), axis, up)  10.2 us
    unnamed x63, local copies, waits for them, and re-layouts  8.74 us
    dot_general x4, matrix products, advance(): jnp.dot(mixing, center.reshape(species, -1), precision=lax.Precision.HIGH...  8.57 us
    pallas_call x2, Pallas kernels, pallas_forces(): pl.pallas_call(functools.partial(forces_kernel, shifts, scale), out_shape...  7.7 us
    pallas_call x1, Pallas kernels, deposit(): pl.pallas_call(deposit_kernel, out_shape=jax.ShapeDtypeStruct((BIN_XY, bi...  6.42 us
  transfers between devices with their start and end apart: 16, of which 0 were waited for; matrix products, arithmetic and copies ran while one was open for 15% of the time, Pallas kernels for 13%

profile of v9, /device:TPU:120, one launch (start us, length us, event | category | flops | bytes accessed | tf_op | source)
XLA Modules:
  0.0 123.0 jit_solution(4379652100544349700)
XLA Ops:
  1.4 1.3 %fusion.65 = (f32[4,4,256]{2,1,0:T(4,128)}, f32[4,1,4,256]{3,2,1,0:T(4,128)S(1)}) fusion(f32[1,1,4,256]{3,2,1,0:T(4,128)S(1)} %multiply_bitcast_fusion, f32[3,1,4,256]{3,2,1,0:T(4,128)} %param.14), kind=kLoop, calls=%fused_computation.144 | loop fusion | flops 4096 | bytes 49152 | tf_op jit(solution)/shard_map/squeeze | solution.py:283
  6.5 3.1 %collective-permute-start = (f32[649,128]{1,0:T(8,128)S(1)}, f32[649,128]{1,0:T(8,128)S(1)}, u32[]{:S(2)}, u32[]{:S(2)}) collective-permute-start(f32[649,128]{1,0:T(8,128)S(1)} %get-tuple-element.54), channel_id=1, source_target_pairs={{16,0},{32,16},{48,32},{64,48},{80,64},{96,80},{112,96},{128,112},... | collective-permute-start | bytes 996872 | tf_op jit(solution)/shard_map/ppermute | solution.py:206
  9.7 6.3 %collective-permute-start.1 = (f32[649,128]{1,0:T(8,128)}, f32[649,128]{1,0:T(8,128)S(1)}, u32[]{:S(2)}, u32[]{:S(2)}) collective-permute-start(f32[649,128]{1,0:T(8,128)} %get-tuple-element.53), channel_id=1, source_target_pairs={{0,16},{16,32},{32,48},{48,64},{64,80},{80,96},{96,112},{112,128},... | collective-permute-start | bytes 996872 | tf_op jit(solution)/shard_map/ppermute | solution.py:205
  16.1 1.9 %collective-permute-start.3 = (f32[163,128]{1,0:T(8,128)S(1)}, f32[163,128]{1,0:T(8,128)S(1)}, u32[]{:S(2)}, u32[]{:S(2)}) collective-permute-start(f32[163,128]{1,0:T(8,128)S(1)} %pad_maximum_fusion.38), channel_id=1, source_target_pairs={{0,1},{1,2},{2,3},{3,4},{4,5},{5,6},{6,7},{7,8},{8,9},{9,10},{10,1... | collective-permute-start | bytes 250376 | tf_op jit(solution)/shard_map/ppermute | solution.py:205
  18.1 5.8 %collective-permute-start.2 = (f32[163,128]{1,0:T(8,128)S(1)}, f32[163,128]{1,0:T(8,128)S(1)}, u32[]{:S(2)}, u32[]{:S(2)}) collective-permute-start(f32[163,128]{1,0:T(8,128)S(1)} %pad_maximum_fusion.37), channel_id=1, source_target_pairs={{1,0},{2,1},{3,2},{4,3},{5,4},{6,5},{7,6},{8,7},{9,8},{10,9},{11,1... | collective-permute-start | bytes 250376 | tf_op jit(solution)/shard_map/ppermute | solution.py:206
  24.5 1.6 %copy.44 = f32[32,4,16,128]{3,0,2,1:T(8,128)} copy(f32[32,4,16,128]{3,2,1,0:T(8,128)S(1)} %copy-done.2) | data formatting | bytes 2097152 | tf_op args[0]
  26.7 1.2 copy.62
  28.1 1.4 %copy.47 = f32[16,4,32,16]{3,2,1,0:T(8,128)} copy(f32[16,4,32,16]{2,0,3,1:T(8,128)S(1)} %bitcast.139) | data formatting | bytes 262144 | tf_op jit(solution)/shard_map/transpose | solution.py:132
  30.3 6.4 %shard_map.121 = f32[4,16,32,128]{3,2,1,0:T(8,128)} custom-call(f32[16,128,16]{2,1,0:T(8,128)} %bitcast.136, f32[16,4,16]{2,1,0:T(4,128)} %bitcast.151), custom_call_target="tpu_custom_call" | custom-call | flops 10000000 | bytes 1300000 | tf_op jit(solution)/shard_map/pallas_call | solution.py:135
  40.1 3.5 %fusion.4 = f32[32,4,16,128]{3,0,2,1:T(8,128)S(1)} fusion(f32[32,4,16,128]{3,0,2,1:T(8,128)S(1)} %copy-done.5, f32[32,1,1,128]{3,0,2,1:T(8,128)S(1)} %broadcast.33, f32[32,1,16,128]{3,0,2,1:T(8,128)S(1)} %bitcast.145, f32[32,1,16,128]{3,0,2,1:T(8,128)S(1)} %bitcast.146, f32[32,4,1,128]{3,0,2,1:T(8,128)} %bitcast.152, f32[32,4,1,128]{3,0,2,1:T(8,128)} %bitcast.153, ...), kind=kOutput, calls=%fused_computation.32 | convolution fusion | flops 107479040 | bytes 4870272 | tf_op jit(solution)/shard_map/dot_general | solution.py:88
  43.9 1.9 %collective-permute-start.4 = (f32[222,128]{1,0:T(8,128)S(1)}, f32[222,128]{1,0:T(8,128)S(1)}, u32[]{:S(2)}, u32[]{:S(2)}) collective-permute-start(f32[222,128]{1,0:T(8,128)S(1)} %pad_maximum_fusion.34), channel_id=1, source_target_pairs={{0,1},{1,2},{2,3},{3,4},{4,5},{5,6},{6,7},{7,8},{8,9},{9,10},{10,1... | collective-permute-start | bytes 341000 | tf_op jit(solution)/shard_map/ppermute | solution.py:205
  45.8 5.8 %collective-permute-start.5 = (f32[222,128]{1,0:T(8,128)S(1)}, f32[222,128]{1,0:T(8,128)S(1)}, u32[]{:S(2)}, u32[]{:S(2)}) collective-permute-start(f32[222,128]{1,0:T(8,128)S(1)} %pad_maximum_fusion.35), channel_id=1, source_target_pairs={{1,0},{2,1},{3,2},{4,3},{5,4},{6,5},{7,6},{8,7},{9,8},{10,9},{11,1... | collective-permute-start | bytes 341000 | tf_op jit(solution)/shard_map/ppermute | solution.py:206
  51.6 3.6 %collective-permute-start.7 = (f32[32,1,16,128]{3,0,2,1:T(8,128)S(1)}, f32[32,1,16,128]{3,0,2,1:T(8,128)S(1)}, u32[]{:S(2)}, u32[]{:S(2)}) collective-permute-start(f32[32,1,16,128]{3,0,2,1:T(8,128)S(1)} %get-tuple-element.34), channel_id=1, source_target_pairs={{0,16},{16,32},{32,48},{48,64},{64,80},{80,96},{96,112},{112,128},... | collective-permute-start | bytes 786440 | tf_op jit(solution)/shard_map/ppermute | solution.py:44
  55.2 3.9 %collective-permute-start.6 = (f32[32,1,16,128]{3,0,2,1:T(8,128)S(1)}, f32[32,1,16,128]{3,0,2,1:T(8,128)}, u32[]{:S(2)}, u32[]{:S(2)}) collective-permute-start(f32[32,1,16,128]{3,0,2,1:T(8,128)S(1)} %get-tuple-element.33), channel_id=1, source_target_pairs={{16,0},{32,16},{48,32},{64,48},{80,64},{96,80},{112,96},{128,112},... | collective-permute-start | bytes 786440 | tf_op jit(solution)/shard_map/ppermute | solution.py:45
  60.5 1.9 %shard_map.122 = f32[8,35,128]{2,1,0:T(8,128)} custom-call(f32[649,128]{1,0:T(8,128)} %copy-done.4, f32[649,128]{1,0:T(8,128)} %copy-done.3, f32[163,128]{1,0:T(8,128)} %copy-done.9, f32[163,128]{1,0:T(8,128)} %copy-done.10, f32[222,128]{1,0:T(8,128)} %copy-done.7, f32[222,128]{1,0:T(8,128)} %copy-done.8), custom_call_target="tpu_custom_call" | custom-call | bytes 300000 | tf_op jit(solution)/shard_map/pallas_call | solution.py:305
  64.4 4.6 %shard_map.123.start_ref = f32[3,40,256]{2,1,0:T(8,128)} custom-call(f32[4,4,256]{2,1,0:T(4,128)} %get-tuple-element.51.own_ref, f32[4,3,6,256]{3,2,1,0:T(8,128)} %pad_maximum_fusion.36.near_ref, f32[4,256]{1,0:T(4,128)} %get-tuple-element.55.occ_ref, f32[3,40,256]{2,1,0:T(8,128)} %broadcast_in_dim.16.start_ref), custom_call_target="tpu_custom_call" | custom-call | flops 6000000 | bytes 150000 | tf_op jit(solution)/shard_map/pallas_call | solution.py:276
  69.7 1.7 %fusion = f32[4,8,64,128]{3,1,2,0:T(8,128)S(1)} fusion(f32[32,32]{1,0:T(8,128)S(1)} %copy-done, f32[4,8,64,128]{3,2,1,0:T(8,128)S(1)} %bitcast.137), kind=kOutput, calls=%fused_computation.27 | convolution fusion | flops 100925440 | bytes 2101248 | tf_op jit(solution)/shard_map/dot_general | solution.py:88
  74.1 2.1 %fusion.24 = f32[32,4,16,128]{3,0,2,1:T(8,128)S(1)} fusion(f32[32,4,16,128]{3,0,2,1:T(8,128)S(1)} %fusion.4, f32[32,1,1,128]{3,0,2,1:T(8,128)S(1)} %broadcast.33, f32[32,6,16,128]{3,0,2,1:T(8,128)S(1)} %constant_dynamic-update-slice_fusion, f32[32,4,1,128]{3,0,2,1:T(8,128)S(1)} %bitcast.143, f32[32,4,1,128]{3,0,2,1:T(8,128)S(1)} %bitcast.144, ...), kind=kLoop, calls=%fused_computation.52 | loop fusion | flops 5505024 | bytes 6439040 | tf_op jit(solution)/shard_map/add | solution.py:92
  77.1 5.7 %collective-permute-start.9 = (f32[32,1,16,128]{3,0,2,1:T(8,128)}, f32[32,1,16,128]{3,0,2,1:T(8,128)S(1)}, u32[]{:S(2)}, u32[]{:S(2)}) collective-permute-start(f32[32,1,16,128]{3,0,2,1:T(8,128)} %get-tuple-element.32), channel_id=1, source_target_pairs={{0,16},{16,32},{32,48},{48,64},{64,80},{80,96},{96,112},{112,128},... | collective-permute-start | bytes 786440 | tf_op jit(solution)/shard_map/ppermute | solution.py:44
  83.4 3.1 %shard_map.124 = f32[3,4,256]{2,1,0:T(4,128)} custom-call(f32[4,4,256]{2,1,0:T(4,128)} %get-tuple-element.51.own_ref, f32[4,3,6,256]{3,2,1,0:T(8,128)} %pad_maximum_fusion.36.near_ref, f32[4,256]{1,0:T(4,128)} %get-tuple-element.55.occ_ref, f32[3,40,256]{2,1,0:T(8,128)} %shard_map.123.start_ref), custom_call_target="tpu_custom_call" | custom-call | flops 3000000 | bytes 150000 | tf_op jit(solution)/shard_map/pallas_call | solution.py:276
  86.5 1.9 %collective-permute-start.8 = (f32[32,1,16,128]{3,0,2,1:T(8,128)}, f32[32,1,16,128]{3,0,2,1:T(8,128)S(1)}, u32[]{:S(2)}, u32[]{:S(2)}) collective-permute-start(f32[32,1,16,128]{3,0,2,1:T(8,128)} %get-tuple-element.31), channel_id=1, source_target_pairs={{16,0},{32,16},{48,32},{64,48},{80,64},{96,80},{112,96},{128,112},... | collective-permute-start | bytes 786440 | tf_op jit(solution)/shard_map/ppermute | solution.py:45
  88.4 1.9 %collective-permute-start.11 = (f32[32,4,1,128]{3,0,2,1:T(8,128)}, f32[32,4,1,128]{3,0,2,1:T(8,128)S(1)}, u32[]{:S(2)}, u32[]{:S(2)}) collective-permute-start(f32[32,4,1,128]{3,0,2,1:T(8,128)} %get-tuple-element.30), channel_id=1, source_target_pairs={{0,1},{1,2},{2,3},{3,4},{4,5},{5,6},{6,7},{7,8},{8,9},{9,10},{10,1... | collective-permute-start | bytes 196616 | tf_op jit(solution)/shard_map/ppermute | solution.py:44
  90.3 5.8 %collective-permute-start.10 = (f32[32,4,1,128]{3,0,2,1:T(8,128)}, f32[32,4,1,128]{3,0,2,1:T(8,128)S(1)}, u32[]{:S(2)}, u32[]{:S(2)}) collective-permute-start(f32[32,4,1,128]{3,0,2,1:T(8,128)} %get-tuple-element.29), channel_id=1, source_target_pairs={{1,0},{2,1},{3,2},{4,3},{5,4},{6,5},{7,6},{8,7},{9,8},{10,9},{11,1... | collective-permute-start | bytes 196616 | tf_op jit(solution)/shard_map/ppermute | solution.py:45
  96.7 1.7 %fusion.1 = f32[4,8,64,128]{3,1,2,0:T(8,128)S(1)} fusion(f32[32,32]{1,0:T(8,128)S(1)} %copy-done, f32[4,8,64,128]{3,2,1,0:T(8,128)S(1)} %bitcast.138), kind=kOutput, calls=%fused_computation.28 | convolution fusion | flops 100925440 | bytes 2101248 | tf_op jit(solution)/shard_map/dot_general | solution.py:88
  98.8 1.2 fusion.35
  100.0 2.8 %collective-permute-start.12 = (f32[32,1,16,128]{3,0,2,1:T(8,128)S(1)}, f32[32,1,16,128]{3,0,2,1:T(8,128)S(1)}, u32[]{:S(2)}, u32[]{:S(2)}) collective-permute-start(f32[32,1,16,128]{3,0,2,1:T(8,128)S(1)} %get-tuple-element.28), channel_id=1, source_target_pairs={{16,0},{32,16},{48,32},{64,48},{80,64},{96,80},{112,96},{128,112},... | collective-permute-start | bytes 786440 | tf_op jit(solution)/shard_map/ppermute | solution.py:45
  102.8 6.9 %collective-permute-start.13 = (f32[32,1,16,128]{3,0,2,1:T(8,128)S(1)}, f32[32,1,16,128]{3,0,2,1:T(8,128)S(1)}, u32[]{:S(2)}, u32[]{:S(2)}) collective-permute-start(f32[32,1,16,128]{3,0,2,1:T(8,128)S(1)} %get-tuple-element.27), channel_id=1, source_target_pairs={{0,16},{16,32},{32,48},{48,64},{64,80},{80,96},{96,112},{112,128},... | collective-permute-start | bytes 786440 | tf_op jit(solution)/shard_map/ppermute | solution.py:44
  110.3 1.9 %collective-permute-start.15 = (f32[32,4,1,128]{3,0,2,1:T(8,128)S(1)}, f32[32,4,1,128]{3,0,2,1:T(8,128)S(1)}, u32[]{:S(2)}, u32[]{:S(2)}) collective-permute-start(f32[32,4,1,128]{3,0,2,1:T(8,128)S(1)} %get-tuple-element.26), channel_id=1, source_target_pairs={{0,1},{1,2},{2,3},{3,4},{4,5},{5,6},{6,7},{7,8},{8,9},{9,10},{10,1... | collective-permute-start | bytes 196616 | tf_op jit(solution)/shard_map/ppermute | solution.py:44
  112.3 5.8 %collective-permute-start.14 = (f32[32,4,1,128]{3,0,2,1:T(8,128)S(1)}, f32[32,4,1,128]{3,0,2,1:T(8,128)S(1)}, u32[]{:S(2)}, u32[]{:S(2)}) collective-permute-start(f32[32,4,1,128]{3,0,2,1:T(8,128)S(1)} %get-tuple-element.25), channel_id=1, source_target_pairs={{1,0},{2,1},{3,2},{4,3},{5,4},{6,5},{7,6},{8,7},{9,8},{10,9},{11,1... | collective-permute-start | bytes 196616 | tf_op jit(solution)/shard_map/ppermute | solution.py:45
  118.0 1.7 %fusion.2 = f32[4,8,64,128]{3,1,2,0:T(8,128)S(1)} fusion(f32[32,32]{1,0:T(8,128)S(1)} %copy-done, f32[4,8,64,128]{3,2,1,0:T(8,128)S(1)} %bitcast.135), kind=kOutput, calls=%fused_computation.29 | convolution fusion | flops 100925440 | bytes 2101248 | tf_op jit(solution)/shard_map/dot_general | solution.py:88
  120.0 1.4 %fusion.46 = f32[32,4,16,128]{3,0,2,1:T(8,128)S(1)} fusion(f32[32,4,16,128]{3,0,2,1:T(8,128)S(1)} %fusion.35, f32[32,1,1,128]{3,0,2,1:T(8,128)S(1)} %broadcast.33, f32[32,1,16,128]{3,0,2,1:T(8,128)S(1)} %collective-permute-done.12, f32[32,1,16,128]{3,0,2,1:T(8,128)S(1)} %collective-permute-done.13, f32[32,4,1,128]{3,0,2,1:T(8,128)S(1)} %collective-permute-done.15, ...), kind=kLoop, calls=%fused_computation.74 | loop fusion | flops 6553600 | bytes 4866176 | tf_op jit(solution)/shard_map/add | solution.py:92
  121.4 1.6 %copy.57 = f32[32,4,16,128]{3,2,1,0:T(8,128)} copy(f32[32,4,16,128]{3,0,2,1:T(8,128)S(1)} %fusion.46) | data formatting | bytes 2097152
  (132 shorter events, 20.2 us)
Async XLA Ops:
  0.6 39.4 %copy-start = (f32[32,32]{1,0:T(8,128)S(1)}, f32[32,32]{1,0:T(8,128)}, u32[]{:S(2)}) copy-start(f32[32,32]{1,0:T(8,128)} %param.12) | copy-start | bytes 12292
  4.4 11.6 %copy-start.2 = (f32[32,4,16,128]{3,2,1,0:T(8,128)S(1)}, f32[32,4,16,128]{3,2,1,0:T(8,128)}, u32[]{:S(2)}) copy-start(f32[32,4,16,128]{3,2,1,0:T(8,128)} %param.10) | copy-start | bytes 3145732
  5.6 18.2 %copy-start.22 = (s32[1,4,256]{2,1,0:T(4,128)S(1)}, s32[1,4,256]{2,1,0:T(4,128)}, u32[]{:S(2)}) copy-start(s32[1,4,256]{2,1,0:T(4,128)} %param.16) | copy-start | bytes 12292
  5.6 18.2 %copy-start.24 = (s32[1,4,256]{2,1,0:T(4,128)S(1)}, s32[1,4,256]{2,1,0:T(4,128)}, u32[]{:S(2)}) copy-start(s32[1,4,256]{2,1,0:T(4,128)} %param.17) | copy-start | bytes 12292
  6.5 31.5 %collective-permute-start = (f32[649,128]{1,0:T(8,128)S(1)}, f32[649,128]{1,0:T(8,128)S(1)}, u32[]{:S(2)}, u32[]{:S(2)}) collective-permute-start(f32[649,128]{1,0:T(8,128)S(1)} %get-tuple-element.54), channel_id=1, source_target_pairs={{16,0},{32,16},{48,32},{64,48},{80,64},{96,80},{112,96},{128,112},... | collective-permute-start | bytes 996872 | tf_op jit(solution)/shard_map/ppermute | solution.py:206
  9.7 28.3 %collective-permute-start.1 = (f32[649,128]{1,0:T(8,128)}, f32[649,128]{1,0:T(8,128)S(1)}, u32[]{:S(2)}, u32[]{:S(2)}) collective-permute-start(f32[649,128]{1,0:T(8,128)} %get-tuple-element.53), channel_id=1, source_target_pairs={{0,16},{16,32},{32,48},{48,64},{64,80},{80,96},{96,112},{112,128},... | collective-permute-start | bytes 996872 | tf_op jit(solution)/shard_map/ppermute | solution.py:205
  16.1 20.5 %collective-permute-start.3 = (f32[163,128]{1,0:T(8,128)S(1)}, f32[163,128]{1,0:T(8,128)S(1)}, u32[]{:S(2)}, u32[]{:S(2)}) collective-permute-start(f32[163,128]{1,0:T(8,128)S(1)} %pad_maximum_fusion.38), channel_id=1, source_target_pairs={{0,1},{1,2},{2,3},{3,4},{4,5},{5,6},{6,7},{7,8},{8,9},{9,10},{10,1... | collective-permute-start | bytes 250376 | tf_op jit(solution)/shard_map/ppermute | solution.py:205
  18.1 19.2 %collective-permute-start.2 = (f32[163,128]{1,0:T(8,128)S(1)}, f32[163,128]{1,0:T(8,128)S(1)}, u32[]{:S(2)}, u32[]{:S(2)}) collective-permute-start(f32[163,128]{1,0:T(8,128)S(1)} %pad_maximum_fusion.37), channel_id=1, source_target_pairs={{1,0},{2,1},{3,2},{4,3},{5,4},{6,5},{7,6},{8,7},{9,8},{10,9},{11,1... | collective-permute-start | bytes 250376 | tf_op jit(solution)/shard_map/ppermute | solution.py:206
  30.3 9.8 %copy-start.5 = (f32[32,4,16,128]{3,0,2,1:T(8,128)S(1)}, f32[32,4,16,128]{3,0,2,1:T(8,128)}, u32[]{:S(2)}) copy-start(f32[32,4,16,128]{3,0,2,1:T(8,128)} %copy.44) | copy-start | bytes 3145732
  36.7 3.4 %copy-start.1 = (f32[4,16,32,128]{3,2,1,0:T(8,128)S(1)}, f32[4,16,32,128]{3,2,1,0:T(8,128)}, u32[]{:S(2)}) copy-start(f32[4,16,32,128]{3,2,1,0:T(8,128)} %shard_map.121) | copy-start | bytes 3145732
  38.0 5.7 %copy-start.3 = (f32[649,128]{1,0:T(8,128)}, f32[649,128]{1,0:T(8,128)S(1)}, u32[]{:S(2)}) copy-start(f32[649,128]{1,0:T(8,128)S(1)} %collective-permute-done.x_above) | copy-start | bytes 996868
  40.1 3.7 %copy-start.12 = (f32[4,1,4,256]{3,2,1,0:T(4,128)S(1)}, f32[4,1,4,256]{3,2,1,0:T(4,128)}, u32[]{:S(2)}) copy-start(f32[4,1,4,256]{3,2,1,0:T(4,128)} %reshape.144) | copy-start | bytes 49156
  40.1 3.7 %copy-start.14 = (f32[4,1,4,256]{3,2,1,0:T(4,128)S(1)}, f32[4,1,4,256]{3,2,1,0:T(4,128)}, u32[]{:S(2)}) copy-start(f32[4,1,4,256]{3,2,1,0:T(4,128)} %reshape.143) | copy-start | bytes 49156
  40.1 3.7 %copy-start.17 = (f32[3,1,4,256]{3,2,1,0:T(4,128)S(1)}, f32[3,1,4,256]{3,2,1,0:T(4,128)}, u32[]{:S(2)}) copy-start(f32[3,1,4,256]{3,2,1,0:T(4,128)} %param.14) | copy-start | bytes 36868
  40.1 3.7 %copy-start.20 = (f32[1,1,4,256]{3,2,1,0:T(4,128)S(1)}, f32[1,1,4,256]{3,2,1,0:T(4,128)}, u32[]{:S(2)}) copy-start(f32[1,1,4,256]{3,2,1,0:T(4,128)} %copy-done.19) | copy-start | bytes 12292
  40.1 3.7 %copy-start.11 = (f32[70,128]{1,0:T(8,128)S(1)}, f32[70,128]{1,0:T(8,128)}, u32[]{:S(2)}) copy-start(f32[70,128]{1,0:T(8,128)} %reshape.146) | copy-start | bytes 107524
  43.7 19.4 %copy-start.13 = (f32[4,1,4,256]{3,2,1,0:T(4,128)S(1)}, f32[4,1,4,256]{3,2,1,0:T(4,128)}, u32[]{:S(2)}) copy-start(f32[4,1,4,256]{3,2,1,0:T(4,128)} %reshape.144) | copy-start | bytes 49156
  43.7 19.4 %copy-start.15 = (f32[4,1,4,256]{3,2,1,0:T(4,128)S(1)}, f32[4,1,4,256]{3,2,1,0:T(4,128)}, u32[]{:S(2)}) copy-start(f32[4,1,4,256]{3,2,1,0:T(4,128)} %reshape.143) | copy-start | bytes 49156
  43.7 19.4 %copy-start.18 = (f32[3,1,4,256]{3,2,1,0:T(4,128)S(1)}, f32[3,1,4,256]{3,2,1,0:T(4,128)}, u32[]{:S(2)}) copy-start(f32[3,1,4,256]{3,2,1,0:T(4,128)} %param.14) | copy-start | bytes 36868
  43.7 19.3 %copy-start.21 = (f32[1,1,4,256]{3,2,1,0:T(4,128)S(1)}, f32[1,1,4,256]{3,2,1,0:T(4,128)}, u32[]{:S(2)}) copy-start(f32[1,1,4,256]{3,2,1,0:T(4,128)} %copy-done.19) | copy-start | bytes 12292
  43.9 15.3 %collective-permute-start.4 = (f32[222,128]{1,0:T(8,128)S(1)}, f32[222,128]{1,0:T(8,128)S(1)}, u32[]{:S(2)}, u32[]{:S(2)}) collective-permute-start(f32[222,128]{1,0:T(8,128)S(1)} %pad_maximum_fusion.34), channel_id=1, source_target_pairs={{0,1},{1,2},{2,3},{3,4},{4,5},{5,6},{6,7},{7,8},{8,9},{9,10},{10,1... | collective-permute-start | bytes 341000 | tf_op jit(solution)/shard_map/ppermute | solution.py:205
  45.8 13.4 %collective-permute-start.5 = (f32[222,128]{1,0:T(8,128)S(1)}, f32[222,128]{1,0:T(8,128)S(1)}, u32[]{:S(2)}, u32[]{:S(2)}) collective-permute-start(f32[222,128]{1,0:T(8,128)S(1)} %pad_maximum_fusion.35), channel_id=1, source_target_pairs={{1,0},{2,1},{3,2},{4,3},{5,4},{6,5},{7,6},{8,7},{9,8},{10,9},{11,1... | collective-permute-start | bytes 341000 | tf_op jit(solution)/shard_map/ppermute | solution.py:206
  51.6 21.3 %collective-permute-start.7 = (f32[32,1,16,128]{3,0,2,1:T(8,128)S(1)}, f32[32,1,16,128]{3,0,2,1:T(8,128)S(1)}, u32[]{:S(2)}, u32[]{:S(2)}) collective-permute-start(f32[32,1,16,128]{3,0,2,1:T(8,128)S(1)} %get-tuple-element.34), channel_id=1, source_target_pairs={{0,16},{16,32},{32,48},{48,64},{64,80},{80,96},{96,112},{112,128},... | collective-permute-start | bytes 786440 | tf_op jit(solution)/shard_map/ppermute | solution.py:44
  55.2 17.8 %collective-permute-start.6 = (f32[32,1,16,128]{3,0,2,1:T(8,128)S(1)}, f32[32,1,16,128]{3,0,2,1:T(8,128)}, u32[]{:S(2)}, u32[]{:S(2)}) collective-permute-start(f32[32,1,16,128]{3,0,2,1:T(8,128)S(1)} %get-tuple-element.33), channel_id=1, source_target_pairs={{16,0},{32,16},{48,32},{64,48},{80,64},{96,80},{112,96},{128,112},... | collective-permute-start | bytes 786440 | tf_op jit(solution)/shard_map/ppermute | solution.py:45
  77.1 21.5 %collective-permute-start.9 = (f32[32,1,16,128]{3,0,2,1:T(8,128)}, f32[32,1,16,128]{3,0,2,1:T(8,128)S(1)}, u32[]{:S(2)}, u32[]{:S(2)}) collective-permute-start(f32[32,1,16,128]{3,0,2,1:T(8,128)} %get-tuple-element.32), channel_id=1, source_target_pairs={{0,16},{16,32},{32,48},{48,64},{64,80},{80,96},{96,112},{112,128},... | collective-permute-start | bytes 786440 | tf_op jit(solution)/shard_map/ppermute | solution.py:44
  86.5 12.2 %collective-permute-start.8 = (f32[32,1,16,128]{3,0,2,1:T(8,128)}, f32[32,1,16,128]{3,0,2,1:T(8,128)S(1)}, u32[]{:S(2)}, u32[]{:S(2)}) collective-permute-start(f32[32,1,16,128]{3,0,2,1:T(8,128)} %get-tuple-element.31), channel_id=1, source_target_pairs={{16,0},{32,16},{48,32},{64,48},{80,64},{96,80},{112,96},{128,112},... | collective-permute-start | bytes 786440 | tf_op jit(solution)/shard_map/ppermute | solution.py:45
  88.4 10.4 %collective-permute-start.11 = (f32[32,4,1,128]{3,0,2,1:T(8,128)}, f32[32,4,1,128]{3,0,2,1:T(8,128)S(1)}, u32[]{:S(2)}, u32[]{:S(2)}) collective-permute-start(f32[32,4,1,128]{3,0,2,1:T(8,128)} %get-tuple-element.30), channel_id=1, source_target_pairs={{0,1},{1,2},{2,3},{3,4},{4,5},{5,6},{6,7},{7,8},{8,9},{9,10},{10,1... | collective-permute-start | bytes 196616 | tf_op jit(solution)/shard_map/ppermute | solution.py:44
  90.3 8.4 %collective-permute-start.10 = (f32[32,4,1,128]{3,0,2,1:T(8,128)}, f32[32,4,1,128]{3,0,2,1:T(8,128)S(1)}, u32[]{:S(2)}, u32[]{:S(2)}) collective-permute-start(f32[32,4,1,128]{3,0,2,1:T(8,128)} %get-tuple-element.29), channel_id=1, source_target_pairs={{1,0},{2,1},{3,2},{4,3},{5,4},{6,5},{7,6},{8,7},{9,8},{10,9},{11,1... | collective-permute-start | bytes 196616 | tf_op jit(solution)/shard_map/ppermute | solution.py:45
  100.0 19.9 %collective-permute-start.12 = (f32[32,1,16,128]{3,0,2,1:T(8,128)S(1)}, f32[32,1,16,128]{3,0,2,1:T(8,128)S(1)}, u32[]{:S(2)}, u32[]{:S(2)}) collective-permute-start(f32[32,1,16,128]{3,0,2,1:T(8,128)S(1)} %get-tuple-element.28), channel_id=1, source_target_pairs={{16,0},{32,16},{48,32},{64,48},{80,64},{96,80},{112,96},{128,112},... | collective-permute-start | bytes 786440 | tf_op jit(solution)/shard_map/ppermute | solution.py:45
  102.8 17.2 %collective-permute-start.13 = (f32[32,1,16,128]{3,0,2,1:T(8,128)S(1)}, f32[32,1,16,128]{3,0,2,1:T(8,128)S(1)}, u32[]{:S(2)}, u32[]{:S(2)}) collective-permute-start(f32[32,1,16,128]{3,0,2,1:T(8,128)S(1)} %get-tuple-element.27), channel_id=1, source_target_pairs={{0,16},{16,32},{32,48},{48,64},{64,80},{80,96},{96,112},{112,128},... | collective-permute-start | bytes 786440 | tf_op jit(solution)/shard_map/ppermute | solution.py:44
  110.3 9.6 %collective-permute-start.15 = (f32[32,4,1,128]{3,0,2,1:T(8,128)S(1)}, f32[32,4,1,128]{3,0,2,1:T(8,128)S(1)}, u32[]{:S(2)}, u32[]{:S(2)}) collective-permute-start(f32[32,4,1,128]{3,0,2,1:T(8,128)S(1)} %get-tuple-element.26), channel_id=1, source_target_pairs={{0,1},{1,2},{2,3},{3,4},{4,5},{5,6},{6,7},{7,8},{8,9},{9,10},{10,1... | collective-permute-start | bytes 196616 | tf_op jit(solution)/shard_map/ppermute | solution.py:44
  112.3 7.7 %collective-permute-start.14 = (f32[32,4,1,128]{3,0,2,1:T(8,128)S(1)}, f32[32,4,1,128]{3,0,2,1:T(8,128)S(1)}, u32[]{:S(2)}, u32[]{:S(2)}) collective-permute-start(f32[32,4,1,128]{3,0,2,1:T(8,128)S(1)} %get-tuple-element.25), channel_id=1, source_target_pairs={{1,0},{2,1},{3,2},{4,3},{5,4},{6,5},{7,6},{8,7},{9,8},{10,9},{11,1... | collective-permute-start | bytes 196616 | tf_op jit(solution)/shard_map/ppermute | solution.py:45
  (11 other events, 17.9 us)

commit v10 on v9

--- a/solution.py
+++ b/solution.py
@@ -60,15 +60,13 @@
     y_low, y_high = halos(current, "gy", 2)
     done = work()
     current, done = lax.optimization_barrier((current, done))
-    padded = framed(current, x_low, x_high, y_low, y_high)
-    return advance(padded, source, rates, mixing), done
+    return fused_step(current, x_low, x_high, y_low, y_high, source, rates, mixing), done
 
 
 def substep(current, source, rates, mixing):
     x_low, x_high = halos(current, "gx", 1)
     y_low, y_high = halos(current, "gy", 2)
-    padded = framed(current, x_low, x_high, y_low, y_high)
-    return advance(padded, source, rates, mixing)
+    return fused_step(current, x_low, x_high, y_low, y_high, source, rates, mixing)
 
 
 def shifted(block, axis, distance):
@@ -94,6 +92,57 @@
         + time_step * mixed
         + time_step * source
     )
+
+
+def step_kernel(width, depth, c_ref, xlo_ref, xhi_ref, ylo_ref, yhi_ref, src_ref, rates_ref, mixing_ref, out_ref):
+    species, total = c_ref.shape
+    lanes = total // (width * depth)
+    plane = depth * lanes
+    chunk = 4 * lanes
+    mixing = mixing_ref[...]
+    rate = rates_ref[...]
+    z = lax.broadcasted_iota(jnp.int32, (species, chunk), 1) % lanes
+    for x in range(width):
+        for part in range(depth // 4):
+            first = x * plane + part * chunk
+            center = c_ref[:, first : first + chunk]
+            if x > 0:
+                below = c_ref[:, first - plane : first - plane + chunk]
+            else:
+                below = xlo_ref[:, part * chunk : (part + 1) * chunk]
+            if x < width - 1:
+                above = c_ref[:, first + plane : first + plane + chunk]
+            else:
+                above = xhi_ref[:, part * chunk : (part + 1) * chunk]
+            if part > 0:
+                left = c_ref[:, first - lanes : first - lanes + chunk]
+            else:
+                left = jnp.concatenate([ylo_ref[:, x * lanes : (x + 1) * lanes], c_ref[:, first : first + chunk - lanes]], axis=1)
+            if part < depth // 4 - 1:
+                right = c_ref[:, first + lanes : first + lanes + chunk]
+            else:
+                right = jnp.concatenate([c_ref[:, first + lanes : first + chunk], yhi_ref[:, x * lanes : (x + 1) * lanes]], axis=1)
+            deeper = jnp.where(z == lanes - 1, 0.0, pltpu.roll(center, chunk - 1, 1))
+            shallower = jnp.where(z == 0, 0.0, pltpu.roll(center, 1, 1))
+            beside = above + below
+            beside = beside + right + left
+            beside = beside + deeper + shallower
+            laplace = beside - 6.0 * center
+            mixed = jnp.dot(mixing, center, precision=lax.Precision.HIGHEST, preferred_element_type=jnp.float32)
+            source = src_ref[:, first : first + chunk]
+            out_ref[:, first : first + chunk] = (
+                center + time_step * (rate * laplace) + time_step * mixed + time_step * source
+            )
+
+
+def fused_step(current, x_low, x_high, y_low, y_high, source, rates, mixing):
+    species, width, depth, lanes = current.shape
+    out = pl.pallas_call(
+        functools.partial(step_kernel, width, depth),
+        out_shape=jax.ShapeDtypeStruct((species, width * depth * lanes), jnp.float32),
+        cost_estimate=pl.CostEstimate(flops=60_000_000, transcendentals=0, bytes_accessed=2_500_000),
+    )(*[part.reshape(species, -1) for part in (current, x_low, x_high, y_low, y_high, source)], rates.reshape(species, 1), mixing)
+    return out.reshape(current.shape)
 
 
 def deposit_kernel(rates_ref, code_ref, out_ref, spread_ref, place_ref):
@@ -119,7 +168,7 @@
         for slot in range(slots):
             hit = place_ref[slot, pl.ds(bin_y, 1), :] == target
             total = total + jnp.where(hit, spread_ref[slot, pl.ds(first, species), :], 0.0)
-        out_ref[cell_x, row_y] = total
+        out_ref[:, pl.ds(pl.multiple_of(index * lanes, lanes), lanes)] = total
         return carry
 
     lax.fori_loop(0, BIN_XY * bins_y * BIN_XY, body, 0)
@@ -134,14 +183,14 @@
     code = jnp.transpose(code, (2, 0, 1))
     out = pl.pallas_call(
         deposit_kernel,
-        out_shape=jax.ShapeDtypeStruct((BIN_XY, bins_y * BIN_XY, species, layers * BIN_Z), jnp.float32),
+        out_shape=jax.ShapeDtypeStruct((species, BIN_XY * bins_y * BIN_XY * layers * BIN_Z), jnp.float32),
         scratch_shapes=[
             pltpu.VMEM((SLOTS, bins_y * species, layers * BIN_Z), jnp.float32),
             pltpu.VMEM((SLOTS, bins_y, layers * BIN_Z), jnp.float32),
         ],
         cost_estimate=pl.CostEstimate(flops=10_000_000, transcendentals=0, bytes_accessed=1_300_000),
     )(rates_slot, code)
-    return jnp.transpose(out, (2, 0, 1, 3))
+    return out.reshape(species, BIN_XY, bins_y * BIN_XY, layers * BIN_Z)
 
 def pair_forces(points, padded, occupancy):
     planes, bins_x, bins_y, lanes = points.shape
@@ -175,8 +224,6 @@
 
 
 def storage_order(piece):
-    if piece.ndim == 4 and piece.shape[0] > 4:
-        return (1, 2, 0, 3)
     return tuple(range(piece.ndim))
 
 
@@ -337,7 +384,7 @@
         [current[:, :, -1:], payload[4:5]],
         [current[:, :, :1], payload[3:4]],
     )
-    current = advance(framed(current, x_low, x_high, y_low, y_high), source, rates, mixing)
+    current = fused_step(current, x_low, x_high, y_low, y_high, source, rates, mixing)
 
     row_points = jnp.concatenate([points_low, points, points_high], axis=1)
     x_low, x_high = halos(current, "gx", 1)
@@ -354,7 +401,7 @@
     arrived = gather_arrived(x_flats, side_flats, corner_flats, *starts, payload.shape[1:])
     partial = pallas_forces(points, bordered, occupancy, None, (-1, 0), False)
     current, arrived, partial = lax.optimization_barrier((current, arrived, partial))
-    current = advance(framed(current, x_low, x_high, y_low, y_high), source, rates, mixing)
+    current = fused_step(current, x_low, x_high, y_low, y_high, source, rates, mixing)
     current, bordered, partial = lax.optimization_barrier((current, bordered, partial))
 
     def later_work():

time: 125 us -> 142 us (1.14)
  Pallas kernels: 16 us -> 31.3 us
  local copies, waits for them, and re-layouts: 21.4 us -> 33 us
  waiting for transfers between devices: 0.04 us -> 10.7 us
  matrix products: 8.57 us -> 0 us
  other arithmetic: 10.5 us -> 3.66 us
  starting transfers between devices: 64.9 us -> 60.7 us
    pallas_call x1 -> x5, Pallas kernels: 6.42 us -> 21.7 us  [the longest x4 15.3 us: fused_step(): pl.pallas_call(functools.partial(step_kernel, width, depth), out_shape=ja...]
    unnamed x63 -> x49, local copies, waits for them, and re-layouts: 8.74 us -> 21.6 us
    dot_general x4 -> x0, matrix products: 8.57 us -> none  [advance(): jnp.dot(mixing, center.reshape(species, -1), precision=lax.Precision.HIGH...]
    ppermute x5, starting transfers between devices: 20.1 us -> 12.5 us  [halos(): high = lax.ppermute(head, axis, [((i + 1) % count, i) for i in range(ends)])]
    ppermute x5, starting transfers between devices: 20 us -> 27.1 us  [halos(): low = lax.ppermute(tail, axis, [(i, (i + 1) % count) for i in range(ends)])]
    ppermute x3, waiting for transfers between devices: 0.01 us -> 6.27 us  [send_pair(): below = lax.ppermute(pack(upward), axis, up)]
    add x3 -> x0, other arithmetic: 4.74 us -> none  [advance(): center + time_step * (rates[:, None, None, None] * laplace)]
    ppermute x5, waiting for transfers between devices: 0.01 us -> 4.44 us  [halos(): low = lax.ppermute(tail, axis, [(i, (i + 1) % count) for i in range(ends)])]
  transfers between devices with their start and end apart: 16 -> 16, of which waited for: 0 -> 2; matrix products, arithmetic and copies ran while one was open for 15% -> 13% of each run, Pallas kernels for 13% -> 11%
where the time goes in v10:
time: 142 us; the launch traced here: 141 us
  starting transfers between devices  60.7 us (43%)
  local copies, waits for them, and re-layouts  33 us (23%)
  Pallas kernels  31.3 us (22%)
  waiting for transfers between devices  10.7 us (8%)
  other arithmetic  3.66 us (3%)
    ppermute x5, starting transfers between devices, halos(): low = lax.ppermute(tail, axis, [(i, (i + 1) % count) for i in range(ends)])  27.1 us
    unnamed x49, local copies, waits for them, and re-layouts  21.6 us
    pallas_call x4, Pallas kernels, fused_step(): pl.pallas_call(functools.partial(step_kernel, width, depth), out_shape=ja...  15.3 us
    ppermute x5, starting transfers between devices, halos(): high = lax.ppermute(head, axis, [((i + 1) % count, i) for i in range(ends)])  12.5 us
    ppermute x3, starting transfers between devices, send_pair(): above = lax.ppermute(pack(downward), axis, down)  10.9 us
    ppermute x3, starting transfers between devices, send_pair(): below = lax.ppermute(pack(upward), axis, up)  10.2 us
    pallas_call x2, Pallas kernels, pallas_forces(): pl.pallas_call(functools.partial(forces_kernel, shifts, scale), out_shape...  7.72 us
    pallas_call x1, Pallas kernels, deposit(): pl.pallas_call(deposit_kernel, out_shape=jax.ShapeDtypeStruct((species, B...  6.37 us
  transfers between devices with their start and end apart: 16, of which 2 were waited for; matrix products, arithmetic and copies ran while one was open for 13% of the time, Pallas kernels for 11%

profile of v10, /device:TPU:120, one launch (start us, length us, event | category | flops | bytes accessed | tf_op | source)
XLA Modules:
  0.0 140.6 jit_solution(18221977906507427336)
XLA Ops:
  4.9 3.1 %collective-permute-start.1 = (f32[649,128]{1,0:T(8,128)S(1)}, f32[649,128]{1,0:T(8,128)S(1)}, u32[]{:S(2)}, u32[]{:S(2)}) collective-permute-start(f32[649,128]{1,0:T(8,128)S(1)} %get-tuple-element.53), channel_id=1, source_target_pairs={{16,0},{32,16},{48,32},{64,48},{80,64},{96,80},{112,96},{128,112},... | collective-permute-start | bytes 996872 | tf_op jit(solution)/shard_map/ppermute | solution.py:253
  8.0 6.3 %collective-permute-start = (f32[649,128]{1,0:T(8,128)S(1)}, f32[649,128]{1,0:T(8,128)S(1)}, u32[]{:S(2)}, u32[]{:S(2)}) collective-permute-start(f32[649,128]{1,0:T(8,128)S(1)} %get-tuple-element.54), channel_id=1, source_target_pairs={{0,16},{16,32},{32,48},{48,64},{64,80},{80,96},{96,112},{112,128},... | collective-permute-start | bytes 996872 | tf_op jit(solution)/shard_map/ppermute | solution.py:252
  14.5 1.9 %collective-permute-start.2 = (f32[163,128]{1,0:T(8,128)S(1)}, f32[163,128]{1,0:T(8,128)S(1)}, u32[]{:S(2)}, u32[]{:S(2)}) collective-permute-start(f32[163,128]{1,0:T(8,128)S(1)} %pad_maximum_fusion.5), channel_id=1, source_target_pairs={{0,1},{1,2},{2,3},{3,4},{4,5},{5,6},{6,7},{7,8},{8,9},{9,10},{10,1... | collective-permute-start | bytes 250376 | tf_op jit(solution)/shard_map/ppermute | solution.py:252
  16.5 5.9 %collective-permute-start.3 = (f32[163,128]{1,0:T(8,128)S(1)}, f32[163,128]{1,0:T(8,128)S(1)}, u32[]{:S(2)}, u32[]{:S(2)}) collective-permute-start(f32[163,128]{1,0:T(8,128)S(1)} %pad_maximum_fusion.6), channel_id=1, source_target_pairs={{1,0},{2,1},{3,2},{4,3},{5,4},{6,5},{7,6},{8,7},{9,8},{10,9},{11,1... | collective-permute-start | bytes 250376 | tf_op jit(solution)/shard_map/ppermute | solution.py:253
  26.7 1.6 %copy.92 = f32[4,8,64,128]{3,1,2,0:T(8,128)} copy(f32[4,8,64,128]{3,2,1,0:T(8,128)S(1)} %bitcast.147) | data formatting | bytes 2097152
  28.3 6.4 %shard_map.121.src_ref = f32[32,8192]{1,0:T(8,128)} custom-call(f32[16,128,16]{2,1,0:T(8,128)} %bitcast.140, f32[16,4,16]{2,1,0:T(4,128)} %bitcast.174), custom_call_target="tpu_custom_call" | custom-call | flops 10000000 | bytes 1300000 | tf_op jit(solution)/shard_map/pallas_call | solution.py:184
  37.6 3.8 %shard_map.122 = f32[32,8192]{1,0:T(8,128)} custom-call(f32[32,8192]{1,0:T(8,128)} %bitcast.141, f32[32,2048]{1,0:T(8,128)} %reshape_reshape.18.xlo_ref, f32[32,2048]{1,0:T(8,128)} %reshape_reshape.19.xhi_ref, f32[32,512]{1,0:T(8,128)} %reshape_reshape.20.ylo_ref, f32[32,512]{1,0:T(8,128)} %reshape_reshape.21.yhi_ref, f32[32,8192]{1,0:T(8,128)} %shard_map.121.src_ref, ...), custom_call_target="tpu_custom_call" | custom-call | flops 60000000 | bytes 2500000 | tf_op jit(solution)/shard_map/pallas_call | solution.py:140
  41.5 1.4 %copy.58 = f32[4,8,64,128]{3,2,1,0:T(8,128)S(1)} copy(f32[4,8,64,128]{3,1,2,0:T(8,128)} %bitcast.145) | data formatting | bytes 2097152
  43.2 1.9 %collective-permute-start.5 = (f32[222,128]{1,0:T(8,128)S(1)}, f32[222,128]{1,0:T(8,128)S(1)}, u32[]{:S(2)}, u32[]{:S(2)}) collective-permute-start(f32[222,128]{1,0:T(8,128)S(1)} %pad_maximum_fusion.3), channel_id=1, source_target_pairs={{1,0},{2,1},{3,2},{4,3},{5,4},{6,5},{7,6},{8,7},{9,8},{10,9},{11,1... | collective-permute-start | bytes 341000 | tf_op jit(solution)/shard_map/ppermute | solution.py:253
  45.2 1.9 %collective-permute-start.7 = (f32[32,1,16,128]{3,2,0,1:T(8,128)S(1)}, f32[32,1,16,128]{3,2,0,1:T(8,128)S(1)}, u32[]{:S(2)}, u32[]{:S(2)}) collective-permute-start(f32[32,1,16,128]{3,2,0,1:T(8,128)S(1)} %get-tuple-element.33), channel_id=1, source_target_pairs={{16,0},{32,16},{48,32},{64,48},{80,64},{96,80},{112,96},{128,112},... | collective-permute-start | bytes 786440 | tf_op jit(solution)/shard_map/ppermute | solution.py:45
  47.1 7.5 %collective-permute-start.6 = (f32[32,1,16,128]{3,2,0,1:T(8,128)S(1)}, f32[32,1,16,128]{3,2,0,1:T(8,128)S(1)}, u32[]{:S(2)}, u32[]{:S(2)}) collective-permute-start(f32[32,1,16,128]{3,2,0,1:T(8,128)S(1)} %get-tuple-element.34), channel_id=1, source_target_pairs={{0,16},{16,32},{32,48},{48,64},{64,80},{80,96},{96,112},{112,128},... | collective-permute-start | bytes 786440 | tf_op jit(solution)/shard_map/ppermute | solution.py:44
  54.7 1.9 %collective-permute-start.4 = (f32[222,128]{1,0:T(8,128)S(1)}, f32[222,128]{1,0:T(8,128)S(1)}, u32[]{:S(2)}, u32[]{:S(2)}) collective-permute-start(f32[222,128]{1,0:T(8,128)S(1)} %pad_maximum_fusion.2), channel_id=1, source_target_pairs={{0,1},{1,2},{2,3},{3,4},{4,5},{5,6},{6,7},{7,8},{8,9},{9,10},{10,1... | collective-permute-start | bytes 341000 | tf_op jit(solution)/shard_map/ppermute | solution.py:252
  56.6 6.3 %collective-permute-done.4.corner_below = f32[222,128]{1,0:T(8,128)S(1)} collective-permute-done((f32[222,128]{1,0:T(8,128)S(1)}, f32[222,128]{1,0:T(8,128)S(1)}, u32[]{:S(2)}, u32[]{:S(2)}) %collective-permute-start.4) | collective-permute-done | bytes 113696 | tf_op jit(solution)/shard_map/ppermute | solution.py:252
  63.5 1.9 %shard_map.123 = f32[8,35,128]{2,1,0:T(8,128)} custom-call(f32[649,128]{1,0:T(8,128)} %copy-done.2, f32[649,128]{1,0:T(8,128)} %copy-done.1, f32[163,128]{1,0:T(8,128)} %copy-done.6, f32[163,128]{1,0:T(8,128)} %copy-done.7, f32[222,128]{1,0:T(8,128)} %copy-done.5, f32[222,128]{1,0:T(8,128)} %copy-done.4), custom_call_target="tpu_custom_call" | custom-call | bytes 300000 | tf_op jit(solution)/shard_map/pallas_call | solution.py:352
  66.7 4.6 %shard_map.124.start_ref = f32[3,40,256]{2,1,0:T(8,128)} custom-call(f32[4,4,256]{2,1,0:T(4,128)} %get-tuple-element.51.own_ref, f32[4,3,6,256]{3,2,1,0:T(8,128)} %pad_maximum_fusion.4.near_ref, f32[4,256]{1,0:T(4,128)} %get-tuple-element.55.occ_ref, f32[3,40,256]{2,1,0:T(8,128)} %broadcast_in_dim.12.start_ref), custom_call_target="tpu_custom_call" | custom-call | flops 6000000 | bytes 150000 | tf_op jit(solution)/shard_map/pallas_call | solution.py:323
  71.4 1.6 %copy.91 = f32[4,8,64,128]{3,1,2,0:T(8,128)} copy(f32[4,8,64,128]{3,2,1,0:T(8,128)S(1)} %copy.58) | data formatting | bytes 2097152
  77.5 3.8 %shard_map.125 = f32[32,8192]{1,0:T(8,128)} custom-call(f32[32,8192]{1,0:T(8,128)} %bitcast.143, f32[32,2048]{1,0:T(8,128)} %bitcast.158, f32[32,2048]{1,0:T(8,128)} %bitcast.155, f32[32,512]{1,0:T(8,128)} %reshape_reshape.22.ylo_ref, f32[32,512]{1,0:T(8,128)} %reshape_reshape.23.yhi_ref, f32[32,8192]{1,0:T(8,128)} %shard_map.121.src_ref, ...), custom_call_target="tpu_custom_call" | custom-call | flops 60000000 | bytes 2500000 | tf_op jit(solution)/shard_map/pallas_call | solution.py:140
  81.3 1.4 %copy.62 = f32[4,8,64,128]{3,2,1,0:T(8,128)S(1)} copy(f32[4,8,64,128]{3,1,2,0:T(8,128)} %bitcast.146) | data formatting | bytes 2097152
  83.2 1.9 %collective-permute-start.9 = (f32[32,1,16,128]{3,2,0,1:T(8,128)S(1)}, f32[32,1,16,128]{3,2,0,1:T(8,128)S(1)}, u32[]{:S(2)}, u32[]{:S(2)}) collective-permute-start(f32[32,1,16,128]{3,2,0,1:T(8,128)S(1)} %get-tuple-element.31), channel_id=1, source_target_pairs={{16,0},{32,16},{48,32},{64,48},{80,64},{96,80},{112,96},{128,112},... | collective-permute-start | bytes 786440 | tf_op jit(solution)/shard_map/ppermute | solution.py:45
  85.1 7.5 %collective-permute-start.8 = (f32[32,1,16,128]{3,2,0,1:T(8,128)S(1)}, f32[32,1,16,128]{3,2,0,1:T(8,128)S(1)}, u32[]{:S(2)}, u32[]{:S(2)}) collective-permute-start(f32[32,1,16,128]{3,2,0,1:T(8,128)S(1)} %get-tuple-element.32), channel_id=1, source_target_pairs={{0,16},{16,32},{32,48},{48,64},{64,80},{80,96},{96,112},{112,128},... | collective-permute-start | bytes 786440 | tf_op jit(solution)/shard_map/ppermute | solution.py:44
  92.7 1.9 %collective-permute-start.11 = (f32[32,4,1,128]{3,1,0,2:T(4,128)S(1)}, f32[32,4,1,128]{3,1,0,2:T(4,128)S(1)}, u32[]{:S(2)}, u32[]{:S(2)}) collective-permute-start(f32[32,4,1,128]{3,1,0,2:T(4,128)S(1)} %get-tuple-element.29), channel_id=1, source_target_pairs={{1,0},{2,1},{3,2},{4,3},{5,4},{6,5},{7,6},{8,7},{9,8},{10,9},{11,1... | collective-permute-start | bytes 196616 | tf_op jit(solution)/shard_map/ppermute | solution.py:45
  94.6 2.6 %collective-permute-start.10 = (f32[32,4,1,128]{3,1,0,2:T(4,128)S(1)}, f32[32,4,1,128]{3,1,0,2:T(4,128)S(1)}, u32[]{:S(2)}, u32[]{:S(2)}) collective-permute-start(f32[32,4,1,128]{3,1,0,2:T(4,128)S(1)} %get-tuple-element.30), channel_id=1, source_target_pairs={{0,1},{1,2},{2,3},{3,4},{4,5},{5,6},{6,7},{7,8},{8,9},{9,10},{10,1... | collective-permute-start | bytes 196616 | tf_op jit(solution)/shard_map/ppermute | solution.py:44
  97.2 3.1 %shard_map.126 = f32[3,4,256]{2,1,0:T(4,128)} custom-call(f32[4,4,256]{2,1,0:T(4,128)} %get-tuple-element.51.own_ref, f32[4,3,6,256]{3,2,1,0:T(8,128)} %pad_maximum_fusion.4.near_ref, f32[4,256]{1,0:T(4,128)} %get-tuple-element.55.occ_ref, f32[3,40,256]{2,1,0:T(8,128)} %shard_map.124.start_ref), custom_call_target="tpu_custom_call" | custom-call | flops 3000000 | bytes 150000 | tf_op jit(solution)/shard_map/pallas_call | solution.py:323
  100.3 1.6 %copy.90 = f32[4,8,64,128]{3,1,2,0:T(8,128)} copy(f32[4,8,64,128]{3,2,1,0:T(8,128)S(1)} %copy.62) | data formatting | bytes 2097152
  104.8 3.8 %shard_map.127.c_ref = f32[32,8192]{1,0:T(8,128)} custom-call(f32[32,8192]{1,0:T(8,128)} %bitcast.142, f32[32,2048]{1,0:T(8,128)} %bitcast.159, f32[32,2048]{1,0:T(8,128)} %bitcast.156, f32[32,512]{1,0:T(8,128)} %bitcast.173, f32[32,512]{1,0:T(8,128)} %bitcast.171, f32[32,8192]{1,0:T(8,128)} %shard_map.121.src_ref, f32[32,1]{1,0:T(8,128)} %copy.35.rates_ref, ...), custom_call_target="tpu_custom_call" | custom-call | flops 60000000 | bytes 2500000 | tf_op jit(solution)/shard_map/pallas_call | solution.py:140
  110.1 2.1 %collective-permute-start.13 = (f32[32,1,16,128]{3,2,0,1:T(8,128)S(1)}, f32[32,1,16,128]{3,2,0,1:T(8,128)S(1)}, u32[]{:S(2)}, u32[]{:S(2)}) collective-permute-start(f32[32,1,16,128]{3,2,0,1:T(8,128)S(1)} %get-tuple-element.27), channel_id=1, source_target_pairs={{16,0},{32,16},{48,32},{64,48},{80,64},{96,80},{112,96},{128,112},... | collective-permute-start | bytes 786440 | tf_op jit(solution)/shard_map/ppermute | solution.py:45
  112.1 7.5 %collective-permute-start.12 = (f32[32,1,16,128]{3,2,0,1:T(8,128)S(1)}, f32[32,1,16,128]{3,2,0,1:T(8,128)S(1)}, u32[]{:S(2)}, u32[]{:S(2)}) collective-permute-start(f32[32,1,16,128]{3,2,0,1:T(8,128)S(1)} %get-tuple-element.28), channel_id=1, source_target_pairs={{0,16},{16,32},{32,48},{48,64},{64,80},{80,96},{96,112},{112,128},... | collective-permute-start | bytes 786440 | tf_op jit(solution)/shard_map/ppermute | solution.py:44
  119.8 4.7 %collective-permute-start.15 = (f32[32,4,1,128]{3,1,0,2:T(4,128)S(1)}, f32[32,4,1,128]{3,1,0,2:T(4,128)S(1)}, u32[]{:S(2)}, u32[]{:S(2)}) collective-permute-start(f32[32,4,1,128]{3,1,0,2:T(4,128)S(1)} %bitcast.180), channel_id=1, source_target_pairs={{1,0},{2,1},{3,2},{4,3},{5,4},{6,5},{7,6},{8,7},{9,8},{10,9},{11,1... | collective-permute-start | bytes 196616 | tf_op jit(solution)/shard_map/ppermute | solution.py:45
  124.5 1.9 %collective-permute-start.14 = (f32[32,4,1,128]{3,1,0,2:T(4,128)S(1)}, f32[32,4,1,128]{3,1,0,2:T(4,128)S(1)}, u32[]{:S(2)}, u32[]{:S(2)}) collective-permute-start(f32[32,4,1,128]{3,1,0,2:T(4,128)S(1)} %bitcast.179), channel_id=1, source_target_pairs={{0,1},{1,2},{2,3},{3,4},{4,5},{5,6},{6,7},{7,8},{8,9},{9,10},{10,1... | collective-permute-start | bytes 196616 | tf_op jit(solution)/shard_map/ppermute | solution.py:44
  127.7 4.4 %collective-permute-done.14 = f32[32,4,1,128]{3,1,0,2:T(4,128)S(1)} collective-permute-done((f32[32,4,1,128]{3,1,0,2:T(4,128)S(1)}, f32[32,4,1,128]{3,1,0,2:T(4,128)S(1)}, u32[]{:S(2)}, u32[]{:S(2)}) %collective-permute-start.14) | collective-permute-done | bytes 65568 | tf_op jit(solution)/shard_map/ppermute | solution.py:44
  134.4 3.8 %shard_map.128 = f32[32,8192]{1,0:T(8,128)} custom-call(f32[32,8192]{1,0:T(8,128)} %shard_map.127.c_ref, f32[32,2048]{1,0:T(8,128)} %bitcast.157, f32[32,2048]{1,0:T(8,128)} %bitcast.154, f32[32,512]{1,0:T(8,128)} %bitcast.172, f32[32,512]{1,0:T(8,128)} %bitcast.170, f32[32,8192]{1,0:T(8,128)} %shard_map.121.src_ref, f32[32,1]{1,0:T(8,128)} %copy.35.rates_ref, ...), custom_call_target="tpu_custom_call" | custom-call | flops 60000000 | bytes 2500000 | tf_op jit(solution)/shard_map/pallas_call | solution.py:140
  138.2 2.4 %copy.73 = f32[4,8,64,128]{3,2,1,0:T(8,128)} copy(f32[4,8,64,128]{3,1,2,0:T(8,128)} %bitcast.144) | data formatting | bytes 2097152
  (111 shorter events, 26.8 us)
Async XLA Ops:
  0.6 0.7 copy-start.9
  2.0 0.7 copy-start.11
  3.6 10.7 %copy-start = (f32[32,4,16,128]{3,2,1,0:T(8,128)S(1)}, f32[32,4,16,128]{3,2,1,0:T(8,128)}, u32[]{:S(2)}) copy-start(f32[32,4,16,128]{3,2,1,0:T(8,128)} %param.10) | copy-start | bytes 3145732
  4.9 31.9 %collective-permute-start.1 = (f32[649,128]{1,0:T(8,128)S(1)}, f32[649,128]{1,0:T(8,128)S(1)}, u32[]{:S(2)}, u32[]{:S(2)}) collective-permute-start(f32[649,128]{1,0:T(8,128)S(1)} %get-tuple-element.53), channel_id=1, source_target_pairs={{16,0},{32,16},{48,32},{64,48},{80,64},{96,80},{112,96},{128,112},... | collective-permute-start | bytes 996872 | tf_op jit(solution)/shard_map/ppermute | solution.py:253
  8.0 27.9 %collective-permute-start = (f32[649,128]{1,0:T(8,128)S(1)}, f32[649,128]{1,0:T(8,128)S(1)}, u32[]{:S(2)}, u32[]{:S(2)}) collective-permute-start(f32[649,128]{1,0:T(8,128)S(1)} %get-tuple-element.54), channel_id=1, source_target_pairs={{0,16},{16,32},{32,48},{48,64},{64,80},{80,96},{96,112},{112,128},... | collective-permute-start | bytes 996872 | tf_op jit(solution)/shard_map/ppermute | solution.py:252
  14.5 20.2 %collective-permute-start.2 = (f32[163,128]{1,0:T(8,128)S(1)}, f32[163,128]{1,0:T(8,128)S(1)}, u32[]{:S(2)}, u32[]{:S(2)}) collective-permute-start(f32[163,128]{1,0:T(8,128)S(1)} %pad_maximum_fusion.5), channel_id=1, source_target_pairs={{0,1},{1,2},{2,3},{3,4},{4,5},{5,6},{6,7},{7,8},{8,9},{9,10},{10,1... | collective-permute-start | bytes 250376 | tf_op jit(solution)/shard_map/ppermute | solution.py:252
  16.4 5.9 %copy-start.10 = (s32[1,4,256]{2,1,0:T(4,128)S(1)}, s32[1,4,256]{2,1,0:T(4,128)}, u32[]{:S(2)}) copy-start(s32[1,4,256]{2,1,0:T(4,128)} %param.16) | copy-start | bytes 12292
  16.4 5.9 %copy-start.12 = (s32[1,4,256]{2,1,0:T(4,128)S(1)}, s32[1,4,256]{2,1,0:T(4,128)}, u32[]{:S(2)}) copy-start(s32[1,4,256]{2,1,0:T(4,128)} %param.17) | copy-start | bytes 12292
  16.4 7.3 %copy-start.8 = (f32[32,1,4,256]{3,2,1,0:T(4,128)S(1)}, f32[32,1,4,256]{3,2,1,0:T(4,128)}, u32[]{:S(2)}) copy-start(f32[32,1,4,256]{3,2,1,0:T(4,128)} %param.13) | copy-start | bytes 393220
  16.5 18.8 %collective-permute-start.3 = (f32[163,128]{1,0:T(8,128)S(1)}, f32[163,128]{1,0:T(8,128)S(1)}, u32[]{:S(2)}, u32[]{:S(2)}) collective-permute-start(f32[163,128]{1,0:T(8,128)S(1)} %pad_maximum_fusion.6), channel_id=1, source_target_pairs={{1,0},{2,1},{3,2},{4,3},{5,4},{6,5},{7,6},{8,7},{9,8},{10,9},{11,1... | collective-permute-start | bytes 250376 | tf_op jit(solution)/shard_map/ppermute | solution.py:253
  25.4 0.7 copy-start.13
  34.7 0.6 copy-start.6
  35.3 0.7 copy-start.7
  36.0 7.1 %copy-start.2 = (f32[649,128]{1,0:T(8,128)}, f32[649,128]{1,0:T(8,128)S(1)}, u32[]{:S(2)}) copy-start(f32[649,128]{1,0:T(8,128)S(1)} %collective-permute-done.x_below) | copy-start | bytes 996868
  36.8 6.3 %copy-start.1 = (f32[649,128]{1,0:T(8,128)}, f32[649,128]{1,0:T(8,128)S(1)}, u32[]{:S(2)}) copy-start(f32[649,128]{1,0:T(8,128)S(1)} %collective-permute-done.1.x_above) | copy-start | bytes 996868
  43.2 13.4 %collective-permute-start.5 = (f32[222,128]{1,0:T(8,128)S(1)}, f32[222,128]{1,0:T(8,128)S(1)}, u32[]{:S(2)}, u32[]{:S(2)}) collective-permute-start(f32[222,128]{1,0:T(8,128)S(1)} %pad_maximum_fusion.3), channel_id=1, source_target_pairs={{1,0},{2,1},{3,2},{4,3},{5,4},{6,5},{7,6},{8,7},{9,8},{10,9},{11,1... | collective-permute-start | bytes 341000 | tf_op jit(solution)/shard_map/ppermute | solution.py:253
  45.2 30.7 %collective-permute-start.7 = (f32[32,1,16,128]{3,2,0,1:T(8,128)S(1)}, f32[32,1,16,128]{3,2,0,1:T(8,128)S(1)}, u32[]{:S(2)}, u32[]{:S(2)}) collective-permute-start(f32[32,1,16,128]{3,2,0,1:T(8,128)S(1)} %get-tuple-element.33), channel_id=1, source_target_pairs={{16,0},{32,16},{48,32},{64,48},{80,64},{96,80},{112,96},{128,112},... | collective-permute-start | bytes 786440 | tf_op jit(solution)/shard_map/ppermute | solution.py:45
  47.1 29.6 %collective-permute-start.6 = (f32[32,1,16,128]{3,2,0,1:T(8,128)S(1)}, f32[32,1,16,128]{3,2,0,1:T(8,128)S(1)}, u32[]{:S(2)}, u32[]{:S(2)}) collective-permute-start(f32[32,1,16,128]{3,2,0,1:T(8,128)S(1)} %get-tuple-element.34), channel_id=1, source_target_pairs={{0,16},{16,32},{32,48},{48,64},{64,80},{80,96},{96,112},{112,128},... | collective-permute-start | bytes 786440 | tf_op jit(solution)/shard_map/ppermute | solution.py:44
  54.7 8.2 %collective-permute-start.4 = (f32[222,128]{1,0:T(8,128)S(1)}, f32[222,128]{1,0:T(8,128)S(1)}, u32[]{:S(2)}, u32[]{:S(2)}) collective-permute-start(f32[222,128]{1,0:T(8,128)S(1)} %pad_maximum_fusion.2), channel_id=1, source_target_pairs={{0,1},{1,2},{2,3},{3,4},{4,5},{5,6},{6,7},{7,8},{8,9},{9,10},{10,1... | collective-permute-start | bytes 341000 | tf_op jit(solution)/shard_map/ppermute | solution.py:252
  56.6 6.3 %copy-start.4 = (f32[222,128]{1,0:T(8,128)}, f32[222,128]{1,0:T(8,128)S(1)}, u32[]{:S(2)}) copy-start(f32[222,128]{1,0:T(8,128)S(1)} %collective-permute-done.5.corner_above) | copy-start | bytes 340996
  62.9 0.6 copy-start.5
  72.9 0.8 slice-start
  74.4 0.8 slice-start.1
  83.2 20.0 %collective-permute-start.9 = (f32[32,1,16,128]{3,2,0,1:T(8,128)S(1)}, f32[32,1,16,128]{3,2,0,1:T(8,128)S(1)}, u32[]{:S(2)}, u32[]{:S(2)}) collective-permute-start(f32[32,1,16,128]{3,2,0,1:T(8,128)S(1)} %get-tuple-element.31), channel_id=1, source_target_pairs={{16,0},{32,16},{48,32},{64,48},{80,64},{96,80},{112,96},{128,112},... | collective-permute-start | bytes 786440 | tf_op jit(solution)/shard_map/ppermute | solution.py:45
  85.1 18.8 %collective-permute-start.8 = (f32[32,1,16,128]{3,2,0,1:T(8,128)S(1)}, f32[32,1,16,128]{3,2,0,1:T(8,128)S(1)}, u32[]{:S(2)}, u32[]{:S(2)}) collective-permute-start(f32[32,1,16,128]{3,2,0,1:T(8,128)S(1)} %get-tuple-element.32), channel_id=1, source_target_pairs={{0,16},{16,32},{32,48},{48,64},{64,80},{80,96},{96,112},{112,128},... | collective-permute-start | bytes 786440 | tf_op jit(solution)/shard_map/ppermute | solution.py:44
  92.7 9.2 %collective-permute-start.11 = (f32[32,4,1,128]{3,1,0,2:T(4,128)S(1)}, f32[32,4,1,128]{3,1,0,2:T(4,128)S(1)}, u32[]{:S(2)}, u32[]{:S(2)}) collective-permute-start(f32[32,4,1,128]{3,1,0,2:T(4,128)S(1)} %get-tuple-element.29), channel_id=1, source_target_pairs={{1,0},{2,1},{3,2},{4,3},{5,4},{6,5},{7,6},{8,7},{9,8},{10,9},{11,1... | collective-permute-start | bytes 196616 | tf_op jit(solution)/shard_map/ppermute | solution.py:45
  94.6 7.9 %collective-permute-start.10 = (f32[32,4,1,128]{3,1,0,2:T(4,128)S(1)}, f32[32,4,1,128]{3,1,0,2:T(4,128)S(1)}, u32[]{:S(2)}, u32[]{:S(2)}) collective-permute-start(f32[32,4,1,128]{3,1,0,2:T(4,128)S(1)} %get-tuple-element.30), channel_id=1, source_target_pairs={{0,1},{1,2},{2,3},{3,4},{4,5},{5,6},{6,7},{7,8},{8,9},{9,10},{10,1... | collective-permute-start | bytes 196616 | tf_op jit(solution)/shard_map/ppermute | solution.py:44
  110.1 16.4 %copy-start.3 = (f32[8,35,128]{2,1,0:T(8,128)S(1)}, f32[8,35,128]{2,1,0:T(8,128)}, u32[]{:S(2)}) copy-start(f32[8,35,128]{2,1,0:T(8,128)} %shard_map.123) | copy-start | bytes 430084
  110.1 22.7 %collective-permute-start.13 = (f32[32,1,16,128]{3,2,0,1:T(8,128)S(1)}, f32[32,1,16,128]{3,2,0,1:T(8,128)S(1)}, u32[]{:S(2)}, u32[]{:S(2)}) collective-permute-start(f32[32,1,16,128]{3,2,0,1:T(8,128)S(1)} %get-tuple-element.27), channel_id=1, source_target_pairs={{16,0},{32,16},{48,32},{64,48},{80,64},{96,80},{112,96},{128,112},... | collective-permute-start | bytes 786440 | tf_op jit(solution)/shard_map/ppermute | solution.py:45
  112.1 21.5 %collective-permute-start.12 = (f32[32,1,16,128]{3,2,0,1:T(8,128)S(1)}, f32[32,1,16,128]{3,2,0,1:T(8,128)S(1)}, u32[]{:S(2)}, u32[]{:S(2)}) collective-permute-start(f32[32,1,16,128]{3,2,0,1:T(8,128)S(1)} %get-tuple-element.28), channel_id=1, source_target_pairs={{0,16},{16,32},{32,48},{48,64},{64,80},{80,96},{96,112},{112,128},... | collective-permute-start | bytes 786440 | tf_op jit(solution)/shard_map/ppermute | solution.py:44
  119.8 7.3 %collective-permute-start.15 = (f32[32,4,1,128]{3,1,0,2:T(4,128)S(1)}, f32[32,4,1,128]{3,1,0,2:T(4,128)S(1)}, u32[]{:S(2)}, u32[]{:S(2)}) collective-permute-start(f32[32,4,1,128]{3,1,0,2:T(4,128)S(1)} %bitcast.180), channel_id=1, source_target_pairs={{1,0},{2,1},{3,2},{4,3},{5,4},{6,5},{7,6},{8,7},{9,8},{10,9},{11,1... | collective-permute-start | bytes 196616 | tf_op jit(solution)/shard_map/ppermute | solution.py:45
  124.5 7.7 %collective-permute-start.14 = (f32[32,4,1,128]{3,1,0,2:T(4,128)S(1)}, f32[32,4,1,128]{3,1,0,2:T(4,128)S(1)}, u32[]{:S(2)}, u32[]{:S(2)}) collective-permute-start(f32[32,4,1,128]{3,1,0,2:T(4,128)S(1)} %bitcast.179), channel_id=1, source_target_pairs={{0,1},{1,2},{2,3},{3,4},{4,5},{5,6},{6,7},{7,8},{8,9},{9,10},{10,1... | collective-permute-start | bytes 196616 | tf_op jit(solution)/shard_map/ppermute | solution.py:44

commit v11 on v9

--- a/solution.py
+++ b/solution.py
@@ -352,16 +352,20 @@
     starts = (field_rows + points.size // 128, side_rows, side_rows + points_low.size // 128)
     rows = points.shape[2]
     arrived = gather_arrived(x_flats, side_flats, corner_flats, *starts, payload.shape[1:])
-    partial = pallas_forces(points, bordered, occupancy, None, (-1, 0), False)
-    current, arrived, partial = lax.optimization_barrier((current, arrived, partial))
+    current, arrived = lax.optimization_barrier((current, arrived))
     current = advance(framed(current, x_low, x_high, y_low, y_high), source, rates, mixing)
-    current, bordered, partial = lax.optimization_barrier((current, bordered, partial))
-
-    def later_work():
+    current, bordered = lax.optimization_barrier((current, bordered))
+
+    def first_work():
+        return pallas_forces(points, bordered, occupancy, None, (-1, 0), False)
+
+    current, partial = substep_beside(current, source, rates, mixing, first_work)
+    current, partial = lax.optimization_barrier((current, partial))
+
+    def last_work():
         return pallas_forces(points, bordered, occupancy, partial, (1,), True)
 
-    current, force = substep_beside(current, source, rates, mixing, later_work)
-    current = substep(current, source, rates, mixing)
+    current, force = substep_beside(current, source, rates, mixing, last_work)
     displacement = force.reshape(3, 1, rows, points.shape[3])
     return (current, displacement, arrived)
 

time: 125 us -> 135 us (1.080)
  the two profiles are of different devices: /device:TPU:120 before, /device:TPU:136 now
where the time goes in v11:
time: 135 us; the launch traced here: 134 us
  starting transfers between devices  59.4 us (44%)
  local copies, waits for them, and re-layouts  22.4 us (17%)
  Pallas kernels  15.9 us (12%)
  other arithmetic  12.2 us (9%)
  waiting for transfers between devices  11.6 us (9%)
  matrix products  11 us (8%)
  between operations  1.54 us (1%)
    ppermute x5, starting transfers between devices, halos(): high = lax.ppermute(head, axis, [((i + 1) % count, i) for i in range(ends)])  23.7 us
    ppermute x5, starting transfers between devices, halos(): low = lax.ppermute(tail, axis, [(i, (i + 1) % count) for i in range(ends)])  15.3 us
    ppermute x3, starting transfers between devices, send_pair(): above = lax.ppermute(pack(downward), axis, down)  12.9 us
    dot_general x4, matrix products, advance(): jnp.dot(mixing, center.reshape(species, -1), precision=lax.Precision.HIGH...  11 us
    ppermute x5, waiting for transfers between devices, halos(): low = lax.ppermute(tail, axis, [(i, (i + 1) % count) for i in range(ends)])  10.7 us
    unnamed x69, local copies, waits for them, and re-layouts  9.35 us
    pallas_call x2, Pallas kernels, pallas_forces(): pl.pallas_call(functools.partial(forces_kernel, shifts, scale), out_shape...  7.71 us
    ppermute x3, starting transfers between devices, send_pair(): below = lax.ppermute(pack(upward), axis, up)  7.56 us
  transfers between devices with their start and end apart: 16, of which 3 were waited for; matrix products, arithmetic and copies ran while one was open for 16% of the time, Pallas kernels for 12%

profile of v11, /device:TPU:136, one launch (start us, length us, event | category | flops | bytes accessed | tf_op | source)
XLA Modules:
  0.0 134.1 jit_solution(5197015655168199014)
XLA Ops:
  1.4 1.3 fusion.65
  6.7 3.7 %collective-permute-start = (f32[649,128]{1,0:T(8,128)}, f32[649,128]{1,0:T(8,128)S(1)}, u32[]{:S(2)}, u32[]{:S(2)}) collective-permute-start(f32[649,128]{1,0:T(8,128)} %get-tuple-element.58), channel_id=1, source_target_pairs={{16,0},{32,16},{48,32},{64,48},{80,64},{96,80},{112,96},{128,112},... | collective-permute-start | bytes 996872 | tf_op jit(solution)/shard_map/ppermute | solution.py:206
  10.4 3.7 %collective-permute-start.1 = (f32[649,128]{1,0:T(8,128)}, f32[649,128]{1,0:T(8,128)S(1)}, u32[]{:S(2)}, u32[]{:S(2)}) collective-permute-start(f32[649,128]{1,0:T(8,128)} %get-tuple-element.57), channel_id=1, source_target_pairs={{0,16},{16,32},{32,48},{48,64},{64,80},{80,96},{96,112},{112,128},... | collective-permute-start | bytes 996872 | tf_op jit(solution)/shard_map/ppermute | solution.py:205
  14.9 3.4 %collective-permute-start.2 = (f32[163,128]{1,0:T(8,128)}, f32[163,128]{1,0:T(8,128)S(1)}, u32[]{:S(2)}, u32[]{:S(2)}) collective-permute-start(f32[163,128]{1,0:T(8,128)} %pad_maximum_fusion.33), channel_id=1, source_target_pairs={{1,0},{2,1},{3,2},{4,3},{5,4},{6,5},{7,6},{8,7},{9,8},{10,9},{11,1... | collective-permute-start | bytes 250376 | tf_op jit(solution)/shard_map/ppermute | solution.py:206
  19.0 1.9 %collective-permute-start.3 = (f32[163,128]{1,0:T(8,128)}, f32[163,128]{1,0:T(8,128)S(1)}, u32[]{:S(2)}, u32[]{:S(2)}) collective-permute-start(f32[163,128]{1,0:T(8,128)} %pad_maximum_fusion.34), channel_id=1, source_target_pairs={{0,1},{1,2},{2,3},{3,4},{4,5},{5,6},{6,7},{7,8},{8,9},{9,10},{10,1... | collective-permute-start | bytes 250376 | tf_op jit(solution)/shard_map/ppermute | solution.py:205
  21.5 1.6 %copy.44 = f32[32,4,16,128]{3,0,2,1:T(8,128)} copy(f32[32,4,16,128]{3,2,1,0:T(8,128)S(1)} %copy-done.2) | data formatting | bytes 2097152 | tf_op args[0]
  24.1 1.4 %copy.47 = f32[16,4,32,16]{3,2,1,0:T(8,128)} copy(f32[16,4,32,16]{2,0,3,1:T(8,128)S(1)} %bitcast.139) | data formatting | bytes 262144 | tf_op jit(solution)/shard_map/transpose | solution.py:132
  26.1 1.2 copy.62
  27.3 6.3 %shard_map.121 = f32[4,16,32,128]{3,2,1,0:T(8,128)} custom-call(f32[16,128,16]{2,1,0:T(8,128)} %bitcast.135, f32[16,4,16]{2,1,0:T(4,128)} %bitcast.153), custom_call_target="tpu_custom_call" | custom-call | flops 10000000 | bytes 1300000 | tf_op jit(solution)/shard_map/pallas_call | solution.py:135
  35.8 5.9 %fusion.4 = f32[32,4,16,128]{3,0,2,1:T(8,128)S(1)} fusion(f32[32,4,16,128]{3,0,2,1:T(8,128)} %copy.44, f32[32,1,1,128]{3,0,2,1:T(8,128)S(1)} %broadcast.33, f32[32,1,16,128]{3,0,2,1:T(8,128)S(1)} %bitcast.147, f32[32,1,16,128]{3,0,2,1:T(8,128)S(1)} %bitcast.148, f32[32,4,1,128]{3,0,2,1:T(8,128)} %bitcast.155, f32[32,4,1,128]{3,0,2,1:T(8,128)} %bitcast.154, ...), kind=kOutput, calls=%fused_computation.32 | convolution fusion | flops 107479040 | bytes 4870272 | tf_op jit(solution)/shard_map/dot_general | solution.py:88
  41.9 5.8 %collective-permute-start.5 = (f32[222,128]{1,0:T(8,128)S(1)}, f32[222,128]{1,0:T(8,128)S(1)}, u32[]{:S(2)}, u32[]{:S(2)}) collective-permute-start(f32[222,128]{1,0:T(8,128)S(1)} %pad_maximum_fusion.31), channel_id=1, source_target_pairs={{1,0},{2,1},{3,2},{4,3},{5,4},{6,5},{7,6},{8,7},{9,8},{10,9},{11,1... | collective-permute-start | bytes 341000 | tf_op jit(solution)/shard_map/ppermute | solution.py:206
  48.5 1.9 %collective-permute-start.4 = (f32[222,128]{1,0:T(8,128)S(1)}, f32[222,128]{1,0:T(8,128)S(1)}, u32[]{:S(2)}, u32[]{:S(2)}) collective-permute-start(f32[222,128]{1,0:T(8,128)S(1)} %pad_maximum_fusion.30), channel_id=1, source_target_pairs={{0,1},{1,2},{2,3},{3,4},{4,5},{5,6},{6,7},{7,8},{8,9},{9,10},{10,1... | collective-permute-start | bytes 341000 | tf_op jit(solution)/shard_map/ppermute | solution.py:205
  51.3 5.4 %collective-permute-start.7 = (f32[32,1,16,128]{3,0,2,1:T(8,128)}, f32[32,1,16,128]{3,0,2,1:T(8,128)S(1)}, u32[]{:S(2)}, u32[]{:S(2)}) collective-permute-start(f32[32,1,16,128]{3,0,2,1:T(8,128)} %get-tuple-element.38), channel_id=1, source_target_pairs={{0,16},{16,32},{32,48},{48,64},{64,80},{80,96},{96,112},{112,128},... | collective-permute-start | bytes 786440 | tf_op jit(solution)/shard_map/ppermute | solution.py:44
  56.7 4.1 %collective-permute-start.6 = (f32[32,1,16,128]{3,0,2,1:T(8,128)}, f32[32,1,16,128]{3,0,2,1:T(8,128)}, u32[]{:S(2)}, u32[]{:S(2)}) collective-permute-start(f32[32,1,16,128]{3,0,2,1:T(8,128)} %get-tuple-element.37), channel_id=1, source_target_pairs={{16,0},{32,16},{48,32},{64,48},{80,64},{96,80},{112,96},{128,112},... | collective-permute-start | bytes 786440 | tf_op jit(solution)/shard_map/ppermute | solution.py:45
  62.0 1.9 %shard_map.122 = f32[8,35,128]{2,1,0:T(8,128)} custom-call(f32[649,128]{1,0:T(8,128)} %copy-done.4, f32[649,128]{1,0:T(8,128)} %copy-done.3, f32[163,128]{1,0:T(8,128)} %copy-done.9, f32[163,128]{1,0:T(8,128)} %copy-done.8, f32[222,128]{1,0:T(8,128)} %copy-done.7, f32[222,128]{1,0:T(8,128)} %copy-done.6), custom_call_target="tpu_custom_call" | custom-call | bytes 300000 | tf_op jit(solution)/shard_map/pallas_call | solution.py:305
  64.6 1.7 %fusion = f32[4,8,64,128]{3,1,2,0:T(8,128)S(1)} fusion(f32[32,32]{1,0:T(8,128)S(1)} %copy-done, f32[4,8,64,128]{3,2,1,0:T(8,128)S(1)} %bitcast.136), kind=kOutput, calls=%fused_computation.27 | convolution fusion | flops 100925440 | bytes 2101248 | tf_op jit(solution)/shard_map/dot_general | solution.py:88
  69.9 2.1 %fusion.24 = f32[32,4,16,128]{3,0,2,1:T(8,128)S(1)} fusion(f32[32,4,16,128]{3,0,2,1:T(8,128)S(1)} %fusion.4, f32[32,1,1,128]{3,0,2,1:T(8,128)S(1)} %broadcast.33, f32[32,6,16,128]{3,0,2,1:T(8,128)S(1)} %constant_dynamic-update-slice_fusion, f32[32,4,1,128]{3,0,2,1:T(8,128)S(1)} %bitcast.146, f32[32,4,1,128]{3,0,2,1:T(8,128)S(1)} %bitcast.144, ...), kind=kLoop, calls=%fused_computation.52 | loop fusion | flops 5505024 | bytes 6439040 | tf_op jit(solution)/shard_map/add | solution.py:92
  72.8 3.7 %collective-permute-start.9 = (f32[32,1,16,128]{3,0,2,1:T(8,128)}, f32[32,1,16,128]{3,0,2,1:T(8,128)S(1)}, u32[]{:S(2)}, u32[]{:S(2)}) collective-permute-start(f32[32,1,16,128]{3,0,2,1:T(8,128)} %get-tuple-element.36), channel_id=1, source_target_pairs={{0,16},{16,32},{32,48},{48,64},{64,80},{80,96},{96,112},{112,128},... | collective-permute-start | bytes 786440 | tf_op jit(solution)/shard_map/ppermute | solution.py:44
  77.8 4.6 %shard_map.123.start_ref = f32[3,40,256]{2,1,0:T(8,128)} custom-call(f32[4,4,256]{2,1,0:T(4,128)} %get-tuple-element.55.own_ref, f32[4,3,6,256]{3,2,1,0:T(8,128)} %pad_maximum_fusion.32.near_ref, f32[4,256]{1,0:T(4,128)} %get-tuple-element.59.occ_ref, f32[3,40,256]{2,1,0:T(8,128)} %broadcast_in_dim.16.start_ref), custom_call_target="tpu_custom_call" | custom-call | flops 6000000 | bytes 150000 | tf_op jit(solution)/shard_map/pallas_call | solution.py:276
  82.4 6.0 %collective-permute-start.8 = (f32[32,1,16,128]{3,0,2,1:T(8,128)}, f32[32,1,16,128]{3,0,2,1:T(8,128)S(1)}, u32[]{:S(2)}, u32[]{:S(2)}) collective-permute-start(f32[32,1,16,128]{3,0,2,1:T(8,128)} %get-tuple-element.35), channel_id=1, source_target_pairs={{16,0},{32,16},{48,32},{64,48},{80,64},{96,80},{112,96},{128,112},... | collective-permute-start | bytes 786440 | tf_op jit(solution)/shard_map/ppermute | solution.py:45
  89.0 1.7 %fusion.1 = f32[4,8,64,128]{3,1,2,0:T(8,128)S(1)} fusion(f32[32,32]{1,0:T(8,128)S(1)} %copy-done, f32[4,8,64,128]{3,2,1,0:T(8,128)S(1)} %bitcast.137), kind=kOutput, calls=%fused_computation.28 | convolution fusion | flops 100925440 | bytes 2101248 | tf_op jit(solution)/shard_map/dot_general | solution.py:88
  91.5 4.2 %collective-permute-start.10 = (f32[32,4,1,128]{3,0,2,1:T(8,128)S(1)}, f32[32,4,1,128]{3,0,2,1:T(8,128)S(1)}, u32[]{:S(2)}, u32[]{:S(2)}) collective-permute-start(f32[32,4,1,128]{3,0,2,1:T(8,128)S(1)} %copy-done.21), channel_id=1, source_target_pairs={{1,0},{2,1},{3,2},{4,3},{5,4},{6,5},{7,6},{8,7},{9,8},{10,9},{11,1... | collective-permute-start | bytes 196616 | tf_op jit(solution)/shard_map/ppermute | solution.py:45
  95.8 1.9 %collective-permute-start.11 = (f32[32,4,1,128]{3,0,2,1:T(8,128)S(1)}, f32[32,4,1,128]{3,0,2,1:T(8,128)S(1)}, u32[]{:S(2)}, u32[]{:S(2)}) collective-permute-start(f32[32,4,1,128]{3,0,2,1:T(8,128)S(1)} %copy-done.19), channel_id=1, source_target_pairs={{0,1},{1,2},{2,3},{3,4},{4,5},{5,6},{6,7},{7,8},{8,9},{9,10},{10,1... | collective-permute-start | bytes 196616 | tf_op jit(solution)/shard_map/ppermute | solution.py:44
  97.9 5.6 %collective-permute-done.11 = f32[32,4,1,128]{3,0,2,1:T(8,128)S(1)} collective-permute-done((f32[32,4,1,128]{3,0,2,1:T(8,128)S(1)}, f32[32,4,1,128]{3,0,2,1:T(8,128)S(1)}, u32[]{:S(2)}, u32[]{:S(2)}) %collective-permute-start.11) | collective-permute-done | bytes 65568 | tf_op jit(solution)/shard_map/ppermute | solution.py:44
  105.5 1.9 %collective-permute-start.13 = (f32[32,1,16,128]{3,0,2,1:T(8,128)}, f32[32,1,16,128]{3,0,2,1:T(8,128)S(1)}, u32[]{:S(2)}, u32[]{:S(2)}) collective-permute-start(f32[32,1,16,128]{3,0,2,1:T(8,128)} %get-tuple-element.32), channel_id=1, source_target_pairs={{0,16},{16,32},{32,48},{48,64},{64,80},{80,96},{96,112},{112,128},... | collective-permute-start | bytes 786440 | tf_op jit(solution)/shard_map/ppermute | solution.py:44
  108.0 3.1 %shard_map.124 = f32[3,4,256]{2,1,0:T(4,128)} custom-call(f32[4,4,256]{2,1,0:T(4,128)} %get-tuple-element.55.own_ref, f32[4,3,6,256]{3,2,1,0:T(8,128)} %pad_maximum_fusion.32.near_ref, f32[4,256]{1,0:T(4,128)} %get-tuple-element.59.occ_ref, f32[3,40,256]{2,1,0:T(8,128)} %shard_map.123.start_ref), custom_call_target="tpu_custom_call" | custom-call | flops 3000000 | bytes 150000 | tf_op jit(solution)/shard_map/pallas_call | solution.py:276
  111.1 7.5 %collective-permute-start.12 = (f32[32,1,16,128]{3,0,2,1:T(8,128)}, f32[32,1,16,128]{3,0,2,1:T(8,128)S(1)}, u32[]{:S(2)}, u32[]{:S(2)}) collective-permute-start(f32[32,1,16,128]{3,0,2,1:T(8,128)} %get-tuple-element.31), channel_id=1, source_target_pairs={{16,0},{32,16},{48,32},{64,48},{80,64},{96,80},{112,96},{128,112},... | collective-permute-start | bytes 786440 | tf_op jit(solution)/shard_map/ppermute | solution.py:45
  119.3 1.7 %fusion.2 = f32[4,8,64,128]{3,1,2,0:T(8,128)S(1)} fusion(f32[32,32]{1,0:T(8,128)S(1)} %copy-done, f32[4,8,64,128]{3,2,1,0:T(8,128)S(1)} %bitcast.138), kind=kOutput, calls=%fused_computation.29 | convolution fusion | flops 100925440 | bytes 2101248 | tf_op jit(solution)/shard_map/dot_general | solution.py:88
  121.8 1.9 %collective-permute-start.14 = (f32[32,4,1,128]{3,0,2,1:T(8,128)S(1)}, f32[32,4,1,128]{3,0,2,1:T(8,128)S(1)}, u32[]{:S(2)}, u32[]{:S(2)}) collective-permute-start(f32[32,4,1,128]{3,0,2,1:T(8,128)S(1)} %copy-done.22), channel_id=1, source_target_pairs={{1,0},{2,1},{3,2},{4,3},{5,4},{6,5},{7,6},{8,7},{9,8},{10,9},{11,1... | collective-permute-start | bytes 196616 | tf_op jit(solution)/shard_map/ppermute | solution.py:45
  123.7 2.4 %collective-permute-start.15 = (f32[32,4,1,128]{3,0,2,1:T(8,128)S(1)}, f32[32,4,1,128]{3,0,2,1:T(8,128)S(1)}, u32[]{:S(2)}, u32[]{:S(2)}) collective-permute-start(f32[32,4,1,128]{3,0,2,1:T(8,128)S(1)} %copy-done.20), channel_id=1, source_target_pairs={{0,1},{1,2},{2,3},{3,4},{4,5},{5,6},{6,7},{7,8},{8,9},{9,10},{10,1... | collective-permute-start | bytes 196616 | tf_op jit(solution)/shard_map/ppermute | solution.py:44
  126.3 5.1 %collective-permute-done.15 = f32[32,4,1,128]{3,0,2,1:T(8,128)S(1)} collective-permute-done((f32[32,4,1,128]{3,0,2,1:T(8,128)S(1)}, f32[32,4,1,128]{3,0,2,1:T(8,128)S(1)}, u32[]{:S(2)}, u32[]{:S(2)}) %collective-permute-start.15) | collective-permute-done | bytes 65568 | tf_op jit(solution)/shard_map/ppermute | solution.py:44
  132.5 1.6 %copy.57 = f32[32,4,16,128]{3,2,1,0:T(8,128)} copy(f32[32,4,16,128]{3,0,2,1:T(8,128)S(1)} %fusion.46) | data formatting | bytes 2097152
  (141 shorter events, 26.3 us)
Async XLA Ops:
  0.6 35.1 %copy-start = (f32[32,32]{1,0:T(8,128)S(1)}, f32[32,32]{1,0:T(8,128)}, u32[]{:S(2)}) copy-start(f32[32,32]{1,0:T(8,128)} %param.12) | copy-start | bytes 12292
  1.4 40.5 %copy-start.17 = (f32[1,1,4,256]{3,2,1,0:T(4,128)}, f32[1,1,4,256]{3,2,1,0:T(4,128)S(1)}, u32[]{:S(2)}) copy-start(f32[1,1,4,256]{3,2,1,0:T(4,128)S(1)} %multiply_bitcast_fusion) | copy-start | bytes 12292
  4.4 9.8 %copy-start.2 = (f32[32,4,16,128]{3,2,1,0:T(8,128)S(1)}, f32[32,4,16,128]{3,2,1,0:T(8,128)}, u32[]{:S(2)}) copy-start(f32[32,4,16,128]{3,2,1,0:T(8,128)} %param.10) | copy-start | bytes 3145732
  5.6 15.4 %copy-start.23 = (s32[1,4,256]{2,1,0:T(4,128)S(1)}, s32[1,4,256]{2,1,0:T(4,128)}, u32[]{:S(2)}) copy-start(s32[1,4,256]{2,1,0:T(4,128)} %param.16) | copy-start | bytes 12292
  5.6 15.4 %copy-start.26 = (s32[1,4,256]{2,1,0:T(4,128)S(1)}, s32[1,4,256]{2,1,0:T(4,128)}, u32[]{:S(2)}) copy-start(s32[1,4,256]{2,1,0:T(4,128)} %param.17) | copy-start | bytes 12292
  6.7 28.3 %collective-permute-start = (f32[649,128]{1,0:T(8,128)}, f32[649,128]{1,0:T(8,128)S(1)}, u32[]{:S(2)}, u32[]{:S(2)}) collective-permute-start(f32[649,128]{1,0:T(8,128)} %get-tuple-element.58), channel_id=1, source_target_pairs={{16,0},{32,16},{48,32},{64,48},{80,64},{96,80},{112,96},{128,112},... | collective-permute-start | bytes 996872 | tf_op jit(solution)/shard_map/ppermute | solution.py:206
  10.4 13.5 %copy-start.14 = (f32[32,1,4,256]{3,2,1,0:T(4,128)S(1)}, f32[32,1,4,256]{3,2,1,0:T(4,128)}, u32[]{:S(2)}) copy-start(f32[32,1,4,256]{3,2,1,0:T(4,128)} %param.13) | copy-start | bytes 393220
  10.4 24.5 %collective-permute-start.1 = (f32[649,128]{1,0:T(8,128)}, f32[649,128]{1,0:T(8,128)S(1)}, u32[]{:S(2)}, u32[]{:S(2)}) collective-permute-start(f32[649,128]{1,0:T(8,128)} %get-tuple-element.57), channel_id=1, source_target_pairs={{0,16},{16,32},{32,48},{48,64},{64,80},{80,96},{96,112},{112,128},... | collective-permute-start | bytes 996872 | tf_op jit(solution)/shard_map/ppermute | solution.py:205
  14.9 18.7 %collective-permute-start.2 = (f32[163,128]{1,0:T(8,128)}, f32[163,128]{1,0:T(8,128)S(1)}, u32[]{:S(2)}, u32[]{:S(2)}) collective-permute-start(f32[163,128]{1,0:T(8,128)} %pad_maximum_fusion.33), channel_id=1, source_target_pairs={{1,0},{2,1},{3,2},{4,3},{5,4},{6,5},{7,6},{8,7},{9,8},{10,9},{11,1... | collective-permute-start | bytes 250376 | tf_op jit(solution)/shard_map/ppermute | solution.py:206
  19.0 15.3 %collective-permute-start.3 = (f32[163,128]{1,0:T(8,128)}, f32[163,128]{1,0:T(8,128)S(1)}, u32[]{:S(2)}, u32[]{:S(2)}) collective-permute-start(f32[163,128]{1,0:T(8,128)} %pad_maximum_fusion.34), channel_id=1, source_target_pairs={{0,1},{1,2},{2,3},{3,4},{4,5},{5,6},{6,7},{7,8},{8,9},{9,10},{10,1... | collective-permute-start | bytes 250376 | tf_op jit(solution)/shard_map/ppermute | solution.py:205
  27.3 8.5 %copy-start.24 = (f32[32]{0:T(128)S(1)}, f32[32]{0:T(128)}, u32[]{:S(2)}) copy-start(f32[32]{0:T(128)} %param.11) | copy-start | bytes 388
  33.6 8.1 %copy-start.8 = (f32[163,128]{1,0:T(8,128)}, f32[163,128]{1,0:T(8,128)S(1)}, u32[]{:S(2)}) copy-start(f32[163,128]{1,0:T(8,128)S(1)} %collective-permute-done.2.side_above) | copy-start | bytes 250372
  34.3 7.5 %copy-start.9 = (f32[163,128]{1,0:T(8,128)}, f32[163,128]{1,0:T(8,128)S(1)}, u32[]{:S(2)}) copy-start(f32[163,128]{1,0:T(8,128)S(1)} %collective-permute-done.3.side_below) | copy-start | bytes 250372
  34.9 6.9 %copy-start.3 = (f32[649,128]{1,0:T(8,128)}, f32[649,128]{1,0:T(8,128)S(1)}, u32[]{:S(2)}) copy-start(f32[649,128]{1,0:T(8,128)S(1)} %collective-permute-done.x_above) | copy-start | bytes 996868
  35.0 6.8 %copy-start.4 = (f32[649,128]{1,0:T(8,128)}, f32[649,128]{1,0:T(8,128)S(1)}, u32[]{:S(2)}) copy-start(f32[649,128]{1,0:T(8,128)S(1)} %collective-permute-done.1.x_below) | copy-start | bytes 996868
  35.8 6.1 %copy-start.15 = (f32[3,1,4,256]{3,2,1,0:T(4,128)S(1)}, f32[3,1,4,256]{3,2,1,0:T(4,128)}, u32[]{:S(2)}) copy-start(f32[3,1,4,256]{3,2,1,0:T(4,128)} %param.14) | copy-start | bytes 36868
  41.8 22.7 %copy-start.10 = (f32[4,1,4,256]{3,2,1,0:T(4,128)}, f32[4,1,4,256]{3,2,1,0:T(4,128)S(1)}, u32[]{:S(2)}) copy-start(f32[4,1,4,256]{3,2,1,0:T(4,128)S(1)} %reshape.143) | copy-start | bytes 49156
  41.9 22.7 %copy-start.12 = (f32[4,1,4,256]{3,2,1,0:T(4,128)}, f32[4,1,4,256]{3,2,1,0:T(4,128)S(1)}, u32[]{:S(2)}) copy-start(f32[4,1,4,256]{3,2,1,0:T(4,128)S(1)} %reshape.144) | copy-start | bytes 49156
  41.9 18.8 %collective-permute-start.5 = (f32[222,128]{1,0:T(8,128)S(1)}, f32[222,128]{1,0:T(8,128)S(1)}, u32[]{:S(2)}, u32[]{:S(2)}) collective-permute-start(f32[222,128]{1,0:T(8,128)S(1)} %pad_maximum_fusion.31), channel_id=1, source_target_pairs={{1,0},{2,1},{3,2},{4,3},{5,4},{6,5},{7,6},{8,7},{9,8},{10,9},{11,1... | collective-permute-start | bytes 341000 | tf_op jit(solution)/shard_map/ppermute | solution.py:206
  48.5 12.3 %collective-permute-start.4 = (f32[222,128]{1,0:T(8,128)S(1)}, f32[222,128]{1,0:T(8,128)S(1)}, u32[]{:S(2)}, u32[]{:S(2)}) collective-permute-start(f32[222,128]{1,0:T(8,128)S(1)} %pad_maximum_fusion.30), channel_id=1, source_target_pairs={{0,1},{1,2},{2,3},{3,4},{4,5},{5,6},{6,7},{7,8},{8,9},{9,10},{10,1... | collective-permute-start | bytes 341000 | tf_op jit(solution)/shard_map/ppermute | solution.py:205
  51.3 16.7 %collective-permute-start.7 = (f32[32,1,16,128]{3,0,2,1:T(8,128)}, f32[32,1,16,128]{3,0,2,1:T(8,128)S(1)}, u32[]{:S(2)}, u32[]{:S(2)}) collective-permute-start(f32[32,1,16,128]{3,0,2,1:T(8,128)} %get-tuple-element.38), channel_id=1, source_target_pairs={{0,16},{16,32},{32,48},{48,64},{64,80},{80,96},{96,112},{112,128},... | collective-permute-start | bytes 786440 | tf_op jit(solution)/shard_map/ppermute | solution.py:44
  56.7 12.2 %collective-permute-start.6 = (f32[32,1,16,128]{3,0,2,1:T(8,128)}, f32[32,1,16,128]{3,0,2,1:T(8,128)}, u32[]{:S(2)}, u32[]{:S(2)}) collective-permute-start(f32[32,1,16,128]{3,0,2,1:T(8,128)} %get-tuple-element.37), channel_id=1, source_target_pairs={{16,0},{32,16},{48,32},{64,48},{80,64},{96,80},{112,96},{128,112},... | collective-permute-start | bytes 786440 | tf_op jit(solution)/shard_map/ppermute | solution.py:45
  72.8 24.9 %collective-permute-start.9 = (f32[32,1,16,128]{3,0,2,1:T(8,128)}, f32[32,1,16,128]{3,0,2,1:T(8,128)S(1)}, u32[]{:S(2)}, u32[]{:S(2)}) collective-permute-start(f32[32,1,16,128]{3,0,2,1:T(8,128)} %get-tuple-element.36), channel_id=1, source_target_pairs={{0,16},{16,32},{32,48},{48,64},{64,80},{80,96},{96,112},{112,128},... | collective-permute-start | bytes 786440 | tf_op jit(solution)/shard_map/ppermute | solution.py:44
  82.4 15.4 %collective-permute-start.8 = (f32[32,1,16,128]{3,0,2,1:T(8,128)}, f32[32,1,16,128]{3,0,2,1:T(8,128)S(1)}, u32[]{:S(2)}, u32[]{:S(2)}) collective-permute-start(f32[32,1,16,128]{3,0,2,1:T(8,128)} %get-tuple-element.35), channel_id=1, source_target_pairs={{16,0},{32,16},{48,32},{64,48},{80,64},{96,80},{112,96},{128,112},... | collective-permute-start | bytes 786440 | tf_op jit(solution)/shard_map/ppermute | solution.py:45
  90.7 5.1 %copy-start.19 = (f32[32,4,1,128]{3,0,2,1:T(8,128)S(1)}, f32[32,4,1,128]{3,0,2,1:T(8,128)}, u32[]{:S(2)}) copy-start(f32[32,4,1,128]{3,0,2,1:T(8,128)} %get-tuple-element.34) | copy-start | bytes 196612
  91.5 6.3 %collective-permute-start.10 = (f32[32,4,1,128]{3,0,2,1:T(8,128)S(1)}, f32[32,4,1,128]{3,0,2,1:T(8,128)S(1)}, u32[]{:S(2)}, u32[]{:S(2)}) collective-permute-start(f32[32,4,1,128]{3,0,2,1:T(8,128)S(1)} %copy-done.21), channel_id=1, source_target_pairs={{1,0},{2,1},{3,2},{4,3},{5,4},{6,5},{7,6},{8,7},{9,8},{10,9},{11,1... | collective-permute-start | bytes 196616 | tf_op jit(solution)/shard_map/ppermute | solution.py:45
  95.8 7.7 %collective-permute-start.11 = (f32[32,4,1,128]{3,0,2,1:T(8,128)S(1)}, f32[32,4,1,128]{3,0,2,1:T(8,128)S(1)}, u32[]{:S(2)}, u32[]{:S(2)}) collective-permute-start(f32[32,4,1,128]{3,0,2,1:T(8,128)S(1)} %copy-done.19), channel_id=1, source_target_pairs={{0,1},{1,2},{2,3},{3,4},{4,5},{5,6},{6,7},{7,8},{8,9},{9,10},{10,1... | collective-permute-start | bytes 196616 | tf_op jit(solution)/shard_map/ppermute | solution.py:44
  105.5 20.7 %collective-permute-start.13 = (f32[32,1,16,128]{3,0,2,1:T(8,128)}, f32[32,1,16,128]{3,0,2,1:T(8,128)S(1)}, u32[]{:S(2)}, u32[]{:S(2)}) collective-permute-start(f32[32,1,16,128]{3,0,2,1:T(8,128)} %get-tuple-element.32), channel_id=1, source_target_pairs={{0,16},{16,32},{32,48},{48,64},{64,80},{80,96},{96,112},{112,128},... | collective-permute-start | bytes 786440 | tf_op jit(solution)/shard_map/ppermute | solution.py:44
  111.1 15.1 %collective-permute-start.12 = (f32[32,1,16,128]{3,0,2,1:T(8,128)}, f32[32,1,16,128]{3,0,2,1:T(8,128)S(1)}, u32[]{:S(2)}, u32[]{:S(2)}) collective-permute-start(f32[32,1,16,128]{3,0,2,1:T(8,128)} %get-tuple-element.31), channel_id=1, source_target_pairs={{16,0},{32,16},{48,32},{64,48},{80,64},{96,80},{112,96},{128,112},... | collective-permute-start | bytes 786440 | tf_op jit(solution)/shard_map/ppermute | solution.py:45
  121.0 2.7 %copy-start.20 = (f32[32,4,1,128]{3,0,2,1:T(8,128)S(1)}, f32[32,4,1,128]{3,0,2,1:T(8,128)}, u32[]{:S(2)}) copy-start(f32[32,4,1,128]{3,0,2,1:T(8,128)} %get-tuple-element.30) | copy-start | bytes 196612
  121.8 4.5 %collective-permute-start.14 = (f32[32,4,1,128]{3,0,2,1:T(8,128)S(1)}, f32[32,4,1,128]{3,0,2,1:T(8,128)S(1)}, u32[]{:S(2)}, u32[]{:S(2)}) collective-permute-start(f32[32,4,1,128]{3,0,2,1:T(8,128)S(1)} %copy-done.22), channel_id=1, source_target_pairs={{1,0},{2,1},{3,2},{4,3},{5,4},{6,5},{7,6},{8,7},{9,8},{10,9},{11,1... | collective-permute-start | bytes 196616 | tf_op jit(solution)/shard_map/ppermute | solution.py:45
  123.7 7.7 %collective-permute-start.15 = (f32[32,4,1,128]{3,0,2,1:T(8,128)S(1)}, f32[32,4,1,128]{3,0,2,1:T(8,128)S(1)}, u32[]{:S(2)}, u32[]{:S(2)}) collective-permute-start(f32[32,4,1,128]{3,0,2,1:T(8,128)S(1)} %copy-done.20), channel_id=1, source_target_pairs={{0,1},{1,2},{2,3},{3,4},{4,5},{5,6},{6,7},{7,8},{8,9},{9,10},{10,1... | collective-permute-start | bytes 196616 | tf_op jit(solution)/shard_map/ppermute | solution.py:44
  (15 other events, 22.4 us)

commit v12 on v9

--- a/solution.py
+++ b/solution.py
@@ -352,15 +352,10 @@
     starts = (field_rows + points.size // 128, side_rows, side_rows + points_low.size // 128)
     rows = points.shape[2]
     arrived = gather_arrived(x_flats, side_flats, corner_flats, *starts, payload.shape[1:])
-    partial = pallas_forces(points, bordered, occupancy, None, (-1, 0), False)
-    current, arrived, partial = lax.optimization_barrier((current, arrived, partial))
+    force = pallas_forces(points, bordered, occupancy, None, (-1, 0, 1), True)
+    current, arrived, force = lax.optimization_barrier((current, arrived, force))
     current = advance(framed(current, x_low, x_high, y_low, y_high), source, rates, mixing)
-    current, bordered, partial = lax.optimization_barrier((current, bordered, partial))
-
-    def later_work():
-        return pallas_forces(points, bordered, occupancy, partial, (1,), True)
-
-    current, force = substep_beside(current, source, rates, mixing, later_work)
+    current = substep(current, source, rates, mixing)
     current = substep(current, source, rates, mixing)
     displacement = force.reshape(3, 1, rows, points.shape[3])
     return (current, displacement, arrived)

time: 125 us -> 123 us (0.984)
  local copies, waits for them, and re-layouts: 21.4 us -> 18.3 us
  matrix products: 8.57 us -> 10.5 us
  starting transfers between devices: 64.9 us -> 66.8 us
  Pallas kernels: 16 us -> 14.3 us
  other arithmetic: 10.5 us -> 9.16 us
    ppermute x5, starting transfers between devices: 20 us -> 22.7 us  [halos(): low = lax.ppermute(tail, axis, [(i, (i + 1) % count) for i in range(ends)])]
    dot_general x4, matrix products: 8.57 us -> 10.5 us  [advance(): jnp.dot(mixing, center.reshape(species, -1), precision=lax.Precision.HIGH...]
    pallas_call x2 -> x1, Pallas kernels: 7.7 us -> 6.08 us  [pallas_forces(): pl.pallas_call(functools.partial(forces_kernel, shifts, scale), out_shape...]
    unnamed x63 -> x41, local copies, waits for them, and re-layouts: 8.74 us -> 9.76 us
  transfers between devices with their start and end apart: 16 -> 16, of which waited for: 0 -> 0; matrix products, arithmetic and copies ran while one was open for 15% -> 14% of each run, Pallas kernels for 13% -> 12%
where the time goes in v12:
time: 123 us; the launch traced here: 121 us
  starting transfers between devices  66.8 us (54%)
  local copies, waits for them, and re-layouts  18.3 us (15%)
  Pallas kernels  14.3 us (12%)
  matrix products  10.5 us (9%)
  other arithmetic  9.16 us (7%)
  between operations  1.44 us (1%)
    ppermute x5, starting transfers between devices, halos(): low = lax.ppermute(tail, axis, [(i, (i + 1) % count) for i in range(ends)])  22.7 us
    ppermute x5, starting transfers between devices, halos(): high = lax.ppermute(head, axis, [((i + 1) % count, i) for i in range(ends)])  19.3 us
    ppermute x3, starting transfers between devices, send_pair(): above = lax.ppermute(pack(downward), axis, down)  14.6 us
    dot_general x4, matrix products, advance(): jnp.dot(mixing, center.reshape(species, -1), precision=lax.Precision.HIGH...  10.5 us
    ppermute x3, starting transfers between devices, send_pair(): below = lax.ppermute(pack(upward), axis, up)  10.2 us
    unnamed x41, local copies, waits for them, and re-layouts  9.76 us
    pallas_call x1, Pallas kernels, deposit(): pl.pallas_call(deposit_kernel, out_shape=jax.ShapeDtypeStruct((BIN_XY, bi...  6.34 us
    pallas_call x1, Pallas kernels, pallas_forces(): pl.pallas_call(functools.partial(forces_kernel, shifts, scale), out_shape...  6.08 us
  transfers between devices with their start and end apart: 16, of which 0 were waited for; matrix products, arithmetic and copies ran while one was open for 14% of the time, Pallas kernels for 12%

profile of v12, /device:TPU:120, one launch (start us, length us, event | category | flops | bytes accessed | tf_op | source)
XLA Modules:
  0.0 120.5 jit_solution(7145802507147951211)
XLA Ops:
  1.4 1.3 %fusion.65 = (f32[4,4,256]{2,1,0:T(4,128)}, f32[4,1,4,256]{3,2,1,0:T(4,128)S(1)}) fusion(f32[1,1,4,256]{3,2,1,0:T(4,128)S(1)} %multiply_bitcast_fusion, f32[3,1,4,256]{3,2,1,0:T(4,128)} %param.14), kind=kLoop, calls=%fused_computation.145 | loop fusion | flops 4096 | bytes 49152 | tf_op jit(solution)/shard_map/squeeze | solution.py:283
  5.8 3.1 %collective-permute-start = (f32[649,128]{1,0:T(8,128)S(1)}, f32[649,128]{1,0:T(8,128)S(1)}, u32[]{:S(2)}, u32[]{:S(2)}) collective-permute-start(f32[649,128]{1,0:T(8,128)S(1)} %get-tuple-element.44), channel_id=1, source_target_pairs={{16,0},{32,16},{48,32},{64,48},{80,64},{96,80},{112,96},{128,112},... | collective-permute-start | bytes 996872 | tf_op jit(solution)/shard_map/ppermute | solution.py:206
  9.0 6.3 %collective-permute-start.1 = (f32[649,128]{1,0:T(8,128)S(1)}, f32[649,128]{1,0:T(8,128)S(1)}, u32[]{:S(2)}, u32[]{:S(2)}) collective-permute-start(f32[649,128]{1,0:T(8,128)S(1)} %get-tuple-element.43), channel_id=1, source_target_pairs={{0,16},{16,32},{32,48},{48,64},{64,80},{80,96},{96,112},{112,128},... | collective-permute-start | bytes 996872 | tf_op jit(solution)/shard_map/ppermute | solution.py:205
  15.4 1.9 %collective-permute-start.3 = (f32[163,128]{1,0:T(8,128)S(1)}, f32[163,128]{1,0:T(8,128)S(1)}, u32[]{:S(2)}, u32[]{:S(2)}) collective-permute-start(f32[163,128]{1,0:T(8,128)S(1)} %pad_maximum_fusion.42), channel_id=1, source_target_pairs={{0,1},{1,2},{2,3},{3,4},{4,5},{5,6},{6,7},{7,8},{8,9},{9,10},{10,1... | collective-permute-start | bytes 250376 | tf_op jit(solution)/shard_map/ppermute | solution.py:205
  17.4 5.8 %collective-permute-start.2 = (f32[163,128]{1,0:T(8,128)S(1)}, f32[163,128]{1,0:T(8,128)S(1)}, u32[]{:S(2)}, u32[]{:S(2)}) collective-permute-start(f32[163,128]{1,0:T(8,128)S(1)} %pad_maximum_fusion.41), channel_id=1, source_target_pairs={{1,0},{2,1},{3,2},{4,3},{5,4},{6,5},{7,6},{8,7},{9,8},{10,9},{11,1... | collective-permute-start | bytes 250376 | tf_op jit(solution)/shard_map/ppermute | solution.py:206
  23.8 1.6 %copy.44 = f32[32,4,16,128]{3,0,2,1:T(8,128)} copy(f32[32,4,16,128]{3,2,1,0:T(8,128)S(1)} %copy-done.2) | data formatting | bytes 2097152 | tf_op args[0]
  26.0 1.2 copy.62
  27.4 1.4 %copy.47 = f32[16,4,32,16]{3,2,1,0:T(8,128)} copy(f32[16,4,32,16]{2,0,3,1:T(8,128)S(1)} %bitcast.139) | data formatting | bytes 262144 | tf_op jit(solution)/shard_map/transpose | solution.py:132
  29.5 6.3 %shard_map.121 = f32[4,16,32,128]{3,2,1,0:T(8,128)} custom-call(f32[16,128,16]{2,1,0:T(8,128)} %bitcast.137, f32[16,4,16]{2,1,0:T(4,128)} %bitcast.151), custom_call_target="tpu_custom_call" | custom-call | flops 10000000 | bytes 1300000 | tf_op jit(solution)/shard_map/pallas_call | solution.py:135
  36.1 1.2 %copy-done.1 = f32[4,16,32,128]{3,2,1,0:T(8,128)S(1)} copy-done((f32[4,16,32,128]{3,2,1,0:T(8,128)S(1)}, f32[4,16,32,128]{3,2,1,0:T(8,128)}, u32[]{:S(2)}) %copy-start.1) | copy-done | bytes 1048600
  37.4 5.5 %fusion.4 = f32[32,4,16,128]{3,0,2,1:T(8,128)S(1)} fusion(f32[32,4,16,128]{3,0,2,1:T(8,128)} %copy.44, f32[32,1,1,128]{3,0,2,1:T(8,128)S(1)} %broadcast.33, f32[32,1,16,128]{3,0,2,1:T(8,128)S(1)} %bitcast.145, f32[32,1,16,128]{3,0,2,1:T(8,128)S(1)} %bitcast.146, f32[32,4,1,128]{3,0,2,1:T(8,128)S(1)} %bitcast.152, f32[32,4,1,128]{3,0,2,1:T(8,128)S(1)} %bitcast.153, ...), kind=kOutput, calls=%fused_computation.32 | convolution fusion | flops 107479040 | bytes 4870272 | tf_op jit(solution)/shard_map/dot_general | solution.py:88
  43.0 1.9 %collective-permute-start.4 = (f32[222,128]{1,0:T(8,128)S(1)}, f32[222,128]{1,0:T(8,128)S(1)}, u32[]{:S(2)}, u32[]{:S(2)}) collective-permute-start(f32[222,128]{1,0:T(8,128)S(1)} %pad_maximum_fusion.38), channel_id=1, source_target_pairs={{0,1},{1,2},{2,3},{3,4},{4,5},{5,6},{6,7},{7,8},{8,9},{9,10},{10,1... | collective-permute-start | bytes 341000 | tf_op jit(solution)/shard_map/ppermute | solution.py:205
  44.9 5.8 %collective-permute-start.5 = (f32[222,128]{1,0:T(8,128)S(1)}, f32[222,128]{1,0:T(8,128)S(1)}, u32[]{:S(2)}, u32[]{:S(2)}) collective-permute-start(f32[222,128]{1,0:T(8,128)S(1)} %pad_maximum_fusion.39), channel_id=1, source_target_pairs={{1,0},{2,1},{3,2},{4,3},{5,4},{6,5},{7,6},{8,7},{9,8},{10,9},{11,1... | collective-permute-start | bytes 341000 | tf_op jit(solution)/shard_map/ppermute | solution.py:206
  51.4 3.6 %collective-permute-start.7 = (f32[32,1,16,128]{3,0,2,1:T(8,128)}, f32[32,1,16,128]{3,0,2,1:T(8,128)S(1)}, u32[]{:S(2)}, u32[]{:S(2)}) collective-permute-start(f32[32,1,16,128]{3,0,2,1:T(8,128)} %get-tuple-element.24), channel_id=1, source_target_pairs={{0,16},{16,32},{32,48},{48,64},{64,80},{80,96},{96,112},{112,128},... | collective-permute-start | bytes 786440 | tf_op jit(solution)/shard_map/ppermute | solution.py:44
  55.0 3.9 %collective-permute-start.6 = (f32[32,1,16,128]{3,0,2,1:T(8,128)S(1)}, f32[32,1,16,128]{3,0,2,1:T(8,128)S(1)}, u32[]{:S(2)}, u32[]{:S(2)}) collective-permute-start(f32[32,1,16,128]{3,0,2,1:T(8,128)S(1)} %get-tuple-element.23), channel_id=1, source_target_pairs={{16,0},{32,16},{48,32},{64,48},{80,64},{96,80},{112,96},{128,112},... | collective-permute-start | bytes 786440 | tf_op jit(solution)/shard_map/ppermute | solution.py:45
  60.3 1.9 %shard_map.122 = f32[8,35,128]{2,1,0:T(8,128)} custom-call(f32[649,128]{1,0:T(8,128)} %copy-done.4, f32[649,128]{1,0:T(8,128)} %copy-done.3, f32[163,128]{1,0:T(8,128)} %copy-done.8, f32[163,128]{1,0:T(8,128)} %copy-done.9, f32[222,128]{1,0:T(8,128)} %copy-done.6, f32[222,128]{1,0:T(8,128)} %copy-done.7), custom_call_target="tpu_custom_call" | custom-call | bytes 300000 | tf_op jit(solution)/shard_map/pallas_call | solution.py:305
  64.2 6.1 %shard_map.123 = f32[3,4,256]{2,1,0:T(4,128)} custom-call(f32[4,4,256]{2,1,0:T(4,128)} %get-tuple-element.41.own_ref, f32[4,3,6,256]{3,2,1,0:T(8,128)} %pad_maximum_fusion.40.near_ref, f32[4,256]{1,0:T(4,128)} %get-tuple-element.45.occ_ref, f32[3,40,256]{2,1,0:T(8,128)} %broadcast_in_dim.16.start_ref), custom_call_target="tpu_custom_call" | custom-call | flops 9000000 | bytes 150000 | tf_op jit(solution)/shard_map/pallas_call | solution.py:276
  70.9 1.7 %fusion = f32[4,8,64,128]{3,1,2,0:T(8,128)S(1)} fusion(f32[32,32]{1,0:T(8,128)S(1)} %copy-done, f32[4,8,64,128]{3,2,1,0:T(8,128)S(1)} %bitcast.138), kind=kOutput, calls=%fused_computation.27 | convolution fusion | flops 100925440 | bytes 2101248 | tf_op jit(solution)/shard_map/dot_general | solution.py:88
  75.0 1.2 fusion.24
  76.3 1.9 %collective-permute-start.8 = (f32[32,1,16,128]{3,0,2,1:T(8,128)S(1)}, f32[32,1,16,128]{3,0,2,1:T(8,128)S(1)}, u32[]{:S(2)}, u32[]{:S(2)}) collective-permute-start(f32[32,1,16,128]{3,0,2,1:T(8,128)S(1)} %get-tuple-element.22), channel_id=1, source_target_pairs={{16,0},{32,16},{48,32},{64,48},{80,64},{96,80},{112,96},{128,112},... | collective-permute-start | bytes 786440 | tf_op jit(solution)/shard_map/ppermute | solution.py:45
  78.2 7.5 %collective-permute-start.9 = (f32[32,1,16,128]{3,0,2,1:T(8,128)S(1)}, f32[32,1,16,128]{3,0,2,1:T(8,128)S(1)}, u32[]{:S(2)}, u32[]{:S(2)}) collective-permute-start(f32[32,1,16,128]{3,0,2,1:T(8,128)S(1)} %get-tuple-element.21), channel_id=1, source_target_pairs={{0,16},{16,32},{32,48},{48,64},{64,80},{80,96},{96,112},{112,128},... | collective-permute-start | bytes 786440 | tf_op jit(solution)/shard_map/ppermute | solution.py:44
  86.4 1.9 %collective-permute-start.11 = (f32[32,4,1,128]{3,0,2,1:T(8,128)S(1)}, f32[32,4,1,128]{3,0,2,1:T(8,128)S(1)}, u32[]{:S(2)}, u32[]{:S(2)}) collective-permute-start(f32[32,4,1,128]{3,0,2,1:T(8,128)S(1)} %get-tuple-element.20), channel_id=1, source_target_pairs={{0,1},{1,2},{2,3},{3,4},{4,5},{5,6},{6,7},{7,8},{8,9},{9,10},{10,1... | collective-permute-start | bytes 196616 | tf_op jit(solution)/shard_map/ppermute | solution.py:44
  88.3 5.8 %collective-permute-start.10 = (f32[32,4,1,128]{3,0,2,1:T(8,128)S(1)}, f32[32,4,1,128]{3,0,2,1:T(8,128)S(1)}, u32[]{:S(2)}, u32[]{:S(2)}) collective-permute-start(f32[32,4,1,128]{3,0,2,1:T(8,128)S(1)} %get-tuple-element.19), channel_id=1, source_target_pairs={{1,0},{2,1},{3,2},{4,3},{5,4},{6,5},{7,6},{8,7},{9,8},{10,9},{11,1... | collective-permute-start | bytes 196616 | tf_op jit(solution)/shard_map/ppermute | solution.py:45
  94.1 1.7 %fusion.1 = f32[4,8,64,128]{3,1,2,0:T(8,128)S(1)} fusion(f32[32,32]{1,0:T(8,128)S(1)} %copy-done, f32[4,8,64,128]{3,2,1,0:T(8,128)S(1)} %bitcast.135), kind=kOutput, calls=%fused_computation.28 | convolution fusion | flops 100925440 | bytes 2101248 | tf_op jit(solution)/shard_map/dot_general | solution.py:88
  96.0 1.5 %fusion.35 = f32[32,4,16,128]{3,0,2,1:T(8,128)S(1)} fusion(f32[32,4,16,128]{3,0,2,1:T(8,128)S(1)} %fusion.24, f32[32,1,1,128]{3,0,2,1:T(8,128)S(1)} %broadcast.33, f32[32,1,16,128]{3,0,2,1:T(8,128)S(1)} %collective-permute-done.8, f32[32,1,16,128]{3,0,2,1:T(8,128)S(1)} %collective-permute-done.9, f32[32,4,1,128]{3,0,2,1:T(8,128)S(1)} %collective-permute-done.11, ...), kind=kLoop, calls=%fused_computation.63 | loop fusion | flops 6553600 | bytes 4866176 | tf_op jit(solution)/shard_map/add | solution.py:92
  97.5 1.9 %collective-permute-start.12 = (f32[32,1,16,128]{3,0,2,1:T(8,128)S(1)}, f32[32,1,16,128]{3,0,2,1:T(8,128)S(1)}, u32[]{:S(2)}, u32[]{:S(2)}) collective-permute-start(f32[32,1,16,128]{3,0,2,1:T(8,128)S(1)} %get-tuple-element.18), channel_id=1, source_target_pairs={{16,0},{32,16},{48,32},{64,48},{80,64},{96,80},{112,96},{128,112},... | collective-permute-start | bytes 786440 | tf_op jit(solution)/shard_map/ppermute | solution.py:45
  99.5 7.8 %collective-permute-start.13 = (f32[32,1,16,128]{3,0,2,1:T(8,128)S(1)}, f32[32,1,16,128]{3,0,2,1:T(8,128)S(1)}, u32[]{:S(2)}, u32[]{:S(2)}) collective-permute-start(f32[32,1,16,128]{3,0,2,1:T(8,128)S(1)} %get-tuple-element.17), channel_id=1, source_target_pairs={{0,16},{16,32},{32,48},{48,64},{64,80},{80,96},{96,112},{112,128},... | collective-permute-start | bytes 786440 | tf_op jit(solution)/shard_map/ppermute | solution.py:44
  107.9 1.9 %collective-permute-start.15 = (f32[32,4,1,128]{3,0,2,1:T(8,128)S(1)}, f32[32,4,1,128]{3,0,2,1:T(8,128)S(1)}, u32[]{:S(2)}, u32[]{:S(2)}) collective-permute-start(f32[32,4,1,128]{3,0,2,1:T(8,128)S(1)} %get-tuple-element.16), channel_id=1, source_target_pairs={{0,1},{1,2},{2,3},{3,4},{4,5},{5,6},{6,7},{7,8},{8,9},{9,10},{10,1... | collective-permute-start | bytes 196616 | tf_op jit(solution)/shard_map/ppermute | solution.py:44
  109.8 5.8 %collective-permute-start.14 = (f32[32,4,1,128]{3,0,2,1:T(8,128)S(1)}, f32[32,4,1,128]{3,0,2,1:T(8,128)S(1)}, u32[]{:S(2)}, u32[]{:S(2)}) collective-permute-start(f32[32,4,1,128]{3,0,2,1:T(8,128)S(1)} %get-tuple-element.15), channel_id=1, source_target_pairs={{1,0},{2,1},{3,2},{4,3},{5,4},{6,5},{7,6},{8,7},{9,8},{10,9},{11,1... | collective-permute-start | bytes 196616 | tf_op jit(solution)/shard_map/ppermute | solution.py:45
  115.6 1.7 %fusion.2 = f32[4,8,64,128]{3,1,2,0:T(8,128)S(1)} fusion(f32[32,32]{1,0:T(8,128)S(1)} %copy-done, f32[4,8,64,128]{3,2,1,0:T(8,128)S(1)} %bitcast.136), kind=kOutput, calls=%fused_computation.29 | convolution fusion | flops 100925440 | bytes 2101248 | tf_op jit(solution)/shard_map/dot_general | solution.py:88
  117.5 1.4 %fusion.46 = f32[32,4,16,128]{3,0,2,1:T(8,128)S(1)} fusion(f32[32,4,16,128]{3,0,2,1:T(8,128)S(1)} %fusion.35, f32[32,1,1,128]{3,0,2,1:T(8,128)S(1)} %broadcast.33, f32[32,1,16,128]{3,0,2,1:T(8,128)S(1)} %collective-permute-done.12, f32[32,1,16,128]{3,0,2,1:T(8,128)S(1)} %collective-permute-done.13, f32[32,4,1,128]{3,0,2,1:T(8,128)S(1)} %collective-permute-done.15, ...), kind=kLoop, calls=%fused_computation.74 | loop fusion | flops 6553600 | bytes 4866176 | tf_op jit(solution)/shard_map/add | solution.py:92
  118.9 1.6 %copy.57 = f32[32,4,16,128]{3,2,1,0:T(8,128)} copy(f32[32,4,16,128]{3,0,2,1:T(8,128)S(1)} %fusion.46) | data formatting | bytes 2097152
  (108 shorter events, 15.1 us)
Async XLA Ops:
  0.6 35.5 %copy-start = (f32[32,32]{1,0:T(8,128)S(1)}, f32[32,32]{1,0:T(8,128)}, u32[]{:S(2)}) copy-start(f32[32,32]{1,0:T(8,128)} %param.12) | copy-start | bytes 12292
  4.3 10.9 %copy-start.2 = (f32[32,4,16,128]{3,2,1,0:T(8,128)S(1)}, f32[32,4,16,128]{3,2,1,0:T(8,128)}, u32[]{:S(2)}) copy-start(f32[32,4,16,128]{3,2,1,0:T(8,128)} %param.10) | copy-start | bytes 3145732
  5.6 17.5 %copy-start.12 = (s32[1,4,256]{2,1,0:T(4,128)S(1)}, s32[1,4,256]{2,1,0:T(4,128)}, u32[]{:S(2)}) copy-start(s32[1,4,256]{2,1,0:T(4,128)} %param.16) | copy-start | bytes 12292
  5.6 17.5 %copy-start.14 = (s32[1,4,256]{2,1,0:T(4,128)S(1)}, s32[1,4,256]{2,1,0:T(4,128)}, u32[]{:S(2)}) copy-start(s32[1,4,256]{2,1,0:T(4,128)} %param.17) | copy-start | bytes 12292
  5.8 30.1 %collective-permute-start = (f32[649,128]{1,0:T(8,128)S(1)}, f32[649,128]{1,0:T(8,128)S(1)}, u32[]{:S(2)}, u32[]{:S(2)}) collective-permute-start(f32[649,128]{1,0:T(8,128)S(1)} %get-tuple-element.44), channel_id=1, source_target_pairs={{16,0},{32,16},{48,32},{64,48},{80,64},{96,80},{112,96},{128,112},... | collective-permute-start | bytes 996872 | tf_op jit(solution)/shard_map/ppermute | solution.py:206
  9.0 26.9 %collective-permute-start.1 = (f32[649,128]{1,0:T(8,128)S(1)}, f32[649,128]{1,0:T(8,128)S(1)}, u32[]{:S(2)}, u32[]{:S(2)}) collective-permute-start(f32[649,128]{1,0:T(8,128)S(1)} %get-tuple-element.43), channel_id=1, source_target_pairs={{0,16},{16,32},{32,48},{48,64},{64,80},{80,96},{96,112},{112,128},... | collective-permute-start | bytes 996872 | tf_op jit(solution)/shard_map/ppermute | solution.py:205
  15.4 20.4 %collective-permute-start.3 = (f32[163,128]{1,0:T(8,128)S(1)}, f32[163,128]{1,0:T(8,128)S(1)}, u32[]{:S(2)}, u32[]{:S(2)}) collective-permute-start(f32[163,128]{1,0:T(8,128)S(1)} %pad_maximum_fusion.42), channel_id=1, source_target_pairs={{0,1},{1,2},{2,3},{3,4},{4,5},{5,6},{6,7},{7,8},{8,9},{9,10},{10,1... | collective-permute-start | bytes 250376 | tf_op jit(solution)/shard_map/ppermute | solution.py:205
  17.4 18.5 %collective-permute-start.2 = (f32[163,128]{1,0:T(8,128)S(1)}, f32[163,128]{1,0:T(8,128)S(1)}, u32[]{:S(2)}, u32[]{:S(2)}) collective-permute-start(f32[163,128]{1,0:T(8,128)S(1)} %pad_maximum_fusion.41), channel_id=1, source_target_pairs={{1,0},{2,1},{3,2},{4,3},{5,4},{6,5},{7,6},{8,7},{9,8},{10,9},{11,1... | collective-permute-start | bytes 250376 | tf_op jit(solution)/shard_map/ppermute | solution.py:206
  26.0 1.2 copy-start.10
  29.5 6.6 %copy-start.13 = (f32[32]{0:T(128)S(1)}, f32[32]{0:T(128)}, u32[]{:S(2)}) copy-start(f32[32]{0:T(128)} %param.11) | copy-start | bytes 388
  35.8 1.5 %copy-start.1 = (f32[4,16,32,128]{3,2,1,0:T(8,128)S(1)}, f32[4,16,32,128]{3,2,1,0:T(8,128)}, u32[]{:S(2)}) copy-start(f32[4,16,32,128]{3,2,1,0:T(8,128)} %shard_map.121) | copy-start | bytes 3145732
  35.8 7.0 %copy-start.8 = (f32[163,128]{1,0:T(8,128)}, f32[163,128]{1,0:T(8,128)S(1)}, u32[]{:S(2)}) copy-start(f32[163,128]{1,0:T(8,128)S(1)} %collective-permute-done.3.side_below) | copy-start | bytes 250372
  35.9 7.0 %copy-start.9 = (f32[163,128]{1,0:T(8,128)}, f32[163,128]{1,0:T(8,128)S(1)}, u32[]{:S(2)}) copy-start(f32[163,128]{1,0:T(8,128)S(1)} %collective-permute-done.2.side_above) | copy-start | bytes 250372
  35.9 7.0 %copy-start.4 = (f32[649,128]{1,0:T(8,128)}, f32[649,128]{1,0:T(8,128)S(1)}, u32[]{:S(2)}) copy-start(f32[649,128]{1,0:T(8,128)S(1)} %collective-permute-done.1.x_below) | copy-start | bytes 996868
  35.9 6.9 %copy-start.3 = (f32[649,128]{1,0:T(8,128)}, f32[649,128]{1,0:T(8,128)S(1)}, u32[]{:S(2)}) copy-start(f32[649,128]{1,0:T(8,128)S(1)} %collective-permute-done.x_above) | copy-start | bytes 996868
  37.4 5.5 %copy-start.11 = (f32[3,1,4,256]{3,2,1,0:T(4,128)S(1)}, f32[3,1,4,256]{3,2,1,0:T(4,128)}, u32[]{:S(2)}) copy-start(f32[3,1,4,256]{3,2,1,0:T(4,128)} %param.14) | copy-start | bytes 36868
  43.0 16.0 %collective-permute-start.4 = (f32[222,128]{1,0:T(8,128)S(1)}, f32[222,128]{1,0:T(8,128)S(1)}, u32[]{:S(2)}, u32[]{:S(2)}) collective-permute-start(f32[222,128]{1,0:T(8,128)S(1)} %pad_maximum_fusion.38), channel_id=1, source_target_pairs={{0,1},{1,2},{2,3},{3,4},{4,5},{5,6},{6,7},{7,8},{8,9},{9,10},{10,1... | collective-permute-start | bytes 341000 | tf_op jit(solution)/shard_map/ppermute | solution.py:205
  44.9 14.0 %collective-permute-start.5 = (f32[222,128]{1,0:T(8,128)S(1)}, f32[222,128]{1,0:T(8,128)S(1)}, u32[]{:S(2)}, u32[]{:S(2)}) collective-permute-start(f32[222,128]{1,0:T(8,128)S(1)} %pad_maximum_fusion.39), channel_id=1, source_target_pairs={{1,0},{2,1},{3,2},{4,3},{5,4},{6,5},{7,6},{8,7},{9,8},{10,9},{11,1... | collective-permute-start | bytes 341000 | tf_op jit(solution)/shard_map/ppermute | solution.py:206
  51.4 22.7 %collective-permute-start.7 = (f32[32,1,16,128]{3,0,2,1:T(8,128)}, f32[32,1,16,128]{3,0,2,1:T(8,128)S(1)}, u32[]{:S(2)}, u32[]{:S(2)}) collective-permute-start(f32[32,1,16,128]{3,0,2,1:T(8,128)} %get-tuple-element.24), channel_id=1, source_target_pairs={{0,16},{16,32},{32,48},{48,64},{64,80},{80,96},{96,112},{112,128},... | collective-permute-start | bytes 786440 | tf_op jit(solution)/shard_map/ppermute | solution.py:44
  55.0 19.3 %collective-permute-start.6 = (f32[32,1,16,128]{3,0,2,1:T(8,128)S(1)}, f32[32,1,16,128]{3,0,2,1:T(8,128)S(1)}, u32[]{:S(2)}, u32[]{:S(2)}) collective-permute-start(f32[32,1,16,128]{3,0,2,1:T(8,128)S(1)} %get-tuple-element.23), channel_id=1, source_target_pairs={{16,0},{32,16},{48,32},{64,48},{80,64},{96,80},{112,96},{128,112},... | collective-permute-start | bytes 786440 | tf_op jit(solution)/shard_map/ppermute | solution.py:45
  59.0 0.7 copy-start.7
  72.6 0.9 copy-start.5
  74.2 0.8 slice-start
  74.2 0.9 slice-start.1
  76.3 19.7 %collective-permute-start.8 = (f32[32,1,16,128]{3,0,2,1:T(8,128)S(1)}, f32[32,1,16,128]{3,0,2,1:T(8,128)S(1)}, u32[]{:S(2)}, u32[]{:S(2)}) collective-permute-start(f32[32,1,16,128]{3,0,2,1:T(8,128)S(1)} %get-tuple-element.22), channel_id=1, source_target_pairs={{16,0},{32,16},{48,32},{64,48},{80,64},{96,80},{112,96},{128,112},... | collective-permute-start | bytes 786440 | tf_op jit(solution)/shard_map/ppermute | solution.py:45
  78.2 17.8 %collective-permute-start.9 = (f32[32,1,16,128]{3,0,2,1:T(8,128)S(1)}, f32[32,1,16,128]{3,0,2,1:T(8,128)S(1)}, u32[]{:S(2)}, u32[]{:S(2)}) collective-permute-start(f32[32,1,16,128]{3,0,2,1:T(8,128)S(1)} %get-tuple-element.21), channel_id=1, source_target_pairs={{0,16},{16,32},{32,48},{48,64},{64,80},{80,96},{96,112},{112,128},... | collective-permute-start | bytes 786440 | tf_op jit(solution)/shard_map/ppermute | solution.py:44
  86.4 9.6 %collective-permute-start.11 = (f32[32,4,1,128]{3,0,2,1:T(8,128)S(1)}, f32[32,4,1,128]{3,0,2,1:T(8,128)S(1)}, u32[]{:S(2)}, u32[]{:S(2)}) collective-permute-start(f32[32,4,1,128]{3,0,2,1:T(8,128)S(1)} %get-tuple-element.20), channel_id=1, source_target_pairs={{0,1},{1,2},{2,3},{3,4},{4,5},{5,6},{6,7},{7,8},{8,9},{9,10},{10,1... | collective-permute-start | bytes 196616 | tf_op jit(solution)/shard_map/ppermute | solution.py:44
  88.3 7.7 %collective-permute-start.10 = (f32[32,4,1,128]{3,0,2,1:T(8,128)S(1)}, f32[32,4,1,128]{3,0,2,1:T(8,128)S(1)}, u32[]{:S(2)}, u32[]{:S(2)}) collective-permute-start(f32[32,4,1,128]{3,0,2,1:T(8,128)S(1)} %get-tuple-element.19), channel_id=1, source_target_pairs={{1,0},{2,1},{3,2},{4,3},{5,4},{6,5},{7,6},{8,7},{9,8},{10,9},{11,1... | collective-permute-start | bytes 196616 | tf_op jit(solution)/shard_map/ppermute | solution.py:45
  97.5 19.9 %collective-permute-start.12 = (f32[32,1,16,128]{3,0,2,1:T(8,128)S(1)}, f32[32,1,16,128]{3,0,2,1:T(8,128)S(1)}, u32[]{:S(2)}, u32[]{:S(2)}) collective-permute-start(f32[32,1,16,128]{3,0,2,1:T(8,128)S(1)} %get-tuple-element.18), channel_id=1, source_target_pairs={{16,0},{32,16},{48,32},{64,48},{80,64},{96,80},{112,96},{128,112},... | collective-permute-start | bytes 786440 | tf_op jit(solution)/shard_map/ppermute | solution.py:45
  99.5 18.0 %collective-permute-start.13 = (f32[32,1,16,128]{3,0,2,1:T(8,128)S(1)}, f32[32,1,16,128]{3,0,2,1:T(8,128)S(1)}, u32[]{:S(2)}, u32[]{:S(2)}) collective-permute-start(f32[32,1,16,128]{3,0,2,1:T(8,128)S(1)} %get-tuple-element.17), channel_id=1, source_target_pairs={{0,16},{16,32},{32,48},{48,64},{64,80},{80,96},{96,112},{112,128},... | collective-permute-start | bytes 786440 | tf_op jit(solution)/shard_map/ppermute | solution.py:44
  107.9 9.6 %collective-permute-start.15 = (f32[32,4,1,128]{3,0,2,1:T(8,128)S(1)}, f32[32,4,1,128]{3,0,2,1:T(8,128)S(1)}, u32[]{:S(2)}, u32[]{:S(2)}) collective-permute-start(f32[32,4,1,128]{3,0,2,1:T(8,128)S(1)} %get-tuple-element.16), channel_id=1, source_target_pairs={{0,1},{1,2},{2,3},{3,4},{4,5},{5,6},{6,7},{7,8},{8,9},{9,10},{10,1... | collective-permute-start | bytes 196616 | tf_op jit(solution)/shard_map/ppermute | solution.py:44
  109.8 7.7 %collective-permute-start.14 = (f32[32,4,1,128]{3,0,2,1:T(8,128)S(1)}, f32[32,4,1,128]{3,0,2,1:T(8,128)S(1)}, u32[]{:S(2)}, u32[]{:S(2)}) collective-permute-start(f32[32,4,1,128]{3,0,2,1:T(8,128)S(1)} %get-tuple-element.15), channel_id=1, source_target_pairs={{1,0},{2,1},{3,2},{4,3},{5,4},{6,5},{7,6},{8,7},{9,8},{10,9},{11,1... | collective-permute-start | bytes 196616 | tf_op jit(solution)/shard_map/ppermute | solution.py:45
  (1 other events, 0.6 us)

commit v13 on v12

--- a/solution.py
+++ b/solution.py
@@ -351,11 +351,15 @@
     side_rows = y_low.size // 128
     starts = (field_rows + points.size // 128, side_rows, side_rows + points_low.size // 128)
     rows = points.shape[2]
-    arrived = gather_arrived(x_flats, side_flats, corner_flats, *starts, payload.shape[1:])
     force = pallas_forces(points, bordered, occupancy, None, (-1, 0, 1), True)
-    current, arrived, force = lax.optimization_barrier((current, arrived, force))
+    current, force = lax.optimization_barrier((current, force))
     current = advance(framed(current, x_low, x_high, y_low, y_high), source, rates, mixing)
-    current = substep(current, source, rates, mixing)
+    current, x_flats, side_flats, corner_flats = lax.optimization_barrier((current, x_flats, side_flats, corner_flats))
+
+    def gather():
+        return gather_arrived(x_flats, side_flats, corner_flats, *starts, payload.shape[1:])
+
+    current, arrived = substep_beside(current, source, rates, mixing, gather)
     current = substep(current, source, rates, mixing)
     displacement = force.reshape(3, 1, rows, points.shape[3])
     return (current, displacement, arrived)

time: 123 us -> 119 us (0.967); the launches traced: 121 us -> 118 us
  starting transfers between devices: 66.8 us -> 56.6 us
  waiting for transfers between devices: 0.04 us -> 7.96 us
  local copies, waits for them, and re-layouts: 18.3 us -> 16.9 us
  other arithmetic: 9.16 us -> 10.4 us
    ppermute x5, starting transfers between devices: 19.3 us -> 12.9 us  [halos(): high = lax.ppermute(head, axis, [((i + 1) % count, i) for i in range(ends)])]
    ppermute x5, waiting for transfers between devices: 0.01 us -> 6.09 us  [halos(): low = lax.ppermute(tail, axis, [(i, (i + 1) % count) for i in range(ends)])]
    ppermute x3, starting transfers between devices: 14.6 us -> 12.6 us  [send_pair(): above = lax.ppermute(pack(downward), axis, down)]
    ppermute x5, starting transfers between devices: 22.7 us -> 20.8 us  [halos(): low = lax.ppermute(tail, axis, [(i, (i + 1) % count) for i in range(ends)])]
    ppermute x5, waiting for transfers between devices: 0.01 us -> 1.85 us  [halos(): high = lax.ppermute(head, axis, [((i + 1) % count, i) for i in range(ends)])]
    unnamed x41 -> x49, local copies, waits for them, and re-layouts: 9.76 us -> 8.42 us
  transfers between devices with their start and end apart: 16 -> 16, of which waited for: 0 -> 3; matrix products, arithmetic and copies ran while one was open for 14% -> 15% of each run, Pallas kernels for 12% -> 12%
where the time goes in v13:
time: 119 us; the launch traced here: 118 us
  starting transfers between devices  56.6 us (48%)
  local copies, waits for them, and re-layouts  16.9 us (14%)
  Pallas kernels  14.3 us (12%)
  matrix products  10.5 us (9%)
  other arithmetic  10.4 us (9%)
  waiting for transfers between devices  7.96 us (7%)
  between operations  1.46 us (1%)
    ppermute x5, starting transfers between devices, halos(): low = lax.ppermute(tail, axis, [(i, (i + 1) % count) for i in range(ends)])  20.8 us
    ppermute x5, starting transfers between devices, halos(): high = lax.ppermute(head, axis, [((i + 1) % count, i) for i in range(ends)])  12.9 us
    ppermute x3, starting transfers between devices, send_pair(): above = lax.ppermute(pack(downward), axis, down)  12.6 us
    dot_general x4, matrix products, advance(): jnp.dot(mixing, center.reshape(species, -1), precision=lax.Precision.HIGH...  10.5 us
    ppermute x3, starting transfers between devices, send_pair(): below = lax.ppermute(pack(upward), axis, up)  10.3 us
    unnamed x49, local copies, waits for them, and re-layouts  8.42 us
    pallas_call x1, Pallas kernels, deposit(): pl.pallas_call(deposit_kernel, out_shape=jax.ShapeDtypeStruct((BIN_XY, bi...  6.33 us
    ppermute x5, waiting for transfers between devices, halos(): low = lax.ppermute(tail, axis, [(i, (i + 1) % count) for i in range(ends)])  6.09 us
  transfers between devices with their start and end apart: 16, of which 3 were waited for; matrix products, arithmetic and copies ran while one was open for 15% of the time, Pallas kernels for 12%

profile of v13, /device:TPU:120, one launch (start us, length us, event | category | flops | bytes accessed | tf_op | source)
XLA Modules:
  0.0 118.2 jit_solution(4883862739733038422)
XLA Ops:
  1.4 1.3 %fusion.65 = (f32[4,4,256]{2,1,0:T(4,128)}, f32[4,1,4,256]{3,2,1,0:T(4,128)S(1)}) fusion(f32[1,1,4,256]{3,2,1,0:T(4,128)S(1)} %multiply_bitcast_fusion, f32[3,1,4,256]{3,2,1,0:T(4,128)} %param.14), kind=kLoop, calls=%fused_computation.144 | loop fusion | flops 4096 | bytes 49152 | tf_op jit(solution)/shard_map/squeeze | solution.py:283
  5.8 3.1 %collective-permute-start = (f32[649,128]{1,0:T(8,128)S(1)}, f32[649,128]{1,0:T(8,128)S(1)}, u32[]{:S(2)}, u32[]{:S(2)}) collective-permute-start(f32[649,128]{1,0:T(8,128)S(1)} %get-tuple-element.60), channel_id=1, source_target_pairs={{16,0},{32,16},{48,32},{64,48},{80,64},{96,80},{112,96},{128,112},... | collective-permute-start | bytes 996872 | tf_op jit(solution)/shard_map/ppermute | solution.py:206
  9.0 6.4 %collective-permute-start.1 = (f32[649,128]{1,0:T(8,128)S(1)}, f32[649,128]{1,0:T(8,128)S(1)}, u32[]{:S(2)}, u32[]{:S(2)}) collective-permute-start(f32[649,128]{1,0:T(8,128)S(1)} %get-tuple-element.59), channel_id=1, source_target_pairs={{0,16},{16,32},{32,48},{48,64},{64,80},{80,96},{96,112},{112,128},... | collective-permute-start | bytes 996872 | tf_op jit(solution)/shard_map/ppermute | solution.py:205
  15.6 3.7 %collective-permute-start.2 = (f32[163,128]{1,0:T(8,128)S(1)}, f32[163,128]{1,0:T(8,128)S(1)}, u32[]{:S(2)}, u32[]{:S(2)}) collective-permute-start(f32[163,128]{1,0:T(8,128)S(1)} %pad_maximum_fusion.37), channel_id=1, source_target_pairs={{1,0},{2,1},{3,2},{4,3},{5,4},{6,5},{7,6},{8,7},{9,8},{10,9},{11,1... | collective-permute-start | bytes 250376 | tf_op jit(solution)/shard_map/ppermute | solution.py:206
  19.3 1.9 %collective-permute-start.3 = (f32[163,128]{1,0:T(8,128)S(1)}, f32[163,128]{1,0:T(8,128)S(1)}, u32[]{:S(2)}, u32[]{:S(2)}) collective-permute-start(f32[163,128]{1,0:T(8,128)S(1)} %pad_maximum_fusion.38), channel_id=1, source_target_pairs={{0,1},{1,2},{2,3},{3,4},{4,5},{5,6},{6,7},{7,8},{8,9},{9,10},{10,1... | collective-permute-start | bytes 250376 | tf_op jit(solution)/shard_map/ppermute | solution.py:205
  21.9 1.6 %copy.48 = f32[32,4,16,128]{3,0,2,1:T(8,128)} copy(f32[32,4,16,128]{3,2,1,0:T(8,128)S(1)} %copy-done.2) | data formatting | bytes 2097152 | tf_op args[0]
  24.5 1.4 %copy.51 = f32[16,4,32,16]{3,2,1,0:T(8,128)} copy(f32[16,4,32,16]{2,0,3,1:T(8,128)S(1)} %bitcast.141) | data formatting | bytes 262144 | tf_op jit(solution)/shard_map/transpose | solution.py:132
  27.6 6.3 %shard_map.121 = f32[4,16,32,128]{3,2,1,0:T(8,128)} custom-call(f32[16,128,16]{2,1,0:T(8,128)} %bitcast.138, f32[16,4,16]{2,1,0:T(4,128)} %bitcast.157), custom_call_target="tpu_custom_call" | custom-call | flops 10000000 | bytes 1300000 | tf_op jit(solution)/shard_map/pallas_call | solution.py:135
  35.3 5.5 %fusion.4 = f32[32,4,16,128]{3,0,2,1:T(8,128)S(1)} fusion(f32[32,4,16,128]{3,0,2,1:T(8,128)} %copy.48, f32[32,1,1,128]{3,0,2,1:T(8,128)S(1)} %broadcast.33, f32[32,1,16,128]{3,0,2,1:T(8,128)S(1)} %bitcast.147, f32[32,1,16,128]{3,0,2,1:T(8,128)S(1)} %bitcast.148, f32[32,4,1,128]{3,0,2,1:T(8,128)} %bitcast.159, f32[32,4,1,128]{3,0,2,1:T(8,128)S(1)} %bitcast.158, ...), kind=kOutput, calls=%fused_computation.32 | convolution fusion | flops 107479040 | bytes 4870272 | tf_op jit(solution)/shard_map/dot_general | solution.py:88
  41.5 1.9 %collective-permute-start.4 = (f32[222,128]{1,0:T(8,128)}, f32[222,128]{1,0:T(8,128)S(1)}, u32[]{:S(2)}, u32[]{:S(2)}) collective-permute-start(f32[222,128]{1,0:T(8,128)} %pad_maximum_fusion.34), channel_id=1, source_target_pairs={{0,1},{1,2},{2,3},{3,4},{4,5},{5,6},{6,7},{7,8},{8,9},{9,10},{10,1... | collective-permute-start | bytes 341000 | tf_op jit(solution)/shard_map/ppermute | solution.py:205
  43.5 5.8 %collective-permute-start.5 = (f32[222,128]{1,0:T(8,128)S(1)}, f32[222,128]{1,0:T(8,128)S(1)}, u32[]{:S(2)}, u32[]{:S(2)}) collective-permute-start(f32[222,128]{1,0:T(8,128)S(1)} %pad_maximum_fusion.35), channel_id=1, source_target_pairs={{1,0},{2,1},{3,2},{4,3},{5,4},{6,5},{7,6},{8,7},{9,8},{10,9},{11,1... | collective-permute-start | bytes 341000 | tf_op jit(solution)/shard_map/ppermute | solution.py:206
  49.3 3.3 %collective-permute-start.7 = (f32[32,1,16,128]{3,0,2,1:T(8,128)S(1)}, f32[32,1,16,128]{3,0,2,1:T(8,128)S(1)}, u32[]{:S(2)}, u32[]{:S(2)}) collective-permute-start(f32[32,1,16,128]{3,0,2,1:T(8,128)S(1)} %get-tuple-element.40), channel_id=1, source_target_pairs={{0,16},{16,32},{32,48},{48,64},{64,80},{80,96},{96,112},{112,128},... | collective-permute-start | bytes 786440 | tf_op jit(solution)/shard_map/ppermute | solution.py:44
  52.6 4.2 %collective-permute-start.6 = (f32[32,1,16,128]{3,0,2,1:T(8,128)S(1)}, f32[32,1,16,128]{3,0,2,1:T(8,128)S(1)}, u32[]{:S(2)}, u32[]{:S(2)}) collective-permute-start(f32[32,1,16,128]{3,0,2,1:T(8,128)S(1)} %get-tuple-element.39), channel_id=1, source_target_pairs={{16,0},{32,16},{48,32},{64,48},{80,64},{96,80},{112,96},{128,112},... | collective-permute-start | bytes 786440 | tf_op jit(solution)/shard_map/ppermute | solution.py:45
  58.3 6.1 %shard_map.122 = f32[3,4,256]{2,1,0:T(4,128)} custom-call(f32[4,4,256]{2,1,0:T(4,128)} %get-tuple-element.57.own_ref, f32[4,3,6,256]{3,2,1,0:T(8,128)} %pad_maximum_fusion.36.near_ref, f32[4,256]{1,0:T(4,128)} %get-tuple-element.61.occ_ref, f32[3,40,256]{2,1,0:T(8,128)} %broadcast_in_dim.16.start_ref), custom_call_target="tpu_custom_call" | custom-call | flops 9000000 | bytes 150000 | tf_op jit(solution)/shard_map/pallas_call | solution.py:276
  65.0 1.7 %fusion = f32[4,8,64,128]{3,1,2,0:T(8,128)S(1)} fusion(f32[32,32]{1,0:T(8,128)S(1)} %copy-done, f32[4,8,64,128]{3,2,1,0:T(8,128)S(1)} %bitcast.139), kind=kOutput, calls=%fused_computation.27 | convolution fusion | flops 100925440 | bytes 2101248 | tf_op jit(solution)/shard_map/dot_general | solution.py:88
  67.7 2.1 %fusion.24 = f32[32,4,16,128]{3,0,2,1:T(8,128)S(1)} fusion(f32[32,4,16,128]{3,0,2,1:T(8,128)S(1)} %fusion.4, f32[32,1,1,128]{3,0,2,1:T(8,128)S(1)} %broadcast.33, f32[32,6,16,128]{3,0,2,1:T(8,128)S(1)} %constant_dynamic-update-slice_fusion, f32[32,4,1,128]{3,0,2,1:T(8,128)S(1)} %bitcast.145, f32[32,4,1,128]{3,0,2,1:T(8,128)S(1)} %bitcast.146, ...), kind=kLoop, calls=%fused_computation.52 | loop fusion | flops 5505024 | bytes 6439040 | tf_op jit(solution)/shard_map/add | solution.py:92
  70.7 5.4 %collective-permute-start.9 = (f32[32,1,16,128]{3,0,2,1:T(8,128)}, f32[32,1,16,128]{3,0,2,1:T(8,128)S(1)}, u32[]{:S(2)}, u32[]{:S(2)}) collective-permute-start(f32[32,1,16,128]{3,0,2,1:T(8,128)} %get-tuple-element.38), channel_id=1, source_target_pairs={{0,16},{16,32},{32,48},{48,64},{64,80},{80,96},{96,112},{112,128},... | collective-permute-start | bytes 786440 | tf_op jit(solution)/shard_map/ppermute | solution.py:44
  76.7 1.9 %shard_map.123 = f32[8,35,128]{2,1,0:T(8,128)} custom-call(f32[649,128]{1,0:T(8,128)} %copy-done.4, f32[649,128]{1,0:T(8,128)} %copy-done.3, f32[163,128]{1,0:T(8,128)} %copy-done.10, f32[163,128]{1,0:T(8,128)} %copy-done.9, f32[222,128]{1,0:T(8,128)} %copy-done.7, f32[222,128]{1,0:T(8,128)} %copy-done.8), custom_call_target="tpu_custom_call" | custom-call | bytes 300000 | tf_op jit(solution)/shard_map/pallas_call | solution.py:305
  78.6 1.9 %collective-permute-start.8 = (f32[32,1,16,128]{3,0,2,1:T(8,128)}, f32[32,1,16,128]{3,0,2,1:T(8,128)S(1)}, u32[]{:S(2)}, u32[]{:S(2)}) collective-permute-start(f32[32,1,16,128]{3,0,2,1:T(8,128)} %get-tuple-element.37), channel_id=1, source_target_pairs={{16,0},{32,16},{48,32},{64,48},{80,64},{96,80},{112,96},{128,112},... | collective-permute-start | bytes 786440 | tf_op jit(solution)/shard_map/ppermute | solution.py:45
  81.2 1.7 %fusion.1 = f32[4,8,64,128]{3,1,2,0:T(8,128)S(1)} fusion(f32[32,32]{1,0:T(8,128)S(1)} %copy-done, f32[4,8,64,128]{3,2,1,0:T(8,128)S(1)} %bitcast.140), kind=kOutput, calls=%fused_computation.28 | convolution fusion | flops 100925440 | bytes 2101248 | tf_op jit(solution)/shard_map/dot_general | solution.py:88
  83.7 1.9 %collective-permute-start.10 = (f32[32,4,1,128]{3,0,2,1:T(8,128)S(1)}, f32[32,4,1,128]{3,0,2,1:T(8,128)S(1)}, u32[]{:S(2)}, u32[]{:S(2)}) collective-permute-start(f32[32,4,1,128]{3,0,2,1:T(8,128)S(1)} %copy-done.14), channel_id=1, source_target_pairs={{1,0},{2,1},{3,2},{4,3},{5,4},{6,5},{7,6},{8,7},{9,8},{10,9},{11,1... | collective-permute-start | bytes 196616 | tf_op jit(solution)/shard_map/ppermute | solution.py:45
  85.6 2.4 %collective-permute-start.11 = (f32[32,4,1,128]{3,0,2,1:T(8,128)S(1)}, f32[32,4,1,128]{3,0,2,1:T(8,128)S(1)}, u32[]{:S(2)}, u32[]{:S(2)}) collective-permute-start(f32[32,4,1,128]{3,0,2,1:T(8,128)S(1)} %copy-done.13), channel_id=1, source_target_pairs={{0,1},{1,2},{2,3},{3,4},{4,5},{5,6},{6,7},{7,8},{8,9},{9,10},{10,1... | collective-permute-start | bytes 196616 | tf_op jit(solution)/shard_map/ppermute | solution.py:44
  88.9 1.8 %collective-permute-done.8 = f32[32,1,16,128]{3,0,2,1:T(8,128)S(1)} collective-permute-done((f32[32,1,16,128]{3,0,2,1:T(8,128)}, f32[32,1,16,128]{3,0,2,1:T(8,128)S(1)}, u32[]{:S(2)}, u32[]{:S(2)}) %collective-permute-start.8) | collective-permute-done | bytes 262176 | tf_op jit(solution)/shard_map/ppermute | solution.py:45
  90.7 2.7 %collective-permute-done.11 = f32[32,4,1,128]{3,0,2,1:T(8,128)S(1)} collective-permute-done((f32[32,4,1,128]{3,0,2,1:T(8,128)S(1)}, f32[32,4,1,128]{3,0,2,1:T(8,128)S(1)}, u32[]{:S(2)}, u32[]{:S(2)}) %collective-permute-start.11) | collective-permute-done | bytes 65568 | tf_op jit(solution)/shard_map/ppermute | solution.py:44
  94.6 3.0 %collective-permute-start.12 = (f32[32,1,16,128]{3,0,2,1:T(8,128)S(1)}, f32[32,1,16,128]{3,0,2,1:T(8,128)S(1)}, u32[]{:S(2)}, u32[]{:S(2)}) collective-permute-start(f32[32,1,16,128]{3,0,2,1:T(8,128)S(1)} %get-tuple-element.34), channel_id=1, source_target_pairs={{16,0},{32,16},{48,32},{64,48},{80,64},{96,80},{112,96},{128,112},... | collective-permute-start | bytes 786440 | tf_op jit(solution)/shard_map/ppermute | solution.py:45
  97.6 7.3 %collective-permute-start.13 = (f32[32,1,16,128]{3,0,2,1:T(8,128)S(1)}, f32[32,1,16,128]{3,0,2,1:T(8,128)S(1)}, u32[]{:S(2)}, u32[]{:S(2)}) collective-permute-start(f32[32,1,16,128]{3,0,2,1:T(8,128)S(1)} %get-tuple-element.33), channel_id=1, source_target_pairs={{0,16},{16,32},{32,48},{48,64},{64,80},{80,96},{96,112},{112,128},... | collective-permute-start | bytes 786440 | tf_op jit(solution)/shard_map/ppermute | solution.py:44
  105.6 1.9 %collective-permute-start.14 = (f32[32,4,1,128]{3,0,2,1:T(8,128)S(1)}, f32[32,4,1,128]{3,0,2,1:T(8,128)S(1)}, u32[]{:S(2)}, u32[]{:S(2)}) collective-permute-start(f32[32,4,1,128]{3,0,2,1:T(8,128)S(1)} %get-tuple-element.31), channel_id=1, source_target_pairs={{1,0},{2,1},{3,2},{4,3},{5,4},{6,5},{7,6},{8,7},{9,8},{10,9},{11,1... | collective-permute-start | bytes 196616 | tf_op jit(solution)/shard_map/ppermute | solution.py:45
  107.5 2.4 %collective-permute-start.15 = (f32[32,4,1,128]{3,0,2,1:T(8,128)S(1)}, f32[32,4,1,128]{3,0,2,1:T(8,128)S(1)}, u32[]{:S(2)}, u32[]{:S(2)}) collective-permute-start(f32[32,4,1,128]{3,0,2,1:T(8,128)S(1)} %get-tuple-element.32), channel_id=1, source_target_pairs={{0,1},{1,2},{2,3},{3,4},{4,5},{5,6},{6,7},{7,8},{8,9},{9,10},{10,1... | collective-permute-start | bytes 196616 | tf_op jit(solution)/shard_map/ppermute | solution.py:44
  109.9 1.7 %fusion.2 = f32[4,8,64,128]{3,1,2,0:T(8,128)S(1)} fusion(f32[32,32]{1,0:T(8,128)S(1)} %copy-done, f32[4,8,64,128]{3,2,1,0:T(8,128)S(1)} %bitcast.137), kind=kOutput, calls=%fused_computation.29 | convolution fusion | flops 100925440 | bytes 2101248 | tf_op jit(solution)/shard_map/dot_general | solution.py:88
  111.8 3.4 %collective-permute-done.15 = f32[32,4,1,128]{3,0,2,1:T(8,128)S(1)} collective-permute-done((f32[32,4,1,128]{3,0,2,1:T(8,128)S(1)}, f32[32,4,1,128]{3,0,2,1:T(8,128)S(1)}, u32[]{:S(2)}, u32[]{:S(2)}) %collective-permute-start.15) | collective-permute-done | bytes 65568 | tf_op jit(solution)/shard_map/ppermute | solution.py:44
  115.2 1.4 %fusion.46 = f32[32,4,16,128]{3,0,2,1:T(8,128)S(1)} fusion(f32[32,4,16,128]{3,0,2,1:T(8,128)S(1)} %fusion.35, f32[32,1,1,128]{3,0,2,1:T(8,128)S(1)} %broadcast.33, f32[32,1,16,128]{3,0,2,1:T(8,128)S(1)} %collective-permute-done.12, f32[32,1,16,128]{3,0,2,1:T(8,128)S(1)} %collective-permute-done.13, f32[32,4,1,128]{3,0,2,1:T(8,128)S(1)} %collective-permute-done.15, ...), kind=kLoop, calls=%fused_computation.74 | loop fusion | flops 6553600 | bytes 4866176 | tf_op jit(solution)/shard_map/add | solution.py:92
  116.6 1.6 %copy.65 = f32[32,4,16,128]{3,2,1,0:T(8,128)} copy(f32[32,4,16,128]{3,0,2,1:T(8,128)S(1)} %fusion.46) | data formatting | bytes 2097152
  (117 shorter events, 18.0 us)
Async XLA Ops:
  0.6 34.2 %copy-start = (f32[32,32]{1,0:T(8,128)S(1)}, f32[32,32]{1,0:T(8,128)}, u32[]{:S(2)}) copy-start(f32[32,32]{1,0:T(8,128)} %param.12) | copy-start | bytes 12292
  4.4 11.1 %copy-start.2 = (f32[32,4,16,128]{3,2,1,0:T(8,128)S(1)}, f32[32,4,16,128]{3,2,1,0:T(8,128)}, u32[]{:S(2)}) copy-start(f32[32,4,16,128]{3,2,1,0:T(8,128)} %param.10) | copy-start | bytes 3145732
  5.5 15.7 %copy-start.15 = (s32[1,4,256]{2,1,0:T(4,128)S(1)}, s32[1,4,256]{2,1,0:T(4,128)}, u32[]{:S(2)}) copy-start(s32[1,4,256]{2,1,0:T(4,128)} %param.16) | copy-start | bytes 12292
  5.6 15.7 %copy-start.17 = (s32[1,4,256]{2,1,0:T(4,128)S(1)}, s32[1,4,256]{2,1,0:T(4,128)}, u32[]{:S(2)}) copy-start(s32[1,4,256]{2,1,0:T(4,128)} %param.17) | copy-start | bytes 12292
  5.8 28.8 %collective-permute-start = (f32[649,128]{1,0:T(8,128)S(1)}, f32[649,128]{1,0:T(8,128)S(1)}, u32[]{:S(2)}, u32[]{:S(2)}) collective-permute-start(f32[649,128]{1,0:T(8,128)S(1)} %get-tuple-element.60), channel_id=1, source_target_pairs={{16,0},{32,16},{48,32},{64,48},{80,64},{96,80},{112,96},{128,112},... | collective-permute-start | bytes 996872 | tf_op jit(solution)/shard_map/ppermute | solution.py:206
  9.0 15.3 %copy-start.11 = (f32[32,1,4,256]{3,2,1,0:T(4,128)S(1)}, f32[32,1,4,256]{3,2,1,0:T(4,128)}, u32[]{:S(2)}) copy-start(f32[32,1,4,256]{3,2,1,0:T(4,128)} %param.13) | copy-start | bytes 393220
  9.0 25.7 %collective-permute-start.1 = (f32[649,128]{1,0:T(8,128)S(1)}, f32[649,128]{1,0:T(8,128)S(1)}, u32[]{:S(2)}, u32[]{:S(2)}) collective-permute-start(f32[649,128]{1,0:T(8,128)S(1)} %get-tuple-element.59), channel_id=1, source_target_pairs={{0,16},{16,32},{32,48},{48,64},{64,80},{80,96},{96,112},{112,128},... | collective-permute-start | bytes 996872 | tf_op jit(solution)/shard_map/ppermute | solution.py:205
  15.6 18.4 %collective-permute-start.2 = (f32[163,128]{1,0:T(8,128)S(1)}, f32[163,128]{1,0:T(8,128)S(1)}, u32[]{:S(2)}, u32[]{:S(2)}) collective-permute-start(f32[163,128]{1,0:T(8,128)S(1)} %pad_maximum_fusion.37), channel_id=1, source_target_pairs={{1,0},{2,1},{3,2},{4,3},{5,4},{6,5},{7,6},{8,7},{9,8},{10,9},{11,1... | collective-permute-start | bytes 250376 | tf_op jit(solution)/shard_map/ppermute | solution.py:206
  19.3 14.6 %collective-permute-start.3 = (f32[163,128]{1,0:T(8,128)S(1)}, f32[163,128]{1,0:T(8,128)S(1)}, u32[]{:S(2)}, u32[]{:S(2)}) collective-permute-start(f32[163,128]{1,0:T(8,128)S(1)} %pad_maximum_fusion.38), channel_id=1, source_target_pairs={{0,1},{1,2},{2,3},{3,4},{4,5},{5,6},{6,7},{7,8},{8,9},{9,10},{10,1... | collective-permute-start | bytes 250376 | tf_op jit(solution)/shard_map/ppermute | solution.py:205
  27.6 7.2 %copy-start.16 = (f32[32]{0:T(128)S(1)}, f32[32]{0:T(128)}, u32[]{:S(2)}) copy-start(f32[32]{0:T(128)} %param.11) | copy-start | bytes 388
  33.9 1.3 %copy-start.1 = (f32[4,16,32,128]{3,2,1,0:T(8,128)S(1)}, f32[4,16,32,128]{3,2,1,0:T(8,128)}, u32[]{:S(2)}) copy-start(f32[4,16,32,128]{3,2,1,0:T(8,128)} %shard_map.121) | copy-start | bytes 3145732
  34.6 6.2 %copy-start.3 = (f32[649,128]{1,0:T(8,128)}, f32[649,128]{1,0:T(8,128)S(1)}, u32[]{:S(2)}) copy-start(f32[649,128]{1,0:T(8,128)S(1)} %collective-permute-done.x_above) | copy-start | bytes 996868
  34.6 6.1 %copy-start.4 = (f32[649,128]{1,0:T(8,128)}, f32[649,128]{1,0:T(8,128)S(1)}, u32[]{:S(2)}) copy-start(f32[649,128]{1,0:T(8,128)S(1)} %collective-permute-done.1.x_below) | copy-start | bytes 996868
  35.2 5.6 %copy-start.12 = (f32[3,1,4,256]{3,2,1,0:T(4,128)S(1)}, f32[3,1,4,256]{3,2,1,0:T(4,128)}, u32[]{:S(2)}) copy-start(f32[3,1,4,256]{3,2,1,0:T(4,128)} %param.14) | copy-start | bytes 36868
  41.5 15.3 %collective-permute-start.4 = (f32[222,128]{1,0:T(8,128)}, f32[222,128]{1,0:T(8,128)S(1)}, u32[]{:S(2)}, u32[]{:S(2)}) collective-permute-start(f32[222,128]{1,0:T(8,128)} %pad_maximum_fusion.34), channel_id=1, source_target_pairs={{0,1},{1,2},{2,3},{3,4},{4,5},{5,6},{6,7},{7,8},{8,9},{9,10},{10,1... | collective-permute-start | bytes 341000 | tf_op jit(solution)/shard_map/ppermute | solution.py:205
  43.5 13.4 %collective-permute-start.5 = (f32[222,128]{1,0:T(8,128)S(1)}, f32[222,128]{1,0:T(8,128)S(1)}, u32[]{:S(2)}, u32[]{:S(2)}) collective-permute-start(f32[222,128]{1,0:T(8,128)S(1)} %pad_maximum_fusion.35), channel_id=1, source_target_pairs={{1,0},{2,1},{3,2},{4,3},{5,4},{6,5},{7,6},{8,7},{9,8},{10,9},{11,1... | collective-permute-start | bytes 341000 | tf_op jit(solution)/shard_map/ppermute | solution.py:206
  49.3 17.6 %collective-permute-start.7 = (f32[32,1,16,128]{3,0,2,1:T(8,128)S(1)}, f32[32,1,16,128]{3,0,2,1:T(8,128)S(1)}, u32[]{:S(2)}, u32[]{:S(2)}) collective-permute-start(f32[32,1,16,128]{3,0,2,1:T(8,128)S(1)} %get-tuple-element.40), channel_id=1, source_target_pairs={{0,16},{16,32},{32,48},{48,64},{64,80},{80,96},{96,112},{112,128},... | collective-permute-start | bytes 786440 | tf_op jit(solution)/shard_map/ppermute | solution.py:44
  52.6 14.4 %collective-permute-start.6 = (f32[32,1,16,128]{3,0,2,1:T(8,128)S(1)}, f32[32,1,16,128]{3,0,2,1:T(8,128)S(1)}, u32[]{:S(2)}, u32[]{:S(2)}) collective-permute-start(f32[32,1,16,128]{3,0,2,1:T(8,128)S(1)} %get-tuple-element.39), channel_id=1, source_target_pairs={{16,0},{32,16},{48,32},{64,48},{80,64},{96,80},{112,96},{128,112},... | collective-permute-start | bytes 786440 | tf_op jit(solution)/shard_map/ppermute | solution.py:45
  56.9 10.0 %copy-start.7 = (f32[222,128]{1,0:T(8,128)}, f32[222,128]{1,0:T(8,128)S(1)}, u32[]{:S(2)}) copy-start(f32[222,128]{1,0:T(8,128)S(1)} %collective-permute-done.4.corner_below) | copy-start | bytes 340996
  56.9 10.0 %copy-start.8 = (f32[222,128]{1,0:T(8,128)}, f32[222,128]{1,0:T(8,128)S(1)}, u32[]{:S(2)}) copy-start(f32[222,128]{1,0:T(8,128)S(1)} %collective-permute-done.5.corner_above) | copy-start | bytes 340996
  66.9 0.9 slice-start
  66.9 0.9 slice-start.1
  70.7 18.1 %collective-permute-start.9 = (f32[32,1,16,128]{3,0,2,1:T(8,128)}, f32[32,1,16,128]{3,0,2,1:T(8,128)S(1)}, u32[]{:S(2)}, u32[]{:S(2)}) collective-permute-start(f32[32,1,16,128]{3,0,2,1:T(8,128)} %get-tuple-element.38), channel_id=1, source_target_pairs={{0,16},{16,32},{32,48},{48,64},{64,80},{80,96},{96,112},{112,128},... | collective-permute-start | bytes 786440 | tf_op jit(solution)/shard_map/ppermute | solution.py:44
  78.6 12.1 %collective-permute-start.8 = (f32[32,1,16,128]{3,0,2,1:T(8,128)}, f32[32,1,16,128]{3,0,2,1:T(8,128)S(1)}, u32[]{:S(2)}, u32[]{:S(2)}) collective-permute-start(f32[32,1,16,128]{3,0,2,1:T(8,128)} %get-tuple-element.37), channel_id=1, source_target_pairs={{16,0},{32,16},{48,32},{64,48},{80,64},{96,80},{112,96},{128,112},... | collective-permute-start | bytes 786440 | tf_op jit(solution)/shard_map/ppermute | solution.py:45
  82.9 2.7 %copy-start.13 = (f32[32,4,1,128]{3,0,2,1:T(8,128)S(1)}, f32[32,4,1,128]{3,0,2,1:T(8,128)}, u32[]{:S(2)}) copy-start(f32[32,4,1,128]{3,0,2,1:T(8,128)} %get-tuple-element.36) | copy-start | bytes 196612
  82.9 5.2 %copy-start.6 = (f32[8,35,128]{2,1,0:T(8,128)S(1)}, f32[8,35,128]{2,1,0:T(8,128)}, u32[]{:S(2)}) copy-start(f32[8,35,128]{2,1,0:T(8,128)} %shard_map.123) | copy-start | bytes 430084
  83.7 7.0 %collective-permute-start.10 = (f32[32,4,1,128]{3,0,2,1:T(8,128)S(1)}, f32[32,4,1,128]{3,0,2,1:T(8,128)S(1)}, u32[]{:S(2)}, u32[]{:S(2)}) collective-permute-start(f32[32,4,1,128]{3,0,2,1:T(8,128)S(1)} %copy-done.14), channel_id=1, source_target_pairs={{1,0},{2,1},{3,2},{4,3},{5,4},{6,5},{7,6},{8,7},{9,8},{10,9},{11,1... | collective-permute-start | bytes 196616 | tf_op jit(solution)/shard_map/ppermute | solution.py:45
  85.6 7.8 %collective-permute-start.11 = (f32[32,4,1,128]{3,0,2,1:T(8,128)S(1)}, f32[32,4,1,128]{3,0,2,1:T(8,128)S(1)}, u32[]{:S(2)}, u32[]{:S(2)}) collective-permute-start(f32[32,4,1,128]{3,0,2,1:T(8,128)S(1)} %copy-done.13), channel_id=1, source_target_pairs={{0,1},{1,2},{2,3},{3,4},{4,5},{5,6},{6,7},{7,8},{8,9},{9,10},{10,1... | collective-permute-start | bytes 196616 | tf_op jit(solution)/shard_map/ppermute | solution.py:44
  94.6 20.5 %collective-permute-start.12 = (f32[32,1,16,128]{3,0,2,1:T(8,128)S(1)}, f32[32,1,16,128]{3,0,2,1:T(8,128)S(1)}, u32[]{:S(2)}, u32[]{:S(2)}) collective-permute-start(f32[32,1,16,128]{3,0,2,1:T(8,128)S(1)} %get-tuple-element.34), channel_id=1, source_target_pairs={{16,0},{32,16},{48,32},{64,48},{80,64},{96,80},{112,96},{128,112},... | collective-permute-start | bytes 786440 | tf_op jit(solution)/shard_map/ppermute | solution.py:45
  97.6 17.6 %collective-permute-start.13 = (f32[32,1,16,128]{3,0,2,1:T(8,128)S(1)}, f32[32,1,16,128]{3,0,2,1:T(8,128)S(1)}, u32[]{:S(2)}, u32[]{:S(2)}) collective-permute-start(f32[32,1,16,128]{3,0,2,1:T(8,128)S(1)} %get-tuple-element.33), channel_id=1, source_target_pairs={{0,16},{16,32},{32,48},{48,64},{64,80},{80,96},{96,112},{112,128},... | collective-permute-start | bytes 786440 | tf_op jit(solution)/shard_map/ppermute | solution.py:44
  105.6 6.2 %collective-permute-start.14 = (f32[32,4,1,128]{3,0,2,1:T(8,128)S(1)}, f32[32,4,1,128]{3,0,2,1:T(8,128)S(1)}, u32[]{:S(2)}, u32[]{:S(2)}) collective-permute-start(f32[32,4,1,128]{3,0,2,1:T(8,128)S(1)} %get-tuple-element.31), channel_id=1, source_target_pairs={{1,0},{2,1},{3,2},{4,3},{5,4},{6,5},{7,6},{8,7},{9,8},{10,9},{11,1... | collective-permute-start | bytes 196616 | tf_op jit(solution)/shard_map/ppermute | solution.py:45
  107.5 7.7 %collective-permute-start.15 = (f32[32,4,1,128]{3,0,2,1:T(8,128)S(1)}, f32[32,4,1,128]{3,0,2,1:T(8,128)S(1)}, u32[]{:S(2)}, u32[]{:S(2)}) collective-permute-start(f32[32,4,1,128]{3,0,2,1:T(8,128)S(1)} %get-tuple-element.32), channel_id=1, source_target_pairs={{0,1},{1,2},{2,3},{3,4},{4,5},{5,6},{6,7},{7,8},{8,9},{9,10},{10,1... | collective-permute-start | bytes 196616 | tf_op jit(solution)/shard_map/ppermute | solution.py:44
  (4 other events, 3.1 us)

commit v14 on v13

--- a/solution.py
+++ b/solution.py
@@ -351,8 +351,8 @@
     side_rows = y_low.size // 128
     starts = (field_rows + points.size // 128, side_rows, side_rows + points_low.size // 128)
     rows = points.shape[2]
-    force = pallas_forces(points, bordered, occupancy, None, (-1, 0, 1), True)
-    current, force = lax.optimization_barrier((current, force))
+    partial = pallas_forces(points, bordered, occupancy, None, (-1, 0), False)
+    current, partial = lax.optimization_barrier((current, partial))
     current = advance(framed(current, x_low, x_high, y_low, y_high), source, rates, mixing)
     current, x_flats, side_flats, corner_flats = lax.optimization_barrier((current, x_flats, side_flats, corner_flats))
 
@@ -360,7 +360,12 @@
         return gather_arrived(x_flats, side_flats, corner_flats, *starts, payload.shape[1:])
 
     current, arrived = substep_beside(current, source, rates, mixing, gather)
-    current = substep(current, source, rates, mixing)
+    current, partial = lax.optimization_barrier((current, partial))
+
+    def finish():
+        return pallas_forces(points, bordered, occupancy, partial, (1,), True)
+
+    current, force = substep_beside(current, source, rates, mixing, finish)
     displacement = force.reshape(3, 1, rows, points.shape[3])
     return (current, displacement, arrived)
 

time: 119 us -> 125 us (1.050)
  the two profiles are of different devices: /device:TPU:120 before, /device:TPU:136 now
where the time goes in v14:
time: 125 us; the launch traced here: 124 us
  starting transfers between devices  58.3 us (47%)
  local copies, waits for them, and re-layouts  17 us (14%)
  Pallas kernels  15.9 us (13%)
  matrix products  10.5 us (8%)
  other arithmetic  10.1 us (8%)
  waiting for transfers between devices  10.1 us (8%)
  between operations  1.5 us (1%)
    ppermute x5, starting transfers between devices, halos(): high = lax.ppermute(head, axis, [((i + 1) % count, i) for i in range(ends)])  22.7 us
    ppermute x5, starting transfers between devices, halos(): low = lax.ppermute(tail, axis, [(i, (i + 1) % count) for i in range(ends)])  15.1 us
    ppermute x3, starting transfers between devices, send_pair(): above = lax.ppermute(pack(downward), axis, down)  12.9 us
    dot_general x4, matrix products, advance(): jnp.dot(mixing, center.reshape(species, -1), precision=lax.Precision.HIGH...  10.5 us
    ppermute x5, waiting for transfers between devices, halos(): low = lax.ppermute(tail, axis, [(i, (i + 1) % count) for i in range(ends)])  10.1 us
    unnamed x51, local copies, waits for them, and re-layouts  8.53 us
    pallas_call x2, Pallas kernels, pallas_forces(): pl.pallas_call(functools.partial(forces_kernel, shifts, scale), out_shape...  7.7 us
    ppermute x3, starting transfers between devices, send_pair(): below = lax.ppermute(pack(upward), axis, up)  7.63 us
  transfers between devices with their start and end apart: 16, of which 2 were waited for; matrix products, arithmetic and copies ran while one was open for 14% of the time, Pallas kernels for 13%

profile of v14, /device:TPU:136, one launch (start us, length us, event | category | flops | bytes accessed | tf_op | source)
XLA Modules:
  0.0 123.6 jit_solution(16133458831765596060)
XLA Ops:
  1.4 1.3 %fusion.65 = (f32[4,4,256]{2,1,0:T(4,128)}, f32[4,1,4,256]{3,2,1,0:T(4,128)S(1)}) fusion(f32[1,1,4,256]{3,2,1,0:T(4,128)S(1)} %multiply_bitcast_fusion, f32[3,1,4,256]{3,2,1,0:T(4,128)} %param.14), kind=kLoop, calls=%fused_computation.143 | loop fusion | flops 4096 | bytes 49152 | tf_op jit(solution)/shard_map/squeeze | solution.py:283
  5.8 3.7 %collective-permute-start = (f32[649,128]{1,0:T(8,128)S(1)}, f32[649,128]{1,0:T(8,128)S(1)}, u32[]{:S(2)}, u32[]{:S(2)}) collective-permute-start(f32[649,128]{1,0:T(8,128)S(1)} %get-tuple-element.68), channel_id=1, source_target_pairs={{16,0},{32,16},{48,32},{64,48},{80,64},{96,80},{112,96},{128,112},... | collective-permute-start | bytes 996872 | tf_op jit(solution)/shard_map/ppermute | solution.py:206
  9.6 3.7 %collective-permute-start.1 = (f32[649,128]{1,0:T(8,128)S(1)}, f32[649,128]{1,0:T(8,128)S(1)}, u32[]{:S(2)}, u32[]{:S(2)}) collective-permute-start(f32[649,128]{1,0:T(8,128)S(1)} %get-tuple-element.67), channel_id=1, source_target_pairs={{0,16},{16,32},{32,48},{48,64},{64,80},{80,96},{96,112},{112,128},... | collective-permute-start | bytes 996872 | tf_op jit(solution)/shard_map/ppermute | solution.py:205
  13.5 3.4 %collective-permute-start.2 = (f32[163,128]{1,0:T(8,128)S(1)}, f32[163,128]{1,0:T(8,128)S(1)}, u32[]{:S(2)}, u32[]{:S(2)}) collective-permute-start(f32[163,128]{1,0:T(8,128)S(1)} %pad_maximum_fusion.33), channel_id=1, source_target_pairs={{1,0},{2,1},{3,2},{4,3},{5,4},{6,5},{7,6},{8,7},{9,8},{10,9},{11,1... | collective-permute-start | bytes 250376 | tf_op jit(solution)/shard_map/ppermute | solution.py:206
  16.9 1.9 %collective-permute-start.3 = (f32[163,128]{1,0:T(8,128)S(1)}, f32[163,128]{1,0:T(8,128)S(1)}, u32[]{:S(2)}, u32[]{:S(2)}) collective-permute-start(f32[163,128]{1,0:T(8,128)S(1)} %pad_maximum_fusion.34), channel_id=1, source_target_pairs={{0,1},{1,2},{2,3},{3,4},{4,5},{5,6},{6,7},{7,8},{8,9},{9,10},{10,1... | collective-permute-start | bytes 250376 | tf_op jit(solution)/shard_map/ppermute | solution.py:205
  19.5 1.6 %copy.44 = f32[32,4,16,128]{3,0,2,1:T(8,128)} copy(f32[32,4,16,128]{3,2,1,0:T(8,128)S(1)} %copy-done.2) | data formatting | bytes 2097152 | tf_op args[0]
  22.1 1.4 %copy.47 = f32[16,4,32,16]{3,2,1,0:T(8,128)} copy(f32[16,4,32,16]{2,0,3,1:T(8,128)S(1)} %bitcast.139) | data formatting | bytes 262144 | tf_op jit(solution)/shard_map/transpose | solution.py:132
  24.0 1.2 copy.62
  25.2 6.3 %shard_map.121 = f32[4,16,32,128]{3,2,1,0:T(8,128)} custom-call(f32[16,128,16]{2,1,0:T(8,128)} %bitcast.135, f32[16,4,16]{2,1,0:T(4,128)} %bitcast.151), custom_call_target="tpu_custom_call" | custom-call | flops 10000000 | bytes 1300000 | tf_op jit(solution)/shard_map/pallas_call | solution.py:135
  32.8 5.5 %fusion.4 = f32[32,4,16,128]{3,0,2,1:T(8,128)S(1)} fusion(f32[32,4,16,128]{3,0,2,1:T(8,128)} %copy.44, f32[32,1,1,128]{3,0,2,1:T(8,128)S(1)} %broadcast.33, f32[32,1,16,128]{3,0,2,1:T(8,128)S(1)} %bitcast.145, f32[32,1,16,128]{3,0,2,1:T(8,128)S(1)} %bitcast.146, f32[32,4,1,128]{3,0,2,1:T(8,128)} %bitcast.153, f32[32,4,1,128]{3,0,2,1:T(8,128)S(1)} %bitcast.152, ...), kind=kOutput, calls=%fused_computation.32 | convolution fusion | flops 107479040 | bytes 4870272 | tf_op jit(solution)/shard_map/dot_general | solution.py:88
  39.1 2.0 %collective-permute-start.4 = (f32[222,128]{1,0:T(8,128)}, f32[222,128]{1,0:T(8,128)S(1)}, u32[]{:S(2)}, u32[]{:S(2)}) collective-permute-start(f32[222,128]{1,0:T(8,128)} %pad_maximum_fusion.30), channel_id=1, source_target_pairs={{0,1},{1,2},{2,3},{3,4},{4,5},{5,6},{6,7},{7,8},{8,9},{9,10},{10,1... | collective-permute-start | bytes 341000 | tf_op jit(solution)/shard_map/ppermute | solution.py:205
  41.2 5.7 %collective-permute-start.5 = (f32[222,128]{1,0:T(8,128)S(1)}, f32[222,128]{1,0:T(8,128)S(1)}, u32[]{:S(2)}, u32[]{:S(2)}) collective-permute-start(f32[222,128]{1,0:T(8,128)S(1)} %pad_maximum_fusion.31), channel_id=1, source_target_pairs={{1,0},{2,1},{3,2},{4,3},{5,4},{6,5},{7,6},{8,7},{9,8},{10,9},{11,1... | collective-permute-start | bytes 341000 | tf_op jit(solution)/shard_map/ppermute | solution.py:206
  46.9 5.4 %collective-permute-start.7 = (f32[32,1,16,128]{3,0,2,1:T(8,128)S(1)}, f32[32,1,16,128]{3,0,2,1:T(8,128)S(1)}, u32[]{:S(2)}, u32[]{:S(2)}) collective-permute-start(f32[32,1,16,128]{3,0,2,1:T(8,128)S(1)} %get-tuple-element.48), channel_id=1, source_target_pairs={{0,16},{16,32},{32,48},{48,64},{64,80},{80,96},{96,112},{112,128},... | collective-permute-start | bytes 786440 | tf_op jit(solution)/shard_map/ppermute | solution.py:44
  52.3 4.2 %collective-permute-start.6 = (f32[32,1,16,128]{3,0,2,1:T(8,128)S(1)}, f32[32,1,16,128]{3,0,2,1:T(8,128)S(1)}, u32[]{:S(2)}, u32[]{:S(2)}) collective-permute-start(f32[32,1,16,128]{3,0,2,1:T(8,128)S(1)} %get-tuple-element.47), channel_id=1, source_target_pairs={{16,0},{32,16},{48,32},{64,48},{80,64},{96,80},{112,96},{128,112},... | collective-permute-start | bytes 786440 | tf_op jit(solution)/shard_map/ppermute | solution.py:45
  58.0 4.6 %shard_map.122.start_ref = f32[3,40,256]{2,1,0:T(8,128)} custom-call(f32[4,4,256]{2,1,0:T(4,128)} %get-tuple-element.65.own_ref, f32[4,3,6,256]{3,2,1,0:T(8,128)} %pad_maximum_fusion.32.near_ref, f32[4,256]{1,0:T(4,128)} %get-tuple-element.69.occ_ref, f32[3,40,256]{2,1,0:T(8,128)} %broadcast_in_dim.16.start_ref), custom_call_target="tpu_custom_call" | custom-call | flops 6000000 | bytes 150000 | tf_op jit(solution)/shard_map/pallas_call | solution.py:276
  63.2 1.7 %fusion = f32[4,8,64,128]{3,1,2,0:T(8,128)S(1)} fusion(f32[32,32]{1,0:T(8,128)S(1)} %copy-done, f32[4,8,64,128]{3,2,1,0:T(8,128)S(1)} %bitcast.136), kind=kOutput, calls=%fused_computation.27 | convolution fusion | flops 100925440 | bytes 2101248 | tf_op jit(solution)/shard_map/dot_general | solution.py:88
  66.0 2.1 %fusion.24 = f32[32,4,16,128]{3,0,2,1:T(8,128)S(1)} fusion(f32[32,4,16,128]{3,0,2,1:T(8,128)S(1)} %fusion.4, f32[32,1,1,128]{3,0,2,1:T(8,128)S(1)} %broadcast.33, f32[32,6,16,128]{3,0,2,1:T(8,128)S(1)} %constant_dynamic-update-slice_fusion, f32[32,4,1,128]{3,0,2,1:T(8,128)S(1)} %bitcast.143, f32[32,4,1,128]{3,0,2,1:T(8,128)S(1)} %bitcast.144, ...), kind=kLoop, calls=%fused_computation.52 | loop fusion | flops 5505024 | bytes 6439040 | tf_op jit(solution)/shard_map/add | solution.py:92
  68.9 3.3 %collective-permute-start.9 = (f32[32,1,16,128]{3,0,2,1:T(8,128)}, f32[32,1,16,128]{3,0,2,1:T(8,128)S(1)}, u32[]{:S(2)}, u32[]{:S(2)}) collective-permute-start(f32[32,1,16,128]{3,0,2,1:T(8,128)} %get-tuple-element.46), channel_id=1, source_target_pairs={{0,16},{16,32},{32,48},{48,64},{64,80},{80,96},{96,112},{112,128},... | collective-permute-start | bytes 786440 | tf_op jit(solution)/shard_map/ppermute | solution.py:44
  72.9 1.9 %shard_map.123 = f32[8,35,128]{2,1,0:T(8,128)} custom-call(f32[649,128]{1,0:T(8,128)} %copy-done.4, f32[649,128]{1,0:T(8,128)} %copy-done.3, f32[163,128]{1,0:T(8,128)} %copy-done.10, f32[163,128]{1,0:T(8,128)} %copy-done.9, f32[222,128]{1,0:T(8,128)} %copy-done.7, f32[222,128]{1,0:T(8,128)} %copy-done.8), custom_call_target="tpu_custom_call" | custom-call | bytes 300000 | tf_op jit(solution)/shard_map/pallas_call | solution.py:305
  74.7 6.2 %collective-permute-start.8 = (f32[32,1,16,128]{3,0,2,1:T(8,128)}, f32[32,1,16,128]{3,0,2,1:T(8,128)S(1)}, u32[]{:S(2)}, u32[]{:S(2)}) collective-permute-start(f32[32,1,16,128]{3,0,2,1:T(8,128)} %get-tuple-element.45), channel_id=1, source_target_pairs={{16,0},{32,16},{48,32},{64,48},{80,64},{96,80},{112,96},{128,112},... | collective-permute-start | bytes 786440 | tf_op jit(solution)/shard_map/ppermute | solution.py:45
  81.5 1.7 %fusion.1 = f32[4,8,64,128]{3,1,2,0:T(8,128)S(1)} fusion(f32[32,32]{1,0:T(8,128)S(1)} %copy-done, f32[4,8,64,128]{3,2,1,0:T(8,128)S(1)} %bitcast.137), kind=kOutput, calls=%fused_computation.28 | convolution fusion | flops 100925440 | bytes 2101248 | tf_op jit(solution)/shard_map/dot_general | solution.py:88
  84.1 2.9 %collective-permute-start.10 = (f32[32,4,1,128]{3,0,2,1:T(8,128)S(1)}, f32[32,4,1,128]{3,0,2,1:T(8,128)S(1)}, u32[]{:S(2)}, u32[]{:S(2)}) collective-permute-start(f32[32,4,1,128]{3,0,2,1:T(8,128)S(1)} %copy-done.14), channel_id=1, source_target_pairs={{1,0},{2,1},{3,2},{4,3},{5,4},{6,5},{7,6},{8,7},{9,8},{10,9},{11,1... | collective-permute-start | bytes 196616 | tf_op jit(solution)/shard_map/ppermute | solution.py:45
  86.9 1.9 %collective-permute-start.11 = (f32[32,4,1,128]{3,0,2,1:T(8,128)S(1)}, f32[32,4,1,128]{3,0,2,1:T(8,128)S(1)}, u32[]{:S(2)}, u32[]{:S(2)}) collective-permute-start(f32[32,4,1,128]{3,0,2,1:T(8,128)S(1)} %copy-done.13), channel_id=1, source_target_pairs={{0,1},{1,2},{2,3},{3,4},{4,5},{5,6},{6,7},{7,8},{8,9},{9,10},{10,1... | collective-permute-start | bytes 196616 | tf_op jit(solution)/shard_map/ppermute | solution.py:44
  89.7 5.0 %collective-permute-done.11 = f32[32,4,1,128]{3,0,2,1:T(8,128)S(1)} collective-permute-done((f32[32,4,1,128]{3,0,2,1:T(8,128)S(1)}, f32[32,4,1,128]{3,0,2,1:T(8,128)S(1)}, u32[]{:S(2)}, u32[]{:S(2)}) %collective-permute-start.11) | collective-permute-done | bytes 65568 | tf_op jit(solution)/shard_map/ppermute | solution.py:44
  95.9 2.1 %collective-permute-start.13 = (f32[32,1,16,128]{3,0,2,1:T(8,128)S(1)}, f32[32,1,16,128]{3,0,2,1:T(8,128)S(1)}, u32[]{:S(2)}, u32[]{:S(2)}) collective-permute-start(f32[32,1,16,128]{3,0,2,1:T(8,128)S(1)} %get-tuple-element.42), channel_id=1, source_target_pairs={{0,16},{16,32},{32,48},{48,64},{64,80},{80,96},{96,112},{112,128},... | collective-permute-start | bytes 786440 | tf_op jit(solution)/shard_map/ppermute | solution.py:44
  98.1 3.1 %shard_map.124 = f32[3,4,256]{2,1,0:T(4,128)} custom-call(f32[4,4,256]{2,1,0:T(4,128)} %get-tuple-element.65.own_ref, f32[4,3,6,256]{3,2,1,0:T(8,128)} %pad_maximum_fusion.32.near_ref, f32[4,256]{1,0:T(4,128)} %get-tuple-element.69.occ_ref, f32[3,40,256]{2,1,0:T(8,128)} %shard_map.122.start_ref), custom_call_target="tpu_custom_call" | custom-call | flops 3000000 | bytes 150000 | tf_op jit(solution)/shard_map/pallas_call | solution.py:276
  101.2 7.5 %collective-permute-start.12 = (f32[32,1,16,128]{3,0,2,1:T(8,128)S(1)}, f32[32,1,16,128]{3,0,2,1:T(8,128)S(1)}, u32[]{:S(2)}, u32[]{:S(2)}) collective-permute-start(f32[32,1,16,128]{3,0,2,1:T(8,128)S(1)} %get-tuple-element.41), channel_id=1, source_target_pairs={{16,0},{32,16},{48,32},{64,48},{80,64},{96,80},{112,96},{128,112},... | collective-permute-start | bytes 786440 | tf_op jit(solution)/shard_map/ppermute | solution.py:45
  109.3 1.7 %fusion.2 = f32[4,8,64,128]{3,1,2,0:T(8,128)S(1)} fusion(f32[32,32]{1,0:T(8,128)S(1)} %copy-done, f32[4,8,64,128]{3,2,1,0:T(8,128)S(1)} %bitcast.138), kind=kOutput, calls=%fused_computation.29 | convolution fusion | flops 100925440 | bytes 2101248 | tf_op jit(solution)/shard_map/dot_general | solution.py:88
  111.2 1.9 %collective-permute-start.14 = (f32[32,4,1,128]{3,0,2,1:T(8,128)S(1)}, f32[32,4,1,128]{3,0,2,1:T(8,128)S(1)}, u32[]{:S(2)}, u32[]{:S(2)}) collective-permute-start(f32[32,4,1,128]{3,0,2,1:T(8,128)S(1)} %get-tuple-element.39), channel_id=1, source_target_pairs={{1,0},{2,1},{3,2},{4,3},{5,4},{6,5},{7,6},{8,7},{9,8},{10,9},{11,1... | collective-permute-start | bytes 196616 | tf_op jit(solution)/shard_map/ppermute | solution.py:45
  113.1 2.4 %collective-permute-start.15 = (f32[32,4,1,128]{3,0,2,1:T(8,128)S(1)}, f32[32,4,1,128]{3,0,2,1:T(8,128)S(1)}, u32[]{:S(2)}, u32[]{:S(2)}) collective-permute-start(f32[32,4,1,128]{3,0,2,1:T(8,128)S(1)} %get-tuple-element.40), channel_id=1, source_target_pairs={{0,1},{1,2},{2,3},{3,4},{4,5},{5,6},{6,7},{7,8},{8,9},{9,10},{10,1... | collective-permute-start | bytes 196616 | tf_op jit(solution)/shard_map/ppermute | solution.py:44
  115.7 5.1 %collective-permute-done.15 = f32[32,4,1,128]{3,0,2,1:T(8,128)S(1)} collective-permute-done((f32[32,4,1,128]{3,0,2,1:T(8,128)S(1)}, f32[32,4,1,128]{3,0,2,1:T(8,128)S(1)}, u32[]{:S(2)}, u32[]{:S(2)}) %collective-permute-start.15) | collective-permute-done | bytes 65568 | tf_op jit(solution)/shard_map/ppermute | solution.py:44
  122.0 1.6 %copy.57 = f32[32,4,16,128]{3,2,1,0:T(8,128)} copy(f32[32,4,16,128]{3,0,2,1:T(8,128)S(1)} %fusion.46) | data formatting | bytes 2097152
  (121 shorter events, 18.1 us)
Async XLA Ops:
  0.6 31.8 %copy-start = (f32[32,32]{1,0:T(8,128)S(1)}, f32[32,32]{1,0:T(8,128)}, u32[]{:S(2)}) copy-start(f32[32,32]{1,0:T(8,128)} %param.12) | copy-start | bytes 12292
  4.4 9.0 %copy-start.2 = (f32[32,4,16,128]{3,2,1,0:T(8,128)S(1)}, f32[32,4,16,128]{3,2,1,0:T(8,128)}, u32[]{:S(2)}) copy-start(f32[32,4,16,128]{3,2,1,0:T(8,128)} %param.10) | copy-start | bytes 3145732
  5.5 13.3 %copy-start.15 = (s32[1,4,256]{2,1,0:T(4,128)S(1)}, s32[1,4,256]{2,1,0:T(4,128)}, u32[]{:S(2)}) copy-start(s32[1,4,256]{2,1,0:T(4,128)} %param.16) | copy-start | bytes 12292
  5.6 13.3 %copy-start.17 = (s32[1,4,256]{2,1,0:T(4,128)S(1)}, s32[1,4,256]{2,1,0:T(4,128)}, u32[]{:S(2)}) copy-start(s32[1,4,256]{2,1,0:T(4,128)} %param.17) | copy-start | bytes 12292
  5.8 26.4 %collective-permute-start = (f32[649,128]{1,0:T(8,128)S(1)}, f32[649,128]{1,0:T(8,128)S(1)}, u32[]{:S(2)}, u32[]{:S(2)}) collective-permute-start(f32[649,128]{1,0:T(8,128)S(1)} %get-tuple-element.68), channel_id=1, source_target_pairs={{16,0},{32,16},{48,32},{64,48},{80,64},{96,80},{112,96},{128,112},... | collective-permute-start | bytes 996872 | tf_op jit(solution)/shard_map/ppermute | solution.py:206
  9.6 12.3 %copy-start.11 = (f32[32,1,4,256]{3,2,1,0:T(4,128)S(1)}, f32[32,1,4,256]{3,2,1,0:T(4,128)}, u32[]{:S(2)}) copy-start(f32[32,1,4,256]{3,2,1,0:T(4,128)} %param.13) | copy-start | bytes 393220
  9.6 22.7 %collective-permute-start.1 = (f32[649,128]{1,0:T(8,128)S(1)}, f32[649,128]{1,0:T(8,128)S(1)}, u32[]{:S(2)}, u32[]{:S(2)}) collective-permute-start(f32[649,128]{1,0:T(8,128)S(1)} %get-tuple-element.67), channel_id=1, source_target_pairs={{0,16},{16,32},{32,48},{48,64},{64,80},{80,96},{96,112},{112,128},... | collective-permute-start | bytes 996872 | tf_op jit(solution)/shard_map/ppermute | solution.py:205
  13.5 18.1 %collective-permute-start.2 = (f32[163,128]{1,0:T(8,128)S(1)}, f32[163,128]{1,0:T(8,128)S(1)}, u32[]{:S(2)}, u32[]{:S(2)}) collective-permute-start(f32[163,128]{1,0:T(8,128)S(1)} %pad_maximum_fusion.33), channel_id=1, source_target_pairs={{1,0},{2,1},{3,2},{4,3},{5,4},{6,5},{7,6},{8,7},{9,8},{10,9},{11,1... | collective-permute-start | bytes 250376 | tf_op jit(solution)/shard_map/ppermute | solution.py:206
  16.9 14.6 %collective-permute-start.3 = (f32[163,128]{1,0:T(8,128)S(1)}, f32[163,128]{1,0:T(8,128)S(1)}, u32[]{:S(2)}, u32[]{:S(2)}) collective-permute-start(f32[163,128]{1,0:T(8,128)S(1)} %pad_maximum_fusion.34), channel_id=1, source_target_pairs={{0,1},{1,2},{2,3},{3,4},{4,5},{5,6},{6,7},{7,8},{8,9},{9,10},{10,1... | collective-permute-start | bytes 250376 | tf_op jit(solution)/shard_map/ppermute | solution.py:205
  25.2 7.2 %copy-start.16 = (f32[32]{0:T(128)S(1)}, f32[32]{0:T(128)}, u32[]{:S(2)}) copy-start(f32[32]{0:T(128)} %param.11) | copy-start | bytes 388
  31.5 1.3 %copy-start.1 = (f32[4,16,32,128]{3,2,1,0:T(8,128)S(1)}, f32[4,16,32,128]{3,2,1,0:T(8,128)}, u32[]{:S(2)}) copy-start(f32[4,16,32,128]{3,2,1,0:T(8,128)} %shard_map.121) | copy-start | bytes 3145732
  32.2 6.2 %copy-start.3 = (f32[649,128]{1,0:T(8,128)}, f32[649,128]{1,0:T(8,128)S(1)}, u32[]{:S(2)}) copy-start(f32[649,128]{1,0:T(8,128)S(1)} %collective-permute-done.x_above) | copy-start | bytes 996868
  32.2 6.1 %copy-start.4 = (f32[649,128]{1,0:T(8,128)}, f32[649,128]{1,0:T(8,128)S(1)}, u32[]{:S(2)}) copy-start(f32[649,128]{1,0:T(8,128)S(1)} %collective-permute-done.1.x_below) | copy-start | bytes 996868
  32.8 5.6 %copy-start.12 = (f32[3,1,4,256]{3,2,1,0:T(4,128)S(1)}, f32[3,1,4,256]{3,2,1,0:T(4,128)}, u32[]{:S(2)}) copy-start(f32[3,1,4,256]{3,2,1,0:T(4,128)} %param.14) | copy-start | bytes 36868
  39.1 17.4 %collective-permute-start.4 = (f32[222,128]{1,0:T(8,128)}, f32[222,128]{1,0:T(8,128)S(1)}, u32[]{:S(2)}, u32[]{:S(2)}) collective-permute-start(f32[222,128]{1,0:T(8,128)} %pad_maximum_fusion.30), channel_id=1, source_target_pairs={{0,1},{1,2},{2,3},{3,4},{4,5},{5,6},{6,7},{7,8},{8,9},{9,10},{10,1... | collective-permute-start | bytes 341000 | tf_op jit(solution)/shard_map/ppermute | solution.py:205
  41.2 15.4 %collective-permute-start.5 = (f32[222,128]{1,0:T(8,128)S(1)}, f32[222,128]{1,0:T(8,128)S(1)}, u32[]{:S(2)}, u32[]{:S(2)}) collective-permute-start(f32[222,128]{1,0:T(8,128)S(1)} %pad_maximum_fusion.31), channel_id=1, source_target_pairs={{1,0},{2,1},{3,2},{4,3},{5,4},{6,5},{7,6},{8,7},{9,8},{10,9},{11,1... | collective-permute-start | bytes 341000 | tf_op jit(solution)/shard_map/ppermute | solution.py:206
  46.9 18.2 %collective-permute-start.7 = (f32[32,1,16,128]{3,0,2,1:T(8,128)S(1)}, f32[32,1,16,128]{3,0,2,1:T(8,128)S(1)}, u32[]{:S(2)}, u32[]{:S(2)}) collective-permute-start(f32[32,1,16,128]{3,0,2,1:T(8,128)S(1)} %get-tuple-element.48), channel_id=1, source_target_pairs={{0,16},{16,32},{32,48},{48,64},{64,80},{80,96},{96,112},{112,128},... | collective-permute-start | bytes 786440 | tf_op jit(solution)/shard_map/ppermute | solution.py:44
  52.3 12.9 %collective-permute-start.6 = (f32[32,1,16,128]{3,0,2,1:T(8,128)S(1)}, f32[32,1,16,128]{3,0,2,1:T(8,128)S(1)}, u32[]{:S(2)}, u32[]{:S(2)}) collective-permute-start(f32[32,1,16,128]{3,0,2,1:T(8,128)S(1)} %get-tuple-element.47), channel_id=1, source_target_pairs={{16,0},{32,16},{48,32},{64,48},{80,64},{96,80},{112,96},{128,112},... | collective-permute-start | bytes 786440 | tf_op jit(solution)/shard_map/ppermute | solution.py:45
  56.6 8.5 %copy-start.7 = (f32[222,128]{1,0:T(8,128)}, f32[222,128]{1,0:T(8,128)S(1)}, u32[]{:S(2)}) copy-start(f32[222,128]{1,0:T(8,128)S(1)} %collective-permute-done.4.corner_below) | copy-start | bytes 340996
  56.6 8.5 %copy-start.8 = (f32[222,128]{1,0:T(8,128)}, f32[222,128]{1,0:T(8,128)S(1)}, u32[]{:S(2)}) copy-start(f32[222,128]{1,0:T(8,128)S(1)} %collective-permute-done.5.corner_above) | copy-start | bytes 340996
  65.1 0.9 slice-start
  65.1 0.9 slice-start.1
  68.9 20.6 %collective-permute-start.9 = (f32[32,1,16,128]{3,0,2,1:T(8,128)}, f32[32,1,16,128]{3,0,2,1:T(8,128)S(1)}, u32[]{:S(2)}, u32[]{:S(2)}) collective-permute-start(f32[32,1,16,128]{3,0,2,1:T(8,128)} %get-tuple-element.46), channel_id=1, source_target_pairs={{0,16},{16,32},{32,48},{48,64},{64,80},{80,96},{96,112},{112,128},... | collective-permute-start | bytes 786440 | tf_op jit(solution)/shard_map/ppermute | solution.py:44
  74.7 14.9 %collective-permute-start.8 = (f32[32,1,16,128]{3,0,2,1:T(8,128)}, f32[32,1,16,128]{3,0,2,1:T(8,128)S(1)}, u32[]{:S(2)}, u32[]{:S(2)}) collective-permute-start(f32[32,1,16,128]{3,0,2,1:T(8,128)} %get-tuple-element.45), channel_id=1, source_target_pairs={{16,0},{32,16},{48,32},{64,48},{80,64},{96,80},{112,96},{128,112},... | collective-permute-start | bytes 786440 | tf_op jit(solution)/shard_map/ppermute | solution.py:45
  83.2 3.7 %copy-start.13 = (f32[32,4,1,128]{3,0,2,1:T(8,128)S(1)}, f32[32,4,1,128]{3,0,2,1:T(8,128)}, u32[]{:S(2)}) copy-start(f32[32,4,1,128]{3,0,2,1:T(8,128)} %get-tuple-element.44) | copy-start | bytes 196612
  83.2 5.6 %copy-start.6 = (f32[8,35,128]{2,1,0:T(8,128)S(1)}, f32[8,35,128]{2,1,0:T(8,128)}, u32[]{:S(2)}) copy-start(f32[8,35,128]{2,1,0:T(8,128)} %shard_map.123) | copy-start | bytes 430084
  84.1 5.7 %collective-permute-start.10 = (f32[32,4,1,128]{3,0,2,1:T(8,128)S(1)}, f32[32,4,1,128]{3,0,2,1:T(8,128)S(1)}, u32[]{:S(2)}, u32[]{:S(2)}) collective-permute-start(f32[32,4,1,128]{3,0,2,1:T(8,128)S(1)} %copy-done.14), channel_id=1, source_target_pairs={{1,0},{2,1},{3,2},{4,3},{5,4},{6,5},{7,6},{8,7},{9,8},{10,9},{11,1... | collective-permute-start | bytes 196616 | tf_op jit(solution)/shard_map/ppermute | solution.py:45
  86.9 7.8 %collective-permute-start.11 = (f32[32,4,1,128]{3,0,2,1:T(8,128)S(1)}, f32[32,4,1,128]{3,0,2,1:T(8,128)S(1)}, u32[]{:S(2)}, u32[]{:S(2)}) collective-permute-start(f32[32,4,1,128]{3,0,2,1:T(8,128)S(1)} %copy-done.13), channel_id=1, source_target_pairs={{0,1},{1,2},{2,3},{3,4},{4,5},{5,6},{6,7},{7,8},{8,9},{9,10},{10,1... | collective-permute-start | bytes 196616 | tf_op jit(solution)/shard_map/ppermute | solution.py:44
  95.9 19.6 %collective-permute-start.13 = (f32[32,1,16,128]{3,0,2,1:T(8,128)S(1)}, f32[32,1,16,128]{3,0,2,1:T(8,128)S(1)}, u32[]{:S(2)}, u32[]{:S(2)}) collective-permute-start(f32[32,1,16,128]{3,0,2,1:T(8,128)S(1)} %get-tuple-element.42), channel_id=1, source_target_pairs={{0,16},{16,32},{32,48},{48,64},{64,80},{80,96},{96,112},{112,128},... | collective-permute-start | bytes 786440 | tf_op jit(solution)/shard_map/ppermute | solution.py:44
  101.2 14.5 %collective-permute-start.12 = (f32[32,1,16,128]{3,0,2,1:T(8,128)S(1)}, f32[32,1,16,128]{3,0,2,1:T(8,128)S(1)}, u32[]{:S(2)}, u32[]{:S(2)}) collective-permute-start(f32[32,1,16,128]{3,0,2,1:T(8,128)S(1)} %get-tuple-element.41), channel_id=1, source_target_pairs={{16,0},{32,16},{48,32},{64,48},{80,64},{96,80},{112,96},{128,112},... | collective-permute-start | bytes 786440 | tf_op jit(solution)/shard_map/ppermute | solution.py:45
  111.2 4.5 %collective-permute-start.14 = (f32[32,4,1,128]{3,0,2,1:T(8,128)S(1)}, f32[32,4,1,128]{3,0,2,1:T(8,128)S(1)}, u32[]{:S(2)}, u32[]{:S(2)}) collective-permute-start(f32[32,4,1,128]{3,0,2,1:T(8,128)S(1)} %get-tuple-element.39), channel_id=1, source_target_pairs={{1,0},{2,1},{3,2},{4,3},{5,4},{6,5},{7,6},{8,7},{9,8},{10,9},{11,1... | collective-permute-start | bytes 196616 | tf_op jit(solution)/shard_map/ppermute | solution.py:45
  113.1 7.7 %collective-permute-start.15 = (f32[32,4,1,128]{3,0,2,1:T(8,128)S(1)}, f32[32,4,1,128]{3,0,2,1:T(8,128)S(1)}, u32[]{:S(2)}, u32[]{:S(2)}) collective-permute-start(f32[32,4,1,128]{3,0,2,1:T(8,128)S(1)} %get-tuple-element.40), channel_id=1, source_target_pairs={{0,1},{1,2},{2,3},{3,4},{4,5},{5,6},{6,7},{7,8},{8,9},{9,10},{10,1... | collective-permute-start | bytes 196616 | tf_op jit(solution)/shard_map/ppermute | solution.py:44
  (4 other events, 3.1 us)

commit v15 on v13

--- a/solution.py
+++ b/solution.py
@@ -359,8 +359,8 @@
     def gather():
         return gather_arrived(x_flats, side_flats, corner_flats, *starts, payload.shape[1:])
 
+    current = substep(current, source, rates, mixing)
     current, arrived = substep_beside(current, source, rates, mixing, gather)
-    current = substep(current, source, rates, mixing)
     displacement = force.reshape(3, 1, rows, points.shape[3])
     return (current, displacement, arrived)
 

time: 119 us -> 121 us (1.017)
  the two profiles are of different devices: /device:TPU:120 before, /device:TPU:136 now
where the time goes in v15:
time: 121 us; the launch traced here: 120 us
  starting transfers between devices  57.9 us (48%)
  local copies, waits for them, and re-layouts  17.3 us (14%)
  Pallas kernels  14.3 us (12%)
  other arithmetic  11.1 us (9%)
  matrix products  10.5 us (9%)
  waiting for transfers between devices  7.27 us (6%)
  between operations  1.46 us (1%)
    ppermute x5, starting transfers between devices, halos(): high = lax.ppermute(head, axis, [((i + 1) % count, i) for i in range(ends)])  22.2 us
    ppermute x5, starting transfers between devices, halos(): low = lax.ppermute(tail, axis, [(i, (i + 1) % count) for i in range(ends)])  15.2 us
    ppermute x3, starting transfers between devices, send_pair(): above = lax.ppermute(pack(downward), axis, down)  12.9 us
    dot_general x4, matrix products, advance(): jnp.dot(mixing, center.reshape(species, -1), precision=lax.Precision.HIGH...  10.5 us
    unnamed x47, local copies, waits for them, and re-layouts  7.9 us
    ppermute x3, starting transfers between devices, send_pair(): below = lax.ppermute(pack(upward), axis, up)  7.63 us
    ppermute x5, waiting for transfers between devices, halos(): low = lax.ppermute(tail, axis, [(i, (i + 1) % count) for i in range(ends)])  7.24 us
    pallas_call x1, Pallas kernels, deposit(): pl.pallas_call(deposit_kernel, out_shape=jax.ShapeDtypeStruct((BIN_XY, bi...  6.34 us
  transfers between devices with their start and end apart: 16, of which 2 were waited for; matrix products, arithmetic and copies ran while one was open for 15% of the time, Pallas kernels for 12%

profile of v15, /device:TPU:136, one launch (start us, length us, event | category | flops | bytes accessed | tf_op | source)
XLA Modules:
  0.0 119.9 jit_solution(16850851137202645914)
XLA Ops:
  1.4 1.3 %fusion.65 = (f32[4,4,256]{2,1,0:T(4,128)}, f32[4,1,4,256]{3,2,1,0:T(4,128)S(1)}) fusion(f32[1,1,4,256]{3,2,1,0:T(4,128)S(1)} %multiply_bitcast_fusion, f32[3,1,4,256]{3,2,1,0:T(4,128)} %param.14), kind=kLoop, calls=%fused_computation.143 | loop fusion | flops 4096 | bytes 49152 | tf_op jit(solution)/shard_map/squeeze | solution.py:283
  5.8 3.7 %collective-permute-start = (f32[649,128]{1,0:T(8,128)S(1)}, f32[649,128]{1,0:T(8,128)S(1)}, u32[]{:S(2)}, u32[]{:S(2)}) collective-permute-start(f32[649,128]{1,0:T(8,128)S(1)} %get-tuple-element.60), channel_id=1, source_target_pairs={{16,0},{32,16},{48,32},{64,48},{80,64},{96,80},{112,96},{128,112},... | collective-permute-start | bytes 996872 | tf_op jit(solution)/shard_map/ppermute | solution.py:206
  9.6 3.7 %collective-permute-start.1 = (f32[649,128]{1,0:T(8,128)S(1)}, f32[649,128]{1,0:T(8,128)S(1)}, u32[]{:S(2)}, u32[]{:S(2)}) collective-permute-start(f32[649,128]{1,0:T(8,128)S(1)} %get-tuple-element.59), channel_id=1, source_target_pairs={{0,16},{16,32},{32,48},{48,64},{64,80},{80,96},{96,112},{112,128},... | collective-permute-start | bytes 996872 | tf_op jit(solution)/shard_map/ppermute | solution.py:205
  13.5 3.4 %collective-permute-start.2 = (f32[163,128]{1,0:T(8,128)S(1)}, f32[163,128]{1,0:T(8,128)S(1)}, u32[]{:S(2)}, u32[]{:S(2)}) collective-permute-start(f32[163,128]{1,0:T(8,128)S(1)} %pad_maximum_fusion.33), channel_id=1, source_target_pairs={{1,0},{2,1},{3,2},{4,3},{5,4},{6,5},{7,6},{8,7},{9,8},{10,9},{11,1... | collective-permute-start | bytes 250376 | tf_op jit(solution)/shard_map/ppermute | solution.py:206
  16.9 1.9 %collective-permute-start.3 = (f32[163,128]{1,0:T(8,128)S(1)}, f32[163,128]{1,0:T(8,128)S(1)}, u32[]{:S(2)}, u32[]{:S(2)}) collective-permute-start(f32[163,128]{1,0:T(8,128)S(1)} %pad_maximum_fusion.34), channel_id=1, source_target_pairs={{0,1},{1,2},{2,3},{3,4},{4,5},{5,6},{6,7},{7,8},{8,9},{9,10},{10,1... | collective-permute-start | bytes 250376 | tf_op jit(solution)/shard_map/ppermute | solution.py:205
  19.5 1.6 %copy.48 = f32[32,4,16,128]{3,0,2,1:T(8,128)} copy(f32[32,4,16,128]{3,2,1,0:T(8,128)S(1)} %copy-done.2) | data formatting | bytes 2097152 | tf_op args[0]
  22.1 1.4 %copy.51 = f32[16,4,32,16]{3,2,1,0:T(8,128)} copy(f32[16,4,32,16]{2,0,3,1:T(8,128)S(1)} %bitcast.141) | data formatting | bytes 262144 | tf_op jit(solution)/shard_map/transpose | solution.py:132
  24.0 1.2 copy.70
  25.2 6.3 %shard_map.121 = f32[4,16,32,128]{3,2,1,0:T(8,128)} custom-call(f32[16,128,16]{2,1,0:T(8,128)} %bitcast.137, f32[16,4,16]{2,1,0:T(4,128)} %bitcast.157), custom_call_target="tpu_custom_call" | custom-call | flops 10000000 | bytes 1300000 | tf_op jit(solution)/shard_map/pallas_call | solution.py:135
  32.9 5.5 %fusion.4 = f32[32,4,16,128]{3,0,2,1:T(8,128)S(1)} fusion(f32[32,4,16,128]{3,0,2,1:T(8,128)} %copy.48, f32[32,1,1,128]{3,0,2,1:T(8,128)S(1)} %broadcast.33, f32[32,1,16,128]{3,0,2,1:T(8,128)S(1)} %bitcast.147, f32[32,1,16,128]{3,0,2,1:T(8,128)S(1)} %bitcast.148, f32[32,4,1,128]{3,0,2,1:T(8,128)} %bitcast.159, f32[32,4,1,128]{3,0,2,1:T(8,128)S(1)} %bitcast.158, ...), kind=kOutput, calls=%fused_computation.32 | convolution fusion | flops 107479040 | bytes 4870272 | tf_op jit(solution)/shard_map/dot_general | solution.py:88
  39.2 2.0 %collective-permute-start.4 = (f32[222,128]{1,0:T(8,128)}, f32[222,128]{1,0:T(8,128)S(1)}, u32[]{:S(2)}, u32[]{:S(2)}) collective-permute-start(f32[222,128]{1,0:T(8,128)} %pad_maximum_fusion.30), channel_id=1, source_target_pairs={{0,1},{1,2},{2,3},{3,4},{4,5},{5,6},{6,7},{7,8},{8,9},{9,10},{10,1... | collective-permute-start | bytes 341000 | tf_op jit(solution)/shard_map/ppermute | solution.py:205
  41.2 5.7 %collective-permute-start.5 = (f32[222,128]{1,0:T(8,128)S(1)}, f32[222,128]{1,0:T(8,128)S(1)}, u32[]{:S(2)}, u32[]{:S(2)}) collective-permute-start(f32[222,128]{1,0:T(8,128)S(1)} %pad_maximum_fusion.31), channel_id=1, source_target_pairs={{1,0},{2,1},{3,2},{4,3},{5,4},{6,5},{7,6},{8,7},{9,8},{10,9},{11,1... | collective-permute-start | bytes 341000 | tf_op jit(solution)/shard_map/ppermute | solution.py:206
  46.9 5.4 %collective-permute-start.7 = (f32[32,1,16,128]{3,0,2,1:T(8,128)S(1)}, f32[32,1,16,128]{3,0,2,1:T(8,128)S(1)}, u32[]{:S(2)}, u32[]{:S(2)}) collective-permute-start(f32[32,1,16,128]{3,0,2,1:T(8,128)S(1)} %get-tuple-element.40), channel_id=1, source_target_pairs={{0,16},{16,32},{32,48},{48,64},{64,80},{80,96},{96,112},{112,128},... | collective-permute-start | bytes 786440 | tf_op jit(solution)/shard_map/ppermute | solution.py:44
  52.3 4.2 %collective-permute-start.6 = (f32[32,1,16,128]{3,0,2,1:T(8,128)S(1)}, f32[32,1,16,128]{3,0,2,1:T(8,128)S(1)}, u32[]{:S(2)}, u32[]{:S(2)}) collective-permute-start(f32[32,1,16,128]{3,0,2,1:T(8,128)S(1)} %get-tuple-element.39), channel_id=1, source_target_pairs={{16,0},{32,16},{48,32},{64,48},{80,64},{96,80},{112,96},{128,112},... | collective-permute-start | bytes 786440 | tf_op jit(solution)/shard_map/ppermute | solution.py:45
  58.0 6.1 %shard_map.122 = f32[3,4,256]{2,1,0:T(4,128)} custom-call(f32[4,4,256]{2,1,0:T(4,128)} %get-tuple-element.57.own_ref, f32[4,3,6,256]{3,2,1,0:T(8,128)} %pad_maximum_fusion.32.near_ref, f32[4,256]{1,0:T(4,128)} %get-tuple-element.61.occ_ref, f32[3,40,256]{2,1,0:T(8,128)} %broadcast_in_dim.16.start_ref), custom_call_target="tpu_custom_call" | custom-call | flops 9000000 | bytes 150000 | tf_op jit(solution)/shard_map/pallas_call | solution.py:276
  64.7 1.7 %fusion = f32[4,8,64,128]{3,1,2,0:T(8,128)S(1)} fusion(f32[32,32]{1,0:T(8,128)S(1)} %copy-done, f32[4,8,64,128]{3,2,1,0:T(8,128)S(1)} %bitcast.139), kind=kOutput, calls=%fused_computation.27 | convolution fusion | flops 100925440 | bytes 2101248 | tf_op jit(solution)/shard_map/dot_general | solution.py:88
  67.5 2.1 %fusion.24 = f32[32,4,16,128]{3,0,2,1:T(8,128)S(1)} fusion(f32[32,4,16,128]{3,0,2,1:T(8,128)S(1)} %fusion.4, f32[32,1,1,128]{3,0,2,1:T(8,128)S(1)} %broadcast.33, f32[32,6,16,128]{3,0,2,1:T(8,128)S(1)} %constant_dynamic-update-slice_fusion, f32[32,4,1,128]{3,0,2,1:T(8,128)S(1)} %bitcast.145, f32[32,4,1,128]{3,0,2,1:T(8,128)S(1)} %bitcast.146, ...), kind=kLoop, calls=%fused_computation.52 | loop fusion | flops 5505024 | bytes 6439040 | tf_op jit(solution)/shard_map/add | solution.py:92
  70.4 3.3 %collective-permute-start.9 = (f32[32,1,16,128]{3,0,2,1:T(8,128)}, f32[32,1,16,128]{3,0,2,1:T(8,128)S(1)}, u32[]{:S(2)}, u32[]{:S(2)}) collective-permute-start(f32[32,1,16,128]{3,0,2,1:T(8,128)} %get-tuple-element.38), channel_id=1, source_target_pairs={{0,16},{16,32},{32,48},{48,64},{64,80},{80,96},{96,112},{112,128},... | collective-permute-start | bytes 786440 | tf_op jit(solution)/shard_map/ppermute | solution.py:44
  75.0 6.2 %collective-permute-start.8 = (f32[32,1,16,128]{3,0,2,1:T(8,128)}, f32[32,1,16,128]{3,0,2,1:T(8,128)}, u32[]{:S(2)}, u32[]{:S(2)}) collective-permute-start(f32[32,1,16,128]{3,0,2,1:T(8,128)} %get-tuple-element.37), channel_id=1, source_target_pairs={{16,0},{32,16},{48,32},{64,48},{80,64},{96,80},{112,96},{128,112},... | collective-permute-start | bytes 786440 | tf_op jit(solution)/shard_map/ppermute | solution.py:45
  81.1 1.7 %fusion.1 = f32[4,8,64,128]{3,1,2,0:T(8,128)S(1)} fusion(f32[32,32]{1,0:T(8,128)S(1)} %copy-done, f32[4,8,64,128]{3,2,1,0:T(8,128)S(1)} %bitcast.138), kind=kOutput, calls=%fused_computation.28 | convolution fusion | flops 100925440 | bytes 2101248 | tf_op jit(solution)/shard_map/dot_general | solution.py:88
  83.0 1.9 %collective-permute-start.10 = (f32[32,4,1,128]{3,0,2,1:T(8,128)}, f32[32,4,1,128]{3,0,2,1:T(8,128)S(1)}, u32[]{:S(2)}, u32[]{:S(2)}) collective-permute-start(f32[32,4,1,128]{3,0,2,1:T(8,128)} %get-tuple-element.35), channel_id=1, source_target_pairs={{1,0},{2,1},{3,2},{4,3},{5,4},{6,5},{7,6},{8,7},{9,8},{10,9},{11,1... | collective-permute-start | bytes 196616 | tf_op jit(solution)/shard_map/ppermute | solution.py:45
  85.0 2.4 %collective-permute-start.11 = (f32[32,4,1,128]{3,0,2,1:T(8,128)}, f32[32,4,1,128]{3,0,2,1:T(8,128)}, u32[]{:S(2)}, u32[]{:S(2)}) collective-permute-start(f32[32,4,1,128]{3,0,2,1:T(8,128)} %get-tuple-element.36), channel_id=1, source_target_pairs={{0,1},{1,2},{2,3},{3,4},{4,5},{5,6},{6,7},{7,8},{8,9},{9,10},{10,1... | collective-permute-start | bytes 196616 | tf_op jit(solution)/shard_map/ppermute | solution.py:44
  87.4 1.9 %shard_map.123 = f32[8,35,128]{2,1,0:T(8,128)} custom-call(f32[649,128]{1,0:T(8,128)} %copy-done.4, f32[649,128]{1,0:T(8,128)} %copy-done.3, f32[163,128]{1,0:T(8,128)} %copy-done.10, f32[163,128]{1,0:T(8,128)} %copy-done.9, f32[222,128]{1,0:T(8,128)} %copy-done.7, f32[222,128]{1,0:T(8,128)} %copy-done.8), custom_call_target="tpu_custom_call" | custom-call | bytes 300000 | tf_op jit(solution)/shard_map/pallas_call | solution.py:305
  90.4 2.6 %collective-permute-done.11 = f32[32,4,1,128]{3,0,2,1:T(8,128)} collective-permute-done((f32[32,4,1,128]{3,0,2,1:T(8,128)}, f32[32,4,1,128]{3,0,2,1:T(8,128)}, u32[]{:S(2)}, u32[]{:S(2)}) %collective-permute-start.11) | collective-permute-done | bytes 65568 | tf_op jit(solution)/shard_map/ppermute | solution.py:44
  93.0 2.2 %fusion.35 = f32[32,4,16,128]{3,0,2,1:T(8,128)S(1)} fusion(f32[32,4,16,128]{3,0,2,1:T(8,128)S(1)} %fusion.24, f32[32,1,1,128]{3,0,2,1:T(8,128)S(1)} %broadcast.33, f32[32,6,16,128]{3,0,2,1:T(8,128)S(1)} %constant_dynamic-update-slice_fusion.3, f32[32,4,1,128]{3,0,2,1:T(8,128)} %collective-permute-done.11, f32[32,4,1,128]{3,0,2,1:T(8,128)S(1)} %collective-permute-done.10, ...), kind=kLoop, calls=%fused_computation.63 | loop fusion | flops 5505024 | bytes 6439040 | tf_op jit(solution)/shard_map/add | solution.py:92
  95.2 1.9 %collective-permute-start.13 = (f32[32,1,16,128]{3,0,2,1:T(8,128)S(1)}, f32[32,1,16,128]{3,0,2,1:T(8,128)S(1)}, u32[]{:S(2)}, u32[]{:S(2)}) collective-permute-start(f32[32,1,16,128]{3,0,2,1:T(8,128)S(1)} %get-tuple-element.34), channel_id=1, source_target_pairs={{0,16},{16,32},{32,48},{48,64},{64,80},{80,96},{96,112},{112,128},... | collective-permute-start | bytes 786440 | tf_op jit(solution)/shard_map/ppermute | solution.py:44
  97.1 7.8 %collective-permute-start.12 = (f32[32,1,16,128]{3,0,2,1:T(8,128)S(1)}, f32[32,1,16,128]{3,0,2,1:T(8,128)S(1)}, u32[]{:S(2)}, u32[]{:S(2)}) collective-permute-start(f32[32,1,16,128]{3,0,2,1:T(8,128)S(1)} %get-tuple-element.33), channel_id=1, source_target_pairs={{16,0},{32,16},{48,32},{64,48},{80,64},{96,80},{112,96},{128,112},... | collective-permute-start | bytes 786440 | tf_op jit(solution)/shard_map/ppermute | solution.py:45
  105.5 1.7 %fusion.2 = f32[4,8,64,128]{3,1,2,0:T(8,128)S(1)} fusion(f32[32,32]{1,0:T(8,128)S(1)} %copy-done, f32[4,8,64,128]{3,2,1,0:T(8,128)S(1)} %bitcast.140), kind=kOutput, calls=%fused_computation.29 | convolution fusion | flops 100925440 | bytes 2101248 | tf_op jit(solution)/shard_map/dot_general | solution.py:88
  107.4 2.1 %collective-permute-start.14 = (f32[32,4,1,128]{3,0,2,1:T(8,128)S(1)}, f32[32,4,1,128]{3,0,2,1:T(8,128)S(1)}, u32[]{:S(2)}, u32[]{:S(2)}) collective-permute-start(f32[32,4,1,128]{3,0,2,1:T(8,128)S(1)} %get-tuple-element.31), channel_id=1, source_target_pairs={{1,0},{2,1},{3,2},{4,3},{5,4},{6,5},{7,6},{8,7},{9,8},{10,9},{11,1... | collective-permute-start | bytes 196616 | tf_op jit(solution)/shard_map/ppermute | solution.py:45
  109.5 2.2 %collective-permute-start.15 = (f32[32,4,1,128]{3,0,2,1:T(8,128)S(1)}, f32[32,4,1,128]{3,0,2,1:T(8,128)S(1)}, u32[]{:S(2)}, u32[]{:S(2)}) collective-permute-start(f32[32,4,1,128]{3,0,2,1:T(8,128)S(1)} %get-tuple-element.32), channel_id=1, source_target_pairs={{0,1},{1,2},{2,3},{3,4},{4,5},{5,6},{6,7},{7,8},{8,9},{9,10},{10,1... | collective-permute-start | bytes 196616 | tf_op jit(solution)/shard_map/ppermute | solution.py:44
  112.6 4.7 %collective-permute-done.15 = f32[32,4,1,128]{3,0,2,1:T(8,128)S(1)} collective-permute-done((f32[32,4,1,128]{3,0,2,1:T(8,128)S(1)}, f32[32,4,1,128]{3,0,2,1:T(8,128)S(1)}, u32[]{:S(2)}, u32[]{:S(2)}) %collective-permute-start.15) | collective-permute-done | bytes 65568 | tf_op jit(solution)/shard_map/ppermute | solution.py:44
  118.3 1.6 %copy.65 = f32[32,4,16,128]{3,2,1,0:T(8,128)} copy(f32[32,4,16,128]{3,0,2,1:T(8,128)S(1)} %fusion.46) | data formatting | bytes 2097152
  (116 shorter events, 17.2 us)
Async XLA Ops:
  0.6 31.8 %copy-start = (f32[32,32]{1,0:T(8,128)S(1)}, f32[32,32]{1,0:T(8,128)}, u32[]{:S(2)}) copy-start(f32[32,32]{1,0:T(8,128)} %param.12) | copy-start | bytes 12292
  4.4 9.0 %copy-start.2 = (f32[32,4,16,128]{3,2,1,0:T(8,128)S(1)}, f32[32,4,16,128]{3,2,1,0:T(8,128)}, u32[]{:S(2)}) copy-start(f32[32,4,16,128]{3,2,1,0:T(8,128)} %param.10) | copy-start | bytes 3145732
  5.5 13.3 %copy-start.13 = (s32[1,4,256]{2,1,0:T(4,128)S(1)}, s32[1,4,256]{2,1,0:T(4,128)}, u32[]{:S(2)}) copy-start(s32[1,4,256]{2,1,0:T(4,128)} %param.16) | copy-start | bytes 12292
  5.6 13.3 %copy-start.15 = (s32[1,4,256]{2,1,0:T(4,128)S(1)}, s32[1,4,256]{2,1,0:T(4,128)}, u32[]{:S(2)}) copy-start(s32[1,4,256]{2,1,0:T(4,128)} %param.17) | copy-start | bytes 12292
  5.8 26.4 %collective-permute-start = (f32[649,128]{1,0:T(8,128)S(1)}, f32[649,128]{1,0:T(8,128)S(1)}, u32[]{:S(2)}, u32[]{:S(2)}) collective-permute-start(f32[649,128]{1,0:T(8,128)S(1)} %get-tuple-element.60), channel_id=1, source_target_pairs={{16,0},{32,16},{48,32},{64,48},{80,64},{96,80},{112,96},{128,112},... | collective-permute-start | bytes 996872 | tf_op jit(solution)/shard_map/ppermute | solution.py:206
  9.6 12.3 %copy-start.11 = (f32[32,1,4,256]{3,2,1,0:T(4,128)S(1)}, f32[32,1,4,256]{3,2,1,0:T(4,128)}, u32[]{:S(2)}) copy-start(f32[32,1,4,256]{3,2,1,0:T(4,128)} %param.13) | copy-start | bytes 393220
  9.6 22.7 %collective-permute-start.1 = (f32[649,128]{1,0:T(8,128)S(1)}, f32[649,128]{1,0:T(8,128)S(1)}, u32[]{:S(2)}, u32[]{:S(2)}) collective-permute-start(f32[649,128]{1,0:T(8,128)S(1)} %get-tuple-element.59), channel_id=1, source_target_pairs={{0,16},{16,32},{32,48},{48,64},{64,80},{80,96},{96,112},{112,128},... | collective-permute-start | bytes 996872 | tf_op jit(solution)/shard_map/ppermute | solution.py:205
  13.5 18.1 %collective-permute-start.2 = (f32[163,128]{1,0:T(8,128)S(1)}, f32[163,128]{1,0:T(8,128)S(1)}, u32[]{:S(2)}, u32[]{:S(2)}) collective-permute-start(f32[163,128]{1,0:T(8,128)S(1)} %pad_maximum_fusion.33), channel_id=1, source_target_pairs={{1,0},{2,1},{3,2},{4,3},{5,4},{6,5},{7,6},{8,7},{9,8},{10,9},{11,1... | collective-permute-start | bytes 250376 | tf_op jit(solution)/shard_map/ppermute | solution.py:206
  16.9 14.7 %collective-permute-start.3 = (f32[163,128]{1,0:T(8,128)S(1)}, f32[163,128]{1,0:T(8,128)S(1)}, u32[]{:S(2)}, u32[]{:S(2)}) collective-permute-start(f32[163,128]{1,0:T(8,128)S(1)} %pad_maximum_fusion.34), channel_id=1, source_target_pairs={{0,1},{1,2},{2,3},{3,4},{4,5},{5,6},{6,7},{7,8},{8,9},{9,10},{10,1... | collective-permute-start | bytes 250376 | tf_op jit(solution)/shard_map/ppermute | solution.py:205
  25.2 7.2 %copy-start.14 = (f32[32]{0:T(128)S(1)}, f32[32]{0:T(128)}, u32[]{:S(2)}) copy-start(f32[32]{0:T(128)} %param.11) | copy-start | bytes 388
  31.6 1.3 %copy-start.1 = (f32[4,16,32,128]{3,2,1,0:T(8,128)S(1)}, f32[4,16,32,128]{3,2,1,0:T(8,128)}, u32[]{:S(2)}) copy-start(f32[4,16,32,128]{3,2,1,0:T(8,128)} %shard_map.121) | copy-start | bytes 3145732
  31.6 0.8 copy-start.9
  32.3 6.2 %copy-start.3 = (f32[649,128]{1,0:T(8,128)}, f32[649,128]{1,0:T(8,128)S(1)}, u32[]{:S(2)}) copy-start(f32[649,128]{1,0:T(8,128)S(1)} %collective-permute-done.x_above) | copy-start | bytes 996868
  32.3 6.1 %copy-start.4 = (f32[649,128]{1,0:T(8,128)}, f32[649,128]{1,0:T(8,128)S(1)}, u32[]{:S(2)}) copy-start(f32[649,128]{1,0:T(8,128)S(1)} %collective-permute-done.1.x_below) | copy-start | bytes 996868
  32.9 5.6 %copy-start.12 = (f32[3,1,4,256]{3,2,1,0:T(4,128)S(1)}, f32[3,1,4,256]{3,2,1,0:T(4,128)}, u32[]{:S(2)}) copy-start(f32[3,1,4,256]{3,2,1,0:T(4,128)} %param.14) | copy-start | bytes 36868
  39.2 17.4 %collective-permute-start.4 = (f32[222,128]{1,0:T(8,128)}, f32[222,128]{1,0:T(8,128)S(1)}, u32[]{:S(2)}, u32[]{:S(2)}) collective-permute-start(f32[222,128]{1,0:T(8,128)} %pad_maximum_fusion.30), channel_id=1, source_target_pairs={{0,1},{1,2},{2,3},{3,4},{4,5},{5,6},{6,7},{7,8},{8,9},{9,10},{10,1... | collective-permute-start | bytes 341000 | tf_op jit(solution)/shard_map/ppermute | solution.py:205
  41.2 15.4 %collective-permute-start.5 = (f32[222,128]{1,0:T(8,128)S(1)}, f32[222,128]{1,0:T(8,128)S(1)}, u32[]{:S(2)}, u32[]{:S(2)}) collective-permute-start(f32[222,128]{1,0:T(8,128)S(1)} %pad_maximum_fusion.31), channel_id=1, source_target_pairs={{1,0},{2,1},{3,2},{4,3},{5,4},{6,5},{7,6},{8,7},{9,8},{10,9},{11,1... | collective-permute-start | bytes 341000 | tf_op jit(solution)/shard_map/ppermute | solution.py:206
  46.9 19.7 %collective-permute-start.7 = (f32[32,1,16,128]{3,0,2,1:T(8,128)S(1)}, f32[32,1,16,128]{3,0,2,1:T(8,128)S(1)}, u32[]{:S(2)}, u32[]{:S(2)}) collective-permute-start(f32[32,1,16,128]{3,0,2,1:T(8,128)S(1)} %get-tuple-element.40), channel_id=1, source_target_pairs={{0,16},{16,32},{32,48},{48,64},{64,80},{80,96},{96,112},{112,128},... | collective-permute-start | bytes 786440 | tf_op jit(solution)/shard_map/ppermute | solution.py:44
  52.3 14.4 %collective-permute-start.6 = (f32[32,1,16,128]{3,0,2,1:T(8,128)S(1)}, f32[32,1,16,128]{3,0,2,1:T(8,128)S(1)}, u32[]{:S(2)}, u32[]{:S(2)}) collective-permute-start(f32[32,1,16,128]{3,0,2,1:T(8,128)S(1)} %get-tuple-element.39), channel_id=1, source_target_pairs={{16,0},{32,16},{48,32},{64,48},{80,64},{96,80},{112,96},{128,112},... | collective-permute-start | bytes 786440 | tf_op jit(solution)/shard_map/ppermute | solution.py:45
  56.6 10.0 %copy-start.7 = (f32[222,128]{1,0:T(8,128)}, f32[222,128]{1,0:T(8,128)S(1)}, u32[]{:S(2)}) copy-start(f32[222,128]{1,0:T(8,128)S(1)} %collective-permute-done.4.corner_below) | copy-start | bytes 340996
  56.6 10.0 %copy-start.8 = (f32[222,128]{1,0:T(8,128)}, f32[222,128]{1,0:T(8,128)S(1)}, u32[]{:S(2)}) copy-start(f32[222,128]{1,0:T(8,128)S(1)} %collective-permute-done.5.corner_above) | copy-start | bytes 340996
  66.6 0.9 slice-start
  66.6 0.9 slice-start.1
  70.4 18.9 %collective-permute-start.9 = (f32[32,1,16,128]{3,0,2,1:T(8,128)}, f32[32,1,16,128]{3,0,2,1:T(8,128)S(1)}, u32[]{:S(2)}, u32[]{:S(2)}) collective-permute-start(f32[32,1,16,128]{3,0,2,1:T(8,128)} %get-tuple-element.38), channel_id=1, source_target_pairs={{0,16},{16,32},{32,48},{48,64},{64,80},{80,96},{96,112},{112,128},... | collective-permute-start | bytes 786440 | tf_op jit(solution)/shard_map/ppermute | solution.py:44
  75.0 14.4 %collective-permute-start.8 = (f32[32,1,16,128]{3,0,2,1:T(8,128)}, f32[32,1,16,128]{3,0,2,1:T(8,128)}, u32[]{:S(2)}, u32[]{:S(2)}) collective-permute-start(f32[32,1,16,128]{3,0,2,1:T(8,128)} %get-tuple-element.37), channel_id=1, source_target_pairs={{16,0},{32,16},{48,32},{64,48},{80,64},{96,80},{112,96},{128,112},... | collective-permute-start | bytes 786440 | tf_op jit(solution)/shard_map/ppermute | solution.py:45
  83.0 7.3 %collective-permute-start.10 = (f32[32,4,1,128]{3,0,2,1:T(8,128)}, f32[32,4,1,128]{3,0,2,1:T(8,128)S(1)}, u32[]{:S(2)}, u32[]{:S(2)}) collective-permute-start(f32[32,4,1,128]{3,0,2,1:T(8,128)} %get-tuple-element.35), channel_id=1, source_target_pairs={{1,0},{2,1},{3,2},{4,3},{5,4},{6,5},{7,6},{8,7},{9,8},{10,9},{11,1... | collective-permute-start | bytes 196616 | tf_op jit(solution)/shard_map/ppermute | solution.py:45
  85.0 8.0 %collective-permute-start.11 = (f32[32,4,1,128]{3,0,2,1:T(8,128)}, f32[32,4,1,128]{3,0,2,1:T(8,128)}, u32[]{:S(2)}, u32[]{:S(2)}) collective-permute-start(f32[32,4,1,128]{3,0,2,1:T(8,128)} %get-tuple-element.36), channel_id=1, source_target_pairs={{0,1},{1,2},{2,3},{3,4},{4,5},{5,6},{6,7},{7,8},{8,9},{9,10},{10,1... | collective-permute-start | bytes 196616 | tf_op jit(solution)/shard_map/ppermute | solution.py:44
  95.2 17.3 %collective-permute-start.13 = (f32[32,1,16,128]{3,0,2,1:T(8,128)S(1)}, f32[32,1,16,128]{3,0,2,1:T(8,128)S(1)}, u32[]{:S(2)}, u32[]{:S(2)}) collective-permute-start(f32[32,1,16,128]{3,0,2,1:T(8,128)S(1)} %get-tuple-element.34), channel_id=1, source_target_pairs={{0,16},{16,32},{32,48},{48,64},{64,80},{80,96},{96,112},{112,128},... | collective-permute-start | bytes 786440 | tf_op jit(solution)/shard_map/ppermute | solution.py:44
  97.1 15.4 %collective-permute-start.12 = (f32[32,1,16,128]{3,0,2,1:T(8,128)S(1)}, f32[32,1,16,128]{3,0,2,1:T(8,128)S(1)}, u32[]{:S(2)}, u32[]{:S(2)}) collective-permute-start(f32[32,1,16,128]{3,0,2,1:T(8,128)S(1)} %get-tuple-element.33), channel_id=1, source_target_pairs={{16,0},{32,16},{48,32},{64,48},{80,64},{96,80},{112,96},{128,112},... | collective-permute-start | bytes 786440 | tf_op jit(solution)/shard_map/ppermute | solution.py:45
  107.2 4.6 %copy-start.6 = (f32[8,35,128]{2,1,0:T(8,128)S(1)}, f32[8,35,128]{2,1,0:T(8,128)}, u32[]{:S(2)}) copy-start(f32[8,35,128]{2,1,0:T(8,128)} %shard_map.123) | copy-start | bytes 430084
  107.4 5.2 %collective-permute-start.14 = (f32[32,4,1,128]{3,0,2,1:T(8,128)S(1)}, f32[32,4,1,128]{3,0,2,1:T(8,128)S(1)}, u32[]{:S(2)}, u32[]{:S(2)}) collective-permute-start(f32[32,4,1,128]{3,0,2,1:T(8,128)S(1)} %get-tuple-element.31), channel_id=1, source_target_pairs={{1,0},{2,1},{3,2},{4,3},{5,4},{6,5},{7,6},{8,7},{9,8},{10,9},{11,1... | collective-permute-start | bytes 196616 | tf_op jit(solution)/shard_map/ppermute | solution.py:45
  109.5 7.7 %collective-permute-start.15 = (f32[32,4,1,128]{3,0,2,1:T(8,128)S(1)}, f32[32,4,1,128]{3,0,2,1:T(8,128)S(1)}, u32[]{:S(2)}, u32[]{:S(2)}) collective-permute-start(f32[32,4,1,128]{3,0,2,1:T(8,128)S(1)} %get-tuple-element.32), channel_id=1, source_target_pairs={{0,1},{1,2},{2,3},{3,4},{4,5},{5,6},{6,7},{7,8},{8,9},{9,10},{10,1... | collective-permute-start | bytes 196616 | tf_op jit(solution)/shard_map/ppermute | solution.py:44
  (2 other events, 1.5 us)
